TPU v7x, 32 devices: a whole 2x2x4 slice. The times are simulated.
32 devices in a mesh: depth: 4 (over y, x), lat: 8 (over z, core).
Axes of the slice: x: 2, y: 2, z: 4, core: 2. Of those that a mesh axis runs over, the one named last changes fastest.
Arguments:
- sources: bfloat16 [4, 8, 32, 2048], P('depth', 'lat'), may hold values from -6 to 6
- coupling: float32 [4, 8, 2048], P('depth', 'lat'), may hold values from 0.2 to 0.6
- merge_ops: bfloat16 [4, 8, 2048, 2048], P('depth', 'lat'), may hold values from -1 to 1.5
Outputs:
- solution: bfloat16 [4, 8, 32, 2048], P('depth', 'lat')
All inputs are finite; a program needn't handle non-finite values.
Results may differ from a plain program's by a relative error of at most 0.03.
Values may be sent and summed in bfloat16 or wider, within the bound.
No kernel may reach another device: no remote copies, remote signals or barrier semaphores. Data moves between devices by JAX's collectives and lax.ppermute only.
A program may use at most 64 MiB of HBM per device.

v0:
```python
import jax
import jax.numpy as jnp
from jax import lax
from jax.sharding import PartitionSpec as P

half_root = 0.7071067811865476


def partner_2(block, axis, apart):
    count = lax.axis_size(axis)
    route = []
    for low in range(count):
        high = low | 1 << apart
        if high != low and high < count:
            route += [(low, high), (high, low)]
    return lax.ppermute(block, axis, route)


def shifted(array, axis, by):
    length = lax.axis_size(axis)
    pairs = [(i, i + by) for i in range(length) if 0 <= i + by < length]
    return lax.ppermute(array, axis, pairs)


def haar_pair(values, partner, lat_index, bit_level):
    is_lower = lat_index // 2**bit_level % 2 == 0
    first = values.astype(jnp.float32)
    second = partner.astype(jnp.float32)
    return jnp.where(is_lower, (first + second) * half_root, (second - first) * half_root).astype(
        jnp.bfloat16
    )


def sweep_layer(leaf_data, merge_op):
    lat_count = lax.axis_size("lat")
    lat_index = lax.axis_index("lat")
    levels = lat_count.bit_length() - 1
    values = leaf_data
    for bit_level in range(levels):
        partner = partner_2(values, "lat", bit_level)
        mixed = haar_pair(values, partner, lat_index, bit_level)
        values = jnp.dot(mixed, merge_op, preferred_element_type=jnp.float32).astype(jnp.bfloat16)
    values = lax.dot_general(
        values, merge_op, (((1,), (1,)), ((), ())), preferred_element_type=jnp.float32
    ).astype(jnp.bfloat16)
    for bit_level in range(levels - 1, -1, -1):
        partner = partner_2(values, "lat", bit_level)
        values = haar_pair(values, partner, lat_index, bit_level)
    return values


def on_device(sources, coupling, merge_ops):
    merge_op = merge_ops[0, 0]
    coupling_row = coupling[0, 0]
    depth_index = lax.axis_index("depth")
    depth_count = lax.axis_size("depth")
    shot_rows = sources[0, 0]
    result = jnp.zeros_like(shot_rows)
    incoming = jnp.zeros_like(shot_rows)
    for sweep_step in range(depth_count):
        leaf_data = (
            shot_rows.astype(jnp.float32) + coupling_row * incoming.astype(jnp.float32)
        ).astype(jnp.bfloat16)
        solved = sweep_layer(leaf_data, merge_op)
        result = jnp.where(depth_index == sweep_step, solved, result)
        if sweep_step + 1 < depth_count:
            incoming = shifted(solved, "depth", 1)
    return result[None, None]


def solution(mesh):
    return jax.shard_map(
        on_device,
        mesh=mesh,
        in_specs=(
            P("depth", "lat", None, None),
            P("depth", "lat", None),
            P("depth", "lat", None, None),
        ),
        out_specs=P("depth", "lat", None, None),
        check_vma=False,
    )
```

profile of v0, /device:TPU:7, one launch (start us, length us, event | category | flops | bytes accessed | tf_op | source)
XLA Modules:
  0.0 217.5 jit_solution(15435499478108927040)
XLA Ops:
  0.0 0.7 broadcast_multiply_fusion
  0.7 0.9 fusion.192
  1.6 0.7 collective-permute-start
  2.4 1.0 collective-permute-done
  3.4 4.9 %fusion.32 = bf16[32,2048]{1,0:T(8,128)(2,1)S(1)} fusion(bf16[1,1,2048,2048]{3,2,1,0:T(8,128)(2,1)} %param.5, bf16[32,2048]{1,0:T(8,128)(2,1)S(1)} %collective-permute-done, bf16[32,2048]{1,0:T(8,128)(2,1)S(1)} %fusion.192, pred[]{:T(512)S(6)} %eq.68), kind=kOutput, calls=%fused_computation.32 | convolution fusion | flops 269025280 | bytes 8781825 | tf_op jit(solution)/shard_map/dot_general | solution.py:42
  8.3 1.3 collective-permute-start.1
  9.6 3.4 %collective-permute-done.1 = bf16[32,2048]{1,0:T(8,128)(2,1)S(1)} collective-permute-done((bf16[32,2048]{1,0:T(8,128)(2,1)S(1)}, bf16[32,2048]{1,0:T(8,128)(2,1)S(1)}, u32[]{:S(2)}, u32[]{:S(2)}) %collective-permute-start.1) | collective-permute-done | bytes 131104 | tf_op jit(solution)/shard_map/ppermute | solution.py:16
  13.0 4.9 %fusion.35 = bf16[32,2048]{1,0:T(8,128)(2,1)S(1)} fusion(bf16[1,1,2048,2048]{3,2,1,0:T(8,128)(2,1)} %param.5, bf16[32,2048]{1,0:T(8,128)(2,1)S(1)} %collective-permute-done.1, bf16[32,2048]{1,0:T(8,128)(2,1)S(1)} %fusion.32, pred[]{:T(512)S(6)} %eq.69), kind=kOutput, calls=%fused_computation.33 | convolution fusion | flops 269025280 | bytes 8781825 | tf_op jit(solution)/shard_map/dot_general | solution.py:42
  17.9 2.4 %collective-permute-start.2 = (bf16[32,2048]{1,0:T(8,128)(2,1)S(1)}, bf16[32,2048]{1,0:T(8,128)(2,1)S(1)}, u32[]{:S(2)}, u32[]{:S(2)}) collective-permute-start(bf16[32,2048]{1,0:T(8,128)(2,1)S(1)} %fusion.35), channel_id=1, source_target_pairs={{0,4},{4,0},{1,5},{5,1},{2,6},{6,2},{3,7},{7,3},{8,12},{12,8},{9,1... | collective-permute-start | bytes 393224 | tf_op jit(solution)/shard_map/ppermute | solution.py:16
  20.3 5.8 %collective-permute-done.2 = bf16[32,2048]{1,0:T(8,128)(2,1)S(1)} collective-permute-done((bf16[32,2048]{1,0:T(8,128)(2,1)S(1)}, bf16[32,2048]{1,0:T(8,128)(2,1)S(1)}, u32[]{:S(2)}, u32[]{:S(2)}) %collective-permute-start.2) | collective-permute-done | bytes 131104 | tf_op jit(solution)/shard_map/ppermute | solution.py:16
  26.1 9.8 %fusion.43 = bf16[32,2048]{1,0:T(8,128)(2,1)S(1)} fusion(bf16[1,1,2048,2048]{3,2,1,0:T(8,128)(2,1)} %param.5, bf16[32,2048]{1,0:T(8,128)(2,1)S(1)} %collective-permute-done.2, bf16[32,2048]{1,0:T(8,128)(2,1)S(1)} %fusion.35, pred[]{:T(512)S(6)} %eq.70), kind=kOutput, calls=%fused_computation.35 | convolution fusion | flops 537526272 | bytes 8781825 | tf_op jit(solution)/shard_map/dot_general | solution.py:43
  35.9 0.1 collective-permute-start.3
  36.0 4.7 %collective-permute-done.3 = bf16[32,2048]{1,0:T(8,128)(2,1)S(1)} collective-permute-done((bf16[32,2048]{1,0:T(8,128)(2,1)S(1)}, bf16[32,2048]{1,0:T(8,128)(2,1)S(1)}, u32[]{:S(2)}, u32[]{:S(2)}) %collective-permute-start.3) | collective-permute-done | bytes 131104 | tf_op jit(solution)/shard_map/ppermute | solution.py:16
  40.7 2.9 %collective-permute-start.4 = (bf16[32,2048]{1,0:T(8,128)(2,1)S(1)}, bf16[32,2048]{1,0:T(8,128)(2,1)S(1)}, u32[]{:S(2)}, u32[]{:S(2)}) collective-permute-start(bf16[32,2048]{1,0:T(8,128)(2,1)S(1)} %fusion.110), channel_id=1, source_target_pairs={{0,2},{2,0},{1,3},{3,1},{4,6},{6,4},{5,7},{7,5},{8,10},{10,8},{9,1... | collective-permute-start | bytes 393224 | tf_op jit(solution)/shard_map/ppermute | solution.py:16
  43.6 2.9 %collective-permute-done.4 = bf16[32,2048]{1,0:T(8,128)(2,1)S(1)} collective-permute-done((bf16[32,2048]{1,0:T(8,128)(2,1)S(1)}, bf16[32,2048]{1,0:T(8,128)(2,1)S(1)}, u32[]{:S(2)}, u32[]{:S(2)}) %collective-permute-start.4) | collective-permute-done | bytes 131104 | tf_op jit(solution)/shard_map/ppermute | solution.py:16
  46.6 4.5 %collective-permute-start.5 = (bf16[32,2048]{1,0:T(8,128)(2,1)S(1)}, bf16[32,2048]{1,0:T(8,128)(2,1)S(1)}, u32[]{:S(2)}, u32[]{:S(2)}) collective-permute-start(bf16[32,2048]{1,0:T(8,128)(2,1)S(1)} %fusion.114), channel_id=1, source_target_pairs={{0,1},{1,0},{2,3},{3,2},{4,5},{5,4},{6,7},{7,6},{8,9},{9,8},{10,11... | collective-permute-start | bytes 393224 | tf_op jit(solution)/shard_map/ppermute | solution.py:16
  51.2 1.0 collective-permute-done.5
  52.2 1.7 collective-permute-start.6
  54.0 5.1 %collective-permute-done.6 = bf16[32,2048]{1,0:T(8,128)(2,1)S(1)} collective-permute-done((bf16[32,2048]{1,0:T(8,128)(2,1)S(1)}, bf16[32,2048]{1,0:T(8,128)(2,1)S(1)}, u32[]{:S(2)}, u32[]{:S(2)}) %collective-permute-start.6) | collective-permute-done | bytes 131104 | tf_op jit(solution)/shard_map/ppermute | solution.py:22
  59.1 1.3 collective-permute-start.7
  60.4 1.0 collective-permute-done.7
  61.4 4.9 %fusion.48 = bf16[32,2048]{1,0:T(8,128)(2,1)S(1)} fusion(bf16[1,1,2048,2048]{3,2,1,0:T(8,128)(2,1)} %param.5, bf16[32,2048]{1,0:T(8,128)(2,1)S(1)} %collective-permute-done.7, bf16[32,2048]{1,0:T(8,128)(2,1)S(1)} %fusion.193, pred[]{:T(512)S(6)} %eq.68), kind=kOutput, calls=%fused_computation.36 | convolution fusion | flops 269025280 | bytes 8781825 | tf_op jit(solution)/shard_map/dot_general | solution.py:42
  66.4 4.7 %collective-permute-done.8 = bf16[32,2048]{1,0:T(8,128)(2,1)S(1)} collective-permute-done((bf16[32,2048]{1,0:T(8,128)(2,1)S(1)}, bf16[32,2048]{1,0:T(8,128)(2,1)S(1)}, u32[]{:S(2)}, u32[]{:S(2)}) %collective-permute-start.8) | collective-permute-done | bytes 131104 | tf_op jit(solution)/shard_map/ppermute | solution.py:16
  71.1 1.5 fusion.51
  72.6 9.1 %collective-permute-done.9 = bf16[32,2048]{1,0:T(8,128)(2,1)S(1)} collective-permute-done((bf16[32,2048]{1,0:T(8,128)(2,1)S(1)}, bf16[32,2048]{1,0:T(8,128)(2,1)S(1)}, u32[]{:S(2)}, u32[]{:S(2)}) %collective-permute-start.9) | collective-permute-done | bytes 131104 | tf_op jit(solution)/shard_map/ppermute | solution.py:16
  81.8 9.8 %fusion.59 = bf16[32,2048]{1,0:T(8,128)(2,1)S(1)} fusion(bf16[1,1,2048,2048]{3,2,1,0:T(8,128)(2,1)} %param.5, bf16[32,2048]{1,0:T(8,128)(2,1)S(1)} %collective-permute-done.9, bf16[32,2048]{1,0:T(8,128)(2,1)S(1)} %fusion.51, pred[]{:T(512)S(6)} %eq.70), kind=kOutput, calls=%fused_computation.39 | convolution fusion | flops 537526272 | bytes 8781825 | tf_op jit(solution)/shard_map/dot_general | solution.py:43
  91.6 0.1 collective-permute-start.10
  91.6 7.7 %collective-permute-done.10 = bf16[32,2048]{1,0:T(8,128)(2,1)S(1)} collective-permute-done((bf16[32,2048]{1,0:T(8,128)(2,1)S(1)}, bf16[32,2048]{1,0:T(8,128)(2,1)S(1)}, u32[]{:S(2)}, u32[]{:S(2)}) %collective-permute-start.10) | collective-permute-done | bytes 131104 | tf_op jit(solution)/shard_map/ppermute | solution.py:16
  99.4 0.1 collective-permute-start.11
  99.4 4.6 %collective-permute-done.11 = bf16[32,2048]{1,0:T(8,128)(2,1)S(1)} collective-permute-done((bf16[32,2048]{1,0:T(8,128)(2,1)S(1)}, bf16[32,2048]{1,0:T(8,128)(2,1)S(1)}, u32[]{:S(2)}, u32[]{:S(2)}) %collective-permute-start.11) | collective-permute-done | bytes 131104 | tf_op jit(solution)/shard_map/ppermute | solution.py:16
  104.1 1.4 collective-permute-start.12
  105.5 1.0 collective-permute-done.12
  106.5 1.8 collective-permute-start.13
  108.3 5.1 %collective-permute-done.13 = bf16[32,2048]{1,0:T(8,128)(2,1)S(1)} collective-permute-done((bf16[32,2048]{1,0:T(8,128)(2,1)S(1)}, bf16[32,2048]{1,0:T(8,128)(2,1)S(1)}, u32[]{:S(2)}, u32[]{:S(2)}) %collective-permute-start.13) | collective-permute-done | bytes 131104 | tf_op jit(solution)/shard_map/ppermute | solution.py:22
  113.5 1.3 collective-permute-start.14
  114.7 1.0 collective-permute-done.14
  115.7 4.9 %fusion.64 = bf16[32,2048]{1,0:T(8,128)(2,1)S(1)} fusion(bf16[1,1,2048,2048]{3,2,1,0:T(8,128)(2,1)} %param.5, bf16[32,2048]{1,0:T(8,128)(2,1)S(1)} %collective-permute-done.14, bf16[32,2048]{1,0:T(8,128)(2,1)S(1)} %fusion.194, pred[]{:T(512)S(6)} %eq.68), kind=kOutput, calls=%fused_computation.40 | convolution fusion | flops 269025280 | bytes 8781825 | tf_op jit(solution)/shard_map/dot_general | solution.py:42
  120.7 4.7 %collective-permute-done.15 = bf16[32,2048]{1,0:T(8,128)(2,1)S(1)} collective-permute-done((bf16[32,2048]{1,0:T(8,128)(2,1)S(1)}, bf16[32,2048]{1,0:T(8,128)(2,1)S(1)}, u32[]{:S(2)}, u32[]{:S(2)}) %collective-permute-start.15) | collective-permute-done | bytes 131104 | tf_op jit(solution)/shard_map/ppermute | solution.py:16
  125.4 1.5 fusion.67
  126.9 1.2 collective-permute-start.16
  128.1 7.9 %collective-permute-done.16 = bf16[32,2048]{1,0:T(8,128)(2,1)S(1)} collective-permute-done((bf16[32,2048]{1,0:T(8,128)(2,1)S(1)}, bf16[32,2048]{1,0:T(8,128)(2,1)S(1)}, u32[]{:S(2)}, u32[]{:S(2)}) %collective-permute-start.16) | collective-permute-done | bytes 131104 | tf_op jit(solution)/shard_map/ppermute | solution.py:16
  136.1 9.8 %fusion.75 = bf16[32,2048]{1,0:T(8,128)(2,1)S(1)} fusion(bf16[1,1,2048,2048]{3,2,1,0:T(8,128)(2,1)} %param.5, bf16[32,2048]{1,0:T(8,128)(2,1)S(1)} %collective-permute-done.16, bf16[32,2048]{1,0:T(8,128)(2,1)S(1)} %fusion.67, pred[]{:T(512)S(6)} %eq.70), kind=kOutput, calls=%fused_computation.43 | convolution fusion | flops 537526272 | bytes 8781825 | tf_op jit(solution)/shard_map/dot_general | solution.py:43
  145.9 0.1 collective-permute-start.17
  145.9 8.7 %collective-permute-done.17 = bf16[32,2048]{1,0:T(8,128)(2,1)S(1)} collective-permute-done((bf16[32,2048]{1,0:T(8,128)(2,1)S(1)}, bf16[32,2048]{1,0:T(8,128)(2,1)S(1)}, u32[]{:S(2)}, u32[]{:S(2)}) %collective-permute-start.17) | collective-permute-done | bytes 131104 | tf_op jit(solution)/shard_map/ppermute | solution.py:16
  154.7 0.1 collective-permute-start.18
  154.8 4.6 %collective-permute-done.18 = bf16[32,2048]{1,0:T(8,128)(2,1)S(1)} collective-permute-done((bf16[32,2048]{1,0:T(8,128)(2,1)S(1)}, bf16[32,2048]{1,0:T(8,128)(2,1)S(1)}, u32[]{:S(2)}, u32[]{:S(2)}) %collective-permute-start.18) | collective-permute-done | bytes 131104 | tf_op jit(solution)/shard_map/ppermute | solution.py:16
  159.4 1.4 collective-permute-start.19
  160.8 1.0 collective-permute-done.19
  161.9 1.8 collective-permute-start.20
  163.7 5.9 %collective-permute-done.20 = bf16[32,2048]{1,0:T(8,128)(2,1)S(1)} collective-permute-done((bf16[32,2048]{1,0:T(8,128)(2,1)S(1)}, bf16[32,2048]{1,0:T(8,128)(2,1)S(1)}, u32[]{:S(2)}, u32[]{:S(2)}) %collective-permute-start.20) | collective-permute-done | bytes 131104 | tf_op jit(solution)/shard_map/ppermute | solution.py:22
  169.6 1.0 collective-permute-start.21
  170.6 1.0 collective-permute-done.21
  171.6 4.9 %fusion.80 = bf16[32,2048]{1,0:T(8,128)(2,1)S(1)} fusion(bf16[1,1,2048,2048]{3,2,1,0:T(8,128)(2,1)} %param.5, bf16[32,2048]{1,0:T(8,128)(2,1)S(1)} %collective-permute-done.21, bf16[32,2048]{1,0:T(8,128)(2,1)S(1)} %fusion.195, pred[]{:T(512)S(6)} %eq.68), kind=kOutput, calls=%fused_computation.44 | convolution fusion | flops 269025280 | bytes 8781825 | tf_op jit(solution)/shard_map/dot_general | solution.py:42
  176.6 4.7 %collective-permute-done.22 = bf16[32,2048]{1,0:T(8,128)(2,1)S(1)} collective-permute-done((bf16[32,2048]{1,0:T(8,128)(2,1)S(1)}, bf16[32,2048]{1,0:T(8,128)(2,1)S(1)}, u32[]{:S(2)}, u32[]{:S(2)}) %collective-permute-start.22) | collective-permute-done | bytes 131104 | tf_op jit(solution)/shard_map/ppermute | solution.py:16
  181.3 1.5 fusion.83
  182.8 0.2 collective-permute-start.23
  183.0 8.5 %collective-permute-done.23 = bf16[32,2048]{1,0:T(8,128)(2,1)S(1)} collective-permute-done((bf16[32,2048]{1,0:T(8,128)(2,1)S(1)}, bf16[32,2048]{1,0:T(8,128)(2,1)S(1)}, u32[]{:S(2)}, u32[]{:S(2)}) %collective-permute-start.23) | collective-permute-done | bytes 131104 | tf_op jit(solution)/shard_map/ppermute | solution.py:16
  191.5 9.8 %fusion.91 = bf16[32,2048]{1,0:T(8,128)(2,1)S(1)} fusion(bf16[1,1,2048,2048]{3,2,1,0:T(8,128)(2,1)} %param.5, bf16[32,2048]{1,0:T(8,128)(2,1)S(1)} %collective-permute-done.23, bf16[32,2048]{1,0:T(8,128)(2,1)S(1)} %fusion.83, pred[]{:T(512)S(6)} %eq.70), kind=kOutput, calls=%fused_computation.47 | convolution fusion | flops 537526272 | bytes 8781825 | tf_op jit(solution)/shard_map/dot_general | solution.py:43
  201.4 8.1 %collective-permute-done.24 = bf16[32,2048]{1,0:T(8,128)(2,1)S(1)} collective-permute-done((bf16[32,2048]{1,0:T(8,128)(2,1)S(1)}, bf16[32,2048]{1,0:T(8,128)(2,1)S(1)}, u32[]{:S(2)}, u32[]{:S(2)}) %collective-permute-start.24) | collective-permute-done | bytes 131104 | tf_op jit(solution)/shard_map/ppermute | solution.py:16
  209.6 0.1 collective-permute-start.25
  209.7 4.5 %collective-permute-done.25 = bf16[32,2048]{1,0:T(8,128)(2,1)S(1)} collective-permute-done((bf16[32,2048]{1,0:T(8,128)(2,1)S(1)}, bf16[32,2048]{1,0:T(8,128)(2,1)S(1)}, u32[]{:S(2)}, u32[]{:S(2)}) %collective-permute-start.25) | collective-permute-done | bytes 131104 | tf_op jit(solution)/shard_map/ppermute | solution.py:16
  214.3 1.4 collective-permute-start.26
  215.7 1.0 collective-permute-done.26
  216.7 0.8 fusion.197
  (38 shorter events, 1.2 us)
Async XLA Ops:
  1.6 1.7 collective-permute-start
  8.3 4.7 %collective-permute-start.1 = (bf16[32,2048]{1,0:T(8,128)(2,1)S(1)}, bf16[32,2048]{1,0:T(8,128)(2,1)S(1)}, u32[]{:S(2)}, u32[]{:S(2)}) collective-permute-start(bf16[32,2048]{1,0:T(8,128)(2,1)S(1)} %fusion.32), channel_id=1, source_target_pairs={{0,2},{2,0},{1,3},{3,1},{4,6},{6,4},{5,7},{7,5},{8,10},{10,8},{9,1... | collective-permute-start | bytes 393224 | tf_op jit(solution)/shard_map/ppermute | solution.py:16
  17.9 8.2 %collective-permute-start.2 = (bf16[32,2048]{1,0:T(8,128)(2,1)S(1)}, bf16[32,2048]{1,0:T(8,128)(2,1)S(1)}, u32[]{:S(2)}, u32[]{:S(2)}) collective-permute-start(bf16[32,2048]{1,0:T(8,128)(2,1)S(1)} %fusion.35), channel_id=1, source_target_pairs={{0,4},{4,0},{1,5},{5,1},{2,6},{6,2},{3,7},{7,3},{8,12},{12,8},{9,1... | collective-permute-start | bytes 393224 | tf_op jit(solution)/shard_map/ppermute | solution.py:16
  20.3 38.8 %copy-start = (bf16[1,1,32,2048]{3,2,1,0:T(8,128)(2,1)S(1)}, bf16[1,1,32,2048]{3,2,1,0:T(8,128)(2,1)}, u32[]{:S(2)}) copy-start(bf16[1,1,32,2048]{3,2,1,0:T(8,128)(2,1)} %param.3) | copy-start | bytes 393220
  20.3 38.8 %copy-start.1 = (f32[1,1,2048]{2,1,0:T(1,128)S(1)}, f32[1,1,2048]{2,1,0:T(1,128)}, u32[]{:S(2)}) copy-start(f32[1,1,2048]{2,1,0:T(1,128)} %param.4) | copy-start | bytes 24580
  35.9 4.8 %collective-permute-start.3 = (bf16[32,2048]{1,0:T(8,128)(2,1)S(1)}, bf16[32,2048]{1,0:T(8,128)(2,1)S(1)}, u32[]{:S(2)}, u32[]{:S(2)}) collective-permute-start(bf16[32,2048]{1,0:T(8,128)(2,1)S(1)} %fusion.43), channel_id=1, source_target_pairs={{0,4},{4,0},{1,5},{5,1},{2,6},{6,2},{3,7},{7,3},{8,12},{12,8},{9,1... | collective-permute-start | bytes 393224 | tf_op jit(solution)/shard_map/ppermute | solution.py:16
  40.7 5.8 %collective-permute-start.4 = (bf16[32,2048]{1,0:T(8,128)(2,1)S(1)}, bf16[32,2048]{1,0:T(8,128)(2,1)S(1)}, u32[]{:S(2)}, u32[]{:S(2)}) collective-permute-start(bf16[32,2048]{1,0:T(8,128)(2,1)S(1)} %fusion.110), channel_id=1, source_target_pairs={{0,2},{2,0},{1,3},{3,1},{4,6},{6,4},{5,7},{7,5},{8,10},{10,8},{9,1... | collective-permute-start | bytes 393224 | tf_op jit(solution)/shard_map/ppermute | solution.py:16
  46.6 5.5 %collective-permute-start.5 = (bf16[32,2048]{1,0:T(8,128)(2,1)S(1)}, bf16[32,2048]{1,0:T(8,128)(2,1)S(1)}, u32[]{:S(2)}, u32[]{:S(2)}) collective-permute-start(bf16[32,2048]{1,0:T(8,128)(2,1)S(1)} %fusion.114), channel_id=1, source_target_pairs={{0,1},{1,0},{2,3},{3,2},{4,5},{5,4},{6,7},{7,6},{8,9},{9,8},{10,11... | collective-permute-start | bytes 393224 | tf_op jit(solution)/shard_map/ppermute | solution.py:16
  52.2 18.9 %slice-start = ((s8[8388608]{0:T(1024)(128)(4,1)}), s8[4194304]{0:T(1024)(128)(4,1)S(1)}, s32[]{:S(2)}) async-start(s8[8388608]{0:T(1024)(128)(4,1)} %bitcast.90), calls=%async_computation | async-start | bytes 8388608
  52.2 6.9 %collective-permute-start.6 = (bf16[32,2048]{1,0:T(8,128)(2,1)S(1)}, bf16[32,2048]{1,0:T(8,128)(2,1)S(1)}, u32[]{:S(2)}, u32[]{:S(2)}) collective-permute-start(bf16[32,2048]{1,0:T(8,128)(2,1)S(1)} %fusion.118), channel_id=1, source_target_pairs={{0,8},{8,16},{16,24},{1,9},{9,17},{17,25},{2,10},{10,18},{18,26},{... | collective-permute-start | bytes 393224 | tf_op jit(solution)/shard_map/ppermute | solution.py:22
  59.1 11.9 %slice-start.1 = ((s8[8388608]{0:T(1024)(128)(4,1)}), s8[4194304]{0:T(1024)(128)(4,1)S(1)}, s32[]{:S(2)}) async-start(s8[8388608]{0:T(1024)(128)(4,1)} %bitcast.90), calls=%async_computation.1 | async-start | bytes 8388608
  59.1 2.3 %collective-permute-start.7 = (bf16[32,2048]{1,0:T(8,128)(2,1)S(1)}, bf16[32,2048]{1,0:T(8,128)(2,1)S(1)}, u32[]{:S(2)}, u32[]{:S(2)}) collective-permute-start(bf16[32,2048]{1,0:T(8,128)(2,1)S(1)} %fusion.193), channel_id=1, source_target_pairs={{0,1},{1,0},{2,3},{3,2},{4,5},{5,4},{6,7},{7,6},{8,9},{9,8},{10,11... | collective-permute-start | bytes 393224 | tf_op jit(solution)/shard_map/ppermute | solution.py:16
  66.3 4.7 %collective-permute-start.8 = (bf16[32,2048]{1,0:T(8,128)(2,1)S(1)}, bf16[32,2048]{1,0:T(8,128)(2,1)S(1)}, u32[]{:S(2)}, u32[]{:S(2)}) collective-permute-start(bf16[32,2048]{1,0:T(8,128)(2,1)S(1)} %fusion.48), channel_id=1, source_target_pairs={{0,2},{2,0},{1,3},{3,1},{4,6},{6,4},{5,7},{7,5},{8,10},{10,8},{9,1... | collective-permute-start | bytes 393224 | tf_op jit(solution)/shard_map/ppermute | solution.py:16
  72.6 9.1 %collective-permute-start.9 = (bf16[32,2048]{1,0:T(8,128)(2,1)S(1)}, bf16[32,2048]{1,0:T(8,128)(2,1)S(1)}, u32[]{:S(2)}, u32[]{:S(2)}) collective-permute-start(bf16[32,2048]{1,0:T(8,128)(2,1)S(1)} %fusion.51), channel_id=1, source_target_pairs={{0,4},{4,0},{1,5},{5,1},{2,6},{6,2},{3,7},{7,3},{8,12},{12,8},{9,1... | collective-permute-start | bytes 393224 | tf_op jit(solution)/shard_map/ppermute | solution.py:16
  91.6 7.7 %collective-permute-start.10 = (bf16[32,2048]{1,0:T(8,128)(2,1)S(1)}, bf16[32,2048]{1,0:T(8,128)(2,1)S(1)}, u32[]{:S(2)}, u32[]{:S(2)}) collective-permute-start(bf16[32,2048]{1,0:T(8,128)(2,1)S(1)} %fusion.59), channel_id=1, source_target_pairs={{0,4},{4,0},{1,5},{5,1},{2,6},{6,2},{3,7},{7,3},{8,12},{12,8},{9,1... | collective-permute-start | bytes 393224 | tf_op jit(solution)/shard_map/ppermute | solution.py:16
  99.4 4.6 %collective-permute-start.11 = (bf16[32,2048]{1,0:T(8,128)(2,1)S(1)}, bf16[32,2048]{1,0:T(8,128)(2,1)S(1)}, u32[]{:S(2)}, u32[]{:S(2)}) collective-permute-start(bf16[32,2048]{1,0:T(8,128)(2,1)S(1)} %fusion.134), channel_id=1, source_target_pairs={{0,2},{2,0},{1,3},{3,1},{4,6},{6,4},{5,7},{7,5},{8,10},{10,8},{9,1... | collective-permute-start | bytes 393224 | tf_op jit(solution)/shard_map/ppermute | solution.py:16
  104.1 2.4 %collective-permute-start.12 = (bf16[32,2048]{1,0:T(8,128)(2,1)S(1)}, bf16[32,2048]{1,0:T(8,128)(2,1)S(1)}, u32[]{:S(2)}, u32[]{:S(2)}) collective-permute-start(bf16[32,2048]{1,0:T(8,128)(2,1)S(1)} %fusion.138), channel_id=1, source_target_pairs={{0,1},{1,0},{2,3},{3,2},{4,5},{5,4},{6,7},{7,6},{8,9},{9,8},{10,11... | collective-permute-start | bytes 393224 | tf_op jit(solution)/shard_map/ppermute | solution.py:16
  106.5 18.9 %slice-start.2 = ((s8[8388608]{0:T(1024)(128)(4,1)}), s8[4194304]{0:T(1024)(128)(4,1)S(1)}, s32[]{:S(2)}) async-start(s8[8388608]{0:T(1024)(128)(4,1)} %bitcast.92), calls=%async_computation.2 | async-start | bytes 8388608
  106.5 6.9 %collective-permute-start.13 = (bf16[32,2048]{1,0:T(8,128)(2,1)S(1)}, bf16[32,2048]{1,0:T(8,128)(2,1)S(1)}, u32[]{:S(2)}, u32[]{:S(2)}) collective-permute-start(bf16[32,2048]{1,0:T(8,128)(2,1)S(1)} %fusion.142), channel_id=1, source_target_pairs={{0,8},{8,16},{16,24},{1,9},{9,17},{17,25},{2,10},{10,18},{18,26},{... | collective-permute-start | bytes 393224 | tf_op jit(solution)/shard_map/ppermute | solution.py:22
  113.4 11.9 %slice-start.3 = ((s8[8388608]{0:T(1024)(128)(4,1)}), s8[4194304]{0:T(1024)(128)(4,1)S(1)}, s32[]{:S(2)}) async-start(s8[8388608]{0:T(1024)(128)(4,1)} %bitcast.92), calls=%async_computation.3 | async-start | bytes 8388608
  113.5 2.3 %collective-permute-start.14 = (bf16[32,2048]{1,0:T(8,128)(2,1)S(1)}, bf16[32,2048]{1,0:T(8,128)(2,1)S(1)}, u32[]{:S(2)}, u32[]{:S(2)}) collective-permute-start(bf16[32,2048]{1,0:T(8,128)(2,1)S(1)} %fusion.194), channel_id=1, source_target_pairs={{0,1},{1,0},{2,3},{3,2},{4,5},{5,4},{6,7},{7,6},{8,9},{9,8},{10,11... | collective-permute-start | bytes 393224 | tf_op jit(solution)/shard_map/ppermute | solution.py:16
  120.6 4.7 %collective-permute-start.15 = (bf16[32,2048]{1,0:T(8,128)(2,1)S(1)}, bf16[32,2048]{1,0:T(8,128)(2,1)S(1)}, u32[]{:S(2)}, u32[]{:S(2)}) collective-permute-start(bf16[32,2048]{1,0:T(8,128)(2,1)S(1)} %fusion.64), channel_id=1, source_target_pairs={{0,2},{2,0},{1,3},{3,1},{4,6},{6,4},{5,7},{7,5},{8,10},{10,8},{9,1... | collective-permute-start | bytes 393224 | tf_op jit(solution)/shard_map/ppermute | solution.py:16
  126.9 9.1 %collective-permute-start.16 = (bf16[32,2048]{1,0:T(8,128)(2,1)S(1)}, bf16[32,2048]{1,0:T(8,128)(2,1)S(1)}, u32[]{:S(2)}, u32[]{:S(2)}) collective-permute-start(bf16[32,2048]{1,0:T(8,128)(2,1)S(1)} %fusion.67), channel_id=1, source_target_pairs={{0,4},{4,0},{1,5},{5,1},{2,6},{6,2},{3,7},{7,3},{8,12},{12,8},{9,1... | collective-permute-start | bytes 393224 | tf_op jit(solution)/shard_map/ppermute | solution.py:16
  145.9 8.7 %collective-permute-start.17 = (bf16[32,2048]{1,0:T(8,128)(2,1)S(1)}, bf16[32,2048]{1,0:T(8,128)(2,1)S(1)}, u32[]{:S(2)}, u32[]{:S(2)}) collective-permute-start(bf16[32,2048]{1,0:T(8,128)(2,1)S(1)} %fusion.75), channel_id=1, source_target_pairs={{0,4},{4,0},{1,5},{5,1},{2,6},{6,2},{3,7},{7,3},{8,12},{12,8},{9,1... | collective-permute-start | bytes 393224 | tf_op jit(solution)/shard_map/ppermute | solution.py:16
  154.7 4.6 %collective-permute-start.18 = (bf16[32,2048]{1,0:T(8,128)(2,1)S(1)}, bf16[32,2048]{1,0:T(8,128)(2,1)S(1)}, u32[]{:S(2)}, u32[]{:S(2)}) collective-permute-start(bf16[32,2048]{1,0:T(8,128)(2,1)S(1)} %fusion.158), channel_id=1, source_target_pairs={{0,2},{2,0},{1,3},{3,1},{4,6},{6,4},{5,7},{7,5},{8,10},{10,8},{9,1... | collective-permute-start | bytes 393224 | tf_op jit(solution)/shard_map/ppermute | solution.py:16
  159.4 2.4 %collective-permute-start.19 = (bf16[32,2048]{1,0:T(8,128)(2,1)S(1)}, bf16[32,2048]{1,0:T(8,128)(2,1)S(1)}, u32[]{:S(2)}, u32[]{:S(2)}) collective-permute-start(bf16[32,2048]{1,0:T(8,128)(2,1)S(1)} %fusion.162), channel_id=1, source_target_pairs={{0,1},{1,0},{2,3},{3,2},{4,5},{5,4},{6,7},{7,6},{8,9},{9,8},{10,11... | collective-permute-start | bytes 393224 | tf_op jit(solution)/shard_map/ppermute | solution.py:16
  161.8 19.4 %slice-start.4 = ((s8[8388608]{0:T(1024)(128)(4,1)}), s8[4194304]{0:T(1024)(128)(4,1)S(1)}, s32[]{:S(2)}) async-start(s8[8388608]{0:T(1024)(128)(4,1)} %bitcast.94), calls=%async_computation.4 | async-start | bytes 8388608
  161.9 7.7 %collective-permute-start.20 = (bf16[32,2048]{1,0:T(8,128)(2,1)S(1)}, bf16[32,2048]{1,0:T(8,128)(2,1)S(1)}, u32[]{:S(2)}, u32[]{:S(2)}) collective-permute-start(bf16[32,2048]{1,0:T(8,128)(2,1)S(1)} %fusion.166), channel_id=1, source_target_pairs={{0,8},{8,16},{16,24},{1,9},{9,17},{17,25},{2,10},{10,18},{18,26},{... | collective-permute-start | bytes 393224 | tf_op jit(solution)/shard_map/ppermute | solution.py:22
  169.6 11.7 %slice-start.5 = ((s8[8388608]{0:T(1024)(128)(4,1)}), s8[4194304]{0:T(1024)(128)(4,1)S(1)}, s32[]{:S(2)}) async-start(s8[8388608]{0:T(1024)(128)(4,1)} %bitcast.94), calls=%async_computation.5 | async-start | bytes 8388608
  169.6 2.0 collective-permute-start.21
  176.5 4.7 %collective-permute-start.22 = (bf16[32,2048]{1,0:T(8,128)(2,1)S(1)}, bf16[32,2048]{1,0:T(8,128)(2,1)S(1)}, u32[]{:S(2)}, u32[]{:S(2)}) collective-permute-start(bf16[32,2048]{1,0:T(8,128)(2,1)S(1)} %fusion.80), channel_id=1, source_target_pairs={{0,2},{2,0},{1,3},{3,1},{4,6},{6,4},{5,7},{7,5},{8,10},{10,8},{9,1... | collective-permute-start | bytes 393224 | tf_op jit(solution)/shard_map/ppermute | solution.py:16
  182.8 8.7 %collective-permute-start.23 = (bf16[32,2048]{1,0:T(8,128)(2,1)S(1)}, bf16[32,2048]{1,0:T(8,128)(2,1)S(1)}, u32[]{:S(2)}, u32[]{:S(2)}) collective-permute-start(bf16[32,2048]{1,0:T(8,128)(2,1)S(1)} %fusion.83), channel_id=1, source_target_pairs={{0,4},{4,0},{1,5},{5,1},{2,6},{6,2},{3,7},{7,3},{8,12},{12,8},{9,1... | collective-permute-start | bytes 393224 | tf_op jit(solution)/shard_map/ppermute | solution.py:16
  201.3 8.2 %collective-permute-start.24 = (bf16[32,2048]{1,0:T(8,128)(2,1)S(1)}, bf16[32,2048]{1,0:T(8,128)(2,1)S(1)}, u32[]{:S(2)}, u32[]{:S(2)}) collective-permute-start(bf16[32,2048]{1,0:T(8,128)(2,1)S(1)} %fusion.91), channel_id=1, source_target_pairs={{0,4},{4,0},{1,5},{5,1},{2,6},{6,2},{3,7},{7,3},{8,12},{12,8},{9,1... | collective-permute-start | bytes 393224 | tf_op jit(solution)/shard_map/ppermute | solution.py:16
  209.6 4.6 %collective-permute-start.25 = (bf16[32,2048]{1,0:T(8,128)(2,1)S(1)}, bf16[32,2048]{1,0:T(8,128)(2,1)S(1)}, u32[]{:S(2)}, u32[]{:S(2)}) collective-permute-start(bf16[32,2048]{1,0:T(8,128)(2,1)S(1)} %fusion.182), channel_id=1, source_target_pairs={{0,2},{2,0},{1,3},{3,1},{4,6},{6,4},{5,7},{7,5},{8,10},{10,8},{9,1... | collective-permute-start | bytes 393224 | tf_op jit(solution)/shard_map/ppermute | solution.py:16
  214.3 2.4 %collective-permute-start.26 = (bf16[32,2048]{1,0:T(8,128)(2,1)S(1)}, bf16[32,2048]{1,0:T(8,128)(2,1)S(1)}, u32[]{:S(2)}, u32[]{:S(2)}) collective-permute-start(bf16[32,2048]{1,0:T(8,128)(2,1)S(1)} %fusion.186), channel_id=1, source_target_pairs={{0,1},{1,0},{2,3},{3,2},{4,5},{5,4},{6,7},{7,6},{8,9},{9,8},{10,11... | collective-permute-start | bytes 393224 | tf_op jit(solution)/shard_map/ppermute | solution.py:16
where the time goes:
time: 220 us; the launch traced here: 217 us
  waiting for transfers between devices  118 us (54%)
  matrix products  68.3 us (31%)
  starting transfers between devices  27 us (12%)
  other arithmetic  3.28 us (1%)
    ppermute x24, waiting for transfers between devices, partner_2(): return lax.ppermute(block, axis, route)  102 us
    dot_general x4, matrix products, sweep_layer(): lax.dot_general(values, merge_op, (((1,), (1,)), ((), ())), preferred_ele...  39.2 us
    dot_general x8, matrix products, sweep_layer(): jnp.dot(mixed, merge_op, preferred_element_type=jnp.float32)  29.2 us
    ppermute x24, starting transfers between devices, partner_2(): return lax.ppermute(block, axis, route)  21.7 us
    ppermute x3, waiting for transfers between devices, shifted(): return lax.ppermute(array, axis, pairs)  16.1 us
    ppermute x3, starting transfers between devices, shifted(): return lax.ppermute(array, axis, pairs)  5.33 us
  transfers between devices with their start and end apart: 27, of which 27 were waited for; matrix products, arithmetic and copies ran while one was open for 0% of the time, Pallas kernels for 0%

commit v1 on v0

--- a/solution.py
+++ b/solution.py
@@ -1,9 +1,14 @@
+import functools
+
 import jax
 import jax.numpy as jnp
 from jax import lax
+from jax.experimental import pallas as pl
+from jax.experimental.pallas import tpu as pltpu
 from jax.sharding import PartitionSpec as P
 
 half_root = 0.7071067811865476
+TILE = 512
 
 
 def partner_2(block, axis, apart):
@@ -22,6 +27,65 @@
     return lax.ppermute(array, axis, pairs)
 
 
+def mixed_dot_kernel(sign_ref, values_ref, partner_ref, op_ref, out_ref):
+    first = values_ref[...].astype(jnp.float32)
+    second = partner_ref[...].astype(jnp.float32)
+    mixed = ((second + sign_ref[...] * first) * half_root).astype(jnp.bfloat16)
+    width = op_ref.shape[1]
+    for start in range(0, width, TILE):
+        out_ref[:, start:start + TILE] = jnp.dot(
+            mixed, op_ref[:, start:start + TILE], preferred_element_type=jnp.float32
+        ).astype(out_ref.dtype)
+
+
+def transposed_dot_kernel(values_ref, op_ref, out_ref):
+    values = values_ref[...]
+    width = op_ref.shape[0]
+    for start in range(0, width, TILE):
+        out_ref[:, start:start + TILE] = lax.dot_general(
+            values,
+            op_ref[start:start + TILE, :],
+            (((1,), (1,)), ((), ())),
+            preferred_element_type=jnp.float32,
+        ).astype(out_ref.dtype)
+
+
+def vmem_spec():
+    return pl.BlockSpec(memory_space=pltpu.VMEM)
+
+
+def cost(rows, width):
+    return pl.CostEstimate(
+        flops=2 * rows * width * width,
+        bytes_accessed=2 * width * width + 6 * rows * width,
+        transcendentals=0,
+    )
+
+
+def mixed_dot(sign, values, partner, merge_op):
+    rows, width = values.shape
+    return pl.pallas_call(
+        mixed_dot_kernel,
+        out_shape=jax.ShapeDtypeStruct(values.shape, jnp.bfloat16),
+        in_specs=[vmem_spec()] * 4,
+        out_specs=vmem_spec(),
+        cost_estimate=cost(rows, width),
+        compiler_params=pltpu.CompilerParams(vmem_limit_bytes=4 * 1024 * 1024),
+    )(sign, values, partner, pltpu.with_memory_space_constraint(merge_op, pltpu.VMEM))
+
+
+def transposed_dot(values, merge_op):
+    rows, width = values.shape
+    return pl.pallas_call(
+        transposed_dot_kernel,
+        out_shape=jax.ShapeDtypeStruct(values.shape, jnp.bfloat16),
+        in_specs=[vmem_spec()] * 2,
+        out_specs=vmem_spec(),
+        cost_estimate=cost(rows, width),
+        compiler_params=pltpu.CompilerParams(vmem_limit_bytes=4 * 1024 * 1024),
+    )(values, pltpu.with_memory_space_constraint(merge_op, pltpu.VMEM))
+
+
 def haar_pair(values, partner, lat_index, bit_level):
     is_lower = lat_index // 2**bit_level % 2 == 0
     first = values.astype(jnp.float32)
@@ -31,18 +95,21 @@
     )
 
 
+def level_sign(lat_index, bit_level, width):
+    is_lower = lat_index // 2**bit_level % 2 == 0
+    return jnp.full((1, width), jnp.where(is_lower, 1.0, -1.0), jnp.float32)
+
+
 def sweep_layer(leaf_data, merge_op):
     lat_count = lax.axis_size("lat")
     lat_index = lax.axis_index("lat")
     levels = lat_count.bit_length() - 1
+    width = leaf_data.shape[1]
     values = leaf_data
     for bit_level in range(levels):
         partner = partner_2(values, "lat", bit_level)
-        mixed = haar_pair(values, partner, lat_index, bit_level)
-        values = jnp.dot(mixed, merge_op, preferred_element_type=jnp.float32).astype(jnp.bfloat16)
-    values = lax.dot_general(
-        values, merge_op, (((1,), (1,)), ((), ())), preferred_element_type=jnp.float32
-    ).astype(jnp.bfloat16)
+        values = mixed_dot(level_sign(lat_index, bit_level, width), values, partner, merge_op)
+    values = transposed_dot(values, merge_op)
     for bit_level in range(levels - 1, -1, -1):
         partner = partner_2(values, "lat", bit_level)
         values = haar_pair(values, partner, lat_index, bit_level)

time: 220 us -> 189 us (0.86)
  matrix products: 68.3 us -> 0 us
  Pallas kernels: 0 us -> 28.5 us
  local copies, waits for them, and re-layouts: 0.05 us -> 10.2 us
    dot_general x12 -> x0, matrix products: 68.3 us -> none  [the longest x4 39.2 us: sweep_layer(): lax.dot_general(values, merge_op, (((1,), (1,)), ((), ())), preferred_ele...]
    pallas_call x0 -> x16, Pallas kernels: none -> 28.5 us  [the longest x12 18.4 us: mixed_dot(): pl.pallas_call(mixed_dot_kernel, out_shape=jax.ShapeDtypeStruct(values.sh...]
    unnamed x16 -> x14, local copies, waits for them, and re-layouts: 0.05 us -> 10.2 us
where the time goes in v1:
time: 189 us; the launch traced here: 187 us
  waiting for transfers between devices  119 us (63%)
  Pallas kernels  28.5 us (15%)
  starting transfers between devices  25.4 us (13%)
  local copies, waits for them, and re-layouts  10.2 us (5%)
  other arithmetic  3.29 us (2%)
    ppermute x24, waiting for transfers between devices, partner_2(): return lax.ppermute(block, axis, route)  102 us
    ppermute x24, starting transfers between devices, partner_2(): return lax.ppermute(block, axis, route)  21.3 us
    pallas_call x12, Pallas kernels, mixed_dot(): pl.pallas_call(mixed_dot_kernel, out_shape=jax.ShapeDtypeStruct(values.sh...  18.4 us
    ppermute x3, waiting for transfers between devices, shifted(): return lax.ppermute(array, axis, pairs)  16.6 us
    pallas_call x4, Pallas kernels, transposed_dot(): pl.pallas_call(transposed_dot_kernel, out_shape=jax.ShapeDtypeStruct(valu...  10.2 us
    unnamed x14, local copies, waits for them, and re-layouts  10.2 us
    ppermute x3, starting transfers between devices, shifted(): return lax.ppermute(array, axis, pairs)  4.06 us
  transfers between devices with their start and end apart: 27, of which 27 were waited for; matrix products, arithmetic and copies ran while one was open for 0% of the time, Pallas kernels for 0%

profile of v1, /device:TPU:7, one launch (start us, length us, event | category | flops | bytes accessed | tf_op | source)
XLA Modules:
  0.0 186.6 jit_solution(16316725866082409166)
XLA Ops:
  0.0 0.7 broadcast_multiply_fusion
  0.7 0.9 fusion.48.values_ref
  1.6 0.7 collective-permute-start
  2.4 1.0 collective-permute-done.partner_ref
  3.4 3.4 %copy-done = bf16[1,1,2048,2048]{3,2,1,0:T(8,128)(2,1)S(1)} copy-done((bf16[1,1,2048,2048]{3,2,1,0:T(8,128)(2,1)S(1)}, bf16[1,1,2048,2048]{3,2,1,0:T(8,128)(2,1)}, u32[]{:S(2)}) %copy-start) | copy-done | bytes 8388632
  6.7 1.5 shard_map.37.values_ref
  8.3 1.3 collective-permute-start.1
  9.6 3.4 %collective-permute-done.1.partner_ref = bf16[32,2048]{1,0:T(8,128)(2,1)S(1)} collective-permute-done((bf16[32,2048]{1,0:T(8,128)(2,1)S(1)}, bf16[32,2048]{1,0:T(8,128)(2,1)S(1)}, u32[]{:S(2)}, u32[]{:S(2)}) %collective-permute-start.1) | collective-permute-done | bytes 131104 | tf_op jit(solution)/shard_map/ppermute | solution.py:21
  13.0 3.4 %copy-done.1 = bf16[1,1,2048,2048]{3,2,1,0:T(8,128)(2,1)S(1)} copy-done((bf16[1,1,2048,2048]{3,2,1,0:T(8,128)(2,1)S(1)}, bf16[1,1,2048,2048]{3,2,1,0:T(8,128)(2,1)}, u32[]{:S(2)}) %copy-start.1) | copy-done | bytes 8388632
  16.4 1.5 shard_map.38.values_ref
  17.9 2.3 %collective-permute-start.2 = (bf16[32,2048]{1,0:T(8,128)(2,1)S(1)}, bf16[32,2048]{1,0:T(8,128)(2,1)S(1)}, u32[]{:S(2)}, u32[]{:S(2)}) collective-permute-start(bf16[32,2048]{1,0:T(8,128)(2,1)S(1)} %shard_map.38.values_ref), channel_id=1, source_target_pairs={{0,4},{4,0},{1,5},{5,1},{2,6},{6,2},{3,7},{7,3},{8,12},{12,8},{9,1... | collective-permute-start | bytes 393224 | tf_op jit(solution)/shard_map/ppermute | solution.py:21
  20.2 5.8 %collective-permute-done.2.partner_ref = bf16[32,2048]{1,0:T(8,128)(2,1)S(1)} collective-permute-done((bf16[32,2048]{1,0:T(8,128)(2,1)S(1)}, bf16[32,2048]{1,0:T(8,128)(2,1)S(1)}, u32[]{:S(2)}, u32[]{:S(2)}) %collective-permute-start.2) | collective-permute-done | bytes 131104 | tf_op jit(solution)/shard_map/ppermute | solution.py:21
  26.1 3.4 %copy-done.2 = bf16[1,1,2048,2048]{3,2,1,0:T(8,128)(2,1)S(1)} copy-done((bf16[1,1,2048,2048]{3,2,1,0:T(8,128)(2,1)S(1)}, bf16[1,1,2048,2048]{3,2,1,0:T(8,128)(2,1)}, u32[]{:S(2)}) %copy-start.2) | copy-done | bytes 8388632
  29.4 1.5 shard_map.39.values_ref
  31.0 2.5 %shard_map.40 = bf16[32,2048]{1,0:T(8,128)(2,1)S(1)} custom-call(bf16[32,2048]{1,0:T(8,128)(2,1)S(1)} %shard_map.39.values_ref, bf16[2048,2048]{1,0:T(8,128)(2,1)S(1)} %bitcast.13), custom_call_target="tpu_custom_call" | custom-call | flops 268435456 | bytes 8781824 | tf_op jit(solution)/shard_map/pallas_call | solution.py:79
  33.5 4.7 %collective-permute-done.3 = bf16[32,2048]{1,0:T(8,128)(2,1)S(1)} collective-permute-done((bf16[32,2048]{1,0:T(8,128)(2,1)S(1)}, bf16[32,2048]{1,0:T(8,128)(2,1)S(1)}, u32[]{:S(2)}, u32[]{:S(2)}) %collective-permute-start.3) | collective-permute-done | bytes 131104 | tf_op jit(solution)/shard_map/ppermute | solution.py:21
  38.3 2.9 %collective-permute-start.4 = (bf16[32,2048]{1,0:T(8,128)(2,1)S(1)}, bf16[32,2048]{1,0:T(8,128)(2,1)S(1)}, u32[]{:S(2)}, u32[]{:S(2)}) collective-permute-start(bf16[32,2048]{1,0:T(8,128)(2,1)S(1)} %fusion.2), channel_id=1, source_target_pairs={{0,2},{2,0},{1,3},{3,1},{4,6},{6,4},{5,7},{7,5},{8,10},{10,8},{9,1... | collective-permute-start | bytes 393224 | tf_op jit(solution)/shard_map/ppermute | solution.py:21
  41.2 2.9 %collective-permute-done.4 = bf16[32,2048]{1,0:T(8,128)(2,1)S(1)} collective-permute-done((bf16[32,2048]{1,0:T(8,128)(2,1)S(1)}, bf16[32,2048]{1,0:T(8,128)(2,1)S(1)}, u32[]{:S(2)}, u32[]{:S(2)}) %collective-permute-start.4) | collective-permute-done | bytes 131104 | tf_op jit(solution)/shard_map/ppermute | solution.py:21
  44.2 4.5 %collective-permute-start.5 = (bf16[32,2048]{1,0:T(8,128)(2,1)S(1)}, bf16[32,2048]{1,0:T(8,128)(2,1)S(1)}, u32[]{:S(2)}, u32[]{:S(2)}) collective-permute-start(bf16[32,2048]{1,0:T(8,128)(2,1)S(1)} %fusion.6), channel_id=1, source_target_pairs={{0,1},{1,0},{2,3},{3,2},{4,5},{5,4},{6,7},{7,6},{8,9},{9,8},{10,11... | collective-permute-start | bytes 393224 | tf_op jit(solution)/shard_map/ppermute | solution.py:21
  48.7 1.0 collective-permute-done.5
  49.8 1.3 collective-permute-start.6
  51.1 5.3 %collective-permute-done.6 = bf16[32,2048]{1,0:T(8,128)(2,1)S(1)} collective-permute-done((bf16[32,2048]{1,0:T(8,128)(2,1)S(1)}, bf16[32,2048]{1,0:T(8,128)(2,1)S(1)}, u32[]{:S(2)}, u32[]{:S(2)}) %collective-permute-start.6) | collective-permute-done | bytes 131104 | tf_op jit(solution)/shard_map/ppermute | solution.py:27
  56.4 1.3 collective-permute-start.7
  57.7 1.0 collective-permute-done.7.partner_ref
  58.7 1.5 shard_map.41.values_ref
  60.3 4.7 %collective-permute-done.8.partner_ref = bf16[32,2048]{1,0:T(8,128)(2,1)S(1)} collective-permute-done((bf16[32,2048]{1,0:T(8,128)(2,1)S(1)}, bf16[32,2048]{1,0:T(8,128)(2,1)S(1)}, u32[]{:S(2)}, u32[]{:S(2)}) %collective-permute-start.8) | collective-permute-done | bytes 131104 | tf_op jit(solution)/shard_map/ppermute | solution.py:21
  65.0 1.5 shard_map.42.values_ref
  66.5 9.1 %collective-permute-done.9.partner_ref = bf16[32,2048]{1,0:T(8,128)(2,1)S(1)} collective-permute-done((bf16[32,2048]{1,0:T(8,128)(2,1)S(1)}, bf16[32,2048]{1,0:T(8,128)(2,1)S(1)}, u32[]{:S(2)}, u32[]{:S(2)}) %collective-permute-start.9) | collective-permute-done | bytes 131104 | tf_op jit(solution)/shard_map/ppermute | solution.py:21
  75.6 1.5 shard_map.43.values_ref
  77.2 2.5 %shard_map.44 = bf16[32,2048]{1,0:T(8,128)(2,1)S(1)} custom-call(bf16[32,2048]{1,0:T(8,128)(2,1)S(1)} %shard_map.43.values_ref, bf16[2048,2048]{1,0:T(8,128)(2,1)S(1)} %bitcast.19), custom_call_target="tpu_custom_call" | custom-call | flops 268435456 | bytes 8781824 | tf_op jit(solution)/shard_map/pallas_call | solution.py:79
  79.7 7.7 %collective-permute-done.10 = bf16[32,2048]{1,0:T(8,128)(2,1)S(1)} collective-permute-done((bf16[32,2048]{1,0:T(8,128)(2,1)S(1)}, bf16[32,2048]{1,0:T(8,128)(2,1)S(1)}, u32[]{:S(2)}, u32[]{:S(2)}) %collective-permute-start.10) | collective-permute-done | bytes 131104 | tf_op jit(solution)/shard_map/ppermute | solution.py:21
  87.5 4.6 %collective-permute-done.11 = bf16[32,2048]{1,0:T(8,128)(2,1)S(1)} collective-permute-done((bf16[32,2048]{1,0:T(8,128)(2,1)S(1)}, bf16[32,2048]{1,0:T(8,128)(2,1)S(1)}, u32[]{:S(2)}, u32[]{:S(2)}) %collective-permute-start.11) | collective-permute-done | bytes 131104 | tf_op jit(solution)/shard_map/ppermute | solution.py:21
  92.2 1.4 collective-permute-start.12
  93.6 1.0 collective-permute-done.12
  94.6 1.5 collective-permute-start.13
  96.1 5.1 %collective-permute-done.13 = bf16[32,2048]{1,0:T(8,128)(2,1)S(1)} collective-permute-done((bf16[32,2048]{1,0:T(8,128)(2,1)S(1)}, bf16[32,2048]{1,0:T(8,128)(2,1)S(1)}, u32[]{:S(2)}, u32[]{:S(2)}) %collective-permute-start.13) | collective-permute-done | bytes 131104 | tf_op jit(solution)/shard_map/ppermute | solution.py:27
  101.3 1.3 collective-permute-start.14
  102.6 1.0 collective-permute-done.14.partner_ref
  103.5 1.5 shard_map.45.values_ref
  105.1 4.7 %collective-permute-done.15.partner_ref = bf16[32,2048]{1,0:T(8,128)(2,1)S(1)} collective-permute-done((bf16[32,2048]{1,0:T(8,128)(2,1)S(1)}, bf16[32,2048]{1,0:T(8,128)(2,1)S(1)}, u32[]{:S(2)}, u32[]{:S(2)}) %collective-permute-start.15) | collective-permute-done | bytes 131104 | tf_op jit(solution)/shard_map/ppermute | solution.py:21
  109.8 1.5 shard_map.46.values_ref
  111.3 1.2 collective-permute-start.16
  112.5 7.9 %collective-permute-done.16.partner_ref = bf16[32,2048]{1,0:T(8,128)(2,1)S(1)} collective-permute-done((bf16[32,2048]{1,0:T(8,128)(2,1)S(1)}, bf16[32,2048]{1,0:T(8,128)(2,1)S(1)}, u32[]{:S(2)}, u32[]{:S(2)}) %collective-permute-start.16) | collective-permute-done | bytes 131104 | tf_op jit(solution)/shard_map/ppermute | solution.py:21
  120.5 1.5 shard_map.47.values_ref
  122.0 2.5 %shard_map.48 = bf16[32,2048]{1,0:T(8,128)(2,1)S(1)} custom-call(bf16[32,2048]{1,0:T(8,128)(2,1)S(1)} %shard_map.47.values_ref, bf16[2048,2048]{1,0:T(8,128)(2,1)S(1)} %bitcast.23), custom_call_target="tpu_custom_call" | custom-call | flops 268435456 | bytes 8781824 | tf_op jit(solution)/shard_map/pallas_call | solution.py:79
  124.6 8.7 %collective-permute-done.17 = bf16[32,2048]{1,0:T(8,128)(2,1)S(1)} collective-permute-done((bf16[32,2048]{1,0:T(8,128)(2,1)S(1)}, bf16[32,2048]{1,0:T(8,128)(2,1)S(1)}, u32[]{:S(2)}, u32[]{:S(2)}) %collective-permute-start.17) | collective-permute-done | bytes 131104 | tf_op jit(solution)/shard_map/ppermute | solution.py:21
  133.4 4.6 %collective-permute-done.18 = bf16[32,2048]{1,0:T(8,128)(2,1)S(1)} collective-permute-done((bf16[32,2048]{1,0:T(8,128)(2,1)S(1)}, bf16[32,2048]{1,0:T(8,128)(2,1)S(1)}, u32[]{:S(2)}, u32[]{:S(2)}) %collective-permute-start.18) | collective-permute-done | bytes 131104 | tf_op jit(solution)/shard_map/ppermute | solution.py:21
  138.0 1.4 collective-permute-start.19
  139.4 1.0 collective-permute-done.19
  140.5 1.3 collective-permute-start.20
  141.8 6.2 %collective-permute-done.20 = bf16[32,2048]{1,0:T(8,128)(2,1)S(1)} collective-permute-done((bf16[32,2048]{1,0:T(8,128)(2,1)S(1)}, bf16[32,2048]{1,0:T(8,128)(2,1)S(1)}, u32[]{:S(2)}, u32[]{:S(2)}) %collective-permute-start.20) | collective-permute-done | bytes 131104 | tf_op jit(solution)/shard_map/ppermute | solution.py:27
  148.0 1.0 collective-permute-start.21
  149.0 1.0 collective-permute-done.21.partner_ref
  150.0 1.5 shard_map.49.values_ref
  151.5 4.7 %collective-permute-done.22.partner_ref = bf16[32,2048]{1,0:T(8,128)(2,1)S(1)} collective-permute-done((bf16[32,2048]{1,0:T(8,128)(2,1)S(1)}, bf16[32,2048]{1,0:T(8,128)(2,1)S(1)}, u32[]{:S(2)}, u32[]{:S(2)}) %collective-permute-start.22) | collective-permute-done | bytes 131104 | tf_op jit(solution)/shard_map/ppermute | solution.py:21
  156.2 1.5 shard_map.50.values_ref
  157.9 8.5 %collective-permute-done.23.partner_ref = bf16[32,2048]{1,0:T(8,128)(2,1)S(1)} collective-permute-done((bf16[32,2048]{1,0:T(8,128)(2,1)S(1)}, bf16[32,2048]{1,0:T(8,128)(2,1)S(1)}, u32[]{:S(2)}, u32[]{:S(2)}) %collective-permute-start.23) | collective-permute-done | bytes 131104 | tf_op jit(solution)/shard_map/ppermute | solution.py:21
  166.5 1.5 shard_map.51.values_ref
  168.0 2.5 %shard_map.52 = bf16[32,2048]{1,0:T(8,128)(2,1)S(1)} custom-call(bf16[32,2048]{1,0:T(8,128)(2,1)S(1)} %shard_map.51.values_ref, bf16[2048,2048]{1,0:T(8,128)(2,1)S(1)} %bitcast.27), custom_call_target="tpu_custom_call" | custom-call | flops 268435456 | bytes 8781824 | tf_op jit(solution)/shard_map/pallas_call | solution.py:79
  170.6 8.1 %collective-permute-done.24 = bf16[32,2048]{1,0:T(8,128)(2,1)S(1)} collective-permute-done((bf16[32,2048]{1,0:T(8,128)(2,1)S(1)}, bf16[32,2048]{1,0:T(8,128)(2,1)S(1)}, u32[]{:S(2)}, u32[]{:S(2)}) %collective-permute-start.24) | collective-permute-done | bytes 131104 | tf_op jit(solution)/shard_map/ppermute | solution.py:21
  178.8 4.5 %collective-permute-done.25 = bf16[32,2048]{1,0:T(8,128)(2,1)S(1)} collective-permute-done((bf16[32,2048]{1,0:T(8,128)(2,1)S(1)}, bf16[32,2048]{1,0:T(8,128)(2,1)S(1)}, u32[]{:S(2)}, u32[]{:S(2)}) %collective-permute-start.25) | collective-permute-done | bytes 131104 | tf_op jit(solution)/shard_map/ppermute | solution.py:21
  183.4 1.4 collective-permute-start.26
  184.8 1.0 collective-permute-done.26
  185.8 0.8 fusion.53
  (41 shorter events, 1.4 us)
Async XLA Ops:
  1.6 1.7 collective-permute-start
  3.4 3.4 %copy-start = (bf16[1,1,2048,2048]{3,2,1,0:T(8,128)(2,1)S(1)}, bf16[1,1,2048,2048]{3,2,1,0:T(8,128)(2,1)}, u32[]{:S(2)}) copy-start(bf16[1,1,2048,2048]{3,2,1,0:T(8,128)(2,1)} %param.5) | copy-start | bytes 25165828
  8.3 4.7 %collective-permute-start.1 = (bf16[32,2048]{1,0:T(8,128)(2,1)S(1)}, bf16[32,2048]{1,0:T(8,128)(2,1)S(1)}, u32[]{:S(2)}, u32[]{:S(2)}) collective-permute-start(bf16[32,2048]{1,0:T(8,128)(2,1)S(1)} %shard_map.37.values_ref), channel_id=1, source_target_pairs={{0,2},{2,0},{1,3},{3,1},{4,6},{6,4},{5,7},{7,5},{8,10},{10,8},{9,1... | collective-permute-start | bytes 393224 | tf_op jit(solution)/shard_map/ppermute | solution.py:21
  13.0 3.4 %copy-start.1 = (bf16[1,1,2048,2048]{3,2,1,0:T(8,128)(2,1)S(1)}, bf16[1,1,2048,2048]{3,2,1,0:T(8,128)(2,1)}, u32[]{:S(2)}) copy-start(bf16[1,1,2048,2048]{3,2,1,0:T(8,128)(2,1)} %param.5) | copy-start | bytes 25165828
  17.9 8.1 %collective-permute-start.2 = (bf16[32,2048]{1,0:T(8,128)(2,1)S(1)}, bf16[32,2048]{1,0:T(8,128)(2,1)S(1)}, u32[]{:S(2)}, u32[]{:S(2)}) collective-permute-start(bf16[32,2048]{1,0:T(8,128)(2,1)S(1)} %shard_map.38.values_ref), channel_id=1, source_target_pairs={{0,4},{4,0},{1,5},{5,1},{2,6},{6,2},{3,7},{7,3},{8,12},{12,8},{9,1... | collective-permute-start | bytes 393224 | tf_op jit(solution)/shard_map/ppermute | solution.py:21
  26.1 3.4 %copy-start.2 = (bf16[1,1,2048,2048]{3,2,1,0:T(8,128)(2,1)S(1)}, bf16[1,1,2048,2048]{3,2,1,0:T(8,128)(2,1)}, u32[]{:S(2)}) copy-start(bf16[1,1,2048,2048]{3,2,1,0:T(8,128)(2,1)} %param.5) | copy-start | bytes 25165828
  29.4 27.0 %copy-start.3 = (bf16[1,1,32,2048]{3,2,1,0:T(8,128)(2,1)S(1)}, bf16[1,1,32,2048]{3,2,1,0:T(8,128)(2,1)}, u32[]{:S(2)}) copy-start(bf16[1,1,32,2048]{3,2,1,0:T(8,128)(2,1)} %param.3) | copy-start | bytes 393220
  29.4 27.0 %copy-start.4 = (f32[1,1,2048]{2,1,0:T(1,128)S(1)}, f32[1,1,2048]{2,1,0:T(1,128)}, u32[]{:S(2)}) copy-start(f32[1,1,2048]{2,1,0:T(1,128)} %param.4) | copy-start | bytes 24580
  29.4 29.3 %slice-start = ((s8[8388608]{0:T(1024)(128)(4,1)}), s8[4194304]{0:T(1024)(128)(4,1)S(1)}, s32[]{:S(2)}) async-start(s8[8388608]{0:T(1024)(128)(4,1)} %bitcast.14), calls=%async_computation | async-start | bytes 8388608
  31.0 27.7 %slice-start.1 = ((s8[8388608]{0:T(1024)(128)(4,1)}), s8[4194304]{0:T(1024)(128)(4,1)S(1)}, s32[]{:S(2)}) async-start(s8[8388608]{0:T(1024)(128)(4,1)} %bitcast.14), calls=%async_computation.1 | async-start | bytes 8388608
  33.5 4.7 %collective-permute-start.3 = (bf16[32,2048]{1,0:T(8,128)(2,1)S(1)}, bf16[32,2048]{1,0:T(8,128)(2,1)S(1)}, u32[]{:S(2)}, u32[]{:S(2)}) collective-permute-start(bf16[32,2048]{1,0:T(8,128)(2,1)S(1)} %shard_map.40), channel_id=1, source_target_pairs={{0,4},{4,0},{1,5},{5,1},{2,6},{6,2},{3,7},{7,3},{8,12},{12,8},{9,1... | collective-permute-start | bytes 393224 | tf_op jit(solution)/shard_map/ppermute | solution.py:21
  38.3 5.8 %collective-permute-start.4 = (bf16[32,2048]{1,0:T(8,128)(2,1)S(1)}, bf16[32,2048]{1,0:T(8,128)(2,1)S(1)}, u32[]{:S(2)}, u32[]{:S(2)}) collective-permute-start(bf16[32,2048]{1,0:T(8,128)(2,1)S(1)} %fusion.2), channel_id=1, source_target_pairs={{0,2},{2,0},{1,3},{3,1},{4,6},{6,4},{5,7},{7,5},{8,10},{10,8},{9,1... | collective-permute-start | bytes 393224 | tf_op jit(solution)/shard_map/ppermute | solution.py:21
  44.2 5.5 %collective-permute-start.5 = (bf16[32,2048]{1,0:T(8,128)(2,1)S(1)}, bf16[32,2048]{1,0:T(8,128)(2,1)S(1)}, u32[]{:S(2)}, u32[]{:S(2)}) collective-permute-start(bf16[32,2048]{1,0:T(8,128)(2,1)S(1)} %fusion.6), channel_id=1, source_target_pairs={{0,1},{1,0},{2,3},{3,2},{4,5},{5,4},{6,7},{7,6},{8,9},{9,8},{10,11... | collective-permute-start | bytes 393224 | tf_op jit(solution)/shard_map/ppermute | solution.py:21
  49.8 6.6 %collective-permute-start.6 = (bf16[32,2048]{1,0:T(8,128)(2,1)S(1)}, bf16[32,2048]{1,0:T(8,128)(2,1)S(1)}, u32[]{:S(2)}, u32[]{:S(2)}) collective-permute-start(bf16[32,2048]{1,0:T(8,128)(2,1)S(1)} %fusion.10), channel_id=1, source_target_pairs={{0,8},{8,16},{16,24},{1,9},{9,17},{17,25},{2,10},{10,18},{18,26},{... | collective-permute-start | bytes 393224 | tf_op jit(solution)/shard_map/ppermute | solution.py:27
  56.4 2.3 %collective-permute-start.7 = (bf16[32,2048]{1,0:T(8,128)(2,1)S(1)}, bf16[32,2048]{1,0:T(8,128)(2,1)S(1)}, u32[]{:S(2)}, u32[]{:S(2)}) collective-permute-start(bf16[32,2048]{1,0:T(8,128)(2,1)S(1)} %fusion.49.values_ref), channel_id=1, source_target_pairs={{0,1},{1,0},{2,3},{3,2},{4,5},{5,4},{6,7},{7,6},{8,9},{9,8},{10,11... | collective-permute-start | bytes 393224 | tf_op jit(solution)/shard_map/ppermute | solution.py:21
  60.2 4.7 %collective-permute-start.8 = (bf16[32,2048]{1,0:T(8,128)(2,1)S(1)}, bf16[32,2048]{1,0:T(8,128)(2,1)S(1)}, u32[]{:S(2)}, u32[]{:S(2)}) collective-permute-start(bf16[32,2048]{1,0:T(8,128)(2,1)S(1)} %shard_map.41.values_ref), channel_id=1, source_target_pairs={{0,2},{2,0},{1,3},{3,1},{4,6},{6,4},{5,7},{7,5},{8,10},{10,8},{9,1... | collective-permute-start | bytes 393224 | tf_op jit(solution)/shard_map/ppermute | solution.py:21
  66.5 9.1 %collective-permute-start.9 = (bf16[32,2048]{1,0:T(8,128)(2,1)S(1)}, bf16[32,2048]{1,0:T(8,128)(2,1)S(1)}, u32[]{:S(2)}, u32[]{:S(2)}) collective-permute-start(bf16[32,2048]{1,0:T(8,128)(2,1)S(1)} %shard_map.42.values_ref), channel_id=1, source_target_pairs={{0,4},{4,0},{1,5},{5,1},{2,6},{6,2},{3,7},{7,3},{8,12},{12,8},{9,1... | collective-permute-start | bytes 393224 | tf_op jit(solution)/shard_map/ppermute | solution.py:21
  79.7 7.7 %collective-permute-start.10 = (bf16[32,2048]{1,0:T(8,128)(2,1)S(1)}, bf16[32,2048]{1,0:T(8,128)(2,1)S(1)}, u32[]{:S(2)}, u32[]{:S(2)}) collective-permute-start(bf16[32,2048]{1,0:T(8,128)(2,1)S(1)} %shard_map.44), channel_id=1, source_target_pairs={{0,4},{4,0},{1,5},{5,1},{2,6},{6,2},{3,7},{7,3},{8,12},{12,8},{9,1... | collective-permute-start | bytes 393224 | tf_op jit(solution)/shard_map/ppermute | solution.py:21
  87.5 4.6 %collective-permute-start.11 = (bf16[32,2048]{1,0:T(8,128)(2,1)S(1)}, bf16[32,2048]{1,0:T(8,128)(2,1)S(1)}, u32[]{:S(2)}, u32[]{:S(2)}) collective-permute-start(bf16[32,2048]{1,0:T(8,128)(2,1)S(1)} %fusion.14), channel_id=1, source_target_pairs={{0,2},{2,0},{1,3},{3,1},{4,6},{6,4},{5,7},{7,5},{8,10},{10,8},{9,1... | collective-permute-start | bytes 393224 | tf_op jit(solution)/shard_map/ppermute | solution.py:21
  92.2 2.4 %collective-permute-start.12 = (bf16[32,2048]{1,0:T(8,128)(2,1)S(1)}, bf16[32,2048]{1,0:T(8,128)(2,1)S(1)}, u32[]{:S(2)}, u32[]{:S(2)}) collective-permute-start(bf16[32,2048]{1,0:T(8,128)(2,1)S(1)} %fusion.18), channel_id=1, source_target_pairs={{0,1},{1,0},{2,3},{3,2},{4,5},{5,4},{6,7},{7,6},{8,9},{9,8},{10,11... | collective-permute-start | bytes 393224 | tf_op jit(solution)/shard_map/ppermute | solution.py:21
  94.6 6.6 %collective-permute-start.13 = (bf16[32,2048]{1,0:T(8,128)(2,1)S(1)}, bf16[32,2048]{1,0:T(8,128)(2,1)S(1)}, u32[]{:S(2)}, u32[]{:S(2)}) collective-permute-start(bf16[32,2048]{1,0:T(8,128)(2,1)S(1)} %fusion.22), channel_id=1, source_target_pairs={{0,8},{8,16},{16,24},{1,9},{9,17},{17,25},{2,10},{10,18},{18,26},{... | collective-permute-start | bytes 393224 | tf_op jit(solution)/shard_map/ppermute | solution.py:27
  101.3 2.3 %collective-permute-start.14 = (bf16[32,2048]{1,0:T(8,128)(2,1)S(1)}, bf16[32,2048]{1,0:T(8,128)(2,1)S(1)}, u32[]{:S(2)}, u32[]{:S(2)}) collective-permute-start(bf16[32,2048]{1,0:T(8,128)(2,1)S(1)} %fusion.50.values_ref), channel_id=1, source_target_pairs={{0,1},{1,0},{2,3},{3,2},{4,5},{5,4},{6,7},{7,6},{8,9},{9,8},{10,11... | collective-permute-start | bytes 393224 | tf_op jit(solution)/shard_map/ppermute | solution.py:21
  105.1 4.7 %collective-permute-start.15 = (bf16[32,2048]{1,0:T(8,128)(2,1)S(1)}, bf16[32,2048]{1,0:T(8,128)(2,1)S(1)}, u32[]{:S(2)}, u32[]{:S(2)}) collective-permute-start(bf16[32,2048]{1,0:T(8,128)(2,1)S(1)} %shard_map.45.values_ref), channel_id=1, source_target_pairs={{0,2},{2,0},{1,3},{3,1},{4,6},{6,4},{5,7},{7,5},{8,10},{10,8},{9,1... | collective-permute-start | bytes 393224 | tf_op jit(solution)/shard_map/ppermute | solution.py:21
  111.3 9.1 %collective-permute-start.16 = (bf16[32,2048]{1,0:T(8,128)(2,1)S(1)}, bf16[32,2048]{1,0:T(8,128)(2,1)S(1)}, u32[]{:S(2)}, u32[]{:S(2)}) collective-permute-start(bf16[32,2048]{1,0:T(8,128)(2,1)S(1)} %shard_map.46.values_ref), channel_id=1, source_target_pairs={{0,4},{4,0},{1,5},{5,1},{2,6},{6,2},{3,7},{7,3},{8,12},{12,8},{9,1... | collective-permute-start | bytes 393224 | tf_op jit(solution)/shard_map/ppermute | solution.py:21
  124.5 8.7 %collective-permute-start.17 = (bf16[32,2048]{1,0:T(8,128)(2,1)S(1)}, bf16[32,2048]{1,0:T(8,128)(2,1)S(1)}, u32[]{:S(2)}, u32[]{:S(2)}) collective-permute-start(bf16[32,2048]{1,0:T(8,128)(2,1)S(1)} %shard_map.48), channel_id=1, source_target_pairs={{0,4},{4,0},{1,5},{5,1},{2,6},{6,2},{3,7},{7,3},{8,12},{12,8},{9,1... | collective-permute-start | bytes 393224 | tf_op jit(solution)/shard_map/ppermute | solution.py:21
  133.3 4.6 %collective-permute-start.18 = (bf16[32,2048]{1,0:T(8,128)(2,1)S(1)}, bf16[32,2048]{1,0:T(8,128)(2,1)S(1)}, u32[]{:S(2)}, u32[]{:S(2)}) collective-permute-start(bf16[32,2048]{1,0:T(8,128)(2,1)S(1)} %fusion.26), channel_id=1, source_target_pairs={{0,2},{2,0},{1,3},{3,1},{4,6},{6,4},{5,7},{7,5},{8,10},{10,8},{9,1... | collective-permute-start | bytes 393224 | tf_op jit(solution)/shard_map/ppermute | solution.py:21
  138.0 2.4 %collective-permute-start.19 = (bf16[32,2048]{1,0:T(8,128)(2,1)S(1)}, bf16[32,2048]{1,0:T(8,128)(2,1)S(1)}, u32[]{:S(2)}, u32[]{:S(2)}) collective-permute-start(bf16[32,2048]{1,0:T(8,128)(2,1)S(1)} %fusion.30), channel_id=1, source_target_pairs={{0,1},{1,0},{2,3},{3,2},{4,5},{5,4},{6,7},{7,6},{8,9},{9,8},{10,11... | collective-permute-start | bytes 393224 | tf_op jit(solution)/shard_map/ppermute | solution.py:21
  140.5 7.5 %collective-permute-start.20 = (bf16[32,2048]{1,0:T(8,128)(2,1)S(1)}, bf16[32,2048]{1,0:T(8,128)(2,1)S(1)}, u32[]{:S(2)}, u32[]{:S(2)}) collective-permute-start(bf16[32,2048]{1,0:T(8,128)(2,1)S(1)} %fusion.34), channel_id=1, source_target_pairs={{0,8},{8,16},{16,24},{1,9},{9,17},{17,25},{2,10},{10,18},{18,26},{... | collective-permute-start | bytes 393224 | tf_op jit(solution)/shard_map/ppermute | solution.py:27
  148.0 2.0 %collective-permute-start.21 = (bf16[32,2048]{1,0:T(8,128)(2,1)S(1)}, bf16[32,2048]{1,0:T(8,128)(2,1)S(1)}, u32[]{:S(2)}, u32[]{:S(2)}) collective-permute-start(bf16[32,2048]{1,0:T(8,128)(2,1)S(1)} %fusion.51.values_ref), channel_id=1, source_target_pairs={{0,1},{1,0},{2,3},{3,2},{4,5},{5,4},{6,7},{7,6},{8,9},{9,8},{10,11... | collective-permute-start | bytes 393224 | tf_op jit(solution)/shard_map/ppermute | solution.py:21
  151.5 4.7 %collective-permute-start.22 = (bf16[32,2048]{1,0:T(8,128)(2,1)S(1)}, bf16[32,2048]{1,0:T(8,128)(2,1)S(1)}, u32[]{:S(2)}, u32[]{:S(2)}) collective-permute-start(bf16[32,2048]{1,0:T(8,128)(2,1)S(1)} %shard_map.49.values_ref), channel_id=1, source_target_pairs={{0,2},{2,0},{1,3},{3,1},{4,6},{6,4},{5,7},{7,5},{8,10},{10,8},{9,1... | collective-permute-start | bytes 393224 | tf_op jit(solution)/shard_map/ppermute | solution.py:21
  157.8 8.7 %collective-permute-start.23 = (bf16[32,2048]{1,0:T(8,128)(2,1)S(1)}, bf16[32,2048]{1,0:T(8,128)(2,1)S(1)}, u32[]{:S(2)}, u32[]{:S(2)}) collective-permute-start(bf16[32,2048]{1,0:T(8,128)(2,1)S(1)} %shard_map.50.values_ref), channel_id=1, source_target_pairs={{0,4},{4,0},{1,5},{5,1},{2,6},{6,2},{3,7},{7,3},{8,12},{12,8},{9,1... | collective-permute-start | bytes 393224 | tf_op jit(solution)/shard_map/ppermute | solution.py:21
  170.5 8.1 %collective-permute-start.24 = (bf16[32,2048]{1,0:T(8,128)(2,1)S(1)}, bf16[32,2048]{1,0:T(8,128)(2,1)S(1)}, u32[]{:S(2)}, u32[]{:S(2)}) collective-permute-start(bf16[32,2048]{1,0:T(8,128)(2,1)S(1)} %shard_map.52), channel_id=1, source_target_pairs={{0,4},{4,0},{1,5},{5,1},{2,6},{6,2},{3,7},{7,3},{8,12},{12,8},{9,1... | collective-permute-start | bytes 393224 | tf_op jit(solution)/shard_map/ppermute | solution.py:21
  178.7 4.6 %collective-permute-start.25 = (bf16[32,2048]{1,0:T(8,128)(2,1)S(1)}, bf16[32,2048]{1,0:T(8,128)(2,1)S(1)}, u32[]{:S(2)}, u32[]{:S(2)}) collective-permute-start(bf16[32,2048]{1,0:T(8,128)(2,1)S(1)} %fusion.38), channel_id=1, source_target_pairs={{0,2},{2,0},{1,3},{3,1},{4,6},{6,4},{5,7},{7,5},{8,10},{10,8},{9,1... | collective-permute-start | bytes 393224 | tf_op jit(solution)/shard_map/ppermute | solution.py:21
  183.4 2.4 %collective-permute-start.26 = (bf16[32,2048]{1,0:T(8,128)(2,1)S(1)}, bf16[32,2048]{1,0:T(8,128)(2,1)S(1)}, u32[]{:S(2)}, u32[]{:S(2)}) collective-permute-start(bf16[32,2048]{1,0:T(8,128)(2,1)S(1)} %fusion.42), channel_id=1, source_target_pairs={{0,1},{1,0},{2,3},{3,2},{4,5},{5,4},{6,7},{7,6},{8,9},{9,8},{10,11... | collective-permute-start | bytes 393224 | tf_op jit(solution)/shard_map/ppermute | solution.py:21

commit v2 on v1

--- a/solution.py
+++ b/solution.py
@@ -9,6 +9,7 @@
 
 half_root = 0.7071067811865476
 TILE = 512
+CHUNKS = 2
 
 
 def partner_2(block, axis, apart):
@@ -122,15 +123,23 @@
     depth_index = lax.axis_index("depth")
     depth_count = lax.axis_size("depth")
     shot_rows = sources[0, 0]
+    rows = shot_rows.shape[0]
+    chunks = CHUNKS
+    chunk = rows // chunks
     result = jnp.zeros_like(shot_rows)
-    incoming = jnp.zeros_like(shot_rows)
-    for sweep_step in range(depth_count):
-        leaf_data = (
-            shot_rows.astype(jnp.float32) + coupling_row * incoming.astype(jnp.float32)
-        ).astype(jnp.bfloat16)
+    incoming = jnp.zeros((chunk, shot_rows.shape[1]), shot_rows.dtype)
+    steps = chunks + depth_count - 1
+    for step in range(steps):
+        position = step - depth_index
+        valid = (position >= 0) & (position < chunks)
+        start = jnp.clip(position, 0, chunks - 1) * chunk
+        own = lax.dynamic_slice_in_dim(shot_rows, start, chunk, 0)
+        leaf_data = (own.astype(jnp.float32) + coupling_row * incoming.astype(jnp.float32)).astype(
+            jnp.bfloat16
+        )
         solved = sweep_layer(leaf_data, merge_op)
-        result = jnp.where(depth_index == sweep_step, solved, result)
-        if sweep_step + 1 < depth_count:
+        result = jnp.where(valid, lax.dynamic_update_slice_in_dim(result, solved, start, 0), result)
+        if step + 1 < steps:
             incoming = shifted(solved, "depth", 1)
     return result[None, None]
 

time: 189 us -> 209 us (1.11)
  waiting for transfers between devices: 119 us -> 58.8 us
  starting transfers between devices: 25.4 us -> 76.5 us
  local copies, waits for them, and re-layouts: 10.2 us -> 37.9 us
    ppermute x24 -> x30, waiting for transfers between devices: 102 us -> 41.9 us  [partner_2(): return lax.ppermute(block, axis, route)]
    ppermute x24 -> x30, starting transfers between devices: 21.3 us -> 70.9 us  [partner_2(): return lax.ppermute(block, axis, route)]
    unnamed x14 -> x27, local copies, waits for them, and re-layouts: 10.2 us -> 37.9 us
    ppermute x3 -> x4, starting transfers between devices: 4.06 us -> 5.57 us  [shifted(): return lax.ppermute(array, axis, pairs)]
    pallas_call x4 -> x5, Pallas kernels: 10.2 us -> 11.4 us  [transposed_dot(): pl.pallas_call(transposed_dot_kernel, out_shape=jax.ShapeDtypeStruct(valu...]
    pallas_call x12 -> x15, Pallas kernels: 18.4 us -> 17.8 us  [mixed_dot(): pl.pallas_call(mixed_dot_kernel, out_shape=jax.ShapeDtypeStruct(values.sh...]
    ppermute x3 -> x4, waiting for transfers between devices: 16.6 us -> 16.9 us  [shifted(): return lax.ppermute(array, axis, pairs)]
  transfers between devices with their start and end apart: 27 -> 34, of which waited for: 27 -> 34; matrix products, arithmetic and copies ran while one was open for 0% -> 0% of each run, Pallas kernels for 0% -> 0%
where the time goes in v2:
time: 209 us; the launch traced here: 205 us
  starting transfers between devices  76.5 us (37%)
  waiting for transfers between devices  58.8 us (28%)
  local copies, waits for them, and re-layouts  37.9 us (18%)
  Pallas kernels  29.2 us (14%)
  other arithmetic  2.87 us (1%)
    ppermute x30, starting transfers between devices, partner_2(): return lax.ppermute(block, axis, route)  70.9 us
    ppermute x30, waiting for transfers between devices, partner_2(): return lax.ppermute(block, axis, route)  41.9 us
    unnamed x27, local copies, waits for them, and re-layouts  37.9 us
    pallas_call x15, Pallas kernels, mixed_dot(): pl.pallas_call(mixed_dot_kernel, out_shape=jax.ShapeDtypeStruct(values.sh...  17.8 us
    ppermute x4, waiting for transfers between devices, shifted(): return lax.ppermute(array, axis, pairs)  16.9 us
    pallas_call x5, Pallas kernels, transposed_dot(): pl.pallas_call(transposed_dot_kernel, out_shape=jax.ShapeDtypeStruct(valu...  11.4 us
    ppermute x4, starting transfers between devices, shifted(): return lax.ppermute(array, axis, pairs)  5.57 us
  transfers between devices with their start and end apart: 34, of which 34 were waited for; matrix products, arithmetic and copies ran while one was open for 0% of the time, Pallas kernels for 0%

profile of v2, /device:TPU:7, one launch (start us, length us, event | category | flops | bytes accessed | tf_op | source)
XLA Modules:
  0.0 205.4 jit_solution(9976929611468270016)
XLA Ops:
  3.2 3.4 %copy-done = bf16[1,1,2048,2048]{3,2,1,0:T(8,128)(2,1)S(1)} copy-done((bf16[1,1,2048,2048]{3,2,1,0:T(8,128)(2,1)S(1)}, bf16[1,1,2048,2048]{3,2,1,0:T(8,128)(2,1)}, u32[]{:S(2)}) %copy-start) | copy-done | bytes 8388632
  9.1 1.8 collective-permute-done.1.partner_ref
  10.9 3.4 %copy-done.1 = bf16[1,1,2048,2048]{3,2,1,0:T(8,128)(2,1)S(1)} copy-done((bf16[1,1,2048,2048]{3,2,1,0:T(8,128)(2,1)S(1)}, bf16[1,1,2048,2048]{3,2,1,0:T(8,128)(2,1)}, u32[]{:S(2)}) %copy-start.1) | copy-done | bytes 8388632
  15.5 2.3 %collective-permute-start.2 = (bf16[16,2048]{1,0:T(8,128)(2,1)S(1)}, bf16[16,2048]{1,0:T(8,128)(2,1)S(1)}, u32[]{:S(2)}, u32[]{:S(2)}) collective-permute-start(bf16[16,2048]{1,0:T(8,128)(2,1)S(1)} %shard_map.38.values_ref), channel_id=1, source_target_pairs={{0,4},{4,0},{1,5},{5,1},{2,6},{6,2},{3,7},{7,3},{8,12},{12,8},{9,1... | collective-permute-start | bytes 196616 | tf_op jit(solution)/shard_map/ppermute | solution.py:22
  17.8 1.7 collective-permute-done.2.partner_ref
  19.5 3.4 %copy-done.2 = bf16[1,1,2048,2048]{3,2,1,0:T(8,128)(2,1)S(1)} copy-done((bf16[1,1,2048,2048]{3,2,1,0:T(8,128)(2,1)S(1)}, bf16[1,1,2048,2048]{3,2,1,0:T(8,128)(2,1)}, u32[]{:S(2)}) %copy-start.2) | copy-done | bytes 8388632
  24.1 2.3 %shard_map.40 = bf16[16,2048]{1,0:T(8,128)(2,1)S(1)} custom-call(bf16[16,2048]{1,0:T(8,128)(2,1)S(1)} %shard_map.39.values_ref, bf16[2048,2048]{1,0:T(8,128)(2,1)S(1)} %bitcast.25), custom_call_target="tpu_custom_call" | custom-call | flops 134217728 | bytes 8585216 | tf_op jit(solution)/shard_map/pallas_call | solution.py:80
  26.4 2.4 %collective-permute-start.3 = (bf16[16,2048]{1,0:T(8,128)(2,1)S(1)}, bf16[16,2048]{1,0:T(8,128)(2,1)S(1)}, u32[]{:S(2)}, u32[]{:S(2)}) collective-permute-start(bf16[16,2048]{1,0:T(8,128)(2,1)S(1)} %shard_map.40), channel_id=1, source_target_pairs={{0,4},{4,0},{1,5},{5,1},{2,6},{6,2},{3,7},{7,3},{8,12},{12,8},{9,1... | collective-permute-start | bytes 196616 | tf_op jit(solution)/shard_map/ppermute | solution.py:22
  28.8 1.7 collective-permute-done.3
  30.4 1.9 collective-permute-start.4
  32.3 1.9 collective-permute-done.4
  34.3 4.4 %collective-permute-start.5 = (bf16[16,2048]{1,0:T(8,128)(2,1)S(1)}, bf16[16,2048]{1,0:T(8,128)(2,1)S(1)}, u32[]{:S(2)}, u32[]{:S(2)}) collective-permute-start(bf16[16,2048]{1,0:T(8,128)(2,1)S(1)} %fusion.6), channel_id=1, source_target_pairs={{0,1},{1,0},{2,3},{3,2},{4,5},{5,4},{6,7},{7,6},{8,9},{9,8},{10,11... | collective-permute-start | bytes 196616 | tf_op jit(solution)/shard_map/ppermute | solution.py:22
  41.0 3.7 %collective-permute-done.6 = bf16[16,2048]{1,0:T(8,128)(2,1)S(1)} collective-permute-done((bf16[16,2048]{1,0:T(8,128)(2,1)S(1)}, bf16[16,2048]{1,0:T(8,128)(2,1)S(1)}, u32[]{:S(2)}, u32[]{:S(2)}) %collective-permute-start.6) | collective-permute-done | bytes 65568 | tf_op jit(solution)/shard_map/ppermute | solution.py:28
  44.7 1.6 collective-permute-start.7
  47.2 3.4 %copy-done.3 = bf16[1,1,2048,2048]{3,2,1,0:T(8,128)(2,1)S(1)} copy-done((bf16[1,1,2048,2048]{3,2,1,0:T(8,128)(2,1)S(1)}, bf16[1,1,2048,2048]{3,2,1,0:T(8,128)(2,1)}, u32[]{:S(2)}) %copy-start.3) | copy-done | bytes 8388632
  53.3 1.7 collective-permute-done.8.partner_ref
  55.0 3.4 %copy-done.4 = bf16[1,1,2048,2048]{3,2,1,0:T(8,128)(2,1)S(1)} copy-done((bf16[1,1,2048,2048]{3,2,1,0:T(8,128)(2,1)S(1)}, bf16[1,1,2048,2048]{3,2,1,0:T(8,128)(2,1)}, u32[]{:S(2)}) %copy-start.4) | copy-done | bytes 8388632
  59.5 3.4 %collective-permute-start.9 = (bf16[16,2048]{1,0:T(8,128)(2,1)S(1)}, bf16[16,2048]{1,0:T(8,128)(2,1)S(1)}, u32[]{:S(2)}, u32[]{:S(2)}) collective-permute-start(bf16[16,2048]{1,0:T(8,128)(2,1)S(1)} %shard_map.42.values_ref), channel_id=1, source_target_pairs={{0,4},{4,0},{1,5},{5,1},{2,6},{6,2},{3,7},{7,3},{8,12},{12,8},{9,1... | collective-permute-start | bytes 196616 | tf_op jit(solution)/shard_map/ppermute | solution.py:22
  62.9 1.7 collective-permute-done.9.partner_ref
  65.7 2.3 %shard_map.44 = bf16[16,2048]{1,0:T(8,128)(2,1)S(1)} custom-call(bf16[16,2048]{1,0:T(8,128)(2,1)S(1)} %shard_map.43.values_ref, bf16[2048,2048]{1,0:T(8,128)(2,1)S(1)} %bitcast.29), custom_call_target="tpu_custom_call" | custom-call | flops 134217728 | bytes 8585216 | tf_op jit(solution)/shard_map/pallas_call | solution.py:80
  68.0 2.5 %collective-permute-start.10 = (bf16[16,2048]{1,0:T(8,128)(2,1)S(1)}, bf16[16,2048]{1,0:T(8,128)(2,1)S(1)}, u32[]{:S(2)}, u32[]{:S(2)}) collective-permute-start(bf16[16,2048]{1,0:T(8,128)(2,1)S(1)} %shard_map.44), channel_id=1, source_target_pairs={{0,4},{4,0},{1,5},{5,1},{2,6},{6,2},{3,7},{7,3},{8,12},{12,8},{9,1... | collective-permute-start | bytes 196616 | tf_op jit(solution)/shard_map/ppermute | solution.py:22
  70.5 1.7 collective-permute-done.10
  72.2 1.7 collective-permute-start.11
  73.9 1.7 collective-permute-done.11
  75.6 4.2 %collective-permute-start.12 = (bf16[16,2048]{1,0:T(8,128)(2,1)S(1)}, bf16[16,2048]{1,0:T(8,128)(2,1)S(1)}, u32[]{:S(2)}, u32[]{:S(2)}) collective-permute-start(bf16[16,2048]{1,0:T(8,128)(2,1)S(1)} %fusion.18), channel_id=1, source_target_pairs={{0,1},{1,0},{2,3},{3,2},{4,5},{5,4},{6,7},{7,6},{8,9},{9,8},{10,11... | collective-permute-start | bytes 196616 | tf_op jit(solution)/shard_map/ppermute | solution.py:22
  82.2 3.5 %collective-permute-done.13 = bf16[16,2048]{1,0:T(8,128)(2,1)S(1)} collective-permute-done((bf16[16,2048]{1,0:T(8,128)(2,1)S(1)}, bf16[16,2048]{1,0:T(8,128)(2,1)S(1)}, u32[]{:S(2)}, u32[]{:S(2)}) %collective-permute-start.13) | collective-permute-done | bytes 65568 | tf_op jit(solution)/shard_map/ppermute | solution.py:28
  88.2 3.4 %copy-done.5 = bf16[1,1,2048,2048]{3,2,1,0:T(8,128)(2,1)S(1)} copy-done((bf16[1,1,2048,2048]{3,2,1,0:T(8,128)(2,1)S(1)}, bf16[1,1,2048,2048]{3,2,1,0:T(8,128)(2,1)}, u32[]{:S(2)}) %copy-start.5) | copy-done | bytes 8388632
  92.8 1.6 collective-permute-start.15
  94.4 1.7 collective-permute-done.15.partner_ref
  96.1 3.4 %copy-done.6 = bf16[1,1,2048,2048]{3,2,1,0:T(8,128)(2,1)S(1)} copy-done((bf16[1,1,2048,2048]{3,2,1,0:T(8,128)(2,1)S(1)}, bf16[1,1,2048,2048]{3,2,1,0:T(8,128)(2,1)}, u32[]{:S(2)}) %copy-start.6) | copy-done | bytes 8388632
  100.6 3.1 %collective-permute-start.16 = (bf16[16,2048]{1,0:T(8,128)(2,1)S(1)}, bf16[16,2048]{1,0:T(8,128)(2,1)S(1)}, u32[]{:S(2)}, u32[]{:S(2)}) collective-permute-start(bf16[16,2048]{1,0:T(8,128)(2,1)S(1)} %shard_map.46.values_ref), channel_id=1, source_target_pairs={{0,4},{4,0},{1,5},{5,1},{2,6},{6,2},{3,7},{7,3},{8,12},{12,8},{9,1... | collective-permute-start | bytes 196616 | tf_op jit(solution)/shard_map/ppermute | solution.py:22
  103.8 1.7 collective-permute-done.16.partner_ref
  106.6 2.3 %shard_map.48 = bf16[16,2048]{1,0:T(8,128)(2,1)S(1)} custom-call(bf16[16,2048]{1,0:T(8,128)(2,1)S(1)} %shard_map.47.values_ref, bf16[2048,2048]{1,0:T(8,128)(2,1)S(1)} %bitcast.33), custom_call_target="tpu_custom_call" | custom-call | flops 134217728 | bytes 8585216 | tf_op jit(solution)/shard_map/pallas_call | solution.py:80
  108.9 2.5 %collective-permute-start.17 = (bf16[16,2048]{1,0:T(8,128)(2,1)S(1)}, bf16[16,2048]{1,0:T(8,128)(2,1)S(1)}, u32[]{:S(2)}, u32[]{:S(2)}) collective-permute-start(bf16[16,2048]{1,0:T(8,128)(2,1)S(1)} %shard_map.48), channel_id=1, source_target_pairs={{0,4},{4,0},{1,5},{5,1},{2,6},{6,2},{3,7},{7,3},{8,12},{12,8},{9,1... | collective-permute-start | bytes 196616 | tf_op jit(solution)/shard_map/ppermute | solution.py:22
  111.4 1.7 collective-permute-done.17
  113.1 1.7 collective-permute-start.18
  114.7 1.7 collective-permute-done.18
  116.4 4.2 %collective-permute-start.19 = (bf16[16,2048]{1,0:T(8,128)(2,1)S(1)}, bf16[16,2048]{1,0:T(8,128)(2,1)S(1)}, u32[]{:S(2)}, u32[]{:S(2)}) collective-permute-start(bf16[16,2048]{1,0:T(8,128)(2,1)S(1)} %fusion.30), channel_id=1, source_target_pairs={{0,1},{1,0},{2,3},{3,2},{4,5},{5,4},{6,7},{7,6},{8,9},{9,8},{10,11... | collective-permute-start | bytes 196616 | tf_op jit(solution)/shard_map/ppermute | solution.py:22
  122.9 4.8 %collective-permute-done.20 = bf16[16,2048]{1,0:T(8,128)(2,1)S(1)} collective-permute-done((bf16[16,2048]{1,0:T(8,128)(2,1)S(1)}, bf16[16,2048]{1,0:T(8,128)(2,1)S(1)}, u32[]{:S(2)}, u32[]{:S(2)}) %collective-permute-start.20) | collective-permute-done | bytes 65568 | tf_op jit(solution)/shard_map/ppermute | solution.py:28
  129.6 3.4 %copy-done.7 = bf16[1,1,2048,2048]{3,2,1,0:T(8,128)(2,1)S(1)} copy-done((bf16[1,1,2048,2048]{3,2,1,0:T(8,128)(2,1)S(1)}, bf16[1,1,2048,2048]{3,2,1,0:T(8,128)(2,1)}, u32[]{:S(2)}) %copy-start.7) | copy-done | bytes 8388632
  134.2 1.6 collective-permute-start.22
  135.8 1.7 collective-permute-done.22.partner_ref
  137.4 3.4 %copy-done.8 = bf16[1,1,2048,2048]{3,2,1,0:T(8,128)(2,1)S(1)} copy-done((bf16[1,1,2048,2048]{3,2,1,0:T(8,128)(2,1)S(1)}, bf16[1,1,2048,2048]{3,2,1,0:T(8,128)(2,1)}, u32[]{:S(2)}) %copy-start.8) | copy-done | bytes 8388632
  142.0 3.1 %collective-permute-start.23 = (bf16[16,2048]{1,0:T(8,128)(2,1)S(1)}, bf16[16,2048]{1,0:T(8,128)(2,1)S(1)}, u32[]{:S(2)}, u32[]{:S(2)}) collective-permute-start(bf16[16,2048]{1,0:T(8,128)(2,1)S(1)} %shard_map.50.values_ref), channel_id=1, source_target_pairs={{0,4},{4,0},{1,5},{5,1},{2,6},{6,2},{3,7},{7,3},{8,12},{12,8},{9,1... | collective-permute-start | bytes 196616 | tf_op jit(solution)/shard_map/ppermute | solution.py:22
  145.1 1.7 collective-permute-done.23.partner_ref
  148.0 2.3 %shard_map.52 = bf16[16,2048]{1,0:T(8,128)(2,1)S(1)} custom-call(bf16[16,2048]{1,0:T(8,128)(2,1)S(1)} %shard_map.51.values_ref, bf16[2048,2048]{1,0:T(8,128)(2,1)S(1)} %bitcast.37), custom_call_target="tpu_custom_call" | custom-call | flops 134217728 | bytes 8585216 | tf_op jit(solution)/shard_map/pallas_call | solution.py:80
  150.3 2.5 %collective-permute-start.24 = (bf16[16,2048]{1,0:T(8,128)(2,1)S(1)}, bf16[16,2048]{1,0:T(8,128)(2,1)S(1)}, u32[]{:S(2)}, u32[]{:S(2)}) collective-permute-start(bf16[16,2048]{1,0:T(8,128)(2,1)S(1)} %shard_map.52), channel_id=1, source_target_pairs={{0,4},{4,0},{1,5},{5,1},{2,6},{6,2},{3,7},{7,3},{8,12},{12,8},{9,1... | collective-permute-start | bytes 196616 | tf_op jit(solution)/shard_map/ppermute | solution.py:22
  152.7 1.7 collective-permute-done.24
  154.4 1.7 collective-permute-start.25
  156.1 1.7 collective-permute-done.25
  157.8 4.2 %collective-permute-start.26 = (bf16[16,2048]{1,0:T(8,128)(2,1)S(1)}, bf16[16,2048]{1,0:T(8,128)(2,1)S(1)}, u32[]{:S(2)}, u32[]{:S(2)}) collective-permute-start(bf16[16,2048]{1,0:T(8,128)(2,1)S(1)} %fusion.42), channel_id=1, source_target_pairs={{0,1},{1,0},{2,3},{3,2},{4,5},{5,4},{6,7},{7,6},{8,9},{9,8},{10,11... | collective-permute-start | bytes 196616 | tf_op jit(solution)/shard_map/ppermute | solution.py:22
  164.5 5.0 %collective-permute-done.27 = bf16[16,2048]{1,0:T(8,128)(2,1)S(1)} collective-permute-done((bf16[16,2048]{1,0:T(8,128)(2,1)S(1)}, bf16[16,2048]{1,0:T(8,128)(2,1)S(1)}, u32[]{:S(2)}, u32[]{:S(2)}) %collective-permute-start.27) | collective-permute-done | bytes 65568 | tf_op jit(solution)/shard_map/ppermute | solution.py:28
  171.4 3.4 %copy-done.9 = bf16[1,1,2048,2048]{3,2,1,0:T(8,128)(2,1)S(1)} copy-done((bf16[1,1,2048,2048]{3,2,1,0:T(8,128)(2,1)S(1)}, bf16[1,1,2048,2048]{3,2,1,0:T(8,128)(2,1)}, u32[]{:S(2)}) %copy-start.9) | copy-done | bytes 8388632
  176.0 1.6 collective-permute-start.29
  177.6 1.7 collective-permute-done.29.partner_ref
  179.2 3.4 %copy-done.10 = bf16[1,1,2048,2048]{3,2,1,0:T(8,128)(2,1)S(1)} copy-done((bf16[1,1,2048,2048]{3,2,1,0:T(8,128)(2,1)S(1)}, bf16[1,1,2048,2048]{3,2,1,0:T(8,128)(2,1)}, u32[]{:S(2)}) %copy-start.10) | copy-done | bytes 8388632
  183.8 3.1 %collective-permute-start.30 = (bf16[16,2048]{1,0:T(8,128)(2,1)S(1)}, bf16[16,2048]{1,0:T(8,128)(2,1)S(1)}, u32[]{:S(2)}, u32[]{:S(2)}) collective-permute-start(bf16[16,2048]{1,0:T(8,128)(2,1)S(1)} %shard_map.54.values_ref), channel_id=1, source_target_pairs={{0,4},{4,0},{1,5},{5,1},{2,6},{6,2},{3,7},{7,3},{8,12},{12,8},{9,1... | collective-permute-start | bytes 196616 | tf_op jit(solution)/shard_map/ppermute | solution.py:22
  186.9 1.7 collective-permute-done.30.partner_ref
  189.8 2.3 %shard_map.56 = bf16[16,2048]{1,0:T(8,128)(2,1)S(1)} custom-call(bf16[16,2048]{1,0:T(8,128)(2,1)S(1)} %shard_map.55.values_ref, bf16[2048,2048]{1,0:T(8,128)(2,1)S(1)} %bitcast.41), custom_call_target="tpu_custom_call" | custom-call | flops 134217728 | bytes 8585216 | tf_op jit(solution)/shard_map/pallas_call | solution.py:80
  192.0 2.5 %collective-permute-start.31 = (bf16[16,2048]{1,0:T(8,128)(2,1)S(1)}, bf16[16,2048]{1,0:T(8,128)(2,1)S(1)}, u32[]{:S(2)}, u32[]{:S(2)}) collective-permute-start(bf16[16,2048]{1,0:T(8,128)(2,1)S(1)} %shard_map.56), channel_id=1, source_target_pairs={{0,4},{4,0},{1,5},{5,1},{2,6},{6,2},{3,7},{7,3},{8,12},{12,8},{9,1... | collective-permute-start | bytes 196616 | tf_op jit(solution)/shard_map/ppermute | solution.py:22
  194.5 1.7 collective-permute-done.31
  196.2 1.7 collective-permute-start.32
  197.9 1.7 collective-permute-done.32
  199.6 4.2 %collective-permute-start.33 = (bf16[16,2048]{1,0:T(8,128)(2,1)S(1)}, bf16[16,2048]{1,0:T(8,128)(2,1)S(1)}, u32[]{:S(2)}, u32[]{:S(2)}) collective-permute-start(bf16[16,2048]{1,0:T(8,128)(2,1)S(1)} %fusion.54), channel_id=1, source_target_pairs={{0,1},{1,0},{2,3},{3,2},{4,5},{5,4},{6,7},{7,6},{8,9},{9,8},{10,11... | collective-permute-start | bytes 196616 | tf_op jit(solution)/shard_map/ppermute | solution.py:22
  (76 shorter events, 42.5 us)
Async XLA Ops:
  1.6 1.6 collective-permute-start
  3.2 3.4 %copy-start = (bf16[1,1,2048,2048]{3,2,1,0:T(8,128)(2,1)S(1)}, bf16[1,1,2048,2048]{3,2,1,0:T(8,128)(2,1)}, u32[]{:S(2)}) copy-start(bf16[1,1,2048,2048]{3,2,1,0:T(8,128)(2,1)} %param.5) | copy-start | bytes 25165828
  7.8 3.1 %collective-permute-start.1 = (bf16[16,2048]{1,0:T(8,128)(2,1)S(1)}, bf16[16,2048]{1,0:T(8,128)(2,1)S(1)}, u32[]{:S(2)}, u32[]{:S(2)}) collective-permute-start(bf16[16,2048]{1,0:T(8,128)(2,1)S(1)} %shard_map.37.values_ref), channel_id=1, source_target_pairs={{0,2},{2,0},{1,3},{3,1},{4,6},{6,4},{5,7},{7,5},{8,10},{10,8},{9,1... | collective-permute-start | bytes 196616 | tf_op jit(solution)/shard_map/ppermute | solution.py:22
  10.9 3.4 %copy-start.1 = (bf16[1,1,2048,2048]{3,2,1,0:T(8,128)(2,1)S(1)}, bf16[1,1,2048,2048]{3,2,1,0:T(8,128)(2,1)}, u32[]{:S(2)}) copy-start(bf16[1,1,2048,2048]{3,2,1,0:T(8,128)(2,1)} %param.5) | copy-start | bytes 25165828
  15.5 4.0 %collective-permute-start.2 = (bf16[16,2048]{1,0:T(8,128)(2,1)S(1)}, bf16[16,2048]{1,0:T(8,128)(2,1)S(1)}, u32[]{:S(2)}, u32[]{:S(2)}) collective-permute-start(bf16[16,2048]{1,0:T(8,128)(2,1)S(1)} %shard_map.38.values_ref), channel_id=1, source_target_pairs={{0,4},{4,0},{1,5},{5,1},{2,6},{6,2},{3,7},{7,3},{8,12},{12,8},{9,1... | collective-permute-start | bytes 196616 | tf_op jit(solution)/shard_map/ppermute | solution.py:22
  19.5 3.4 %copy-start.2 = (bf16[1,1,2048,2048]{3,2,1,0:T(8,128)(2,1)S(1)}, bf16[1,1,2048,2048]{3,2,1,0:T(8,128)(2,1)}, u32[]{:S(2)}) copy-start(bf16[1,1,2048,2048]{3,2,1,0:T(8,128)(2,1)} %param.5) | copy-start | bytes 25165828
  22.9 21.8 %copy-start.11 = (bf16[1,1,32,2048]{3,2,1,0:T(8,128)(2,1)S(1)}, bf16[1,1,32,2048]{3,2,1,0:T(8,128)(2,1)}, u32[]{:S(2)}) copy-start(bf16[1,1,32,2048]{3,2,1,0:T(8,128)(2,1)} %param.3) | copy-start | bytes 393220
  22.9 21.8 %copy-start.12 = (f32[1,1,2048]{2,1,0:T(1,128)S(1)}, f32[1,1,2048]{2,1,0:T(1,128)}, u32[]{:S(2)}) copy-start(f32[1,1,2048]{2,1,0:T(1,128)} %param.4) | copy-start | bytes 24580
  26.4 4.0 %collective-permute-start.3 = (bf16[16,2048]{1,0:T(8,128)(2,1)S(1)}, bf16[16,2048]{1,0:T(8,128)(2,1)S(1)}, u32[]{:S(2)}, u32[]{:S(2)}) collective-permute-start(bf16[16,2048]{1,0:T(8,128)(2,1)S(1)} %shard_map.40), channel_id=1, source_target_pairs={{0,4},{4,0},{1,5},{5,1},{2,6},{6,2},{3,7},{7,3},{8,12},{12,8},{9,1... | collective-permute-start | bytes 196616 | tf_op jit(solution)/shard_map/ppermute | solution.py:22
  30.4 3.8 %collective-permute-start.4 = (bf16[16,2048]{1,0:T(8,128)(2,1)S(1)}, bf16[16,2048]{1,0:T(8,128)(2,1)S(1)}, u32[]{:S(2)}, u32[]{:S(2)}) collective-permute-start(bf16[16,2048]{1,0:T(8,128)(2,1)S(1)} %fusion.2), channel_id=1, source_target_pairs={{0,2},{2,0},{1,3},{3,1},{4,6},{6,4},{5,7},{7,5},{8,10},{10,8},{9,1... | collective-permute-start | bytes 196616 | tf_op jit(solution)/shard_map/ppermute | solution.py:22
  34.3 5.3 %collective-permute-start.5 = (bf16[16,2048]{1,0:T(8,128)(2,1)S(1)}, bf16[16,2048]{1,0:T(8,128)(2,1)S(1)}, u32[]{:S(2)}, u32[]{:S(2)}) collective-permute-start(bf16[16,2048]{1,0:T(8,128)(2,1)S(1)} %fusion.6), channel_id=1, source_target_pairs={{0,1},{1,0},{2,3},{3,2},{4,5},{5,4},{6,7},{7,6},{8,9},{9,8},{10,11... | collective-permute-start | bytes 196616 | tf_op jit(solution)/shard_map/ppermute | solution.py:22
  39.7 5.0 %collective-permute-start.6 = (bf16[16,2048]{1,0:T(8,128)(2,1)S(1)}, bf16[16,2048]{1,0:T(8,128)(2,1)S(1)}, u32[]{:S(2)}, u32[]{:S(2)}) collective-permute-start(bf16[16,2048]{1,0:T(8,128)(2,1)S(1)} %get-tuple-element.12), channel_id=1, source_target_pairs={{0,8},{8,16},{16,24},{1,9},{9,17},{17,25},{2,10},{10,18},{18,26},{... | collective-permute-start | bytes 196616 | tf_op jit(solution)/shard_map/ppermute | solution.py:28
  44.7 2.5 %collective-permute-start.7 = (bf16[16,2048]{1,0:T(8,128)(2,1)S(1)}, bf16[16,2048]{1,0:T(8,128)(2,1)S(1)}, u32[]{:S(2)}, u32[]{:S(2)}) collective-permute-start(bf16[16,2048]{1,0:T(8,128)(2,1)S(1)} %fusion.63.values_ref), channel_id=1, source_target_pairs={{0,1},{1,0},{2,3},{3,2},{4,5},{5,4},{6,7},{7,6},{8,9},{9,8},{10,11... | collective-permute-start | bytes 196616 | tf_op jit(solution)/shard_map/ppermute | solution.py:22
  47.2 3.4 %copy-start.3 = (bf16[1,1,2048,2048]{3,2,1,0:T(8,128)(2,1)S(1)}, bf16[1,1,2048,2048]{3,2,1,0:T(8,128)(2,1)}, u32[]{:S(2)}) copy-start(bf16[1,1,2048,2048]{3,2,1,0:T(8,128)(2,1)} %param.5) | copy-start | bytes 25165828
  51.8 3.2 %collective-permute-start.8 = (bf16[16,2048]{1,0:T(8,128)(2,1)S(1)}, bf16[16,2048]{1,0:T(8,128)(2,1)S(1)}, u32[]{:S(2)}, u32[]{:S(2)}) collective-permute-start(bf16[16,2048]{1,0:T(8,128)(2,1)S(1)} %shard_map.41.values_ref), channel_id=1, source_target_pairs={{0,2},{2,0},{1,3},{3,1},{4,6},{6,4},{5,7},{7,5},{8,10},{10,8},{9,1... | collective-permute-start | bytes 196616 | tf_op jit(solution)/shard_map/ppermute | solution.py:22
  55.0 3.4 %copy-start.4 = (bf16[1,1,2048,2048]{3,2,1,0:T(8,128)(2,1)S(1)}, bf16[1,1,2048,2048]{3,2,1,0:T(8,128)(2,1)}, u32[]{:S(2)}) copy-start(bf16[1,1,2048,2048]{3,2,1,0:T(8,128)(2,1)} %param.5) | copy-start | bytes 25165828
  59.5 5.0 %collective-permute-start.9 = (bf16[16,2048]{1,0:T(8,128)(2,1)S(1)}, bf16[16,2048]{1,0:T(8,128)(2,1)S(1)}, u32[]{:S(2)}, u32[]{:S(2)}) collective-permute-start(bf16[16,2048]{1,0:T(8,128)(2,1)S(1)} %shard_map.42.values_ref), channel_id=1, source_target_pairs={{0,4},{4,0},{1,5},{5,1},{2,6},{6,2},{3,7},{7,3},{8,12},{12,8},{9,1... | collective-permute-start | bytes 196616 | tf_op jit(solution)/shard_map/ppermute | solution.py:22
  68.0 4.1 %collective-permute-start.10 = (bf16[16,2048]{1,0:T(8,128)(2,1)S(1)}, bf16[16,2048]{1,0:T(8,128)(2,1)S(1)}, u32[]{:S(2)}, u32[]{:S(2)}) collective-permute-start(bf16[16,2048]{1,0:T(8,128)(2,1)S(1)} %shard_map.44), channel_id=1, source_target_pairs={{0,4},{4,0},{1,5},{5,1},{2,6},{6,2},{3,7},{7,3},{8,12},{12,8},{9,1... | collective-permute-start | bytes 196616 | tf_op jit(solution)/shard_map/ppermute | solution.py:22
  72.2 3.3 %collective-permute-start.11 = (bf16[16,2048]{1,0:T(8,128)(2,1)S(1)}, bf16[16,2048]{1,0:T(8,128)(2,1)S(1)}, u32[]{:S(2)}, u32[]{:S(2)}) collective-permute-start(bf16[16,2048]{1,0:T(8,128)(2,1)S(1)} %fusion.14), channel_id=1, source_target_pairs={{0,2},{2,0},{1,3},{3,1},{4,6},{6,4},{5,7},{7,5},{8,10},{10,8},{9,1... | collective-permute-start | bytes 196616 | tf_op jit(solution)/shard_map/ppermute | solution.py:22
  75.6 5.1 %collective-permute-start.12 = (bf16[16,2048]{1,0:T(8,128)(2,1)S(1)}, bf16[16,2048]{1,0:T(8,128)(2,1)S(1)}, u32[]{:S(2)}, u32[]{:S(2)}) collective-permute-start(bf16[16,2048]{1,0:T(8,128)(2,1)S(1)} %fusion.18), channel_id=1, source_target_pairs={{0,1},{1,0},{2,3},{3,2},{4,5},{5,4},{6,7},{7,6},{8,9},{9,8},{10,11... | collective-permute-start | bytes 196616 | tf_op jit(solution)/shard_map/ppermute | solution.py:22
  80.7 5.0 %collective-permute-start.13 = (bf16[16,2048]{1,0:T(8,128)(2,1)S(1)}, bf16[16,2048]{1,0:T(8,128)(2,1)S(1)}, u32[]{:S(2)}, u32[]{:S(2)}) collective-permute-start(bf16[16,2048]{1,0:T(8,128)(2,1)S(1)} %get-tuple-element.10), channel_id=1, source_target_pairs={{0,8},{8,16},{16,24},{1,9},{9,17},{17,25},{2,10},{10,18},{18,26},{... | collective-permute-start | bytes 196616 | tf_op jit(solution)/shard_map/ppermute | solution.py:28
  85.8 2.5 %collective-permute-start.14 = (bf16[16,2048]{1,0:T(8,128)(2,1)S(1)}, bf16[16,2048]{1,0:T(8,128)(2,1)S(1)}, u32[]{:S(2)}, u32[]{:S(2)}) collective-permute-start(bf16[16,2048]{1,0:T(8,128)(2,1)S(1)} %fusion.62.values_ref), channel_id=1, source_target_pairs={{0,1},{1,0},{2,3},{3,2},{4,5},{5,4},{6,7},{7,6},{8,9},{9,8},{10,11... | collective-permute-start | bytes 196616 | tf_op jit(solution)/shard_map/ppermute | solution.py:22
  88.2 3.4 %copy-start.5 = (bf16[1,1,2048,2048]{3,2,1,0:T(8,128)(2,1)S(1)}, bf16[1,1,2048,2048]{3,2,1,0:T(8,128)(2,1)}, u32[]{:S(2)}) copy-start(bf16[1,1,2048,2048]{3,2,1,0:T(8,128)(2,1)} %param.5) | copy-start | bytes 25165828
  92.8 3.2 %collective-permute-start.15 = (bf16[16,2048]{1,0:T(8,128)(2,1)S(1)}, bf16[16,2048]{1,0:T(8,128)(2,1)S(1)}, u32[]{:S(2)}, u32[]{:S(2)}) collective-permute-start(bf16[16,2048]{1,0:T(8,128)(2,1)S(1)} %shard_map.45.values_ref), channel_id=1, source_target_pairs={{0,2},{2,0},{1,3},{3,1},{4,6},{6,4},{5,7},{7,5},{8,10},{10,8},{9,1... | collective-permute-start | bytes 196616 | tf_op jit(solution)/shard_map/ppermute | solution.py:22
  96.1 3.4 %copy-start.6 = (bf16[1,1,2048,2048]{3,2,1,0:T(8,128)(2,1)S(1)}, bf16[1,1,2048,2048]{3,2,1,0:T(8,128)(2,1)}, u32[]{:S(2)}) copy-start(bf16[1,1,2048,2048]{3,2,1,0:T(8,128)(2,1)} %param.5) | copy-start | bytes 25165828
  100.6 4.8 %collective-permute-start.16 = (bf16[16,2048]{1,0:T(8,128)(2,1)S(1)}, bf16[16,2048]{1,0:T(8,128)(2,1)S(1)}, u32[]{:S(2)}, u32[]{:S(2)}) collective-permute-start(bf16[16,2048]{1,0:T(8,128)(2,1)S(1)} %shard_map.46.values_ref), channel_id=1, source_target_pairs={{0,4},{4,0},{1,5},{5,1},{2,6},{6,2},{3,7},{7,3},{8,12},{12,8},{9,1... | collective-permute-start | bytes 196616 | tf_op jit(solution)/shard_map/ppermute | solution.py:22
  108.9 4.1 %collective-permute-start.17 = (bf16[16,2048]{1,0:T(8,128)(2,1)S(1)}, bf16[16,2048]{1,0:T(8,128)(2,1)S(1)}, u32[]{:S(2)}, u32[]{:S(2)}) collective-permute-start(bf16[16,2048]{1,0:T(8,128)(2,1)S(1)} %shard_map.48), channel_id=1, source_target_pairs={{0,4},{4,0},{1,5},{5,1},{2,6},{6,2},{3,7},{7,3},{8,12},{12,8},{9,1... | collective-permute-start | bytes 196616 | tf_op jit(solution)/shard_map/ppermute | solution.py:22
  113.1 3.3 %collective-permute-start.18 = (bf16[16,2048]{1,0:T(8,128)(2,1)S(1)}, bf16[16,2048]{1,0:T(8,128)(2,1)S(1)}, u32[]{:S(2)}, u32[]{:S(2)}) collective-permute-start(bf16[16,2048]{1,0:T(8,128)(2,1)S(1)} %fusion.26), channel_id=1, source_target_pairs={{0,2},{2,0},{1,3},{3,1},{4,6},{6,4},{5,7},{7,5},{8,10},{10,8},{9,1... | collective-permute-start | bytes 196616 | tf_op jit(solution)/shard_map/ppermute | solution.py:22
  116.4 5.1 %collective-permute-start.19 = (bf16[16,2048]{1,0:T(8,128)(2,1)S(1)}, bf16[16,2048]{1,0:T(8,128)(2,1)S(1)}, u32[]{:S(2)}, u32[]{:S(2)}) collective-permute-start(bf16[16,2048]{1,0:T(8,128)(2,1)S(1)} %fusion.30), channel_id=1, source_target_pairs={{0,1},{1,0},{2,3},{3,2},{4,5},{5,4},{6,7},{7,6},{8,9},{9,8},{10,11... | collective-permute-start | bytes 196616 | tf_op jit(solution)/shard_map/ppermute | solution.py:22
  121.6 6.1 %collective-permute-start.20 = (bf16[16,2048]{1,0:T(8,128)(2,1)S(1)}, bf16[16,2048]{1,0:T(8,128)(2,1)S(1)}, u32[]{:S(2)}, u32[]{:S(2)}) collective-permute-start(bf16[16,2048]{1,0:T(8,128)(2,1)S(1)} %get-tuple-element.8), channel_id=1, source_target_pairs={{0,8},{8,16},{16,24},{1,9},{9,17},{17,25},{2,10},{10,18},{18,26},{... | collective-permute-start | bytes 196616 | tf_op jit(solution)/shard_map/ppermute | solution.py:28
  127.7 1.9 collective-permute-start.21
  129.6 3.4 %copy-start.7 = (bf16[1,1,2048,2048]{3,2,1,0:T(8,128)(2,1)S(1)}, bf16[1,1,2048,2048]{3,2,1,0:T(8,128)(2,1)}, u32[]{:S(2)}) copy-start(bf16[1,1,2048,2048]{3,2,1,0:T(8,128)(2,1)} %param.5) | copy-start | bytes 25165828
  134.2 3.2 %collective-permute-start.22 = (bf16[16,2048]{1,0:T(8,128)(2,1)S(1)}, bf16[16,2048]{1,0:T(8,128)(2,1)S(1)}, u32[]{:S(2)}, u32[]{:S(2)}) collective-permute-start(bf16[16,2048]{1,0:T(8,128)(2,1)S(1)} %shard_map.49.values_ref), channel_id=1, source_target_pairs={{0,2},{2,0},{1,3},{3,1},{4,6},{6,4},{5,7},{7,5},{8,10},{10,8},{9,1... | collective-permute-start | bytes 196616 | tf_op jit(solution)/shard_map/ppermute | solution.py:22
  137.4 3.4 %copy-start.8 = (bf16[1,1,2048,2048]{3,2,1,0:T(8,128)(2,1)S(1)}, bf16[1,1,2048,2048]{3,2,1,0:T(8,128)(2,1)}, u32[]{:S(2)}) copy-start(bf16[1,1,2048,2048]{3,2,1,0:T(8,128)(2,1)} %param.5) | copy-start | bytes 25165828
  142.0 4.8 %collective-permute-start.23 = (bf16[16,2048]{1,0:T(8,128)(2,1)S(1)}, bf16[16,2048]{1,0:T(8,128)(2,1)S(1)}, u32[]{:S(2)}, u32[]{:S(2)}) collective-permute-start(bf16[16,2048]{1,0:T(8,128)(2,1)S(1)} %shard_map.50.values_ref), channel_id=1, source_target_pairs={{0,4},{4,0},{1,5},{5,1},{2,6},{6,2},{3,7},{7,3},{8,12},{12,8},{9,1... | collective-permute-start | bytes 196616 | tf_op jit(solution)/shard_map/ppermute | solution.py:22
  150.3 4.1 %collective-permute-start.24 = (bf16[16,2048]{1,0:T(8,128)(2,1)S(1)}, bf16[16,2048]{1,0:T(8,128)(2,1)S(1)}, u32[]{:S(2)}, u32[]{:S(2)}) collective-permute-start(bf16[16,2048]{1,0:T(8,128)(2,1)S(1)} %shard_map.52), channel_id=1, source_target_pairs={{0,4},{4,0},{1,5},{5,1},{2,6},{6,2},{3,7},{7,3},{8,12},{12,8},{9,1... | collective-permute-start | bytes 196616 | tf_op jit(solution)/shard_map/ppermute | solution.py:22
  154.4 3.3 %collective-permute-start.25 = (bf16[16,2048]{1,0:T(8,128)(2,1)S(1)}, bf16[16,2048]{1,0:T(8,128)(2,1)S(1)}, u32[]{:S(2)}, u32[]{:S(2)}) collective-permute-start(bf16[16,2048]{1,0:T(8,128)(2,1)S(1)} %fusion.38), channel_id=1, source_target_pairs={{0,2},{2,0},{1,3},{3,1},{4,6},{6,4},{5,7},{7,5},{8,10},{10,8},{9,1... | collective-permute-start | bytes 196616 | tf_op jit(solution)/shard_map/ppermute | solution.py:22
  157.8 5.1 %collective-permute-start.26 = (bf16[16,2048]{1,0:T(8,128)(2,1)S(1)}, bf16[16,2048]{1,0:T(8,128)(2,1)S(1)}, u32[]{:S(2)}, u32[]{:S(2)}) collective-permute-start(bf16[16,2048]{1,0:T(8,128)(2,1)S(1)} %fusion.42), channel_id=1, source_target_pairs={{0,1},{1,0},{2,3},{3,2},{4,5},{5,4},{6,7},{7,6},{8,9},{9,8},{10,11... | collective-permute-start | bytes 196616 | tf_op jit(solution)/shard_map/ppermute | solution.py:22
  163.0 6.5 %collective-permute-start.27 = (bf16[16,2048]{1,0:T(8,128)(2,1)S(1)}, bf16[16,2048]{1,0:T(8,128)(2,1)S(1)}, u32[]{:S(2)}, u32[]{:S(2)}) collective-permute-start(bf16[16,2048]{1,0:T(8,128)(2,1)S(1)} %get-tuple-element.6), channel_id=1, source_target_pairs={{0,8},{8,16},{16,24},{1,9},{9,17},{17,25},{2,10},{10,18},{18,26},{... | collective-permute-start | bytes 196616 | tf_op jit(solution)/shard_map/ppermute | solution.py:28
  169.5 1.9 collective-permute-start.28
  171.4 3.4 %copy-start.9 = (bf16[1,1,2048,2048]{3,2,1,0:T(8,128)(2,1)S(1)}, bf16[1,1,2048,2048]{3,2,1,0:T(8,128)(2,1)}, u32[]{:S(2)}) copy-start(bf16[1,1,2048,2048]{3,2,1,0:T(8,128)(2,1)} %param.5) | copy-start | bytes 25165828
  176.0 3.2 %collective-permute-start.29 = (bf16[16,2048]{1,0:T(8,128)(2,1)S(1)}, bf16[16,2048]{1,0:T(8,128)(2,1)S(1)}, u32[]{:S(2)}, u32[]{:S(2)}) collective-permute-start(bf16[16,2048]{1,0:T(8,128)(2,1)S(1)} %shard_map.53.values_ref), channel_id=1, source_target_pairs={{0,2},{2,0},{1,3},{3,1},{4,6},{6,4},{5,7},{7,5},{8,10},{10,8},{9,1... | collective-permute-start | bytes 196616 | tf_op jit(solution)/shard_map/ppermute | solution.py:22
  179.2 3.4 %copy-start.10 = (bf16[1,1,2048,2048]{3,2,1,0:T(8,128)(2,1)S(1)}, bf16[1,1,2048,2048]{3,2,1,0:T(8,128)(2,1)}, u32[]{:S(2)}) copy-start(bf16[1,1,2048,2048]{3,2,1,0:T(8,128)(2,1)} %param.5) | copy-start | bytes 25165828
  183.8 4.8 %collective-permute-start.30 = (bf16[16,2048]{1,0:T(8,128)(2,1)S(1)}, bf16[16,2048]{1,0:T(8,128)(2,1)S(1)}, u32[]{:S(2)}, u32[]{:S(2)}) collective-permute-start(bf16[16,2048]{1,0:T(8,128)(2,1)S(1)} %shard_map.54.values_ref), channel_id=1, source_target_pairs={{0,4},{4,0},{1,5},{5,1},{2,6},{6,2},{3,7},{7,3},{8,12},{12,8},{9,1... | collective-permute-start | bytes 196616 | tf_op jit(solution)/shard_map/ppermute | solution.py:22
  192.0 4.1 %collective-permute-start.31 = (bf16[16,2048]{1,0:T(8,128)(2,1)S(1)}, bf16[16,2048]{1,0:T(8,128)(2,1)S(1)}, u32[]{:S(2)}, u32[]{:S(2)}) collective-permute-start(bf16[16,2048]{1,0:T(8,128)(2,1)S(1)} %shard_map.56), channel_id=1, source_target_pairs={{0,4},{4,0},{1,5},{5,1},{2,6},{6,2},{3,7},{7,3},{8,12},{12,8},{9,1... | collective-permute-start | bytes 196616 | tf_op jit(solution)/shard_map/ppermute | solution.py:22
  196.2 3.3 %collective-permute-start.32 = (bf16[16,2048]{1,0:T(8,128)(2,1)S(1)}, bf16[16,2048]{1,0:T(8,128)(2,1)S(1)}, u32[]{:S(2)}, u32[]{:S(2)}) collective-permute-start(bf16[16,2048]{1,0:T(8,128)(2,1)S(1)} %fusion.50), channel_id=1, source_target_pairs={{0,2},{2,0},{1,3},{3,1},{4,6},{6,4},{5,7},{7,5},{8,10},{10,8},{9,1... | collective-permute-start | bytes 196616 | tf_op jit(solution)/shard_map/ppermute | solution.py:22
  199.6 5.1 %collective-permute-start.33 = (bf16[16,2048]{1,0:T(8,128)(2,1)S(1)}, bf16[16,2048]{1,0:T(8,128)(2,1)S(1)}, u32[]{:S(2)}, u32[]{:S(2)}) collective-permute-start(bf16[16,2048]{1,0:T(8,128)(2,1)S(1)} %fusion.54), channel_id=1, source_target_pairs={{0,1},{1,0},{2,3},{3,2},{4,5},{5,4},{6,7},{7,6},{8,9},{9,8},{10,11... | collective-permute-start | bytes 196616 | tf_op jit(solution)/shard_map/ppermute | solution.py:22

commit v3 on v1

--- a/solution.py
+++ b/solution.py
@@ -110,10 +110,22 @@
         partner = partner_2(values, "lat", bit_level)
         values = mixed_dot(level_sign(lat_index, bit_level, width), values, partner, merge_op)
     values = transposed_dot(values, merge_op)
-    for bit_level in range(levels - 1, -1, -1):
-        partner = partner_2(values, "lat", bit_level)
-        values = haar_pair(values, partner, lat_index, bit_level)
-    return values
+    return pushed_down(values, lat_index, lat_count, levels)
+
+
+def pushed_down(values, lat_index, lat_count, levels):
+    gathered = lax.all_gather(values, "lat", axis=0, tiled=False)
+    bits = [(lat_index >> level) & 1 for level in range(levels)]
+    total = None
+    for other in range(lat_count):
+        parity = 0
+        for level in range(levels):
+            if other >> level & 1:
+                parity = parity ^ bits[level]
+        sign = (1 - 2 * parity).astype(jnp.float32) if other else jnp.float32(1.0)
+        term = sign * gathered[other].astype(jnp.float32)
+        total = term if total is None else total + term
+    return (total * (half_root**levels)).astype(jnp.bfloat16)
 
 
 def on_device(sources, coupling, merge_ops):

time: 189 us -> 260 us (1.38)
  waiting for transfers between devices: 119 us -> 152 us
  local copies, waits for them, and re-layouts: 10.2 us -> 30.5 us
  between operations: 0.2 us -> 13.3 us
  other arithmetic: 3.29 us -> 9.1 us
  starting transfers between devices: 25.4 us -> 21.4 us
  Pallas kernels: 28.5 us -> 31.3 us
    all_gather x0 -> x4, waiting for transfers between devices: none -> 94 us  [pushed_down(): gathered = lax.all_gather(values, 'lat', axis=0, tiled=False)]
    ppermute x24 -> x12, waiting for transfers between devices: 102 us -> 42.5 us  [partner_2(): return lax.ppermute(block, axis, route)]
    unnamed x14 -> x28, local copies, waits for them, and re-layouts: 10.2 us -> 30.5 us
    ppermute x24 -> x12, starting transfers between devices: 21.3 us -> 17.2 us  [partner_2(): return lax.ppermute(block, axis, route)]
    convert_element_type x11 -> x3, other arithmetic: 0.74 us -> 4.47 us  [pushed_down(): return (total * half_root ** levels).astype(jnp.bfloat16)]
    select_n x0 -> x1, other arithmetic: none -> 2.87 us  [on_device(): result = jnp.where(depth_index == sweep_step, solved, result)]
    pallas_call x4, Pallas kernels: 10.2 us -> 12.9 us  [transposed_dot(): pl.pallas_call(transposed_dot_kernel, out_shape=jax.ShapeDtypeStruct(valu...]
  transfers between devices with their start and end apart: 27 -> 19, of which waited for: 27 -> 19; matrix products, arithmetic and copies ran while one was open for 0% -> 0% of each run, Pallas kernels for 0% -> 0%
where the time goes in v3:
time: 260 us; the launch traced here: 258 us
  waiting for transfers between devices  152 us (58%)
  Pallas kernels  31.3 us (12%)
  local copies, waits for them, and re-layouts  30.5 us (12%)
  starting transfers between devices  21.4 us (8%)
  between operations  13.3 us (5%)
  other arithmetic  9.1 us (4%)
    all_gather x4, waiting for transfers between devices, pushed_down(): gathered = lax.all_gather(values, 'lat', axis=0, tiled=False)  94 us
    ppermute x12, waiting for transfers between devices, partner_2(): return lax.ppermute(block, axis, route)  42.5 us
    unnamed x28, local copies, waits for them, and re-layouts  30.5 us
    pallas_call x12, Pallas kernels, mixed_dot(): pl.pallas_call(mixed_dot_kernel, out_shape=jax.ShapeDtypeStruct(values.sh...  18.4 us
    ppermute x12, starting transfers between devices, partner_2(): return lax.ppermute(block, axis, route)  17.2 us
    ppermute x3, waiting for transfers between devices, shifted(): return lax.ppermute(array, axis, pairs)  15.9 us
    pallas_call x4, Pallas kernels, transposed_dot(): pl.pallas_call(transposed_dot_kernel, out_shape=jax.ShapeDtypeStruct(valu...  12.9 us
  transfers between devices with their start and end apart: 19, of which 19 were waited for; matrix products, arithmetic and copies ran while one was open for 0% of the time, Pallas kernels for 0%

profile of v3, /device:TPU:7, one launch (start us, length us, event | category | flops | bytes accessed | tf_op | source)
XLA Modules:
  0.0 257.9 jit_solution(14278668509456527899)
XLA Ops:
  7.2 0.9 fusion.values_ref
  8.2 0.7 collective-permute-start
  8.9 1.0 collective-permute-done.partner_ref
  9.9 3.4 %copy-done = bf16[1,1,2048,2048]{3,2,1,0:T(8,128)(2,1)S(1)} copy-done((bf16[1,1,2048,2048]{3,2,1,0:T(8,128)(2,1)S(1)}, bf16[1,1,2048,2048]{3,2,1,0:T(8,128)(2,1)}, u32[]{:S(2)}) %copy-start) | copy-done | bytes 8388632
  13.3 1.5 shard_map.37.values_ref
  14.8 1.3 collective-permute-start.1
  16.1 3.4 %collective-permute-done.1.partner_ref = bf16[32,2048]{1,0:T(8,128)(2,1)S(1)} collective-permute-done((bf16[32,2048]{1,0:T(8,128)(2,1)S(1)}, bf16[32,2048]{1,0:T(8,128)(2,1)S(1)}, u32[]{:S(2)}, u32[]{:S(2)}) %collective-permute-start.1) | collective-permute-done | bytes 131104 | tf_op jit(solution)/shard_map/ppermute | solution.py:21
  19.5 3.4 %copy-done.1 = bf16[1,1,2048,2048]{3,2,1,0:T(8,128)(2,1)S(1)} copy-done((bf16[1,1,2048,2048]{3,2,1,0:T(8,128)(2,1)S(1)}, bf16[1,1,2048,2048]{3,2,1,0:T(8,128)(2,1)}, u32[]{:S(2)}) %copy-start.1) | copy-done | bytes 8388632
  22.9 1.5 shard_map.38.values_ref
  24.4 2.3 collective-permute-start.2
  26.8 5.8 %collective-permute-done.2.partner_ref = bf16[32,2048]{1,0:T(8,128)(2,1)S(1)} collective-permute-done((bf16[32,2048]{1,0:T(8,128)(2,1)S(1)}, bf16[32,2048]{1,0:T(8,128)(2,1)S(1)}, u32[]{:S(2)}, u32[]{:S(2)}) %collective-permute-start.2) | collective-permute-done | bytes 131104 | tf_op jit(solution)/shard_map/ppermute | solution.py:21
  32.6 3.4 %copy-done.2 = bf16[1,1,2048,2048]{3,2,1,0:T(8,128)(2,1)S(1)} copy-done((bf16[1,1,2048,2048]{3,2,1,0:T(8,128)(2,1)S(1)}, bf16[1,1,2048,2048]{3,2,1,0:T(8,128)(2,1)}, u32[]{:S(2)}) %copy-start.2) | copy-done | bytes 8388632
  36.0 1.5 shard_map.39.values_ref
  37.5 3.2 %shard_map.40 = bf16[32,2048]{1,0:T(8,128)(2,1)} custom-call(bf16[32,2048]{1,0:T(8,128)(2,1)S(1)} %shard_map.39.values_ref, bf16[2048,2048]{1,0:T(8,128)(2,1)S(1)} %bitcast.109), custom_call_target="tpu_custom_call" | custom-call | flops 268435456 | bytes 8781824 | tf_op jit(solution)/shard_map/pallas_call | solution.py:79
  40.8 24.6 %all-gather.9.cloned.1.call-done = bf16[256,2048]{1,0:T(8,128)(2,1)} async-done(((bf16[32,2048]{1,0:T(8,128)(2,1)}), bf16[256,2048]{1,0:T(8,128)(2,1)}) %all-gather.9.cloned.1.call-update) | async-done | bytes 1048592 | tf_op jit(solution)/shard_map/all_gather | solution.py:117
  65.4 1.5 fusion.14
  66.9 1.3 collective-permute-start.3
  68.2 5.4 %collective-permute-done.3 = bf16[32,2048]{1,0:T(8,128)(2,1)S(1)} collective-permute-done((bf16[32,2048]{1,0:T(8,128)(2,1)S(1)}, bf16[32,2048]{1,0:T(8,128)(2,1)S(1)}, u32[]{:S(2)}, u32[]{:S(2)}) %collective-permute-start.3) | collective-permute-done | bytes 131104 | tf_op jit(solution)/shard_map/ppermute | solution.py:27
  73.6 1.2 collective-permute-start.4
  74.8 1.0 collective-permute-done.4.partner_ref
  75.8 3.4 %copy-done.3 = bf16[1,1,2048,2048]{3,2,1,0:T(8,128)(2,1)S(1)} copy-done((bf16[1,1,2048,2048]{3,2,1,0:T(8,128)(2,1)S(1)}, bf16[1,1,2048,2048]{3,2,1,0:T(8,128)(2,1)}, u32[]{:S(2)}) %copy-start.3) | copy-done | bytes 8388632
  79.2 1.5 shard_map.41.values_ref
  80.8 1.3 collective-permute-start.5
  82.1 3.4 %collective-permute-done.5.partner_ref = bf16[32,2048]{1,0:T(8,128)(2,1)S(1)} collective-permute-done((bf16[32,2048]{1,0:T(8,128)(2,1)S(1)}, bf16[32,2048]{1,0:T(8,128)(2,1)S(1)}, u32[]{:S(2)}, u32[]{:S(2)}) %collective-permute-start.5) | collective-permute-done | bytes 131104 | tf_op jit(solution)/shard_map/ppermute | solution.py:21
  85.5 3.4 %copy-done.4 = bf16[1,1,2048,2048]{3,2,1,0:T(8,128)(2,1)S(1)} copy-done((bf16[1,1,2048,2048]{3,2,1,0:T(8,128)(2,1)S(1)}, bf16[1,1,2048,2048]{3,2,1,0:T(8,128)(2,1)}, u32[]{:S(2)}) %copy-start.4) | copy-done | bytes 8388632
  88.9 1.5 shard_map.42.values_ref
  90.4 1.8 collective-permute-start.6
  92.1 6.4 %collective-permute-done.6.partner_ref = bf16[32,2048]{1,0:T(8,128)(2,1)S(1)} collective-permute-done((bf16[32,2048]{1,0:T(8,128)(2,1)S(1)}, bf16[32,2048]{1,0:T(8,128)(2,1)S(1)}, u32[]{:S(2)}, u32[]{:S(2)}) %collective-permute-start.6) | collective-permute-done | bytes 131104 | tf_op jit(solution)/shard_map/ppermute | solution.py:21
  98.5 1.5 shard_map.43.values_ref
  100.0 3.2 %shard_map.44 = bf16[32,2048]{1,0:T(8,128)(2,1)} custom-call(bf16[32,2048]{1,0:T(8,128)(2,1)S(1)} %shard_map.43.values_ref, bf16[2048,2048]{1,0:T(8,128)(2,1)S(1)} %bitcast.113), custom_call_target="tpu_custom_call" | custom-call | flops 268435456 | bytes 8781824 | tf_op jit(solution)/shard_map/pallas_call | solution.py:79
  103.3 23.1 %all-gather.11.cloned.1.call-done = bf16[256,2048]{1,0:T(8,128)(2,1)} async-done(((bf16[32,2048]{1,0:T(8,128)(2,1)}), bf16[256,2048]{1,0:T(8,128)(2,1)}) %all-gather.11.cloned.1.call-update) | async-done | bytes 1048592 | tf_op jit(solution)/shard_map/all_gather | solution.py:117
  126.4 1.5 fusion.13
  127.9 1.5 collective-permute-start.7
  129.4 5.2 %collective-permute-done.7 = bf16[32,2048]{1,0:T(8,128)(2,1)S(1)} collective-permute-done((bf16[32,2048]{1,0:T(8,128)(2,1)S(1)}, bf16[32,2048]{1,0:T(8,128)(2,1)S(1)}, u32[]{:S(2)}, u32[]{:S(2)}) %collective-permute-start.7) | collective-permute-done | bytes 131104 | tf_op jit(solution)/shard_map/ppermute | solution.py:27
  134.6 1.2 collective-permute-start.8
  135.8 1.0 collective-permute-done.8.partner_ref
  136.8 3.4 %copy-done.5 = bf16[1,1,2048,2048]{3,2,1,0:T(8,128)(2,1)S(1)} copy-done((bf16[1,1,2048,2048]{3,2,1,0:T(8,128)(2,1)S(1)}, bf16[1,1,2048,2048]{3,2,1,0:T(8,128)(2,1)}, u32[]{:S(2)}) %copy-start.5) | copy-done | bytes 8388632
  140.2 1.5 shard_map.45.values_ref
  141.7 1.3 collective-permute-start.9
  143.1 3.4 %collective-permute-done.9.partner_ref = bf16[32,2048]{1,0:T(8,128)(2,1)S(1)} collective-permute-done((bf16[32,2048]{1,0:T(8,128)(2,1)S(1)}, bf16[32,2048]{1,0:T(8,128)(2,1)S(1)}, u32[]{:S(2)}, u32[]{:S(2)}) %collective-permute-start.9) | collective-permute-done | bytes 131104 | tf_op jit(solution)/shard_map/ppermute | solution.py:21
  146.5 3.4 %copy-done.6 = bf16[1,1,2048,2048]{3,2,1,0:T(8,128)(2,1)S(1)} copy-done((bf16[1,1,2048,2048]{3,2,1,0:T(8,128)(2,1)S(1)}, bf16[1,1,2048,2048]{3,2,1,0:T(8,128)(2,1)}, u32[]{:S(2)}) %copy-start.6) | copy-done | bytes 8388632
  149.8 1.5 shard_map.46.values_ref
  151.4 1.8 collective-permute-start.10
  153.1 6.4 %collective-permute-done.10.partner_ref = bf16[32,2048]{1,0:T(8,128)(2,1)S(1)} collective-permute-done((bf16[32,2048]{1,0:T(8,128)(2,1)S(1)}, bf16[32,2048]{1,0:T(8,128)(2,1)S(1)}, u32[]{:S(2)}, u32[]{:S(2)}) %collective-permute-start.10) | collective-permute-done | bytes 131104 | tf_op jit(solution)/shard_map/ppermute | solution.py:21
  159.5 1.5 shard_map.47.values_ref
  161.0 3.2 %shard_map.48 = bf16[32,2048]{1,0:T(8,128)(2,1)} custom-call(bf16[32,2048]{1,0:T(8,128)(2,1)S(1)} %shard_map.47.values_ref, bf16[2048,2048]{1,0:T(8,128)(2,1)S(1)} %bitcast.117), custom_call_target="tpu_custom_call" | custom-call | flops 268435456 | bytes 8781824 | tf_op jit(solution)/shard_map/pallas_call | solution.py:79
  164.3 23.1 %all-gather.13.cloned.1.call-done = bf16[256,2048]{1,0:T(8,128)(2,1)} async-done(((bf16[32,2048]{1,0:T(8,128)(2,1)}), bf16[256,2048]{1,0:T(8,128)(2,1)}) %all-gather.13.cloned.1.call-update) | async-done | bytes 1048592 | tf_op jit(solution)/shard_map/all_gather | solution.py:117
  187.4 1.5 fusion.12
  188.9 1.3 collective-permute-start.11
  190.2 5.4 %collective-permute-done.11 = bf16[32,2048]{1,0:T(8,128)(2,1)S(1)} collective-permute-done((bf16[32,2048]{1,0:T(8,128)(2,1)S(1)}, bf16[32,2048]{1,0:T(8,128)(2,1)S(1)}, u32[]{:S(2)}, u32[]{:S(2)}) %collective-permute-start.11) | collective-permute-done | bytes 131104 | tf_op jit(solution)/shard_map/ppermute | solution.py:27
  195.6 1.2 collective-permute-start.12
  196.9 1.0 collective-permute-done.12.partner_ref
  197.8 3.4 %copy-done.7 = bf16[1,1,2048,2048]{3,2,1,0:T(8,128)(2,1)S(1)} copy-done((bf16[1,1,2048,2048]{3,2,1,0:T(8,128)(2,1)S(1)}, bf16[1,1,2048,2048]{3,2,1,0:T(8,128)(2,1)}, u32[]{:S(2)}) %copy-start.7) | copy-done | bytes 8388632
  201.2 1.5 shard_map.49.values_ref
  202.8 1.3 collective-permute-start.13
  204.1 3.4 %collective-permute-done.13.partner_ref = bf16[32,2048]{1,0:T(8,128)(2,1)S(1)} collective-permute-done((bf16[32,2048]{1,0:T(8,128)(2,1)S(1)}, bf16[32,2048]{1,0:T(8,128)(2,1)S(1)}, u32[]{:S(2)}, u32[]{:S(2)}) %collective-permute-start.13) | collective-permute-done | bytes 131104 | tf_op jit(solution)/shard_map/ppermute | solution.py:21
  207.5 3.4 %copy-done.8 = bf16[1,1,2048,2048]{3,2,1,0:T(8,128)(2,1)S(1)} copy-done((bf16[1,1,2048,2048]{3,2,1,0:T(8,128)(2,1)S(1)}, bf16[1,1,2048,2048]{3,2,1,0:T(8,128)(2,1)}, u32[]{:S(2)}) %copy-start.8) | copy-done | bytes 8388632
  210.9 1.5 shard_map.50.values_ref
  212.4 1.7 collective-permute-start.14
  214.1 6.5 %collective-permute-done.14.partner_ref = bf16[32,2048]{1,0:T(8,128)(2,1)S(1)} collective-permute-done((bf16[32,2048]{1,0:T(8,128)(2,1)S(1)}, bf16[32,2048]{1,0:T(8,128)(2,1)S(1)}, u32[]{:S(2)}, u32[]{:S(2)}) %collective-permute-start.14) | collective-permute-done | bytes 131104 | tf_op jit(solution)/shard_map/ppermute | solution.py:21
  220.6 1.5 shard_map.51.values_ref
  222.1 3.2 %shard_map.52 = bf16[32,2048]{1,0:T(8,128)(2,1)} custom-call(bf16[32,2048]{1,0:T(8,128)(2,1)S(1)} %shard_map.51.values_ref, bf16[2048,2048]{1,0:T(8,128)(2,1)S(1)} %bitcast.121), custom_call_target="tpu_custom_call" | custom-call | flops 268435456 | bytes 8781824 | tf_op jit(solution)/shard_map/pallas_call | solution.py:79
  225.4 23.2 %all-gather.15.cloned.1.call-done = bf16[256,2048]{1,0:T(8,128)(2,1)} async-done(((bf16[32,2048]{1,0:T(8,128)(2,1)}), bf16[256,2048]{1,0:T(8,128)(2,1)}) %all-gather.15.cloned.1.call-update) | async-done | bytes 1048592 | tf_op jit(solution)/shard_map/all_gather | solution.py:117
  248.5 2.9 %select_bitcast_fusion = bf16[1,1,32,2048]{3,2,1,0:T(8,128)(2,1)} fusion(bf16[256,2048]{1,0:T(8,128)(2,1)} %all-gather.15.cloned.1.call-done, f32[]{:T(128)S(6)} %convert_element_type.514, f32[]{:T(128)S(6)} %convert_element_type.512, f32[]{:T(128)S(6)} %convert_element_type.510, f32[]{:T(128)S(6)} %convert_element_type.508, f32[]{:T(128)S(6)} %convert_element_type.506, ...), kind=kLoop, calls=%fused_computation.24 | loop fusion | flops 6553600 | bytes 4325408 | tf_op jit(solution)/shard_map/jit(_where)/select_n | solution.py:144
  (34 shorter events, 1.1 us)
Async XLA Ops:
  6.5 58.9 %all-gather.9.cloned.1.call-start = ((), (), s32[]{:S(2)}) async-start(), calls=%async_computation | async-start | bytes 1179648 | tf_op jit(solution)/shard_map/all_gather | solution.py:117
  8.2 1.7 collective-permute-start
  9.9 3.4 %copy-start = (bf16[1,1,2048,2048]{3,2,1,0:T(8,128)(2,1)S(1)}, bf16[1,1,2048,2048]{3,2,1,0:T(8,128)(2,1)}, u32[]{:S(2)}) copy-start(bf16[1,1,2048,2048]{3,2,1,0:T(8,128)(2,1)} %param.5) | copy-start | bytes 25165828
  14.8 4.7 %collective-permute-start.1 = (bf16[32,2048]{1,0:T(8,128)(2,1)S(1)}, bf16[32,2048]{1,0:T(8,128)(2,1)S(1)}, u32[]{:S(2)}, u32[]{:S(2)}) collective-permute-start(bf16[32,2048]{1,0:T(8,128)(2,1)S(1)} %shard_map.37.values_ref), channel_id=1, source_target_pairs={{0,2},{2,0},{1,3},{3,1},{4,6},{6,4},{5,7},{7,5},{8,10},{10,8},{9,1... | collective-permute-start | bytes 393224 | tf_op jit(solution)/shard_map/ppermute | solution.py:21
  19.5 3.4 %copy-start.1 = (bf16[1,1,2048,2048]{3,2,1,0:T(8,128)(2,1)S(1)}, bf16[1,1,2048,2048]{3,2,1,0:T(8,128)(2,1)}, u32[]{:S(2)}) copy-start(bf16[1,1,2048,2048]{3,2,1,0:T(8,128)(2,1)} %param.5) | copy-start | bytes 25165828
  24.4 8.1 %collective-permute-start.2 = (bf16[32,2048]{1,0:T(8,128)(2,1)S(1)}, bf16[32,2048]{1,0:T(8,128)(2,1)S(1)}, u32[]{:S(2)}, u32[]{:S(2)}) collective-permute-start(bf16[32,2048]{1,0:T(8,128)(2,1)S(1)} %shard_map.38.values_ref), channel_id=1, source_target_pairs={{0,4},{4,0},{1,5},{5,1},{2,6},{6,2},{3,7},{7,3},{8,12},{12,8},{9,1... | collective-permute-start | bytes 393224 | tf_op jit(solution)/shard_map/ppermute | solution.py:21
  32.6 3.4 %copy-start.2 = (bf16[1,1,2048,2048]{3,2,1,0:T(8,128)(2,1)S(1)}, bf16[1,1,2048,2048]{3,2,1,0:T(8,128)(2,1)}, u32[]{:S(2)}) copy-start(bf16[1,1,2048,2048]{3,2,1,0:T(8,128)(2,1)} %param.5) | copy-start | bytes 25165828
  36.0 37.6 %copy-start.12 = (bf16[1,1,32,2048]{3,2,1,0:T(8,128)(2,1)S(1)}, bf16[1,1,32,2048]{3,2,1,0:T(8,128)(2,1)}, u32[]{:S(2)}) copy-start(bf16[1,1,32,2048]{3,2,1,0:T(8,128)(2,1)} %param.3) | copy-start | bytes 393220
  36.0 37.6 %copy-start.13 = (f32[1,1,2048]{2,1,0:T(1,128)S(1)}, f32[1,1,2048]{2,1,0:T(1,128)}, u32[]{:S(2)}) copy-start(f32[1,1,2048]{2,1,0:T(1,128)} %param.4) | copy-start | bytes 24580
  40.7 85.7 %all-gather.11.cloned.1.call-start = ((), (), s32[]{:S(2)}) async-start(), calls=%async_computation.1 | async-start | bytes 1179648 | tf_op jit(solution)/shard_map/all_gather | solution.py:117
  66.9 6.7 %collective-permute-start.3 = (bf16[32,2048]{1,0:T(8,128)(2,1)S(1)}, bf16[32,2048]{1,0:T(8,128)(2,1)S(1)}, u32[]{:S(2)}, u32[]{:S(2)}) collective-permute-start(bf16[32,2048]{1,0:T(8,128)(2,1)S(1)} %fusion.14), channel_id=1, source_target_pairs={{0,8},{8,16},{16,24},{1,9},{9,17},{17,25},{2,10},{10,18},{18,26},{... | collective-permute-start | bytes 393224 | tf_op jit(solution)/shard_map/ppermute | solution.py:27
  73.6 2.2 collective-permute-start.4
  75.8 3.4 %copy-start.3 = (bf16[1,1,2048,2048]{3,2,1,0:T(8,128)(2,1)S(1)}, bf16[1,1,2048,2048]{3,2,1,0:T(8,128)(2,1)}, u32[]{:S(2)}) copy-start(bf16[1,1,2048,2048]{3,2,1,0:T(8,128)(2,1)} %param.5) | copy-start | bytes 25165828
  80.8 4.7 %collective-permute-start.5 = (bf16[32,2048]{1,0:T(8,128)(2,1)S(1)}, bf16[32,2048]{1,0:T(8,128)(2,1)S(1)}, u32[]{:S(2)}, u32[]{:S(2)}) collective-permute-start(bf16[32,2048]{1,0:T(8,128)(2,1)S(1)} %shard_map.41.values_ref), channel_id=1, source_target_pairs={{0,2},{2,0},{1,3},{3,1},{4,6},{6,4},{5,7},{7,5},{8,10},{10,8},{9,1... | collective-permute-start | bytes 393224 | tf_op jit(solution)/shard_map/ppermute | solution.py:21
  85.5 3.4 %copy-start.4 = (bf16[1,1,2048,2048]{3,2,1,0:T(8,128)(2,1)S(1)}, bf16[1,1,2048,2048]{3,2,1,0:T(8,128)(2,1)}, u32[]{:S(2)}) copy-start(bf16[1,1,2048,2048]{3,2,1,0:T(8,128)(2,1)} %param.5) | copy-start | bytes 25165828
  90.4 8.1 %collective-permute-start.6 = (bf16[32,2048]{1,0:T(8,128)(2,1)S(1)}, bf16[32,2048]{1,0:T(8,128)(2,1)S(1)}, u32[]{:S(2)}, u32[]{:S(2)}) collective-permute-start(bf16[32,2048]{1,0:T(8,128)(2,1)S(1)} %shard_map.42.values_ref), channel_id=1, source_target_pairs={{0,4},{4,0},{1,5},{5,1},{2,6},{6,2},{3,7},{7,3},{8,12},{12,8},{9,1... | collective-permute-start | bytes 393224 | tf_op jit(solution)/shard_map/ppermute | solution.py:21
  103.3 84.2 %all-gather.13.cloned.1.call-start = ((), (), s32[]{:S(2)}) async-start(), calls=%async_computation.2 | async-start | bytes 1179648 | tf_op jit(solution)/shard_map/all_gather | solution.py:117
  127.9 6.7 %collective-permute-start.7 = (bf16[32,2048]{1,0:T(8,128)(2,1)S(1)}, bf16[32,2048]{1,0:T(8,128)(2,1)S(1)}, u32[]{:S(2)}, u32[]{:S(2)}) collective-permute-start(bf16[32,2048]{1,0:T(8,128)(2,1)S(1)} %fusion.13), channel_id=1, source_target_pairs={{0,8},{8,16},{16,24},{1,9},{9,17},{17,25},{2,10},{10,18},{18,26},{... | collective-permute-start | bytes 393224 | tf_op jit(solution)/shard_map/ppermute | solution.py:27
  134.6 2.2 collective-permute-start.8
  136.8 3.4 %copy-start.5 = (bf16[1,1,2048,2048]{3,2,1,0:T(8,128)(2,1)S(1)}, bf16[1,1,2048,2048]{3,2,1,0:T(8,128)(2,1)}, u32[]{:S(2)}) copy-start(bf16[1,1,2048,2048]{3,2,1,0:T(8,128)(2,1)} %param.5) | copy-start | bytes 25165828
  141.7 4.7 %collective-permute-start.9 = (bf16[32,2048]{1,0:T(8,128)(2,1)S(1)}, bf16[32,2048]{1,0:T(8,128)(2,1)S(1)}, u32[]{:S(2)}, u32[]{:S(2)}) collective-permute-start(bf16[32,2048]{1,0:T(8,128)(2,1)S(1)} %shard_map.45.values_ref), channel_id=1, source_target_pairs={{0,2},{2,0},{1,3},{3,1},{4,6},{6,4},{5,7},{7,5},{8,10},{10,8},{9,1... | collective-permute-start | bytes 393224 | tf_op jit(solution)/shard_map/ppermute | solution.py:21
  146.5 3.4 %copy-start.6 = (bf16[1,1,2048,2048]{3,2,1,0:T(8,128)(2,1)S(1)}, bf16[1,1,2048,2048]{3,2,1,0:T(8,128)(2,1)}, u32[]{:S(2)}) copy-start(bf16[1,1,2048,2048]{3,2,1,0:T(8,128)(2,1)} %param.5) | copy-start | bytes 25165828
  151.4 8.1 %collective-permute-start.10 = (bf16[32,2048]{1,0:T(8,128)(2,1)S(1)}, bf16[32,2048]{1,0:T(8,128)(2,1)S(1)}, u32[]{:S(2)}, u32[]{:S(2)}) collective-permute-start(bf16[32,2048]{1,0:T(8,128)(2,1)S(1)} %shard_map.46.values_ref), channel_id=1, source_target_pairs={{0,4},{4,0},{1,5},{5,1},{2,6},{6,2},{3,7},{7,3},{8,12},{12,8},{9,1... | collective-permute-start | bytes 393224 | tf_op jit(solution)/shard_map/ppermute | solution.py:21
  164.3 84.3 %all-gather.15.cloned.1.call-start = ((), (), s32[]{:S(2)}) async-start(), calls=%async_computation.3 | async-start | bytes 1179648 | tf_op jit(solution)/shard_map/all_gather | solution.py:117
  188.9 6.7 %collective-permute-start.11 = (bf16[32,2048]{1,0:T(8,128)(2,1)S(1)}, bf16[32,2048]{1,0:T(8,128)(2,1)S(1)}, u32[]{:S(2)}, u32[]{:S(2)}) collective-permute-start(bf16[32,2048]{1,0:T(8,128)(2,1)S(1)} %fusion.12), channel_id=1, source_target_pairs={{0,8},{8,16},{16,24},{1,9},{9,17},{17,25},{2,10},{10,18},{18,26},{... | collective-permute-start | bytes 393224 | tf_op jit(solution)/shard_map/ppermute | solution.py:27
  195.6 2.2 collective-permute-start.12
  197.8 3.4 %copy-start.7 = (bf16[1,1,2048,2048]{3,2,1,0:T(8,128)(2,1)S(1)}, bf16[1,1,2048,2048]{3,2,1,0:T(8,128)(2,1)}, u32[]{:S(2)}) copy-start(bf16[1,1,2048,2048]{3,2,1,0:T(8,128)(2,1)} %param.5) | copy-start | bytes 25165828
  202.8 4.7 %collective-permute-start.13 = (bf16[32,2048]{1,0:T(8,128)(2,1)S(1)}, bf16[32,2048]{1,0:T(8,128)(2,1)S(1)}, u32[]{:S(2)}, u32[]{:S(2)}) collective-permute-start(bf16[32,2048]{1,0:T(8,128)(2,1)S(1)} %shard_map.49.values_ref), channel_id=1, source_target_pairs={{0,2},{2,0},{1,3},{3,1},{4,6},{6,4},{5,7},{7,5},{8,10},{10,8},{9,1... | collective-permute-start | bytes 393224 | tf_op jit(solution)/shard_map/ppermute | solution.py:21
  207.5 3.4 %copy-start.8 = (bf16[1,1,2048,2048]{3,2,1,0:T(8,128)(2,1)S(1)}, bf16[1,1,2048,2048]{3,2,1,0:T(8,128)(2,1)}, u32[]{:S(2)}) copy-start(bf16[1,1,2048,2048]{3,2,1,0:T(8,128)(2,1)} %param.5) | copy-start | bytes 25165828
  212.4 36.1 %copy-start.9 = (bf16[256,2048]{1,0:T(8,128)(2,1)S(1)}, bf16[256,2048]{1,0:T(8,128)(2,1)}, u32[]{:S(2)}) copy-start(bf16[256,2048]{1,0:T(8,128)(2,1)} %all-gather.9.cloned.1.call-done) | copy-start | bytes 3145732
  212.4 36.1 %copy-start.10 = (bf16[256,2048]{1,0:T(8,128)(2,1)S(1)}, bf16[256,2048]{1,0:T(8,128)(2,1)}, u32[]{:S(2)}) copy-start(bf16[256,2048]{1,0:T(8,128)(2,1)} %all-gather.11.cloned.1.call-done) | copy-start | bytes 3145732
  212.4 36.1 %copy-start.11 = (bf16[256,2048]{1,0:T(8,128)(2,1)S(1)}, bf16[256,2048]{1,0:T(8,128)(2,1)}, u32[]{:S(2)}) copy-start(bf16[256,2048]{1,0:T(8,128)(2,1)} %all-gather.13.cloned.1.call-done) | copy-start | bytes 3145732
  212.4 8.2 %collective-permute-start.14 = (bf16[32,2048]{1,0:T(8,128)(2,1)S(1)}, bf16[32,2048]{1,0:T(8,128)(2,1)S(1)}, u32[]{:S(2)}, u32[]{:S(2)}) collective-permute-start(bf16[32,2048]{1,0:T(8,128)(2,1)S(1)} %shard_map.50.values_ref), channel_id=1, source_target_pairs={{0,4},{4,0},{1,5},{5,1},{2,6},{6,2},{3,7},{7,3},{8,12},{12,8},{9,1... | collective-permute-start | bytes 393224 | tf_op jit(solution)/shard_map/ppermute | solution.py:21
Sparse Core Ops, SparseCore 0:
  40.9 24.5 all-gather.8
  103.4 22.9 all-gather.10
  164.4 23.0 all-gather.12
  225.5 22.9 all-gather.14

commit v4 on v1

--- a/solution.py
+++ b/solution.py
@@ -86,6 +86,60 @@
     )(values, pltpu.with_memory_space_constraint(merge_op, pltpu.VMEM))
 
 
+def streamed_mixed_kernel(sign_ref, values_ref, partner_ref, op_ref, out_ref, mixed_ref):
+    @pl.when(pl.program_id(0) == 0)
+    def _():
+        first = values_ref[...].astype(jnp.float32)
+        second = partner_ref[...].astype(jnp.float32)
+        mixed_ref[...] = ((second + sign_ref[...] * first) * half_root).astype(jnp.bfloat16)
+
+    out_ref[...] = jnp.dot(mixed_ref[...], op_ref[...], preferred_element_type=jnp.float32).astype(
+        out_ref.dtype
+    )
+
+
+def streamed_transposed_kernel(values_ref, op_ref, out_ref):
+    out_ref[...] = lax.dot_general(
+        values_ref[...], op_ref[...], (((1,), (1,)), ((), ())), preferred_element_type=jnp.float32
+    ).astype(out_ref.dtype)
+
+
+def whole(shape):
+    return pl.BlockSpec(shape, lambda j: (0,) * len(shape))
+
+
+def streamed_mixed_dot(sign, values, partner, merge_op):
+    rows, width = values.shape
+    return pl.pallas_call(
+        streamed_mixed_kernel,
+        out_shape=jax.ShapeDtypeStruct(values.shape, jnp.bfloat16),
+        grid=(width // TILE,),
+        in_specs=[
+            whole(sign.shape),
+            whole(values.shape),
+            whole(partner.shape),
+            pl.BlockSpec((width, TILE), lambda j: (0, j)),
+        ],
+        out_specs=pl.BlockSpec((rows, TILE), lambda j: (0, j)),
+        scratch_shapes=[pltpu.VMEM(values.shape, jnp.bfloat16)],
+        cost_estimate=cost(rows, width),
+        compiler_params=pltpu.CompilerParams(vmem_limit_bytes=16 * 1024 * 1024),
+    )(sign, values, partner, pltpu.with_memory_space_constraint(merge_op, pltpu.HBM))
+
+
+def streamed_transposed_dot(values, merge_op):
+    rows, width = values.shape
+    return pl.pallas_call(
+        streamed_transposed_kernel,
+        out_shape=jax.ShapeDtypeStruct(values.shape, jnp.bfloat16),
+        grid=(width // TILE,),
+        in_specs=[whole(values.shape), pl.BlockSpec((TILE, width), lambda j: (j, 0))],
+        out_specs=pl.BlockSpec((rows, TILE), lambda j: (0, j)),
+        cost_estimate=cost(rows, width),
+        compiler_params=pltpu.CompilerParams(vmem_limit_bytes=16 * 1024 * 1024),
+    )(values, pltpu.with_memory_space_constraint(merge_op, pltpu.HBM))
+
+
 def haar_pair(values, partner, lat_index, bit_level):
     is_lower = lat_index // 2**bit_level % 2 == 0
     first = values.astype(jnp.float32)
@@ -100,7 +154,7 @@
     return jnp.full((1, width), jnp.where(is_lower, 1.0, -1.0), jnp.float32)
 
 
-def sweep_layer(leaf_data, merge_op):
+def sweep_layer(leaf_data, merge_op, streamed):
     lat_count = lax.axis_size("lat")
     lat_index = lax.axis_index("lat")
     levels = lat_count.bit_length() - 1
@@ -108,8 +162,15 @@
     values = leaf_data
     for bit_level in range(levels):
         partner = partner_2(values, "lat", bit_level)
-        values = mixed_dot(level_sign(lat_index, bit_level, width), values, partner, merge_op)
-    values = transposed_dot(values, merge_op)
+        sign = level_sign(lat_index, bit_level, width)
+        if streamed:
+            values = streamed_mixed_dot(sign, values, partner, merge_op)
+        else:
+            values = mixed_dot(sign, values, partner, merge_op)
+    if streamed:
+        values = streamed_transposed_dot(values, merge_op)
+    else:
+        values = transposed_dot(values, merge_op)
     for bit_level in range(levels - 1, -1, -1):
         partner = partner_2(values, "lat", bit_level)
         values = haar_pair(values, partner, lat_index, bit_level)
@@ -128,7 +189,7 @@
         leaf_data = (
             shot_rows.astype(jnp.float32) + coupling_row * incoming.astype(jnp.float32)
         ).astype(jnp.bfloat16)
-        solved = sweep_layer(leaf_data, merge_op)
+        solved = sweep_layer(leaf_data, merge_op, sweep_step == 0)
         result = jnp.where(depth_index == sweep_step, solved, result)
         if sweep_step + 1 < depth_count:
             incoming = shifted(solved, "depth", 1)

time: 189 us -> 193 us (1.021)
  Pallas kernels: 28.5 us -> 42.4 us
  local copies, waits for them, and re-layouts: 10.2 us -> 0.04 us
    pallas_call x0 -> x4, Pallas kernels: none -> 21 us  [the longest x3 15.3 us: streamed_mixed_dot(): pl.pallas_call(streamed_mixed_kernel, out_shape=jax.ShapeDtypeStruct(valu...]
    unnamed x14 -> x8, local copies, waits for them, and re-layouts: 10.2 us -> 0.03 us
    pallas_call x12 -> x9, Pallas kernels: 18.4 us -> 13.8 us  [mixed_dot(): pl.pallas_call(mixed_dot_kernel, out_shape=jax.ShapeDtypeStruct(values.sh...]
    pallas_call x4 -> x3, Pallas kernels: 10.2 us -> 7.63 us  [transposed_dot(): pl.pallas_call(transposed_dot_kernel, out_shape=jax.ShapeDtypeStruct(valu...]
where the time goes in v4:
time: 193 us; the launch traced here: 191 us
  waiting for transfers between devices  119 us (62%)
  Pallas kernels  42.4 us (22%)
  starting transfers between devices  25.5 us (13%)
  other arithmetic  3.29 us (2%)
    ppermute x24, waiting for transfers between devices, partner_2(): return lax.ppermute(block, axis, route)  102 us
    ppermute x24, starting transfers between devices, partner_2(): return lax.ppermute(block, axis, route)  21.5 us
    ppermute x3, waiting for transfers between devices, shifted(): return lax.ppermute(array, axis, pairs)  16.5 us
    pallas_call x3, Pallas kernels, streamed_mixed_dot(): pl.pallas_call(streamed_mixed_kernel, out_shape=jax.ShapeDtypeStruct(valu...  15.3 us
    pallas_call x9, Pallas kernels, mixed_dot(): pl.pallas_call(mixed_dot_kernel, out_shape=jax.ShapeDtypeStruct(values.sh...  13.8 us
    pallas_call x3, Pallas kernels, transposed_dot(): pl.pallas_call(transposed_dot_kernel, out_shape=jax.ShapeDtypeStruct(valu...  7.63 us
    pallas_call x1, Pallas kernels, streamed_transposed_dot(): pl.pallas_call(streamed_transposed_kernel, out_shape=jax.ShapeDtypeStruct...  5.74 us
    ppermute x3, starting transfers between devices, shifted(): return lax.ppermute(array, axis, pairs)  4.06 us
  transfers between devices with their start and end apart: 27, of which 27 were waited for; matrix products, arithmetic and copies ran while one was open for 0% of the time, Pallas kernels for 0%

profile of v4, /device:TPU:7, one launch (start us, length us, event | category | flops | bytes accessed | tf_op | source)
XLA Modules:
  0.0 190.6 jit_solution(10244892423147418541)
XLA Ops:
  0.0 0.7 broadcast_multiply_fusion
  0.7 0.9 fusion.48.values_ref
  1.6 0.7 collective-permute-start
  2.4 1.0 collective-permute-done.partner_ref
  3.4 5.0 %shard_map.37.values_ref = bf16[32,2048]{1,0:T(8,128)(2,1)S(1)} custom-call(f32[1,2048]{1,0:T(1,128)S(1)} %broadcast_in_dim.12.sign_ref, bf16[32,2048]{1,0:T(8,128)(2,1)S(1)} %fusion.48.values_ref, bf16[32,2048]{1,0:T(8,128)(2,1)S(1)} %collective-permute-done.partner_ref, bf16[2048,2048]{1,0:T(8,128)(2,1)} %bitcast.10), custom_call_target="tpu_custom_call" | custom-call | flops 268435456 | bytes 8781824 | tf_op jit(solution)/shard_map/pallas_call | solution.py:113
  8.3 1.4 collective-permute-start.1
  9.7 3.4 %collective-permute-done.1.partner_ref = bf16[32,2048]{1,0:T(8,128)(2,1)S(1)} collective-permute-done((bf16[32,2048]{1,0:T(8,128)(2,1)S(1)}, bf16[32,2048]{1,0:T(8,128)(2,1)S(1)}, u32[]{:S(2)}, u32[]{:S(2)}) %collective-permute-start.1) | collective-permute-done | bytes 131104 | tf_op jit(solution)/shard_map/ppermute | solution.py:21
  13.1 5.0 %shard_map.38.values_ref = bf16[32,2048]{1,0:T(8,128)(2,1)S(1)} custom-call(f32[1,2048]{1,0:T(1,128)S(1)} %broadcast_in_dim.11.sign_ref, bf16[32,2048]{1,0:T(8,128)(2,1)S(1)} %shard_map.37.values_ref, bf16[32,2048]{1,0:T(8,128)(2,1)S(1)} %collective-permute-done.1.partner_ref, bf16[2048,2048]{1,0:T(8,128)(2,1)} %bitcast.11), custom_call_target="tpu_custom_call" | custom-call | flops 268435456 | bytes 8781824 | tf_op jit(solution)/shard_map/pallas_call | solution.py:113
  18.1 2.4 %collective-permute-start.2 = (bf16[32,2048]{1,0:T(8,128)(2,1)S(1)}, bf16[32,2048]{1,0:T(8,128)(2,1)S(1)}, u32[]{:S(2)}, u32[]{:S(2)}) collective-permute-start(bf16[32,2048]{1,0:T(8,128)(2,1)S(1)} %shard_map.38.values_ref), channel_id=1, source_target_pairs={{0,4},{4,0},{1,5},{5,1},{2,6},{6,2},{3,7},{7,3},{8,12},{12,8},{9,1... | collective-permute-start | bytes 393224 | tf_op jit(solution)/shard_map/ppermute | solution.py:21
  20.4 5.8 %collective-permute-done.2.partner_ref = bf16[32,2048]{1,0:T(8,128)(2,1)S(1)} collective-permute-done((bf16[32,2048]{1,0:T(8,128)(2,1)S(1)}, bf16[32,2048]{1,0:T(8,128)(2,1)S(1)}, u32[]{:S(2)}, u32[]{:S(2)}) %collective-permute-start.2) | collective-permute-done | bytes 131104 | tf_op jit(solution)/shard_map/ppermute | solution.py:21
  26.3 5.4 %shard_map.39.values_ref = bf16[32,2048]{1,0:T(8,128)(2,1)S(1)} custom-call(f32[1,2048]{1,0:T(1,128)S(1)} %broadcast_in_dim.10.sign_ref, bf16[32,2048]{1,0:T(8,128)(2,1)S(1)} %shard_map.38.values_ref, bf16[32,2048]{1,0:T(8,128)(2,1)S(1)} %collective-permute-done.2.partner_ref, bf16[2048,2048]{1,0:T(8,128)(2,1)} %bitcast.12), custom_call_target="tpu_custom_call" | custom-call | flops 268435456 | bytes 8781824 | tf_op jit(solution)/shard_map/pallas_call | solution.py:113
  31.6 5.7 %shard_map.40 = bf16[32,2048]{1,0:T(8,128)(2,1)S(1)} custom-call(bf16[32,2048]{1,0:T(8,128)(2,1)S(1)} %shard_map.39.values_ref, bf16[2048,2048]{1,0:T(8,128)(2,1)} %bitcast.13), custom_call_target="tpu_custom_call" | custom-call | flops 268435456 | bytes 8781824 | tf_op jit(solution)/shard_map/pallas_call | solution.py:132
  37.4 0.1 collective-permute-start.3
  37.5 4.7 %collective-permute-done.3 = bf16[32,2048]{1,0:T(8,128)(2,1)S(1)} collective-permute-done((bf16[32,2048]{1,0:T(8,128)(2,1)S(1)}, bf16[32,2048]{1,0:T(8,128)(2,1)S(1)}, u32[]{:S(2)}, u32[]{:S(2)}) %collective-permute-start.3) | collective-permute-done | bytes 131104 | tf_op jit(solution)/shard_map/ppermute | solution.py:21
  42.2 2.9 %collective-permute-start.4 = (bf16[32,2048]{1,0:T(8,128)(2,1)S(1)}, bf16[32,2048]{1,0:T(8,128)(2,1)S(1)}, u32[]{:S(2)}, u32[]{:S(2)}) collective-permute-start(bf16[32,2048]{1,0:T(8,128)(2,1)S(1)} %fusion.2), channel_id=1, source_target_pairs={{0,2},{2,0},{1,3},{3,1},{4,6},{6,4},{5,7},{7,5},{8,10},{10,8},{9,1... | collective-permute-start | bytes 393224 | tf_op jit(solution)/shard_map/ppermute | solution.py:21
  45.2 2.9 %collective-permute-done.4 = bf16[32,2048]{1,0:T(8,128)(2,1)S(1)} collective-permute-done((bf16[32,2048]{1,0:T(8,128)(2,1)S(1)}, bf16[32,2048]{1,0:T(8,128)(2,1)S(1)}, u32[]{:S(2)}, u32[]{:S(2)}) %collective-permute-start.4) | collective-permute-done | bytes 131104 | tf_op jit(solution)/shard_map/ppermute | solution.py:21
  48.1 4.5 %collective-permute-start.5 = (bf16[32,2048]{1,0:T(8,128)(2,1)S(1)}, bf16[32,2048]{1,0:T(8,128)(2,1)S(1)}, u32[]{:S(2)}, u32[]{:S(2)}) collective-permute-start(bf16[32,2048]{1,0:T(8,128)(2,1)S(1)} %fusion.6), channel_id=1, source_target_pairs={{0,1},{1,0},{2,3},{3,2},{4,5},{5,4},{6,7},{7,6},{8,9},{9,8},{10,11... | collective-permute-start | bytes 393224 | tf_op jit(solution)/shard_map/ppermute | solution.py:21
  52.7 1.0 collective-permute-done.5
  53.7 1.3 collective-permute-start.6
  55.0 5.3 %collective-permute-done.6 = bf16[32,2048]{1,0:T(8,128)(2,1)S(1)} collective-permute-done((bf16[32,2048]{1,0:T(8,128)(2,1)S(1)}, bf16[32,2048]{1,0:T(8,128)(2,1)S(1)}, u32[]{:S(2)}, u32[]{:S(2)}) %collective-permute-start.6) | collective-permute-done | bytes 131104 | tf_op jit(solution)/shard_map/ppermute | solution.py:27
  60.4 1.3 collective-permute-start.7
  61.6 1.0 collective-permute-done.7.partner_ref
  62.6 1.5 shard_map.41.values_ref
  64.2 4.7 %collective-permute-done.8.partner_ref = bf16[32,2048]{1,0:T(8,128)(2,1)S(1)} collective-permute-done((bf16[32,2048]{1,0:T(8,128)(2,1)S(1)}, bf16[32,2048]{1,0:T(8,128)(2,1)S(1)}, u32[]{:S(2)}, u32[]{:S(2)}) %collective-permute-start.8) | collective-permute-done | bytes 131104 | tf_op jit(solution)/shard_map/ppermute | solution.py:21
  68.9 1.5 shard_map.42.values_ref
  70.4 9.1 %collective-permute-done.9.partner_ref = bf16[32,2048]{1,0:T(8,128)(2,1)S(1)} collective-permute-done((bf16[32,2048]{1,0:T(8,128)(2,1)S(1)}, bf16[32,2048]{1,0:T(8,128)(2,1)S(1)}, u32[]{:S(2)}, u32[]{:S(2)}) %collective-permute-start.9) | collective-permute-done | bytes 131104 | tf_op jit(solution)/shard_map/ppermute | solution.py:21
  79.6 1.5 shard_map.43.values_ref
  81.1 2.5 %shard_map.44 = bf16[32,2048]{1,0:T(8,128)(2,1)S(1)} custom-call(bf16[32,2048]{1,0:T(8,128)(2,1)S(1)} %shard_map.43.values_ref, bf16[2048,2048]{1,0:T(8,128)(2,1)S(1)} %bitcast.19), custom_call_target="tpu_custom_call" | custom-call | flops 268435456 | bytes 8781824 | tf_op jit(solution)/shard_map/pallas_call | solution.py:79
  83.7 7.7 %collective-permute-done.10 = bf16[32,2048]{1,0:T(8,128)(2,1)S(1)} collective-permute-done((bf16[32,2048]{1,0:T(8,128)(2,1)S(1)}, bf16[32,2048]{1,0:T(8,128)(2,1)S(1)}, u32[]{:S(2)}, u32[]{:S(2)}) %collective-permute-start.10) | collective-permute-done | bytes 131104 | tf_op jit(solution)/shard_map/ppermute | solution.py:21
  91.5 4.6 %collective-permute-done.11 = bf16[32,2048]{1,0:T(8,128)(2,1)S(1)} collective-permute-done((bf16[32,2048]{1,0:T(8,128)(2,1)S(1)}, bf16[32,2048]{1,0:T(8,128)(2,1)S(1)}, u32[]{:S(2)}, u32[]{:S(2)}) %collective-permute-start.11) | collective-permute-done | bytes 131104 | tf_op jit(solution)/shard_map/ppermute | solution.py:21
  96.1 1.4 collective-permute-start.12
  97.5 1.0 collective-permute-done.12
  98.6 1.3 collective-permute-start.13
  99.9 5.3 %collective-permute-done.13 = bf16[32,2048]{1,0:T(8,128)(2,1)S(1)} collective-permute-done((bf16[32,2048]{1,0:T(8,128)(2,1)S(1)}, bf16[32,2048]{1,0:T(8,128)(2,1)S(1)}, u32[]{:S(2)}, u32[]{:S(2)}) %collective-permute-start.13) | collective-permute-done | bytes 131104 | tf_op jit(solution)/shard_map/ppermute | solution.py:27
  105.2 1.3 collective-permute-start.14
  106.5 1.0 collective-permute-done.14.partner_ref
  107.5 1.5 shard_map.45.values_ref
  109.0 4.7 %collective-permute-done.15.partner_ref = bf16[32,2048]{1,0:T(8,128)(2,1)S(1)} collective-permute-done((bf16[32,2048]{1,0:T(8,128)(2,1)S(1)}, bf16[32,2048]{1,0:T(8,128)(2,1)S(1)}, u32[]{:S(2)}, u32[]{:S(2)}) %collective-permute-start.15) | collective-permute-done | bytes 131104 | tf_op jit(solution)/shard_map/ppermute | solution.py:21
  113.7 1.5 shard_map.46.values_ref
  115.3 1.2 collective-permute-start.16
  116.5 7.9 %collective-permute-done.16.partner_ref = bf16[32,2048]{1,0:T(8,128)(2,1)S(1)} collective-permute-done((bf16[32,2048]{1,0:T(8,128)(2,1)S(1)}, bf16[32,2048]{1,0:T(8,128)(2,1)S(1)}, u32[]{:S(2)}, u32[]{:S(2)}) %collective-permute-start.16) | collective-permute-done | bytes 131104 | tf_op jit(solution)/shard_map/ppermute | solution.py:21
  124.4 1.5 shard_map.47.values_ref
  125.9 2.5 %shard_map.48 = bf16[32,2048]{1,0:T(8,128)(2,1)S(1)} custom-call(bf16[32,2048]{1,0:T(8,128)(2,1)S(1)} %shard_map.47.values_ref, bf16[2048,2048]{1,0:T(8,128)(2,1)S(1)} %bitcast.23), custom_call_target="tpu_custom_call" | custom-call | flops 268435456 | bytes 8781824 | tf_op jit(solution)/shard_map/pallas_call | solution.py:79
  128.5 8.7 %collective-permute-done.17 = bf16[32,2048]{1,0:T(8,128)(2,1)S(1)} collective-permute-done((bf16[32,2048]{1,0:T(8,128)(2,1)S(1)}, bf16[32,2048]{1,0:T(8,128)(2,1)S(1)}, u32[]{:S(2)}, u32[]{:S(2)}) %collective-permute-start.17) | collective-permute-done | bytes 131104 | tf_op jit(solution)/shard_map/ppermute | solution.py:21
  137.2 0.1 collective-permute-start.18
  137.3 4.6 %collective-permute-done.18 = bf16[32,2048]{1,0:T(8,128)(2,1)S(1)} collective-permute-done((bf16[32,2048]{1,0:T(8,128)(2,1)S(1)}, bf16[32,2048]{1,0:T(8,128)(2,1)S(1)}, u32[]{:S(2)}, u32[]{:S(2)}) %collective-permute-start.18) | collective-permute-done | bytes 131104 | tf_op jit(solution)/shard_map/ppermute | solution.py:21
  142.0 1.4 collective-permute-start.19
  143.4 1.0 collective-permute-done.19
  144.4 1.5 collective-permute-start.20
  145.9 6.0 %collective-permute-done.20 = bf16[32,2048]{1,0:T(8,128)(2,1)S(1)} collective-permute-done((bf16[32,2048]{1,0:T(8,128)(2,1)S(1)}, bf16[32,2048]{1,0:T(8,128)(2,1)S(1)}, u32[]{:S(2)}, u32[]{:S(2)}) %collective-permute-start.20) | collective-permute-done | bytes 131104 | tf_op jit(solution)/shard_map/ppermute | solution.py:27
  151.9 1.0 collective-permute-start.21
  152.9 1.0 collective-permute-done.21.partner_ref
  153.9 1.5 shard_map.49.values_ref
  155.5 4.7 %collective-permute-done.22.partner_ref = bf16[32,2048]{1,0:T(8,128)(2,1)S(1)} collective-permute-done((bf16[32,2048]{1,0:T(8,128)(2,1)S(1)}, bf16[32,2048]{1,0:T(8,128)(2,1)S(1)}, u32[]{:S(2)}, u32[]{:S(2)}) %collective-permute-start.22) | collective-permute-done | bytes 131104 | tf_op jit(solution)/shard_map/ppermute | solution.py:21
  160.2 1.5 shard_map.50.values_ref
  161.7 0.2 collective-permute-start.23
  161.9 8.5 %collective-permute-done.23.partner_ref = bf16[32,2048]{1,0:T(8,128)(2,1)S(1)} collective-permute-done((bf16[32,2048]{1,0:T(8,128)(2,1)S(1)}, bf16[32,2048]{1,0:T(8,128)(2,1)S(1)}, u32[]{:S(2)}, u32[]{:S(2)}) %collective-permute-start.23) | collective-permute-done | bytes 131104 | tf_op jit(solution)/shard_map/ppermute | solution.py:21
  170.4 1.5 shard_map.51.values_ref
  171.9 2.5 %shard_map.52 = bf16[32,2048]{1,0:T(8,128)(2,1)S(1)} custom-call(bf16[32,2048]{1,0:T(8,128)(2,1)S(1)} %shard_map.51.values_ref, bf16[2048,2048]{1,0:T(8,128)(2,1)S(1)} %bitcast.27), custom_call_target="tpu_custom_call" | custom-call | flops 268435456 | bytes 8781824 | tf_op jit(solution)/shard_map/pallas_call | solution.py:79
  174.5 8.1 %collective-permute-done.24 = bf16[32,2048]{1,0:T(8,128)(2,1)S(1)} collective-permute-done((bf16[32,2048]{1,0:T(8,128)(2,1)S(1)}, bf16[32,2048]{1,0:T(8,128)(2,1)S(1)}, u32[]{:S(2)}, u32[]{:S(2)}) %collective-permute-start.24) | collective-permute-done | bytes 131104 | tf_op jit(solution)/shard_map/ppermute | solution.py:21
  182.7 4.5 %collective-permute-done.25 = bf16[32,2048]{1,0:T(8,128)(2,1)S(1)} collective-permute-done((bf16[32,2048]{1,0:T(8,128)(2,1)S(1)}, bf16[32,2048]{1,0:T(8,128)(2,1)S(1)}, u32[]{:S(2)}, u32[]{:S(2)}) %collective-permute-start.25) | collective-permute-done | bytes 131104 | tf_op jit(solution)/shard_map/ppermute | solution.py:21
  187.4 1.4 collective-permute-start.26
  188.8 1.0 collective-permute-done.26
  189.8 0.8 fusion.53
  (35 shorter events, 1.2 us)
Async XLA Ops:
  1.6 1.7 collective-permute-start
  8.3 4.8 %collective-permute-start.1 = (bf16[32,2048]{1,0:T(8,128)(2,1)S(1)}, bf16[32,2048]{1,0:T(8,128)(2,1)S(1)}, u32[]{:S(2)}, u32[]{:S(2)}) collective-permute-start(bf16[32,2048]{1,0:T(8,128)(2,1)S(1)} %shard_map.37.values_ref), channel_id=1, source_target_pairs={{0,2},{2,0},{1,3},{3,1},{4,6},{6,4},{5,7},{7,5},{8,10},{10,8},{9,1... | collective-permute-start | bytes 393224 | tf_op jit(solution)/shard_map/ppermute | solution.py:21
  18.1 8.2 %collective-permute-start.2 = (bf16[32,2048]{1,0:T(8,128)(2,1)S(1)}, bf16[32,2048]{1,0:T(8,128)(2,1)S(1)}, u32[]{:S(2)}, u32[]{:S(2)}) collective-permute-start(bf16[32,2048]{1,0:T(8,128)(2,1)S(1)} %shard_map.38.values_ref), channel_id=1, source_target_pairs={{0,4},{4,0},{1,5},{5,1},{2,6},{6,2},{3,7},{7,3},{8,12},{12,8},{9,1... | collective-permute-start | bytes 393224 | tf_op jit(solution)/shard_map/ppermute | solution.py:21
  26.2 34.1 %copy-start = (bf16[1,1,32,2048]{3,2,1,0:T(8,128)(2,1)S(1)}, bf16[1,1,32,2048]{3,2,1,0:T(8,128)(2,1)}, u32[]{:S(2)}) copy-start(bf16[1,1,32,2048]{3,2,1,0:T(8,128)(2,1)} %param.3) | copy-start | bytes 393220
  26.2 34.1 %copy-start.1 = (f32[1,1,2048]{2,1,0:T(1,128)S(1)}, f32[1,1,2048]{2,1,0:T(1,128)}, u32[]{:S(2)}) copy-start(f32[1,1,2048]{2,1,0:T(1,128)} %param.4) | copy-start | bytes 24580
  26.3 36.4 %slice-start = ((s8[8388608]{0:T(1024)(128)(4,1)}), s8[4194304]{0:T(1024)(128)(4,1)S(1)}, s32[]{:S(2)}) async-start(s8[8388608]{0:T(1024)(128)(4,1)} %bitcast.14), calls=%async_computation | async-start | bytes 8388608
  31.6 31.0 %slice-start.1 = ((s8[8388608]{0:T(1024)(128)(4,1)}), s8[4194304]{0:T(1024)(128)(4,1)S(1)}, s32[]{:S(2)}) async-start(s8[8388608]{0:T(1024)(128)(4,1)} %bitcast.14), calls=%async_computation.1 | async-start | bytes 8388608
  37.4 4.8 %collective-permute-start.3 = (bf16[32,2048]{1,0:T(8,128)(2,1)S(1)}, bf16[32,2048]{1,0:T(8,128)(2,1)S(1)}, u32[]{:S(2)}, u32[]{:S(2)}) collective-permute-start(bf16[32,2048]{1,0:T(8,128)(2,1)S(1)} %shard_map.40), channel_id=1, source_target_pairs={{0,4},{4,0},{1,5},{5,1},{2,6},{6,2},{3,7},{7,3},{8,12},{12,8},{9,1... | collective-permute-start | bytes 393224 | tf_op jit(solution)/shard_map/ppermute | solution.py:21
  42.2 5.8 %collective-permute-start.4 = (bf16[32,2048]{1,0:T(8,128)(2,1)S(1)}, bf16[32,2048]{1,0:T(8,128)(2,1)S(1)}, u32[]{:S(2)}, u32[]{:S(2)}) collective-permute-start(bf16[32,2048]{1,0:T(8,128)(2,1)S(1)} %fusion.2), channel_id=1, source_target_pairs={{0,2},{2,0},{1,3},{3,1},{4,6},{6,4},{5,7},{7,5},{8,10},{10,8},{9,1... | collective-permute-start | bytes 393224 | tf_op jit(solution)/shard_map/ppermute | solution.py:21
  48.1 5.5 %collective-permute-start.5 = (bf16[32,2048]{1,0:T(8,128)(2,1)S(1)}, bf16[32,2048]{1,0:T(8,128)(2,1)S(1)}, u32[]{:S(2)}, u32[]{:S(2)}) collective-permute-start(bf16[32,2048]{1,0:T(8,128)(2,1)S(1)} %fusion.6), channel_id=1, source_target_pairs={{0,1},{1,0},{2,3},{3,2},{4,5},{5,4},{6,7},{7,6},{8,9},{9,8},{10,11... | collective-permute-start | bytes 393224 | tf_op jit(solution)/shard_map/ppermute | solution.py:21
  53.7 6.6 %collective-permute-start.6 = (bf16[32,2048]{1,0:T(8,128)(2,1)S(1)}, bf16[32,2048]{1,0:T(8,128)(2,1)S(1)}, u32[]{:S(2)}, u32[]{:S(2)}) collective-permute-start(bf16[32,2048]{1,0:T(8,128)(2,1)S(1)} %fusion.10), channel_id=1, source_target_pairs={{0,8},{8,16},{16,24},{1,9},{9,17},{17,25},{2,10},{10,18},{18,26},{... | collective-permute-start | bytes 393224 | tf_op jit(solution)/shard_map/ppermute | solution.py:27
  60.4 2.3 %collective-permute-start.7 = (bf16[32,2048]{1,0:T(8,128)(2,1)S(1)}, bf16[32,2048]{1,0:T(8,128)(2,1)S(1)}, u32[]{:S(2)}, u32[]{:S(2)}) collective-permute-start(bf16[32,2048]{1,0:T(8,128)(2,1)S(1)} %fusion.49.values_ref), channel_id=1, source_target_pairs={{0,1},{1,0},{2,3},{3,2},{4,5},{5,4},{6,7},{7,6},{8,9},{9,8},{10,11... | collective-permute-start | bytes 393224 | tf_op jit(solution)/shard_map/ppermute | solution.py:21
  64.2 4.7 %collective-permute-start.8 = (bf16[32,2048]{1,0:T(8,128)(2,1)S(1)}, bf16[32,2048]{1,0:T(8,128)(2,1)S(1)}, u32[]{:S(2)}, u32[]{:S(2)}) collective-permute-start(bf16[32,2048]{1,0:T(8,128)(2,1)S(1)} %shard_map.41.values_ref), channel_id=1, source_target_pairs={{0,2},{2,0},{1,3},{3,1},{4,6},{6,4},{5,7},{7,5},{8,10},{10,8},{9,1... | collective-permute-start | bytes 393224 | tf_op jit(solution)/shard_map/ppermute | solution.py:21
  70.4 9.1 %collective-permute-start.9 = (bf16[32,2048]{1,0:T(8,128)(2,1)S(1)}, bf16[32,2048]{1,0:T(8,128)(2,1)S(1)}, u32[]{:S(2)}, u32[]{:S(2)}) collective-permute-start(bf16[32,2048]{1,0:T(8,128)(2,1)S(1)} %shard_map.42.values_ref), channel_id=1, source_target_pairs={{0,4},{4,0},{1,5},{5,1},{2,6},{6,2},{3,7},{7,3},{8,12},{12,8},{9,1... | collective-permute-start | bytes 393224 | tf_op jit(solution)/shard_map/ppermute | solution.py:21
  83.6 7.7 %collective-permute-start.10 = (bf16[32,2048]{1,0:T(8,128)(2,1)S(1)}, bf16[32,2048]{1,0:T(8,128)(2,1)S(1)}, u32[]{:S(2)}, u32[]{:S(2)}) collective-permute-start(bf16[32,2048]{1,0:T(8,128)(2,1)S(1)} %shard_map.44), channel_id=1, source_target_pairs={{0,4},{4,0},{1,5},{5,1},{2,6},{6,2},{3,7},{7,3},{8,12},{12,8},{9,1... | collective-permute-start | bytes 393224 | tf_op jit(solution)/shard_map/ppermute | solution.py:21
  91.4 4.6 %collective-permute-start.11 = (bf16[32,2048]{1,0:T(8,128)(2,1)S(1)}, bf16[32,2048]{1,0:T(8,128)(2,1)S(1)}, u32[]{:S(2)}, u32[]{:S(2)}) collective-permute-start(bf16[32,2048]{1,0:T(8,128)(2,1)S(1)} %fusion.14), channel_id=1, source_target_pairs={{0,2},{2,0},{1,3},{3,1},{4,6},{6,4},{5,7},{7,5},{8,10},{10,8},{9,1... | collective-permute-start | bytes 393224 | tf_op jit(solution)/shard_map/ppermute | solution.py:21
  96.1 2.4 %collective-permute-start.12 = (bf16[32,2048]{1,0:T(8,128)(2,1)S(1)}, bf16[32,2048]{1,0:T(8,128)(2,1)S(1)}, u32[]{:S(2)}, u32[]{:S(2)}) collective-permute-start(bf16[32,2048]{1,0:T(8,128)(2,1)S(1)} %fusion.18), channel_id=1, source_target_pairs={{0,1},{1,0},{2,3},{3,2},{4,5},{5,4},{6,7},{7,6},{8,9},{9,8},{10,11... | collective-permute-start | bytes 393224 | tf_op jit(solution)/shard_map/ppermute | solution.py:21
  98.6 6.6 %collective-permute-start.13 = (bf16[32,2048]{1,0:T(8,128)(2,1)S(1)}, bf16[32,2048]{1,0:T(8,128)(2,1)S(1)}, u32[]{:S(2)}, u32[]{:S(2)}) collective-permute-start(bf16[32,2048]{1,0:T(8,128)(2,1)S(1)} %fusion.22), channel_id=1, source_target_pairs={{0,8},{8,16},{16,24},{1,9},{9,17},{17,25},{2,10},{10,18},{18,26},{... | collective-permute-start | bytes 393224 | tf_op jit(solution)/shard_map/ppermute | solution.py:27
  105.2 2.3 %collective-permute-start.14 = (bf16[32,2048]{1,0:T(8,128)(2,1)S(1)}, bf16[32,2048]{1,0:T(8,128)(2,1)S(1)}, u32[]{:S(2)}, u32[]{:S(2)}) collective-permute-start(bf16[32,2048]{1,0:T(8,128)(2,1)S(1)} %fusion.50.values_ref), channel_id=1, source_target_pairs={{0,1},{1,0},{2,3},{3,2},{4,5},{5,4},{6,7},{7,6},{8,9},{9,8},{10,11... | collective-permute-start | bytes 393224 | tf_op jit(solution)/shard_map/ppermute | solution.py:21
  109.0 4.7 %collective-permute-start.15 = (bf16[32,2048]{1,0:T(8,128)(2,1)S(1)}, bf16[32,2048]{1,0:T(8,128)(2,1)S(1)}, u32[]{:S(2)}, u32[]{:S(2)}) collective-permute-start(bf16[32,2048]{1,0:T(8,128)(2,1)S(1)} %shard_map.45.values_ref), channel_id=1, source_target_pairs={{0,2},{2,0},{1,3},{3,1},{4,6},{6,4},{5,7},{7,5},{8,10},{10,8},{9,1... | collective-permute-start | bytes 393224 | tf_op jit(solution)/shard_map/ppermute | solution.py:21
  115.3 9.1 %collective-permute-start.16 = (bf16[32,2048]{1,0:T(8,128)(2,1)S(1)}, bf16[32,2048]{1,0:T(8,128)(2,1)S(1)}, u32[]{:S(2)}, u32[]{:S(2)}) collective-permute-start(bf16[32,2048]{1,0:T(8,128)(2,1)S(1)} %shard_map.46.values_ref), channel_id=1, source_target_pairs={{0,4},{4,0},{1,5},{5,1},{2,6},{6,2},{3,7},{7,3},{8,12},{12,8},{9,1... | collective-permute-start | bytes 393224 | tf_op jit(solution)/shard_map/ppermute | solution.py:21
  128.5 8.7 %collective-permute-start.17 = (bf16[32,2048]{1,0:T(8,128)(2,1)S(1)}, bf16[32,2048]{1,0:T(8,128)(2,1)S(1)}, u32[]{:S(2)}, u32[]{:S(2)}) collective-permute-start(bf16[32,2048]{1,0:T(8,128)(2,1)S(1)} %shard_map.48), channel_id=1, source_target_pairs={{0,4},{4,0},{1,5},{5,1},{2,6},{6,2},{3,7},{7,3},{8,12},{12,8},{9,1... | collective-permute-start | bytes 393224 | tf_op jit(solution)/shard_map/ppermute | solution.py:21
  137.2 4.6 %collective-permute-start.18 = (bf16[32,2048]{1,0:T(8,128)(2,1)S(1)}, bf16[32,2048]{1,0:T(8,128)(2,1)S(1)}, u32[]{:S(2)}, u32[]{:S(2)}) collective-permute-start(bf16[32,2048]{1,0:T(8,128)(2,1)S(1)} %fusion.26), channel_id=1, source_target_pairs={{0,2},{2,0},{1,3},{3,1},{4,6},{6,4},{5,7},{7,5},{8,10},{10,8},{9,1... | collective-permute-start | bytes 393224 | tf_op jit(solution)/shard_map/ppermute | solution.py:21
  142.0 2.4 %collective-permute-start.19 = (bf16[32,2048]{1,0:T(8,128)(2,1)S(1)}, bf16[32,2048]{1,0:T(8,128)(2,1)S(1)}, u32[]{:S(2)}, u32[]{:S(2)}) collective-permute-start(bf16[32,2048]{1,0:T(8,128)(2,1)S(1)} %fusion.30), channel_id=1, source_target_pairs={{0,1},{1,0},{2,3},{3,2},{4,5},{5,4},{6,7},{7,6},{8,9},{9,8},{10,11... | collective-permute-start | bytes 393224 | tf_op jit(solution)/shard_map/ppermute | solution.py:21
  144.4 7.4 %collective-permute-start.20 = (bf16[32,2048]{1,0:T(8,128)(2,1)S(1)}, bf16[32,2048]{1,0:T(8,128)(2,1)S(1)}, u32[]{:S(2)}, u32[]{:S(2)}) collective-permute-start(bf16[32,2048]{1,0:T(8,128)(2,1)S(1)} %fusion.34), channel_id=1, source_target_pairs={{0,8},{8,16},{16,24},{1,9},{9,17},{17,25},{2,10},{10,18},{18,26},{... | collective-permute-start | bytes 393224 | tf_op jit(solution)/shard_map/ppermute | solution.py:27
  151.9 2.0 %collective-permute-start.21 = (bf16[32,2048]{1,0:T(8,128)(2,1)S(1)}, bf16[32,2048]{1,0:T(8,128)(2,1)S(1)}, u32[]{:S(2)}, u32[]{:S(2)}) collective-permute-start(bf16[32,2048]{1,0:T(8,128)(2,1)S(1)} %fusion.51.values_ref), channel_id=1, source_target_pairs={{0,1},{1,0},{2,3},{3,2},{4,5},{5,4},{6,7},{7,6},{8,9},{9,8},{10,11... | collective-permute-start | bytes 393224 | tf_op jit(solution)/shard_map/ppermute | solution.py:21
  155.4 4.7 %collective-permute-start.22 = (bf16[32,2048]{1,0:T(8,128)(2,1)S(1)}, bf16[32,2048]{1,0:T(8,128)(2,1)S(1)}, u32[]{:S(2)}, u32[]{:S(2)}) collective-permute-start(bf16[32,2048]{1,0:T(8,128)(2,1)S(1)} %shard_map.49.values_ref), channel_id=1, source_target_pairs={{0,2},{2,0},{1,3},{3,1},{4,6},{6,4},{5,7},{7,5},{8,10},{10,8},{9,1... | collective-permute-start | bytes 393224 | tf_op jit(solution)/shard_map/ppermute | solution.py:21
  161.7 8.7 %collective-permute-start.23 = (bf16[32,2048]{1,0:T(8,128)(2,1)S(1)}, bf16[32,2048]{1,0:T(8,128)(2,1)S(1)}, u32[]{:S(2)}, u32[]{:S(2)}) collective-permute-start(bf16[32,2048]{1,0:T(8,128)(2,1)S(1)} %shard_map.50.values_ref), channel_id=1, source_target_pairs={{0,4},{4,0},{1,5},{5,1},{2,6},{6,2},{3,7},{7,3},{8,12},{12,8},{9,1... | collective-permute-start | bytes 393224 | tf_op jit(solution)/shard_map/ppermute | solution.py:21
  174.5 8.1 %collective-permute-start.24 = (bf16[32,2048]{1,0:T(8,128)(2,1)S(1)}, bf16[32,2048]{1,0:T(8,128)(2,1)S(1)}, u32[]{:S(2)}, u32[]{:S(2)}) collective-permute-start(bf16[32,2048]{1,0:T(8,128)(2,1)S(1)} %shard_map.52), channel_id=1, source_target_pairs={{0,4},{4,0},{1,5},{5,1},{2,6},{6,2},{3,7},{7,3},{8,12},{12,8},{9,1... | collective-permute-start | bytes 393224 | tf_op jit(solution)/shard_map/ppermute | solution.py:21
  182.7 4.6 %collective-permute-start.25 = (bf16[32,2048]{1,0:T(8,128)(2,1)S(1)}, bf16[32,2048]{1,0:T(8,128)(2,1)S(1)}, u32[]{:S(2)}, u32[]{:S(2)}) collective-permute-start(bf16[32,2048]{1,0:T(8,128)(2,1)S(1)} %fusion.38), channel_id=1, source_target_pairs={{0,2},{2,0},{1,3},{3,1},{4,6},{6,4},{5,7},{7,5},{8,10},{10,8},{9,1... | collective-permute-start | bytes 393224 | tf_op jit(solution)/shard_map/ppermute | solution.py:21
  187.4 2.4 %collective-permute-start.26 = (bf16[32,2048]{1,0:T(8,128)(2,1)S(1)}, bf16[32,2048]{1,0:T(8,128)(2,1)S(1)}, u32[]{:S(2)}, u32[]{:S(2)}) collective-permute-start(bf16[32,2048]{1,0:T(8,128)(2,1)S(1)} %fusion.42), channel_id=1, source_target_pairs={{0,1},{1,0},{2,3},{3,2},{4,5},{5,4},{6,7},{7,6},{8,9},{9,8},{10,11... | collective-permute-start | bytes 393224 | tf_op jit(solution)/shard_map/ppermute | solution.py:21

commit v5 on v1

--- a/solution.py
+++ b/solution.py
@@ -100,17 +100,17 @@
     return jnp.full((1, width), jnp.where(is_lower, 1.0, -1.0), jnp.float32)
 
 
-def sweep_layer(leaf_data, merge_op):
+def sweep_layer(leaf_data, partner_leaf, merge_op):
     lat_count = lax.axis_size("lat")
     lat_index = lax.axis_index("lat")
     levels = lat_count.bit_length() - 1
     width = leaf_data.shape[1]
     values = leaf_data
     for bit_level in range(levels):
-        partner = partner_2(values, "lat", bit_level)
+        partner = partner_leaf if bit_level == 0 else partner_2(values, "lat", bit_level)
         values = mixed_dot(level_sign(lat_index, bit_level, width), values, partner, merge_op)
     values = transposed_dot(values, merge_op)
-    for bit_level in range(levels - 1, -1, -1):
+    for bit_level in range(levels - 1, 0, -1):
         partner = partner_2(values, "lat", bit_level)
         values = haar_pair(values, partner, lat_index, bit_level)
     return values
@@ -121,17 +121,30 @@
     coupling_row = coupling[0, 0]
     depth_index = lax.axis_index("depth")
     depth_count = lax.axis_size("depth")
+    lat_index = lax.axis_index("lat")
     shot_rows = sources[0, 0]
+    partner_rows = partner_2(shot_rows, "lat", 0)
+    partner_coupling = partner_2(coupling_row[None], "lat", 0)[0]
     result = jnp.zeros_like(shot_rows)
     incoming = jnp.zeros_like(shot_rows)
+    partner_incoming = jnp.zeros_like(shot_rows)
     for sweep_step in range(depth_count):
         leaf_data = (
             shot_rows.astype(jnp.float32) + coupling_row * incoming.astype(jnp.float32)
         ).astype(jnp.bfloat16)
-        solved = sweep_layer(leaf_data, merge_op)
+        partner_leaf = (
+            partner_rows.astype(jnp.float32) + partner_coupling * partner_incoming.astype(jnp.float32)
+        ).astype(jnp.bfloat16)
+        level_one = sweep_layer(leaf_data, partner_leaf, merge_op)
+        if sweep_step + 1 < depth_count:
+            arrived = shifted(level_one, "depth", 1)
+            level_one = jnp.where(depth_index == sweep_step, level_one, arrived)
+        other = partner_2(level_one, "lat", 0)
+        solved = haar_pair(level_one, other, lat_index, 0)
+        partner_solved = haar_pair(other, level_one, lat_index ^ 1, 0)
         result = jnp.where(depth_index == sweep_step, solved, result)
-        if sweep_step + 1 < depth_count:
-            incoming = shifted(solved, "depth", 1)
+        incoming = solved
+        partner_incoming = partner_solved
     return result[None, None]
 
 

time: 189 us -> 203 us (1.074)
  local copies, waits for them, and re-layouts: 10.2 us -> 30.4 us
  waiting for transfers between devices: 119 us -> 112 us
    unnamed x14 -> x22, local copies, waits for them, and re-layouts: 10.2 us -> 30.4 us
    ppermute x24 -> x22, waiting for transfers between devices: 102 us -> 98.4 us  [partner_2(): return lax.ppermute(block, axis, route)]
    ppermute x3, waiting for transfers between devices: 16.6 us -> 13.6 us  [shifted(): return lax.ppermute(array, axis, pairs)]
    ppermute x24 -> x22, starting transfers between devices: 21.3 us -> 20.7 us  [partner_2(): return lax.ppermute(block, axis, route)]
  transfers between devices with their start and end apart: 27 -> 25, of which waited for: 27 -> 23; matrix products, arithmetic and copies ran while one was open for 0% -> 1% of each run, Pallas kernels for 0% -> 0%
where the time goes in v5:
time: 203 us; the launch traced here: 200 us
  waiting for transfers between devices  112 us (55%)
  local copies, waits for them, and re-layouts  30.4 us (15%)
  Pallas kernels  28.6 us (14%)
  starting transfers between devices  24.8 us (12%)
  other arithmetic  3.63 us (2%)
    ppermute x22, waiting for transfers between devices, partner_2(): return lax.ppermute(block, axis, route)  98.4 us
    unnamed x22, local copies, waits for them, and re-layouts  30.4 us
    ppermute x22, starting transfers between devices, partner_2(): return lax.ppermute(block, axis, route)  20.7 us
    pallas_call x12, Pallas kernels, mixed_dot(): pl.pallas_call(mixed_dot_kernel, out_shape=jax.ShapeDtypeStruct(values.sh...  18.4 us
    ppermute x3, waiting for transfers between devices, shifted(): return lax.ppermute(array, axis, pairs)  13.6 us
    pallas_call x4, Pallas kernels, transposed_dot(): pl.pallas_call(transposed_dot_kernel, out_shape=jax.ShapeDtypeStruct(valu...  10.2 us
  transfers between devices with their start and end apart: 25, of which 23 were waited for; matrix products, arithmetic and copies ran while one was open for 1% of the time, Pallas kernels for 0%

profile of v5, /device:TPU:7, one launch (start us, length us, event | category | flops | bytes accessed | tf_op | source)
XLA Modules:
  0.0 199.7 jit_solution(15817307452785059269)
XLA Ops:
  0.0 0.7 collective-permute-start.1
  0.7 0.7 broadcast_multiply_fusion.1
  1.4 0.9 fusion.57.values_ref
  2.4 3.4 %copy-done = bf16[1,1,2048,2048]{3,2,1,0:T(8,128)(2,1)S(1)} copy-done((bf16[1,1,2048,2048]{3,2,1,0:T(8,128)(2,1)S(1)}, bf16[1,1,2048,2048]{3,2,1,0:T(8,128)(2,1)}, u32[]{:S(2)}) %copy-start) | copy-done | bytes 8388632
  5.8 1.5 shard_map.37.values_ref
  7.3 1.3 collective-permute-start.2
  8.6 3.2 %collective-permute-done.2.partner_ref = bf16[32,2048]{1,0:T(8,128)(2,1)S(1)} collective-permute-done((bf16[32,2048]{1,0:T(8,128)(2,1)S(1)}, bf16[32,2048]{1,0:T(8,128)(2,1)S(1)}, u32[]{:S(2)}, u32[]{:S(2)}) %collective-permute-start.2) | collective-permute-done | bytes 131104 | tf_op jit(solution)/shard_map/ppermute | solution.py:21
  11.9 3.4 %copy-done.1 = bf16[1,1,2048,2048]{3,2,1,0:T(8,128)(2,1)S(1)} copy-done((bf16[1,1,2048,2048]{3,2,1,0:T(8,128)(2,1)S(1)}, bf16[1,1,2048,2048]{3,2,1,0:T(8,128)(2,1)}, u32[]{:S(2)}) %copy-start.1) | copy-done | bytes 8388632
  15.3 1.5 shard_map.38.values_ref
  16.8 2.3 %collective-permute-start.3 = (bf16[32,2048]{1,0:T(8,128)(2,1)S(1)}, bf16[32,2048]{1,0:T(8,128)(2,1)S(1)}, u32[]{:S(2)}, u32[]{:S(2)}) collective-permute-start(bf16[32,2048]{1,0:T(8,128)(2,1)S(1)} %shard_map.38.values_ref), channel_id=1, source_target_pairs={{0,4},{4,0},{1,5},{5,1},{2,6},{6,2},{3,7},{7,3},{8,12},{12,8},{9,1... | collective-permute-start | bytes 393224 | tf_op jit(solution)/shard_map/ppermute | solution.py:21
  19.1 5.8 %collective-permute-done.3.partner_ref = bf16[32,2048]{1,0:T(8,128)(2,1)S(1)} collective-permute-done((bf16[32,2048]{1,0:T(8,128)(2,1)S(1)}, bf16[32,2048]{1,0:T(8,128)(2,1)S(1)}, u32[]{:S(2)}, u32[]{:S(2)}) %collective-permute-start.3) | collective-permute-done | bytes 131104 | tf_op jit(solution)/shard_map/ppermute | solution.py:21
  25.0 3.4 %copy-done.2 = bf16[1,1,2048,2048]{3,2,1,0:T(8,128)(2,1)S(1)} copy-done((bf16[1,1,2048,2048]{3,2,1,0:T(8,128)(2,1)S(1)}, bf16[1,1,2048,2048]{3,2,1,0:T(8,128)(2,1)}, u32[]{:S(2)}) %copy-start.2) | copy-done | bytes 8388632
  28.3 1.5 shard_map.39.values_ref
  29.9 2.5 %shard_map.40 = bf16[32,2048]{1,0:T(8,128)(2,1)S(1)} custom-call(bf16[32,2048]{1,0:T(8,128)(2,1)S(1)} %shard_map.39.values_ref, bf16[2048,2048]{1,0:T(8,128)(2,1)S(1)} %bitcast.14), custom_call_target="tpu_custom_call" | custom-call | flops 268435456 | bytes 8781824 | tf_op jit(solution)/shard_map/pallas_call | solution.py:79
  32.4 4.7 %collective-permute-done.4 = bf16[32,2048]{1,0:T(8,128)(2,1)S(1)} collective-permute-done((bf16[32,2048]{1,0:T(8,128)(2,1)S(1)}, bf16[32,2048]{1,0:T(8,128)(2,1)S(1)}, u32[]{:S(2)}, u32[]{:S(2)}) %collective-permute-start.4) | collective-permute-done | bytes 131104 | tf_op jit(solution)/shard_map/ppermute | solution.py:21
  37.2 2.6 %collective-permute-start.5 = (bf16[32,2048]{1,0:T(8,128)(2,1)S(1)}, bf16[32,2048]{1,0:T(8,128)(2,1)S(1)}, u32[]{:S(2)}, u32[]{:S(2)}) collective-permute-start(bf16[32,2048]{1,0:T(8,128)(2,1)S(1)} %fusion.2), channel_id=1, source_target_pairs={{0,2},{2,0},{1,3},{3,1},{4,6},{6,4},{5,7},{7,5},{8,10},{10,8},{9,1... | collective-permute-start | bytes 393224 | tf_op jit(solution)/shard_map/ppermute | solution.py:21
  39.8 3.1 %collective-permute-done.5 = bf16[32,2048]{1,0:T(8,128)(2,1)S(1)} collective-permute-done((bf16[32,2048]{1,0:T(8,128)(2,1)S(1)}, bf16[32,2048]{1,0:T(8,128)(2,1)S(1)}, u32[]{:S(2)}, u32[]{:S(2)}) %collective-permute-start.5) | collective-permute-done | bytes 131104 | tf_op jit(solution)/shard_map/ppermute | solution.py:21
  43.0 1.3 collective-permute-start.6
  44.3 4.4 %collective-permute-done.6 = bf16[32,2048]{1,0:T(8,128)(2,1)S(1)} collective-permute-done((bf16[32,2048]{1,0:T(8,128)(2,1)S(1)}, bf16[32,2048]{1,0:T(8,128)(2,1)S(1)}, u32[]{:S(2)}, u32[]{:S(2)}) %collective-permute-start.6) | collective-permute-done | bytes 131104 | tf_op jit(solution)/shard_map/ppermute | solution.py:27
  48.7 5.7 %collective-permute-start.7 = (bf16[32,2048]{1,0:T(8,128)(2,1)S(1)}, bf16[32,2048]{1,0:T(8,128)(2,1)S(1)}, u32[]{:S(2)}, u32[]{:S(2)}) collective-permute-start(bf16[32,2048]{1,0:T(8,128)(2,1)S(1)} %broadcast_select_fusion), channel_id=1, source_target_pairs={{0,1},{1,0},{2,3},{3,2},{4,5},{5,4},{6,7},{7,6},{8,9},{9,8},{10,11... | collective-permute-start | bytes 393224 | tf_op jit(solution)/shard_map/ppermute | solution.py:21
  54.4 1.0 collective-permute-done.7
  55.5 3.4 %copy-done.3 = bf16[1,1,2048,2048]{3,2,1,0:T(8,128)(2,1)S(1)} copy-done((bf16[1,1,2048,2048]{3,2,1,0:T(8,128)(2,1)S(1)}, bf16[1,1,2048,2048]{3,2,1,0:T(8,128)(2,1)}, u32[]{:S(2)}) %copy-start.3) | copy-done | bytes 8388632
  58.9 1.5 shard_map.41.values_ref
  60.5 4.7 %collective-permute-done.8.partner_ref = bf16[32,2048]{1,0:T(8,128)(2,1)S(1)} collective-permute-done((bf16[32,2048]{1,0:T(8,128)(2,1)S(1)}, bf16[32,2048]{1,0:T(8,128)(2,1)S(1)}, u32[]{:S(2)}, u32[]{:S(2)}) %collective-permute-start.8) | collective-permute-done | bytes 131104 | tf_op jit(solution)/shard_map/ppermute | solution.py:21
  65.2 3.4 %copy-done.4 = bf16[1,1,2048,2048]{3,2,1,0:T(8,128)(2,1)S(1)} copy-done((bf16[1,1,2048,2048]{3,2,1,0:T(8,128)(2,1)S(1)}, bf16[1,1,2048,2048]{3,2,1,0:T(8,128)(2,1)}, u32[]{:S(2)}) %copy-start.4) | copy-done | bytes 8388632
  68.5 1.5 shard_map.42.values_ref
  70.1 0.3 collective-permute-start.9
  70.4 8.9 %collective-permute-done.9.partner_ref = bf16[32,2048]{1,0:T(8,128)(2,1)S(1)} collective-permute-done((bf16[32,2048]{1,0:T(8,128)(2,1)S(1)}, bf16[32,2048]{1,0:T(8,128)(2,1)S(1)}, u32[]{:S(2)}, u32[]{:S(2)}) %collective-permute-start.9) | collective-permute-done | bytes 131104 | tf_op jit(solution)/shard_map/ppermute | solution.py:21
  79.2 1.5 shard_map.43.values_ref
  80.8 2.5 %shard_map.44 = bf16[32,2048]{1,0:T(8,128)(2,1)S(1)} custom-call(bf16[32,2048]{1,0:T(8,128)(2,1)S(1)} %shard_map.43.values_ref, bf16[2048,2048]{1,0:T(8,128)(2,1)S(1)} %bitcast.18), custom_call_target="tpu_custom_call" | custom-call | flops 268435456 | bytes 8781824 | tf_op jit(solution)/shard_map/pallas_call | solution.py:79
  83.3 7.9 %collective-permute-done.10 = bf16[32,2048]{1,0:T(8,128)(2,1)S(1)} collective-permute-done((bf16[32,2048]{1,0:T(8,128)(2,1)S(1)}, bf16[32,2048]{1,0:T(8,128)(2,1)S(1)}, u32[]{:S(2)}, u32[]{:S(2)}) %collective-permute-start.10) | collective-permute-done | bytes 131104 | tf_op jit(solution)/shard_map/ppermute | solution.py:21
  91.4 4.6 %collective-permute-done.11 = bf16[32,2048]{1,0:T(8,128)(2,1)S(1)} collective-permute-done((bf16[32,2048]{1,0:T(8,128)(2,1)S(1)}, bf16[32,2048]{1,0:T(8,128)(2,1)S(1)}, u32[]{:S(2)}, u32[]{:S(2)}) %collective-permute-start.11) | collective-permute-done | bytes 131104 | tf_op jit(solution)/shard_map/ppermute | solution.py:21
  96.0 1.5 collective-permute-start.12
  97.5 4.2 %collective-permute-done.12 = bf16[32,2048]{1,0:T(8,128)(2,1)S(1)} collective-permute-done((bf16[32,2048]{1,0:T(8,128)(2,1)S(1)}, bf16[32,2048]{1,0:T(8,128)(2,1)S(1)}, u32[]{:S(2)}, u32[]{:S(2)}) %collective-permute-start.12) | collective-permute-done | bytes 131104 | tf_op jit(solution)/shard_map/ppermute | solution.py:27
  101.8 2.6 %collective-permute-start.13 = (bf16[32,2048]{1,0:T(8,128)(2,1)S(1)}, bf16[32,2048]{1,0:T(8,128)(2,1)S(1)}, u32[]{:S(2)}, u32[]{:S(2)}) collective-permute-start(bf16[32,2048]{1,0:T(8,128)(2,1)S(1)} %broadcast_select_fusion.1), channel_id=1, source_target_pairs={{0,1},{1,0},{2,3},{3,2},{4,5},{5,4},{6,7},{7,6},{8,9},{9,8},{10,11... | collective-permute-start | bytes 393224 | tf_op jit(solution)/shard_map/ppermute | solution.py:21
  104.3 1.0 collective-permute-done.13
  105.5 3.4 %copy-done.5 = bf16[1,1,2048,2048]{3,2,1,0:T(8,128)(2,1)S(1)} copy-done((bf16[1,1,2048,2048]{3,2,1,0:T(8,128)(2,1)S(1)}, bf16[1,1,2048,2048]{3,2,1,0:T(8,128)(2,1)}, u32[]{:S(2)}) %copy-start.5) | copy-done | bytes 8388632
  108.8 1.5 shard_map.45.values_ref
  110.4 4.7 %collective-permute-done.14.partner_ref = bf16[32,2048]{1,0:T(8,128)(2,1)S(1)} collective-permute-done((bf16[32,2048]{1,0:T(8,128)(2,1)S(1)}, bf16[32,2048]{1,0:T(8,128)(2,1)S(1)}, u32[]{:S(2)}, u32[]{:S(2)}) %collective-permute-start.14) | collective-permute-done | bytes 131104 | tf_op jit(solution)/shard_map/ppermute | solution.py:21
  115.1 3.4 %copy-done.6 = bf16[1,1,2048,2048]{3,2,1,0:T(8,128)(2,1)S(1)} copy-done((bf16[1,1,2048,2048]{3,2,1,0:T(8,128)(2,1)S(1)}, bf16[1,1,2048,2048]{3,2,1,0:T(8,128)(2,1)}, u32[]{:S(2)}) %copy-start.6) | copy-done | bytes 8388632
  118.5 1.5 shard_map.46.values_ref
  120.0 0.9 collective-permute-start.15
  120.9 7.8 %collective-permute-done.15.partner_ref = bf16[32,2048]{1,0:T(8,128)(2,1)S(1)} collective-permute-done((bf16[32,2048]{1,0:T(8,128)(2,1)S(1)}, bf16[32,2048]{1,0:T(8,128)(2,1)S(1)}, u32[]{:S(2)}, u32[]{:S(2)}) %collective-permute-start.15) | collective-permute-done | bytes 131104 | tf_op jit(solution)/shard_map/ppermute | solution.py:21
  128.7 1.5 shard_map.47.values_ref
  130.3 2.5 %shard_map.48 = bf16[32,2048]{1,0:T(8,128)(2,1)S(1)} custom-call(bf16[32,2048]{1,0:T(8,128)(2,1)S(1)} %shard_map.47.values_ref, bf16[2048,2048]{1,0:T(8,128)(2,1)S(1)} %bitcast.22), custom_call_target="tpu_custom_call" | custom-call | flops 268435456 | bytes 8781824 | tf_op jit(solution)/shard_map/pallas_call | solution.py:79
  132.8 8.8 %collective-permute-done.16 = bf16[32,2048]{1,0:T(8,128)(2,1)S(1)} collective-permute-done((bf16[32,2048]{1,0:T(8,128)(2,1)S(1)}, bf16[32,2048]{1,0:T(8,128)(2,1)S(1)}, u32[]{:S(2)}, u32[]{:S(2)}) %collective-permute-start.16) | collective-permute-done | bytes 131104 | tf_op jit(solution)/shard_map/ppermute | solution.py:21
  141.8 4.5 %collective-permute-done.17 = bf16[32,2048]{1,0:T(8,128)(2,1)S(1)} collective-permute-done((bf16[32,2048]{1,0:T(8,128)(2,1)S(1)}, bf16[32,2048]{1,0:T(8,128)(2,1)S(1)}, u32[]{:S(2)}, u32[]{:S(2)}) %collective-permute-start.17) | collective-permute-done | bytes 131104 | tf_op jit(solution)/shard_map/ppermute | solution.py:21
  146.4 1.3 collective-permute-start.18
  147.7 5.0 %collective-permute-done.18 = bf16[32,2048]{1,0:T(8,128)(2,1)S(1)} collective-permute-done((bf16[32,2048]{1,0:T(8,128)(2,1)S(1)}, bf16[32,2048]{1,0:T(8,128)(2,1)S(1)}, u32[]{:S(2)}, u32[]{:S(2)}) %collective-permute-start.18) | collective-permute-done | bytes 131104 | tf_op jit(solution)/shard_map/ppermute | solution.py:27
  152.8 2.3 %collective-permute-start.19 = (bf16[32,2048]{1,0:T(8,128)(2,1)S(1)}, bf16[32,2048]{1,0:T(8,128)(2,1)S(1)}, u32[]{:S(2)}, u32[]{:S(2)}) collective-permute-start(bf16[32,2048]{1,0:T(8,128)(2,1)S(1)} %broadcast_select_fusion.2), channel_id=1, source_target_pairs={{0,1},{1,0},{2,3},{3,2},{4,5},{5,4},{6,7},{7,6},{8,9},{9,8},{10,11... | collective-permute-start | bytes 393224 | tf_op jit(solution)/shard_map/ppermute | solution.py:21
  155.0 1.0 collective-permute-done.19
  156.2 3.4 %copy-done.7 = bf16[1,1,2048,2048]{3,2,1,0:T(8,128)(2,1)S(1)} copy-done((bf16[1,1,2048,2048]{3,2,1,0:T(8,128)(2,1)S(1)}, bf16[1,1,2048,2048]{3,2,1,0:T(8,128)(2,1)}, u32[]{:S(2)}) %copy-start.7) | copy-done | bytes 8388632
  159.6 1.5 shard_map.49.values_ref
  161.3 4.5 %collective-permute-done.20.partner_ref = bf16[32,2048]{1,0:T(8,128)(2,1)S(1)} collective-permute-done((bf16[32,2048]{1,0:T(8,128)(2,1)S(1)}, bf16[32,2048]{1,0:T(8,128)(2,1)S(1)}, u32[]{:S(2)}, u32[]{:S(2)}) %collective-permute-start.20) | collective-permute-done | bytes 131104 | tf_op jit(solution)/shard_map/ppermute | solution.py:21
  165.8 3.4 %copy-done.8 = bf16[1,1,2048,2048]{3,2,1,0:T(8,128)(2,1)S(1)} copy-done((bf16[1,1,2048,2048]{3,2,1,0:T(8,128)(2,1)S(1)}, bf16[1,1,2048,2048]{3,2,1,0:T(8,128)(2,1)}, u32[]{:S(2)}) %copy-start.8) | copy-done | bytes 8388632
  169.2 1.5 shard_map.50.values_ref
  170.9 8.7 %collective-permute-done.21.partner_ref = bf16[32,2048]{1,0:T(8,128)(2,1)S(1)} collective-permute-done((bf16[32,2048]{1,0:T(8,128)(2,1)S(1)}, bf16[32,2048]{1,0:T(8,128)(2,1)S(1)}, u32[]{:S(2)}, u32[]{:S(2)}) %collective-permute-start.21) | collective-permute-done | bytes 131104 | tf_op jit(solution)/shard_map/ppermute | solution.py:21
  179.6 1.5 shard_map.51.values_ref
  181.1 2.5 %shard_map.52 = bf16[32,2048]{1,0:T(8,128)(2,1)S(1)} custom-call(bf16[32,2048]{1,0:T(8,128)(2,1)S(1)} %shard_map.51.values_ref, bf16[2048,2048]{1,0:T(8,128)(2,1)S(1)} %bitcast.26), custom_call_target="tpu_custom_call" | custom-call | flops 268435456 | bytes 8781824 | tf_op jit(solution)/shard_map/pallas_call | solution.py:79
  183.7 7.9 %collective-permute-done.22 = bf16[32,2048]{1,0:T(8,128)(2,1)S(1)} collective-permute-done((bf16[32,2048]{1,0:T(8,128)(2,1)S(1)}, bf16[32,2048]{1,0:T(8,128)(2,1)S(1)}, u32[]{:S(2)}, u32[]{:S(2)}) %collective-permute-start.22) | collective-permute-done | bytes 131104 | tf_op jit(solution)/shard_map/ppermute | solution.py:21
  191.8 4.5 %collective-permute-done.23 = bf16[32,2048]{1,0:T(8,128)(2,1)S(1)} collective-permute-done((bf16[32,2048]{1,0:T(8,128)(2,1)S(1)}, bf16[32,2048]{1,0:T(8,128)(2,1)S(1)}, u32[]{:S(2)}, u32[]{:S(2)}) %collective-permute-start.23) | collective-permute-done | bytes 131104 | tf_op jit(solution)/shard_map/ppermute | solution.py:21
  196.4 1.4 collective-permute-start.24
  197.8 1.0 collective-permute-done.24
  198.8 0.9 fusion.66
  (46 shorter events, 1.8 us)
Async XLA Ops:
  0.0 2.3 %collective-permute-start.1 = (f32[1,2048]{1,0:T(1,128)}, f32[1,2048]{1,0:T(1,128)S(1)}, u32[]{:S(2)}, u32[]{:S(2)}) collective-permute-start(f32[1,2048]{1,0:T(1,128)} %bitcast.28), channel_id=1, source_target_pairs={{0,1},{1,0},{2,3},{3,2},{4,5},{5,4},{6,7},{7,6},{8,9},{9,8},{10,11... | collective-permute-start | bytes 24584 | tf_op jit(solution)/shard_map/ppermute | solution.py:21
  0.7 1.7 collective-permute-start
  2.4 3.4 %copy-start = (bf16[1,1,2048,2048]{3,2,1,0:T(8,128)(2,1)S(1)}, bf16[1,1,2048,2048]{3,2,1,0:T(8,128)(2,1)}, u32[]{:S(2)}) copy-start(bf16[1,1,2048,2048]{3,2,1,0:T(8,128)(2,1)} %param.5) | copy-start | bytes 25165828
  7.3 4.6 %collective-permute-start.2 = (bf16[32,2048]{1,0:T(8,128)(2,1)S(1)}, bf16[32,2048]{1,0:T(8,128)(2,1)S(1)}, u32[]{:S(2)}, u32[]{:S(2)}) collective-permute-start(bf16[32,2048]{1,0:T(8,128)(2,1)S(1)} %shard_map.37.values_ref), channel_id=1, source_target_pairs={{0,2},{2,0},{1,3},{3,1},{4,6},{6,4},{5,7},{7,5},{8,10},{10,8},{9,1... | collective-permute-start | bytes 393224 | tf_op jit(solution)/shard_map/ppermute | solution.py:21
  11.9 3.4 %copy-start.1 = (bf16[1,1,2048,2048]{3,2,1,0:T(8,128)(2,1)S(1)}, bf16[1,1,2048,2048]{3,2,1,0:T(8,128)(2,1)}, u32[]{:S(2)}) copy-start(bf16[1,1,2048,2048]{3,2,1,0:T(8,128)(2,1)} %param.5) | copy-start | bytes 25165828
  16.8 8.1 %collective-permute-start.3 = (bf16[32,2048]{1,0:T(8,128)(2,1)S(1)}, bf16[32,2048]{1,0:T(8,128)(2,1)S(1)}, u32[]{:S(2)}, u32[]{:S(2)}) collective-permute-start(bf16[32,2048]{1,0:T(8,128)(2,1)S(1)} %shard_map.38.values_ref), channel_id=1, source_target_pairs={{0,4},{4,0},{1,5},{5,1},{2,6},{6,2},{3,7},{7,3},{8,12},{12,8},{9,1... | collective-permute-start | bytes 393224 | tf_op jit(solution)/shard_map/ppermute | solution.py:21
  25.0 3.4 %copy-start.2 = (bf16[1,1,2048,2048]{3,2,1,0:T(8,128)(2,1)S(1)}, bf16[1,1,2048,2048]{3,2,1,0:T(8,128)(2,1)}, u32[]{:S(2)}) copy-start(bf16[1,1,2048,2048]{3,2,1,0:T(8,128)(2,1)} %param.5) | copy-start | bytes 25165828
  28.3 27.0 %copy-start.9 = (bf16[1,1,32,2048]{3,2,1,0:T(8,128)(2,1)S(1)}, bf16[1,1,32,2048]{3,2,1,0:T(8,128)(2,1)}, u32[]{:S(2)}) copy-start(bf16[1,1,32,2048]{3,2,1,0:T(8,128)(2,1)} %param.3) | copy-start | bytes 393220
  28.3 27.0 %copy-start.10 = (f32[1,1,2048]{2,1,0:T(1,128)S(1)}, f32[1,1,2048]{2,1,0:T(1,128)}, u32[]{:S(2)}) copy-start(f32[1,1,2048]{2,1,0:T(1,128)} %param.4) | copy-start | bytes 24580
  32.4 4.7 %collective-permute-start.4 = (bf16[32,2048]{1,0:T(8,128)(2,1)S(1)}, bf16[32,2048]{1,0:T(8,128)(2,1)S(1)}, u32[]{:S(2)}, u32[]{:S(2)}) collective-permute-start(bf16[32,2048]{1,0:T(8,128)(2,1)S(1)} %shard_map.40), channel_id=1, source_target_pairs={{0,4},{4,0},{1,5},{5,1},{2,6},{6,2},{3,7},{7,3},{8,12},{12,8},{9,1... | collective-permute-start | bytes 393224 | tf_op jit(solution)/shard_map/ppermute | solution.py:21
  37.2 5.7 %collective-permute-start.5 = (bf16[32,2048]{1,0:T(8,128)(2,1)S(1)}, bf16[32,2048]{1,0:T(8,128)(2,1)S(1)}, u32[]{:S(2)}, u32[]{:S(2)}) collective-permute-start(bf16[32,2048]{1,0:T(8,128)(2,1)S(1)} %fusion.2), channel_id=1, source_target_pairs={{0,2},{2,0},{1,3},{3,1},{4,6},{6,4},{5,7},{7,5},{8,10},{10,8},{9,1... | collective-permute-start | bytes 393224 | tf_op jit(solution)/shard_map/ppermute | solution.py:21
  43.0 5.7 %collective-permute-start.6 = (bf16[32,2048]{1,0:T(8,128)(2,1)S(1)}, bf16[32,2048]{1,0:T(8,128)(2,1)S(1)}, u32[]{:S(2)}, u32[]{:S(2)}) collective-permute-start(bf16[32,2048]{1,0:T(8,128)(2,1)S(1)} %fusion.6), channel_id=1, source_target_pairs={{0,8},{8,16},{16,24},{1,9},{9,17},{17,25},{2,10},{10,18},{18,26},{... | collective-permute-start | bytes 393224 | tf_op jit(solution)/shard_map/ppermute | solution.py:27
  48.7 6.7 %collective-permute-start.7 = (bf16[32,2048]{1,0:T(8,128)(2,1)S(1)}, bf16[32,2048]{1,0:T(8,128)(2,1)S(1)}, u32[]{:S(2)}, u32[]{:S(2)}) collective-permute-start(bf16[32,2048]{1,0:T(8,128)(2,1)S(1)} %broadcast_select_fusion), channel_id=1, source_target_pairs={{0,1},{1,0},{2,3},{3,2},{4,5},{5,4},{6,7},{7,6},{8,9},{9,8},{10,11... | collective-permute-start | bytes 393224 | tf_op jit(solution)/shard_map/ppermute | solution.py:21
  55.5 3.4 %copy-start.3 = (bf16[1,1,2048,2048]{3,2,1,0:T(8,128)(2,1)S(1)}, bf16[1,1,2048,2048]{3,2,1,0:T(8,128)(2,1)}, u32[]{:S(2)}) copy-start(bf16[1,1,2048,2048]{3,2,1,0:T(8,128)(2,1)} %param.5) | copy-start | bytes 25165828
  60.5 4.7 %collective-permute-start.8 = (bf16[32,2048]{1,0:T(8,128)(2,1)S(1)}, bf16[32,2048]{1,0:T(8,128)(2,1)S(1)}, u32[]{:S(2)}, u32[]{:S(2)}) collective-permute-start(bf16[32,2048]{1,0:T(8,128)(2,1)S(1)} %shard_map.41.values_ref), channel_id=1, source_target_pairs={{0,2},{2,0},{1,3},{3,1},{4,6},{6,4},{5,7},{7,5},{8,10},{10,8},{9,1... | collective-permute-start | bytes 393224 | tf_op jit(solution)/shard_map/ppermute | solution.py:21
  65.2 3.4 %copy-start.4 = (bf16[1,1,2048,2048]{3,2,1,0:T(8,128)(2,1)S(1)}, bf16[1,1,2048,2048]{3,2,1,0:T(8,128)(2,1)}, u32[]{:S(2)}) copy-start(bf16[1,1,2048,2048]{3,2,1,0:T(8,128)(2,1)} %param.5) | copy-start | bytes 25165828
  70.1 9.1 %collective-permute-start.9 = (bf16[32,2048]{1,0:T(8,128)(2,1)S(1)}, bf16[32,2048]{1,0:T(8,128)(2,1)S(1)}, u32[]{:S(2)}, u32[]{:S(2)}) collective-permute-start(bf16[32,2048]{1,0:T(8,128)(2,1)S(1)} %shard_map.42.values_ref), channel_id=1, source_target_pairs={{0,4},{4,0},{1,5},{5,1},{2,6},{6,2},{3,7},{7,3},{8,12},{12,8},{9,1... | collective-permute-start | bytes 393224 | tf_op jit(solution)/shard_map/ppermute | solution.py:21
  83.3 8.0 %collective-permute-start.10 = (bf16[32,2048]{1,0:T(8,128)(2,1)S(1)}, bf16[32,2048]{1,0:T(8,128)(2,1)S(1)}, u32[]{:S(2)}, u32[]{:S(2)}) collective-permute-start(bf16[32,2048]{1,0:T(8,128)(2,1)S(1)} %shard_map.44), channel_id=1, source_target_pairs={{0,4},{4,0},{1,5},{5,1},{2,6},{6,2},{3,7},{7,3},{8,12},{12,8},{9,1... | collective-permute-start | bytes 393224 | tf_op jit(solution)/shard_map/ppermute | solution.py:21
  91.3 4.6 %collective-permute-start.11 = (bf16[32,2048]{1,0:T(8,128)(2,1)S(1)}, bf16[32,2048]{1,0:T(8,128)(2,1)S(1)}, u32[]{:S(2)}, u32[]{:S(2)}) collective-permute-start(bf16[32,2048]{1,0:T(8,128)(2,1)S(1)} %fusion.10), channel_id=1, source_target_pairs={{0,2},{2,0},{1,3},{3,1},{4,6},{6,4},{5,7},{7,5},{8,10},{10,8},{9,1... | collective-permute-start | bytes 393224 | tf_op jit(solution)/shard_map/ppermute | solution.py:21
  96.0 5.7 %collective-permute-start.12 = (bf16[32,2048]{1,0:T(8,128)(2,1)S(1)}, bf16[32,2048]{1,0:T(8,128)(2,1)S(1)}, u32[]{:S(2)}, u32[]{:S(2)}) collective-permute-start(bf16[32,2048]{1,0:T(8,128)(2,1)S(1)} %fusion.14), channel_id=1, source_target_pairs={{0,8},{8,16},{16,24},{1,9},{9,17},{17,25},{2,10},{10,18},{18,26},{... | collective-permute-start | bytes 393224 | tf_op jit(solution)/shard_map/ppermute | solution.py:27
  101.8 3.5 %collective-permute-start.13 = (bf16[32,2048]{1,0:T(8,128)(2,1)S(1)}, bf16[32,2048]{1,0:T(8,128)(2,1)S(1)}, u32[]{:S(2)}, u32[]{:S(2)}) collective-permute-start(bf16[32,2048]{1,0:T(8,128)(2,1)S(1)} %broadcast_select_fusion.1), channel_id=1, source_target_pairs={{0,1},{1,0},{2,3},{3,2},{4,5},{5,4},{6,7},{7,6},{8,9},{9,8},{10,11... | collective-permute-start | bytes 393224 | tf_op jit(solution)/shard_map/ppermute | solution.py:21
  105.5 3.4 %copy-start.5 = (bf16[1,1,2048,2048]{3,2,1,0:T(8,128)(2,1)S(1)}, bf16[1,1,2048,2048]{3,2,1,0:T(8,128)(2,1)}, u32[]{:S(2)}) copy-start(bf16[1,1,2048,2048]{3,2,1,0:T(8,128)(2,1)} %param.5) | copy-start | bytes 25165828
  110.4 4.7 %collective-permute-start.14 = (bf16[32,2048]{1,0:T(8,128)(2,1)S(1)}, bf16[32,2048]{1,0:T(8,128)(2,1)S(1)}, u32[]{:S(2)}, u32[]{:S(2)}) collective-permute-start(bf16[32,2048]{1,0:T(8,128)(2,1)S(1)} %shard_map.45.values_ref), channel_id=1, source_target_pairs={{0,2},{2,0},{1,3},{3,1},{4,6},{6,4},{5,7},{7,5},{8,10},{10,8},{9,1... | collective-permute-start | bytes 393224 | tf_op jit(solution)/shard_map/ppermute | solution.py:21
  115.1 3.4 %copy-start.6 = (bf16[1,1,2048,2048]{3,2,1,0:T(8,128)(2,1)S(1)}, bf16[1,1,2048,2048]{3,2,1,0:T(8,128)(2,1)}, u32[]{:S(2)}) copy-start(bf16[1,1,2048,2048]{3,2,1,0:T(8,128)(2,1)} %param.5) | copy-start | bytes 25165828
  120.0 8.7 %collective-permute-start.15 = (bf16[32,2048]{1,0:T(8,128)(2,1)S(1)}, bf16[32,2048]{1,0:T(8,128)(2,1)S(1)}, u32[]{:S(2)}, u32[]{:S(2)}) collective-permute-start(bf16[32,2048]{1,0:T(8,128)(2,1)S(1)} %shard_map.46.values_ref), channel_id=1, source_target_pairs={{0,4},{4,0},{1,5},{5,1},{2,6},{6,2},{3,7},{7,3},{8,12},{12,8},{9,1... | collective-permute-start | bytes 393224 | tf_op jit(solution)/shard_map/ppermute | solution.py:21
  132.8 8.9 %collective-permute-start.16 = (bf16[32,2048]{1,0:T(8,128)(2,1)S(1)}, bf16[32,2048]{1,0:T(8,128)(2,1)S(1)}, u32[]{:S(2)}, u32[]{:S(2)}) collective-permute-start(bf16[32,2048]{1,0:T(8,128)(2,1)S(1)} %shard_map.48), channel_id=1, source_target_pairs={{0,4},{4,0},{1,5},{5,1},{2,6},{6,2},{3,7},{7,3},{8,12},{12,8},{9,1... | collective-permute-start | bytes 393224 | tf_op jit(solution)/shard_map/ppermute | solution.py:21
  141.7 4.6 %collective-permute-start.17 = (bf16[32,2048]{1,0:T(8,128)(2,1)S(1)}, bf16[32,2048]{1,0:T(8,128)(2,1)S(1)}, u32[]{:S(2)}, u32[]{:S(2)}) collective-permute-start(bf16[32,2048]{1,0:T(8,128)(2,1)S(1)} %fusion.18), channel_id=1, source_target_pairs={{0,2},{2,0},{1,3},{3,1},{4,6},{6,4},{5,7},{7,5},{8,10},{10,8},{9,1... | collective-permute-start | bytes 393224 | tf_op jit(solution)/shard_map/ppermute | solution.py:21
  146.4 6.3 %collective-permute-start.18 = (bf16[32,2048]{1,0:T(8,128)(2,1)S(1)}, bf16[32,2048]{1,0:T(8,128)(2,1)S(1)}, u32[]{:S(2)}, u32[]{:S(2)}) collective-permute-start(bf16[32,2048]{1,0:T(8,128)(2,1)S(1)} %fusion.22), channel_id=1, source_target_pairs={{0,8},{8,16},{16,24},{1,9},{9,17},{17,25},{2,10},{10,18},{18,26},{... | collective-permute-start | bytes 393224 | tf_op jit(solution)/shard_map/ppermute | solution.py:27
  152.8 3.3 %collective-permute-start.19 = (bf16[32,2048]{1,0:T(8,128)(2,1)S(1)}, bf16[32,2048]{1,0:T(8,128)(2,1)S(1)}, u32[]{:S(2)}, u32[]{:S(2)}) collective-permute-start(bf16[32,2048]{1,0:T(8,128)(2,1)S(1)} %broadcast_select_fusion.2), channel_id=1, source_target_pairs={{0,1},{1,0},{2,3},{3,2},{4,5},{5,4},{6,7},{7,6},{8,9},{9,8},{10,11... | collective-permute-start | bytes 393224 | tf_op jit(solution)/shard_map/ppermute | solution.py:21
  156.2 3.4 %copy-start.7 = (bf16[1,1,2048,2048]{3,2,1,0:T(8,128)(2,1)S(1)}, bf16[1,1,2048,2048]{3,2,1,0:T(8,128)(2,1)}, u32[]{:S(2)}) copy-start(bf16[1,1,2048,2048]{3,2,1,0:T(8,128)(2,1)} %param.5) | copy-start | bytes 25165828
  161.1 4.7 %collective-permute-start.20 = (bf16[32,2048]{1,0:T(8,128)(2,1)S(1)}, bf16[32,2048]{1,0:T(8,128)(2,1)S(1)}, u32[]{:S(2)}, u32[]{:S(2)}) collective-permute-start(bf16[32,2048]{1,0:T(8,128)(2,1)S(1)} %shard_map.49.values_ref), channel_id=1, source_target_pairs={{0,2},{2,0},{1,3},{3,1},{4,6},{6,4},{5,7},{7,5},{8,10},{10,8},{9,1... | collective-permute-start | bytes 393224 | tf_op jit(solution)/shard_map/ppermute | solution.py:21
  165.8 3.4 %copy-start.8 = (bf16[1,1,2048,2048]{3,2,1,0:T(8,128)(2,1)S(1)}, bf16[1,1,2048,2048]{3,2,1,0:T(8,128)(2,1)}, u32[]{:S(2)}) copy-start(bf16[1,1,2048,2048]{3,2,1,0:T(8,128)(2,1)} %param.5) | copy-start | bytes 25165828
  170.7 8.8 %collective-permute-start.21 = (bf16[32,2048]{1,0:T(8,128)(2,1)S(1)}, bf16[32,2048]{1,0:T(8,128)(2,1)S(1)}, u32[]{:S(2)}, u32[]{:S(2)}) collective-permute-start(bf16[32,2048]{1,0:T(8,128)(2,1)S(1)} %shard_map.50.values_ref), channel_id=1, source_target_pairs={{0,4},{4,0},{1,5},{5,1},{2,6},{6,2},{3,7},{7,3},{8,12},{12,8},{9,1... | collective-permute-start | bytes 393224 | tf_op jit(solution)/shard_map/ppermute | solution.py:21
  183.7 8.0 %collective-permute-start.22 = (bf16[32,2048]{1,0:T(8,128)(2,1)S(1)}, bf16[32,2048]{1,0:T(8,128)(2,1)S(1)}, u32[]{:S(2)}, u32[]{:S(2)}) collective-permute-start(bf16[32,2048]{1,0:T(8,128)(2,1)S(1)} %shard_map.52), channel_id=1, source_target_pairs={{0,4},{4,0},{1,5},{5,1},{2,6},{6,2},{3,7},{7,3},{8,12},{12,8},{9,1... | collective-permute-start | bytes 393224 | tf_op jit(solution)/shard_map/ppermute | solution.py:21
  191.7 4.6 %collective-permute-start.23 = (bf16[32,2048]{1,0:T(8,128)(2,1)S(1)}, bf16[32,2048]{1,0:T(8,128)(2,1)S(1)}, u32[]{:S(2)}, u32[]{:S(2)}) collective-permute-start(bf16[32,2048]{1,0:T(8,128)(2,1)S(1)} %fusion.26), channel_id=1, source_target_pairs={{0,2},{2,0},{1,3},{3,1},{4,6},{6,4},{5,7},{7,5},{8,10},{10,8},{9,1... | collective-permute-start | bytes 393224 | tf_op jit(solution)/shard_map/ppermute | solution.py:21
  196.4 2.4 %collective-permute-start.24 = (bf16[32,2048]{1,0:T(8,128)(2,1)S(1)}, bf16[32,2048]{1,0:T(8,128)(2,1)S(1)}, u32[]{:S(2)}, u32[]{:S(2)}) collective-permute-start(bf16[32,2048]{1,0:T(8,128)(2,1)S(1)} %fusion.30), channel_id=1, source_target_pairs={{0,1},{1,0},{2,3},{3,2},{4,5},{5,4},{6,7},{7,6},{8,9},{9,8},{10,11... | collective-permute-start | bytes 393224 | tf_op jit(solution)/shard_map/ppermute | solution.py:21

commit v6 on v1

--- a/solution.py
+++ b/solution.py
@@ -21,10 +21,8 @@
     return lax.ppermute(block, axis, route)
 
 
-def shifted(array, axis, by):
-    length = lax.axis_size(axis)
-    pairs = [(i, i + by) for i in range(length) if 0 <= i + by < length]
-    return lax.ppermute(array, axis, pairs)
+def handed_down(array, axis, layer):
+    return lax.ppermute(array, axis, [(layer, layer + 1)])
 
 
 def mixed_dot_kernel(sign_ref, values_ref, partner_ref, op_ref, out_ref):
@@ -131,7 +129,7 @@
         solved = sweep_layer(leaf_data, merge_op)
         result = jnp.where(depth_index == sweep_step, solved, result)
         if sweep_step + 1 < depth_count:
-            incoming = shifted(solved, "depth", 1)
+            incoming = handed_down(solved, "depth", sweep_step)
     return result[None, None]
 
 

time: 189 us -> 184 us (0.974)
  starting transfers between devices: 25.4 us -> 22.4 us
  transfers between devices with their start and end apart: 27 -> 27, of which waited for: 27 -> 25; matrix products, arithmetic and copies ran while one was open for 0% -> 0% of each run, Pallas kernels for 0% -> 0%
where the time goes in v6:
time: 184 us; the launch traced here: 183 us
  waiting for transfers between devices  119 us (65%)
  Pallas kernels  28.5 us (15%)
  starting transfers between devices  22.4 us (12%)
  local copies, waits for them, and re-layouts  10.2 us (6%)
  other arithmetic  3.29 us (2%)
    ppermute x24, waiting for transfers between devices, partner_2(): return lax.ppermute(block, axis, route)  102 us
    ppermute x24, starting transfers between devices, partner_2(): return lax.ppermute(block, axis, route)  19.6 us
    pallas_call x12, Pallas kernels, mixed_dot(): pl.pallas_call(mixed_dot_kernel, out_shape=jax.ShapeDtypeStruct(values.sh...  18.4 us
    ppermute x3, waiting for transfers between devices, handed_down(): return lax.ppermute(array, axis, [(layer, layer + 1)])  16.2 us
    pallas_call x4, Pallas kernels, transposed_dot(): pl.pallas_call(transposed_dot_kernel, out_shape=jax.ShapeDtypeStruct(valu...  10.2 us
    unnamed x14, local copies, waits for them, and re-layouts  10.2 us
  transfers between devices with their start and end apart: 27, of which 25 were waited for; matrix products, arithmetic and copies ran while one was open for 0% of the time, Pallas kernels for 0%

profile of v6, /device:TPU:7, one launch (start us, length us, event | category | flops | bytes accessed | tf_op | source)
XLA Modules:
  0.0 183.3 jit_solution(6013424769702675337)
XLA Ops:
  0.0 0.7 broadcast_multiply_fusion
  0.7 0.9 fusion.48.values_ref
  1.6 0.7 collective-permute-start
  2.4 1.0 collective-permute-done.partner_ref
  3.4 3.4 %copy-done = bf16[1,1,2048,2048]{3,2,1,0:T(8,128)(2,1)S(1)} copy-done((bf16[1,1,2048,2048]{3,2,1,0:T(8,128)(2,1)S(1)}, bf16[1,1,2048,2048]{3,2,1,0:T(8,128)(2,1)}, u32[]{:S(2)}) %copy-start) | copy-done | bytes 8388632
  6.7 1.5 shard_map.37.values_ref
  8.3 1.3 collective-permute-start.1
  9.6 3.4 %collective-permute-done.1.partner_ref = bf16[32,2048]{1,0:T(8,128)(2,1)S(1)} collective-permute-done((bf16[32,2048]{1,0:T(8,128)(2,1)S(1)}, bf16[32,2048]{1,0:T(8,128)(2,1)S(1)}, u32[]{:S(2)}, u32[]{:S(2)}) %collective-permute-start.1) | collective-permute-done | bytes 131104 | tf_op jit(solution)/shard_map/ppermute | solution.py:21
  13.0 3.4 %copy-done.1 = bf16[1,1,2048,2048]{3,2,1,0:T(8,128)(2,1)S(1)} copy-done((bf16[1,1,2048,2048]{3,2,1,0:T(8,128)(2,1)S(1)}, bf16[1,1,2048,2048]{3,2,1,0:T(8,128)(2,1)}, u32[]{:S(2)}) %copy-start.1) | copy-done | bytes 8388632
  16.4 1.5 shard_map.38.values_ref
  17.9 2.3 %collective-permute-start.2 = (bf16[32,2048]{1,0:T(8,128)(2,1)S(1)}, bf16[32,2048]{1,0:T(8,128)(2,1)S(1)}, u32[]{:S(2)}, u32[]{:S(2)}) collective-permute-start(bf16[32,2048]{1,0:T(8,128)(2,1)S(1)} %shard_map.38.values_ref), channel_id=1, source_target_pairs={{0,4},{4,0},{1,5},{5,1},{2,6},{6,2},{3,7},{7,3},{8,12},{12,8},{9,1... | collective-permute-start | bytes 393224 | tf_op jit(solution)/shard_map/ppermute | solution.py:21
  20.2 5.8 %collective-permute-done.2.partner_ref = bf16[32,2048]{1,0:T(8,128)(2,1)S(1)} collective-permute-done((bf16[32,2048]{1,0:T(8,128)(2,1)S(1)}, bf16[32,2048]{1,0:T(8,128)(2,1)S(1)}, u32[]{:S(2)}, u32[]{:S(2)}) %collective-permute-start.2) | collective-permute-done | bytes 131104 | tf_op jit(solution)/shard_map/ppermute | solution.py:21
  26.1 3.4 %copy-done.2 = bf16[1,1,2048,2048]{3,2,1,0:T(8,128)(2,1)S(1)} copy-done((bf16[1,1,2048,2048]{3,2,1,0:T(8,128)(2,1)S(1)}, bf16[1,1,2048,2048]{3,2,1,0:T(8,128)(2,1)}, u32[]{:S(2)}) %copy-start.2) | copy-done | bytes 8388632
  29.4 1.5 shard_map.39.values_ref
  31.0 2.5 %shard_map.40 = bf16[32,2048]{1,0:T(8,128)(2,1)S(1)} custom-call(bf16[32,2048]{1,0:T(8,128)(2,1)S(1)} %shard_map.39.values_ref, bf16[2048,2048]{1,0:T(8,128)(2,1)S(1)} %bitcast.13), custom_call_target="tpu_custom_call" | custom-call | flops 268435456 | bytes 8781824 | tf_op jit(solution)/shard_map/pallas_call | solution.py:77
  33.5 4.7 %collective-permute-done.3 = bf16[32,2048]{1,0:T(8,128)(2,1)S(1)} collective-permute-done((bf16[32,2048]{1,0:T(8,128)(2,1)S(1)}, bf16[32,2048]{1,0:T(8,128)(2,1)S(1)}, u32[]{:S(2)}, u32[]{:S(2)}) %collective-permute-start.3) | collective-permute-done | bytes 131104 | tf_op jit(solution)/shard_map/ppermute | solution.py:21
  38.3 2.9 %collective-permute-start.4 = (bf16[32,2048]{1,0:T(8,128)(2,1)S(1)}, bf16[32,2048]{1,0:T(8,128)(2,1)S(1)}, u32[]{:S(2)}, u32[]{:S(2)}) collective-permute-start(bf16[32,2048]{1,0:T(8,128)(2,1)S(1)} %fusion.2), channel_id=1, source_target_pairs={{0,2},{2,0},{1,3},{3,1},{4,6},{6,4},{5,7},{7,5},{8,10},{10,8},{9,1... | collective-permute-start | bytes 393224 | tf_op jit(solution)/shard_map/ppermute | solution.py:21
  41.2 2.9 %collective-permute-done.4 = bf16[32,2048]{1,0:T(8,128)(2,1)S(1)} collective-permute-done((bf16[32,2048]{1,0:T(8,128)(2,1)S(1)}, bf16[32,2048]{1,0:T(8,128)(2,1)S(1)}, u32[]{:S(2)}, u32[]{:S(2)}) %collective-permute-start.4) | collective-permute-done | bytes 131104 | tf_op jit(solution)/shard_map/ppermute | solution.py:21
  44.2 4.5 %collective-permute-start.5 = (bf16[32,2048]{1,0:T(8,128)(2,1)S(1)}, bf16[32,2048]{1,0:T(8,128)(2,1)S(1)}, u32[]{:S(2)}, u32[]{:S(2)}) collective-permute-start(bf16[32,2048]{1,0:T(8,128)(2,1)S(1)} %fusion.6), channel_id=1, source_target_pairs={{0,1},{1,0},{2,3},{3,2},{4,5},{5,4},{6,7},{7,6},{8,9},{9,8},{10,11... | collective-permute-start | bytes 393224 | tf_op jit(solution)/shard_map/ppermute | solution.py:21
  48.7 1.0 collective-permute-done.5
  49.8 0.7 collective-permute-start.6
  50.6 0.4 collective-permute-start.7
  51.0 1.0 collective-permute-done.7.partner_ref
  52.0 1.5 shard_map.41.values_ref
  53.5 4.7 %collective-permute-done.8.partner_ref = bf16[32,2048]{1,0:T(8,128)(2,1)S(1)} collective-permute-done((bf16[32,2048]{1,0:T(8,128)(2,1)S(1)}, bf16[32,2048]{1,0:T(8,128)(2,1)S(1)}, u32[]{:S(2)}, u32[]{:S(2)}) %collective-permute-start.8) | collective-permute-done | bytes 131104 | tf_op jit(solution)/shard_map/ppermute | solution.py:21
  58.2 1.5 shard_map.42.values_ref
  59.8 9.1 %collective-permute-done.9.partner_ref = bf16[32,2048]{1,0:T(8,128)(2,1)S(1)} collective-permute-done((bf16[32,2048]{1,0:T(8,128)(2,1)S(1)}, bf16[32,2048]{1,0:T(8,128)(2,1)S(1)}, u32[]{:S(2)}, u32[]{:S(2)}) %collective-permute-start.9) | collective-permute-done | bytes 131104 | tf_op jit(solution)/shard_map/ppermute | solution.py:21
  68.9 1.5 shard_map.43.values_ref
  70.4 2.5 %shard_map.44 = bf16[32,2048]{1,0:T(8,128)(2,1)S(1)} custom-call(bf16[32,2048]{1,0:T(8,128)(2,1)S(1)} %shard_map.43.values_ref, bf16[2048,2048]{1,0:T(8,128)(2,1)S(1)} %bitcast.19), custom_call_target="tpu_custom_call" | custom-call | flops 268435456 | bytes 8781824 | tf_op jit(solution)/shard_map/pallas_call | solution.py:77
  73.0 7.7 %collective-permute-done.10 = bf16[32,2048]{1,0:T(8,128)(2,1)S(1)} collective-permute-done((bf16[32,2048]{1,0:T(8,128)(2,1)S(1)}, bf16[32,2048]{1,0:T(8,128)(2,1)S(1)}, u32[]{:S(2)}, u32[]{:S(2)}) %collective-permute-start.10) | collective-permute-done | bytes 131104 | tf_op jit(solution)/shard_map/ppermute | solution.py:21
  80.8 4.6 %collective-permute-done.11 = bf16[32,2048]{1,0:T(8,128)(2,1)S(1)} collective-permute-done((bf16[32,2048]{1,0:T(8,128)(2,1)S(1)}, bf16[32,2048]{1,0:T(8,128)(2,1)S(1)}, u32[]{:S(2)}, u32[]{:S(2)}) %collective-permute-start.11) | collective-permute-done | bytes 131104 | tf_op jit(solution)/shard_map/ppermute | solution.py:21
  85.4 1.4 collective-permute-start.12
  86.8 1.0 collective-permute-done.12
  87.9 0.8 collective-permute-start.13
  88.8 0.4 collective-permute-start.14
  89.2 1.0 collective-permute-done.14.partner_ref
  90.2 1.5 shard_map.45.values_ref
  91.8 4.7 %collective-permute-done.15.partner_ref = bf16[32,2048]{1,0:T(8,128)(2,1)S(1)} collective-permute-done((bf16[32,2048]{1,0:T(8,128)(2,1)S(1)}, bf16[32,2048]{1,0:T(8,128)(2,1)S(1)}, u32[]{:S(2)}, u32[]{:S(2)}) %collective-permute-start.15) | collective-permute-done | bytes 131104 | tf_op jit(solution)/shard_map/ppermute | solution.py:21
  96.5 1.5 shard_map.46.values_ref
  98.0 1.2 collective-permute-start.16
  99.2 7.9 %collective-permute-done.16.partner_ref = bf16[32,2048]{1,0:T(8,128)(2,1)S(1)} collective-permute-done((bf16[32,2048]{1,0:T(8,128)(2,1)S(1)}, bf16[32,2048]{1,0:T(8,128)(2,1)S(1)}, u32[]{:S(2)}, u32[]{:S(2)}) %collective-permute-start.16) | collective-permute-done | bytes 131104 | tf_op jit(solution)/shard_map/ppermute | solution.py:21
  107.1 1.5 shard_map.47.values_ref
  108.7 2.5 %shard_map.48 = bf16[32,2048]{1,0:T(8,128)(2,1)S(1)} custom-call(bf16[32,2048]{1,0:T(8,128)(2,1)S(1)} %shard_map.47.values_ref, bf16[2048,2048]{1,0:T(8,128)(2,1)S(1)} %bitcast.23), custom_call_target="tpu_custom_call" | custom-call | flops 268435456 | bytes 8781824 | tf_op jit(solution)/shard_map/pallas_call | solution.py:77
  111.2 8.7 %collective-permute-done.17 = bf16[32,2048]{1,0:T(8,128)(2,1)S(1)} collective-permute-done((bf16[32,2048]{1,0:T(8,128)(2,1)S(1)}, bf16[32,2048]{1,0:T(8,128)(2,1)S(1)}, u32[]{:S(2)}, u32[]{:S(2)}) %collective-permute-start.17) | collective-permute-done | bytes 131104 | tf_op jit(solution)/shard_map/ppermute | solution.py:21
  120.0 0.1 collective-permute-start.18
  120.0 4.6 %collective-permute-done.18 = bf16[32,2048]{1,0:T(8,128)(2,1)S(1)} collective-permute-done((bf16[32,2048]{1,0:T(8,128)(2,1)S(1)}, bf16[32,2048]{1,0:T(8,128)(2,1)S(1)}, u32[]{:S(2)}, u32[]{:S(2)}) %collective-permute-start.18) | collective-permute-done | bytes 131104 | tf_op jit(solution)/shard_map/ppermute | solution.py:21
  124.7 1.4 collective-permute-start.19
  126.1 1.0 collective-permute-done.19
  127.1 1.3 collective-permute-start.20
  128.4 16.1 %collective-permute-done.20 = bf16[32,2048]{1,0:T(8,128)(2,1)S(1)} collective-permute-done((bf16[32,2048]{1,0:T(8,128)(2,1)S(1)}, bf16[32,2048]{1,0:T(8,128)(2,1)S(1)}, u32[]{:S(2)}, u32[]{:S(2)}) %collective-permute-start.20) | collective-permute-done | bytes 131104 | tf_op jit(solution)/shard_map/ppermute | solution.py:25
  144.6 1.0 collective-permute-start.21
  145.6 1.0 collective-permute-done.21.partner_ref
  146.6 1.5 shard_map.49.values_ref
  148.2 4.7 %collective-permute-done.22.partner_ref = bf16[32,2048]{1,0:T(8,128)(2,1)S(1)} collective-permute-done((bf16[32,2048]{1,0:T(8,128)(2,1)S(1)}, bf16[32,2048]{1,0:T(8,128)(2,1)S(1)}, u32[]{:S(2)}, u32[]{:S(2)}) %collective-permute-start.22) | collective-permute-done | bytes 131104 | tf_op jit(solution)/shard_map/ppermute | solution.py:21
  152.9 1.5 shard_map.50.values_ref
  154.4 0.2 collective-permute-start.23
  154.6 8.5 %collective-permute-done.23.partner_ref = bf16[32,2048]{1,0:T(8,128)(2,1)S(1)} collective-permute-done((bf16[32,2048]{1,0:T(8,128)(2,1)S(1)}, bf16[32,2048]{1,0:T(8,128)(2,1)S(1)}, u32[]{:S(2)}, u32[]{:S(2)}) %collective-permute-start.23) | collective-permute-done | bytes 131104 | tf_op jit(solution)/shard_map/ppermute | solution.py:21
  163.1 1.5 shard_map.51.values_ref
  164.6 2.5 %shard_map.52 = bf16[32,2048]{1,0:T(8,128)(2,1)S(1)} custom-call(bf16[32,2048]{1,0:T(8,128)(2,1)S(1)} %shard_map.51.values_ref, bf16[2048,2048]{1,0:T(8,128)(2,1)S(1)} %bitcast.27), custom_call_target="tpu_custom_call" | custom-call | flops 268435456 | bytes 8781824 | tf_op jit(solution)/shard_map/pallas_call | solution.py:77
  167.2 8.1 %collective-permute-done.24 = bf16[32,2048]{1,0:T(8,128)(2,1)S(1)} collective-permute-done((bf16[32,2048]{1,0:T(8,128)(2,1)S(1)}, bf16[32,2048]{1,0:T(8,128)(2,1)S(1)}, u32[]{:S(2)}, u32[]{:S(2)}) %collective-permute-start.24) | collective-permute-done | bytes 131104 | tf_op jit(solution)/shard_map/ppermute | solution.py:21
  175.5 4.5 %collective-permute-done.25 = bf16[32,2048]{1,0:T(8,128)(2,1)S(1)} collective-permute-done((bf16[32,2048]{1,0:T(8,128)(2,1)S(1)}, bf16[32,2048]{1,0:T(8,128)(2,1)S(1)}, u32[]{:S(2)}, u32[]{:S(2)}) %collective-permute-start.25) | collective-permute-done | bytes 131104 | tf_op jit(solution)/shard_map/ppermute | solution.py:21
  180.1 1.4 collective-permute-start.26
  181.5 1.0 collective-permute-done.26
  182.5 0.8 fusion.53
  (41 shorter events, 1.2 us)
Async XLA Ops:
  1.6 1.7 collective-permute-start
  3.4 3.4 %copy-start = (bf16[1,1,2048,2048]{3,2,1,0:T(8,128)(2,1)S(1)}, bf16[1,1,2048,2048]{3,2,1,0:T(8,128)(2,1)}, u32[]{:S(2)}) copy-start(bf16[1,1,2048,2048]{3,2,1,0:T(8,128)(2,1)} %param.5) | copy-start | bytes 25165828
  8.3 4.7 %collective-permute-start.1 = (bf16[32,2048]{1,0:T(8,128)(2,1)S(1)}, bf16[32,2048]{1,0:T(8,128)(2,1)S(1)}, u32[]{:S(2)}, u32[]{:S(2)}) collective-permute-start(bf16[32,2048]{1,0:T(8,128)(2,1)S(1)} %shard_map.37.values_ref), channel_id=1, source_target_pairs={{0,2},{2,0},{1,3},{3,1},{4,6},{6,4},{5,7},{7,5},{8,10},{10,8},{9,1... | collective-permute-start | bytes 393224 | tf_op jit(solution)/shard_map/ppermute | solution.py:21
  13.0 3.4 %copy-start.1 = (bf16[1,1,2048,2048]{3,2,1,0:T(8,128)(2,1)S(1)}, bf16[1,1,2048,2048]{3,2,1,0:T(8,128)(2,1)}, u32[]{:S(2)}) copy-start(bf16[1,1,2048,2048]{3,2,1,0:T(8,128)(2,1)} %param.5) | copy-start | bytes 25165828
  17.9 8.1 %collective-permute-start.2 = (bf16[32,2048]{1,0:T(8,128)(2,1)S(1)}, bf16[32,2048]{1,0:T(8,128)(2,1)S(1)}, u32[]{:S(2)}, u32[]{:S(2)}) collective-permute-start(bf16[32,2048]{1,0:T(8,128)(2,1)S(1)} %shard_map.38.values_ref), channel_id=1, source_target_pairs={{0,4},{4,0},{1,5},{5,1},{2,6},{6,2},{3,7},{7,3},{8,12},{12,8},{9,1... | collective-permute-start | bytes 393224 | tf_op jit(solution)/shard_map/ppermute | solution.py:21
  26.1 3.4 %copy-start.2 = (bf16[1,1,2048,2048]{3,2,1,0:T(8,128)(2,1)S(1)}, bf16[1,1,2048,2048]{3,2,1,0:T(8,128)(2,1)}, u32[]{:S(2)}) copy-start(bf16[1,1,2048,2048]{3,2,1,0:T(8,128)(2,1)} %param.5) | copy-start | bytes 25165828
  29.4 21.1 %copy-start.3 = (bf16[1,1,32,2048]{3,2,1,0:T(8,128)(2,1)S(1)}, bf16[1,1,32,2048]{3,2,1,0:T(8,128)(2,1)}, u32[]{:S(2)}) copy-start(bf16[1,1,32,2048]{3,2,1,0:T(8,128)(2,1)} %param.3) | copy-start | bytes 393220
  29.4 21.1 %copy-start.4 = (f32[1,1,2048]{2,1,0:T(1,128)S(1)}, f32[1,1,2048]{2,1,0:T(1,128)}, u32[]{:S(2)}) copy-start(f32[1,1,2048]{2,1,0:T(1,128)} %param.4) | copy-start | bytes 24580
  29.4 22.5 %slice-start = ((s8[8388608]{0:T(1024)(128)(4,1)}), s8[4194304]{0:T(1024)(128)(4,1)S(1)}, s32[]{:S(2)}) async-start(s8[8388608]{0:T(1024)(128)(4,1)} %bitcast.14), calls=%async_computation | async-start | bytes 8388608
  31.0 21.0 %slice-start.1 = ((s8[8388608]{0:T(1024)(128)(4,1)}), s8[4194304]{0:T(1024)(128)(4,1)S(1)}, s32[]{:S(2)}) async-start(s8[8388608]{0:T(1024)(128)(4,1)} %bitcast.14), calls=%async_computation.1 | async-start | bytes 8388608
  33.5 4.7 %collective-permute-start.3 = (bf16[32,2048]{1,0:T(8,128)(2,1)S(1)}, bf16[32,2048]{1,0:T(8,128)(2,1)S(1)}, u32[]{:S(2)}, u32[]{:S(2)}) collective-permute-start(bf16[32,2048]{1,0:T(8,128)(2,1)S(1)} %shard_map.40), channel_id=1, source_target_pairs={{0,4},{4,0},{1,5},{5,1},{2,6},{6,2},{3,7},{7,3},{8,12},{12,8},{9,1... | collective-permute-start | bytes 393224 | tf_op jit(solution)/shard_map/ppermute | solution.py:21
  38.3 5.8 %collective-permute-start.4 = (bf16[32,2048]{1,0:T(8,128)(2,1)S(1)}, bf16[32,2048]{1,0:T(8,128)(2,1)S(1)}, u32[]{:S(2)}, u32[]{:S(2)}) collective-permute-start(bf16[32,2048]{1,0:T(8,128)(2,1)S(1)} %fusion.2), channel_id=1, source_target_pairs={{0,2},{2,0},{1,3},{3,1},{4,6},{6,4},{5,7},{7,5},{8,10},{10,8},{9,1... | collective-permute-start | bytes 393224 | tf_op jit(solution)/shard_map/ppermute | solution.py:21
  44.2 5.5 %collective-permute-start.5 = (bf16[32,2048]{1,0:T(8,128)(2,1)S(1)}, bf16[32,2048]{1,0:T(8,128)(2,1)S(1)}, u32[]{:S(2)}, u32[]{:S(2)}) collective-permute-start(bf16[32,2048]{1,0:T(8,128)(2,1)S(1)} %fusion.6), channel_id=1, source_target_pairs={{0,1},{1,0},{2,3},{3,2},{4,5},{5,4},{6,7},{7,6},{8,9},{9,8},{10,11... | collective-permute-start | bytes 393224 | tf_op jit(solution)/shard_map/ppermute | solution.py:21
  49.8 0.7 collective-permute-start.6
  50.6 1.4 collective-permute-start.7
  53.5 4.7 %collective-permute-start.8 = (bf16[32,2048]{1,0:T(8,128)(2,1)S(1)}, bf16[32,2048]{1,0:T(8,128)(2,1)S(1)}, u32[]{:S(2)}, u32[]{:S(2)}) collective-permute-start(bf16[32,2048]{1,0:T(8,128)(2,1)S(1)} %shard_map.41.values_ref), channel_id=1, source_target_pairs={{0,2},{2,0},{1,3},{3,1},{4,6},{6,4},{5,7},{7,5},{8,10},{10,8},{9,1... | collective-permute-start | bytes 393224 | tf_op jit(solution)/shard_map/ppermute | solution.py:21
  59.8 9.1 %collective-permute-start.9 = (bf16[32,2048]{1,0:T(8,128)(2,1)S(1)}, bf16[32,2048]{1,0:T(8,128)(2,1)S(1)}, u32[]{:S(2)}, u32[]{:S(2)}) collective-permute-start(bf16[32,2048]{1,0:T(8,128)(2,1)S(1)} %shard_map.42.values_ref), channel_id=1, source_target_pairs={{0,4},{4,0},{1,5},{5,1},{2,6},{6,2},{3,7},{7,3},{8,12},{12,8},{9,1... | collective-permute-start | bytes 393224 | tf_op jit(solution)/shard_map/ppermute | solution.py:21
  73.0 7.7 %collective-permute-start.10 = (bf16[32,2048]{1,0:T(8,128)(2,1)S(1)}, bf16[32,2048]{1,0:T(8,128)(2,1)S(1)}, u32[]{:S(2)}, u32[]{:S(2)}) collective-permute-start(bf16[32,2048]{1,0:T(8,128)(2,1)S(1)} %shard_map.44), channel_id=1, source_target_pairs={{0,4},{4,0},{1,5},{5,1},{2,6},{6,2},{3,7},{7,3},{8,12},{12,8},{9,1... | collective-permute-start | bytes 393224 | tf_op jit(solution)/shard_map/ppermute | solution.py:21
  80.7 4.6 %collective-permute-start.11 = (bf16[32,2048]{1,0:T(8,128)(2,1)S(1)}, bf16[32,2048]{1,0:T(8,128)(2,1)S(1)}, u32[]{:S(2)}, u32[]{:S(2)}) collective-permute-start(bf16[32,2048]{1,0:T(8,128)(2,1)S(1)} %fusion.14), channel_id=1, source_target_pairs={{0,2},{2,0},{1,3},{3,1},{4,6},{6,4},{5,7},{7,5},{8,10},{10,8},{9,1... | collective-permute-start | bytes 393224 | tf_op jit(solution)/shard_map/ppermute | solution.py:21
  85.4 2.4 %collective-permute-start.12 = (bf16[32,2048]{1,0:T(8,128)(2,1)S(1)}, bf16[32,2048]{1,0:T(8,128)(2,1)S(1)}, u32[]{:S(2)}, u32[]{:S(2)}) collective-permute-start(bf16[32,2048]{1,0:T(8,128)(2,1)S(1)} %fusion.18), channel_id=1, source_target_pairs={{0,1},{1,0},{2,3},{3,2},{4,5},{5,4},{6,7},{7,6},{8,9},{9,8},{10,11... | collective-permute-start | bytes 393224 | tf_op jit(solution)/shard_map/ppermute | solution.py:21
  87.9 0.9 collective-permute-start.13
  88.8 1.4 collective-permute-start.14
  91.8 4.7 %collective-permute-start.15 = (bf16[32,2048]{1,0:T(8,128)(2,1)S(1)}, bf16[32,2048]{1,0:T(8,128)(2,1)S(1)}, u32[]{:S(2)}, u32[]{:S(2)}) collective-permute-start(bf16[32,2048]{1,0:T(8,128)(2,1)S(1)} %shard_map.45.values_ref), channel_id=1, source_target_pairs={{0,2},{2,0},{1,3},{3,1},{4,6},{6,4},{5,7},{7,5},{8,10},{10,8},{9,1... | collective-permute-start | bytes 393224 | tf_op jit(solution)/shard_map/ppermute | solution.py:21
  98.0 9.1 %collective-permute-start.16 = (bf16[32,2048]{1,0:T(8,128)(2,1)S(1)}, bf16[32,2048]{1,0:T(8,128)(2,1)S(1)}, u32[]{:S(2)}, u32[]{:S(2)}) collective-permute-start(bf16[32,2048]{1,0:T(8,128)(2,1)S(1)} %shard_map.46.values_ref), channel_id=1, source_target_pairs={{0,4},{4,0},{1,5},{5,1},{2,6},{6,2},{3,7},{7,3},{8,12},{12,8},{9,1... | collective-permute-start | bytes 393224 | tf_op jit(solution)/shard_map/ppermute | solution.py:21
  111.2 8.7 %collective-permute-start.17 = (bf16[32,2048]{1,0:T(8,128)(2,1)S(1)}, bf16[32,2048]{1,0:T(8,128)(2,1)S(1)}, u32[]{:S(2)}, u32[]{:S(2)}) collective-permute-start(bf16[32,2048]{1,0:T(8,128)(2,1)S(1)} %shard_map.48), channel_id=1, source_target_pairs={{0,4},{4,0},{1,5},{5,1},{2,6},{6,2},{3,7},{7,3},{8,12},{12,8},{9,1... | collective-permute-start | bytes 393224 | tf_op jit(solution)/shard_map/ppermute | solution.py:21
  120.0 4.6 %collective-permute-start.18 = (bf16[32,2048]{1,0:T(8,128)(2,1)S(1)}, bf16[32,2048]{1,0:T(8,128)(2,1)S(1)}, u32[]{:S(2)}, u32[]{:S(2)}) collective-permute-start(bf16[32,2048]{1,0:T(8,128)(2,1)S(1)} %fusion.26), channel_id=1, source_target_pairs={{0,2},{2,0},{1,3},{3,1},{4,6},{6,4},{5,7},{7,5},{8,10},{10,8},{9,1... | collective-permute-start | bytes 393224 | tf_op jit(solution)/shard_map/ppermute | solution.py:21
  124.7 2.4 %collective-permute-start.19 = (bf16[32,2048]{1,0:T(8,128)(2,1)S(1)}, bf16[32,2048]{1,0:T(8,128)(2,1)S(1)}, u32[]{:S(2)}, u32[]{:S(2)}) collective-permute-start(bf16[32,2048]{1,0:T(8,128)(2,1)S(1)} %fusion.30), channel_id=1, source_target_pairs={{0,1},{1,0},{2,3},{3,2},{4,5},{5,4},{6,7},{7,6},{8,9},{9,8},{10,11... | collective-permute-start | bytes 393224 | tf_op jit(solution)/shard_map/ppermute | solution.py:21
  127.1 17.4 %collective-permute-start.20 = (bf16[32,2048]{1,0:T(8,128)(2,1)S(1)}, bf16[32,2048]{1,0:T(8,128)(2,1)S(1)}, u32[]{:S(2)}, u32[]{:S(2)}) collective-permute-start(bf16[32,2048]{1,0:T(8,128)(2,1)S(1)} %fusion.34), channel_id=1, source_target_pairs={{16,24},{17,25},{18,26},{19,27},{20,28},{21,29},{22,30},{23,31}} | collective-permute-start | bytes 393224 | tf_op jit(solution)/shard_map/ppermute | solution.py:25
  144.6 2.0 %collective-permute-start.21 = (bf16[32,2048]{1,0:T(8,128)(2,1)S(1)}, bf16[32,2048]{1,0:T(8,128)(2,1)S(1)}, u32[]{:S(2)}, u32[]{:S(2)}) collective-permute-start(bf16[32,2048]{1,0:T(8,128)(2,1)S(1)} %fusion.51.values_ref), channel_id=1, source_target_pairs={{0,1},{1,0},{2,3},{3,2},{4,5},{5,4},{6,7},{7,6},{8,9},{9,8},{10,11... | collective-permute-start | bytes 393224 | tf_op jit(solution)/shard_map/ppermute | solution.py:21
  148.2 4.7 %collective-permute-start.22 = (bf16[32,2048]{1,0:T(8,128)(2,1)S(1)}, bf16[32,2048]{1,0:T(8,128)(2,1)S(1)}, u32[]{:S(2)}, u32[]{:S(2)}) collective-permute-start(bf16[32,2048]{1,0:T(8,128)(2,1)S(1)} %shard_map.49.values_ref), channel_id=1, source_target_pairs={{0,2},{2,0},{1,3},{3,1},{4,6},{6,4},{5,7},{7,5},{8,10},{10,8},{9,1... | collective-permute-start | bytes 393224 | tf_op jit(solution)/shard_map/ppermute | solution.py:21
  154.4 8.7 %collective-permute-start.23 = (bf16[32,2048]{1,0:T(8,128)(2,1)S(1)}, bf16[32,2048]{1,0:T(8,128)(2,1)S(1)}, u32[]{:S(2)}, u32[]{:S(2)}) collective-permute-start(bf16[32,2048]{1,0:T(8,128)(2,1)S(1)} %shard_map.50.values_ref), channel_id=1, source_target_pairs={{0,4},{4,0},{1,5},{5,1},{2,6},{6,2},{3,7},{7,3},{8,12},{12,8},{9,1... | collective-permute-start | bytes 393224 | tf_op jit(solution)/shard_map/ppermute | solution.py:21
  167.2 8.1 %collective-permute-start.24 = (bf16[32,2048]{1,0:T(8,128)(2,1)S(1)}, bf16[32,2048]{1,0:T(8,128)(2,1)S(1)}, u32[]{:S(2)}, u32[]{:S(2)}) collective-permute-start(bf16[32,2048]{1,0:T(8,128)(2,1)S(1)} %shard_map.52), channel_id=1, source_target_pairs={{0,4},{4,0},{1,5},{5,1},{2,6},{6,2},{3,7},{7,3},{8,12},{12,8},{9,1... | collective-permute-start | bytes 393224 | tf_op jit(solution)/shard_map/ppermute | solution.py:21
  175.4 4.6 %collective-permute-start.25 = (bf16[32,2048]{1,0:T(8,128)(2,1)S(1)}, bf16[32,2048]{1,0:T(8,128)(2,1)S(1)}, u32[]{:S(2)}, u32[]{:S(2)}) collective-permute-start(bf16[32,2048]{1,0:T(8,128)(2,1)S(1)} %fusion.38), channel_id=1, source_target_pairs={{0,2},{2,0},{1,3},{3,1},{4,6},{6,4},{5,7},{7,5},{8,10},{10,8},{9,1... | collective-permute-start | bytes 393224 | tf_op jit(solution)/shard_map/ppermute | solution.py:21
  180.1 2.4 %collective-permute-start.26 = (bf16[32,2048]{1,0:T(8,128)(2,1)S(1)}, bf16[32,2048]{1,0:T(8,128)(2,1)S(1)}, u32[]{:S(2)}, u32[]{:S(2)}) collective-permute-start(bf16[32,2048]{1,0:T(8,128)(2,1)S(1)} %fusion.42), channel_id=1, source_target_pairs={{0,1},{1,0},{2,3},{3,2},{4,5},{5,4},{6,7},{7,6},{8,9},{9,8},{10,11... | collective-permute-start | bytes 393224 | tf_op jit(solution)/shard_map/ppermute | solution.py:21

commit v7 on v6

--- a/solution.py
+++ b/solution.py
@@ -84,6 +84,58 @@
     )(values, pltpu.with_memory_space_constraint(merge_op, pltpu.VMEM))
 
 
+CHUNK = 256
+
+
+def fetched_dot_kernel(mix, *refs):
+    if mix:
+        sign_ref, values_ref, partner_ref, op_hbm_ref, out_ref, op_ref, sems = refs
+    else:
+        values_ref, op_hbm_ref, out_ref, op_ref, sems = refs
+    width = op_ref.shape[0]
+    copies = []
+    for index in range(width // CHUNK):
+        rows = pl.ds(index * CHUNK, CHUNK)
+        copy = pltpu.make_async_copy(op_hbm_ref.at[rows, :], op_ref.at[rows, :], sems.at[index])
+        copy.start()
+        copies.append(copy)
+    if mix:
+        first = values_ref[...].astype(jnp.float32)
+        second = partner_ref[...].astype(jnp.float32)
+        mixed = ((second + sign_ref[...] * first) * half_root).astype(jnp.bfloat16)
+        total = jnp.zeros(out_ref.shape, jnp.float32)
+        for index, copy in enumerate(copies):
+            copy.wait()
+            rows = slice(index * CHUNK, (index + 1) * CHUNK)
+            total = total + jnp.dot(mixed[:, rows], op_ref[rows, :], preferred_element_type=jnp.float32)
+        out_ref[...] = total.astype(out_ref.dtype)
+    else:
+        values = values_ref[...]
+        for index, copy in enumerate(copies):
+            copy.wait()
+            rows = slice(index * CHUNK, (index + 1) * CHUNK)
+            out_ref[:, rows] = lax.dot_general(
+                values, op_ref[rows, :], (((1,), (1,)), ((), ())), preferred_element_type=jnp.float32
+            ).astype(out_ref.dtype)
+
+
+def fetched_dot(operands, merge_op, mix):
+    values = operands[1] if mix else operands[0]
+    rows, width = values.shape
+    return pl.pallas_call(
+        functools.partial(fetched_dot_kernel, mix),
+        out_shape=jax.ShapeDtypeStruct(values.shape, jnp.bfloat16),
+        in_specs=[vmem_spec()] * len(operands) + [pl.BlockSpec(memory_space=pl.ANY)],
+        out_specs=vmem_spec(),
+        scratch_shapes=[
+            pltpu.VMEM(merge_op.shape, merge_op.dtype),
+            pltpu.SemaphoreType.DMA((width // CHUNK,)),
+        ],
+        cost_estimate=cost(rows, width),
+        compiler_params=pltpu.CompilerParams(vmem_limit_bytes=16 * 1024 * 1024),
+    )(*operands, pltpu.with_memory_space_constraint(merge_op, pltpu.HBM))
+
+
 def haar_pair(values, partner, lat_index, bit_level):
     is_lower = lat_index // 2**bit_level % 2 == 0
     first = values.astype(jnp.float32)
@@ -98,7 +150,7 @@
     return jnp.full((1, width), jnp.where(is_lower, 1.0, -1.0), jnp.float32)
 
 
-def sweep_layer(leaf_data, merge_op):
+def sweep_layer(leaf_data, merge_op, fetch):
     lat_count = lax.axis_size("lat")
     lat_index = lax.axis_index("lat")
     levels = lat_count.bit_length() - 1
@@ -106,8 +158,15 @@
     values = leaf_data
     for bit_level in range(levels):
         partner = partner_2(values, "lat", bit_level)
-        values = mixed_dot(level_sign(lat_index, bit_level, width), values, partner, merge_op)
-    values = transposed_dot(values, merge_op)
+        sign = level_sign(lat_index, bit_level, width)
+        if fetch:
+            values = fetched_dot((sign, values, partner), merge_op, True)
+        else:
+            values = mixed_dot(sign, values, partner, merge_op)
+    if fetch:
+        values = fetched_dot((values,), merge_op, False)
+    else:
+        values = transposed_dot(values, merge_op)
     for bit_level in range(levels - 1, -1, -1):
         partner = partner_2(values, "lat", bit_level)
         values = haar_pair(values, partner, lat_index, bit_level)
@@ -126,7 +185,7 @@
         leaf_data = (
             shot_rows.astype(jnp.float32) + coupling_row * incoming.astype(jnp.float32)
         ).astype(jnp.bfloat16)
-        solved = sweep_layer(leaf_data, merge_op)
+        solved = sweep_layer(leaf_data, merge_op, sweep_step == 0)
         result = jnp.where(depth_index == sweep_step, solved, result)
         if sweep_step + 1 < depth_count:
             incoming = handed_down(solved, "depth", sweep_step)

time: 184 us -> 185 us (level)
  Pallas kernels: 28.5 us -> 39.8 us
  local copies, waits for them, and re-layouts: 10.2 us -> 0.04 us
    pallas_call x0 -> x4, Pallas kernels: none -> 18.4 us  [fetched_dot(): pl.pallas_call(functools.partial(fetched_dot_kernel, mix), out_shape=jax....]
    unnamed x14 -> x8, local copies, waits for them, and re-layouts: 10.2 us -> 0.03 us
    pallas_call x12 -> x9, Pallas kernels: 18.4 us -> 13.8 us  [mixed_dot(): pl.pallas_call(mixed_dot_kernel, out_shape=jax.ShapeDtypeStruct(values.sh...]
    pallas_call x4 -> x3, Pallas kernels: 10.2 us -> 7.63 us  [transposed_dot(): pl.pallas_call(transposed_dot_kernel, out_shape=jax.ShapeDtypeStruct(valu...]
where the time goes in v7:
time: 185 us
  waiting for transfers between devices  119 us (64%)
  Pallas kernels  39.8 us (22%)
  starting transfers between devices  22.6 us (12%)
  other arithmetic  3.29 us (2%)
    ppermute x24, waiting for transfers between devices, partner_2(): return lax.ppermute(block, axis, route)  102 us
    ppermute x24, starting transfers between devices, partner_2(): return lax.ppermute(block, axis, route)  19.8 us
    pallas_call x4, Pallas kernels, fetched_dot(): pl.pallas_call(functools.partial(fetched_dot_kernel, mix), out_shape=jax....  18.4 us
    ppermute x3, waiting for transfers between devices, handed_down(): return lax.ppermute(array, axis, [(layer, layer + 1)])  16.1 us
    pallas_call x9, Pallas kernels, mixed_dot(): pl.pallas_call(mixed_dot_kernel, out_shape=jax.ShapeDtypeStruct(values.sh...  13.8 us
    pallas_call x3, Pallas kernels, transposed_dot(): pl.pallas_call(transposed_dot_kernel, out_shape=jax.ShapeDtypeStruct(valu...  7.63 us
  transfers between devices with their start and end apart: 27, of which 25 were waited for; matrix products, arithmetic and copies ran while one was open for 0% of the time, Pallas kernels for 0%

profile of v7, /device:TPU:7, one launch (start us, length us, event | category | flops | bytes accessed | tf_op | source)
XLA Modules:
  0.0 184.6 jit_solution(13933028922300456047)
XLA Ops:
  0.0 0.7 broadcast_multiply_fusion
  0.7 0.9 fusion.48.refs_1_
  1.6 0.7 collective-permute-start
  2.4 1.0 collective-permute-done.refs_2_
  3.4 3.8 %shard_map.37.refs_1_ = bf16[32,2048]{1,0:T(8,128)(2,1)S(1)} custom-call(f32[1,2048]{1,0:T(1,128)S(1)} %broadcast_in_dim.12.refs_0_.sign_ref, bf16[32,2048]{1,0:T(8,128)(2,1)S(1)} %fusion.48.refs_1_, bf16[32,2048]{1,0:T(8,128)(2,1)S(1)} %collective-permute-done.refs_2_, bf16[2048,2048]{1,0:T(8,128)(2,1)} %bitcast.10), custom_call_target="tpu_custom_call" | custom-call | flops 268435456 | bytes 8781824 | tf_op jit(solution)/shard_map/pallas_call | solution.py:125
  7.1 1.4 collective-permute-start.1
  8.5 3.4 %collective-permute-done.1.refs_2_ = bf16[32,2048]{1,0:T(8,128)(2,1)S(1)} collective-permute-done((bf16[32,2048]{1,0:T(8,128)(2,1)S(1)}, bf16[32,2048]{1,0:T(8,128)(2,1)S(1)}, u32[]{:S(2)}, u32[]{:S(2)}) %collective-permute-start.1) | collective-permute-done | bytes 131104 | tf_op jit(solution)/shard_map/ppermute | solution.py:21
  11.9 3.8 %shard_map.38.refs_1_ = bf16[32,2048]{1,0:T(8,128)(2,1)S(1)} custom-call(f32[1,2048]{1,0:T(1,128)S(1)} %broadcast_in_dim.11.refs_0_.sign_ref, bf16[32,2048]{1,0:T(8,128)(2,1)S(1)} %shard_map.37.refs_1_, bf16[32,2048]{1,0:T(8,128)(2,1)S(1)} %collective-permute-done.1.refs_2_, bf16[2048,2048]{1,0:T(8,128)(2,1)} %bitcast.11), custom_call_target="tpu_custom_call" | custom-call | flops 268435456 | bytes 8781824 | tf_op jit(solution)/shard_map/pallas_call | solution.py:125
  15.7 2.4 %collective-permute-start.2 = (bf16[32,2048]{1,0:T(8,128)(2,1)S(1)}, bf16[32,2048]{1,0:T(8,128)(2,1)S(1)}, u32[]{:S(2)}, u32[]{:S(2)}) collective-permute-start(bf16[32,2048]{1,0:T(8,128)(2,1)S(1)} %shard_map.38.refs_1_), channel_id=1, source_target_pairs={{0,4},{4,0},{1,5},{5,1},{2,6},{6,2},{3,7},{7,3},{8,12},{12,8},{9,1... | collective-permute-start | bytes 393224 | tf_op jit(solution)/shard_map/ppermute | solution.py:21
  18.1 5.8 %collective-permute-done.2.refs_2_ = bf16[32,2048]{1,0:T(8,128)(2,1)S(1)} collective-permute-done((bf16[32,2048]{1,0:T(8,128)(2,1)S(1)}, bf16[32,2048]{1,0:T(8,128)(2,1)S(1)}, u32[]{:S(2)}, u32[]{:S(2)}) %collective-permute-start.2) | collective-permute-done | bytes 131104 | tf_op jit(solution)/shard_map/ppermute | solution.py:21
  23.9 4.1 %shard_map.39.refs_0_ = bf16[32,2048]{1,0:T(8,128)(2,1)S(1)} custom-call(f32[1,2048]{1,0:T(1,128)S(1)} %broadcast_in_dim.10.refs_0_.sign_ref, bf16[32,2048]{1,0:T(8,128)(2,1)S(1)} %shard_map.38.refs_1_, bf16[32,2048]{1,0:T(8,128)(2,1)S(1)} %collective-permute-done.2.refs_2_, bf16[2048,2048]{1,0:T(8,128)(2,1)} %bitcast.12), custom_call_target="tpu_custom_call" | custom-call | flops 268435456 | bytes 8781824 | tf_op jit(solution)/shard_map/pallas_call | solution.py:125
  28.0 6.7 %shard_map.40 = bf16[32,2048]{1,0:T(8,128)(2,1)S(1)} custom-call(bf16[32,2048]{1,0:T(8,128)(2,1)S(1)} %shard_map.39.refs_0_, bf16[2048,2048]{1,0:T(8,128)(2,1)} %bitcast.13), custom_call_target="tpu_custom_call" | custom-call | flops 268435456 | bytes 8781824 | tf_op jit(solution)/shard_map/pallas_call | solution.py:125
  34.8 0.1 collective-permute-start.3
  34.9 4.7 %collective-permute-done.3 = bf16[32,2048]{1,0:T(8,128)(2,1)S(1)} collective-permute-done((bf16[32,2048]{1,0:T(8,128)(2,1)S(1)}, bf16[32,2048]{1,0:T(8,128)(2,1)S(1)}, u32[]{:S(2)}, u32[]{:S(2)}) %collective-permute-start.3) | collective-permute-done | bytes 131104 | tf_op jit(solution)/shard_map/ppermute | solution.py:21
  39.6 2.9 %collective-permute-start.4 = (bf16[32,2048]{1,0:T(8,128)(2,1)S(1)}, bf16[32,2048]{1,0:T(8,128)(2,1)S(1)}, u32[]{:S(2)}, u32[]{:S(2)}) collective-permute-start(bf16[32,2048]{1,0:T(8,128)(2,1)S(1)} %fusion.2), channel_id=1, source_target_pairs={{0,2},{2,0},{1,3},{3,1},{4,6},{6,4},{5,7},{7,5},{8,10},{10,8},{9,1... | collective-permute-start | bytes 393224 | tf_op jit(solution)/shard_map/ppermute | solution.py:21
  42.5 2.9 %collective-permute-done.4 = bf16[32,2048]{1,0:T(8,128)(2,1)S(1)} collective-permute-done((bf16[32,2048]{1,0:T(8,128)(2,1)S(1)}, bf16[32,2048]{1,0:T(8,128)(2,1)S(1)}, u32[]{:S(2)}, u32[]{:S(2)}) %collective-permute-start.4) | collective-permute-done | bytes 131104 | tf_op jit(solution)/shard_map/ppermute | solution.py:21
  45.5 4.5 %collective-permute-start.5 = (bf16[32,2048]{1,0:T(8,128)(2,1)S(1)}, bf16[32,2048]{1,0:T(8,128)(2,1)S(1)}, u32[]{:S(2)}, u32[]{:S(2)}) collective-permute-start(bf16[32,2048]{1,0:T(8,128)(2,1)S(1)} %fusion.6), channel_id=1, source_target_pairs={{0,1},{1,0},{2,3},{3,2},{4,5},{5,4},{6,7},{7,6},{8,9},{9,8},{10,11... | collective-permute-start | bytes 393224 | tf_op jit(solution)/shard_map/ppermute | solution.py:21
  50.1 1.0 collective-permute-done.5
  51.1 0.7 collective-permute-start.6
  51.9 0.4 collective-permute-start.7
  52.3 1.0 collective-permute-done.7.partner_ref
  53.3 1.5 shard_map.41.values_ref
  54.8 4.7 %collective-permute-done.8.partner_ref = bf16[32,2048]{1,0:T(8,128)(2,1)S(1)} collective-permute-done((bf16[32,2048]{1,0:T(8,128)(2,1)S(1)}, bf16[32,2048]{1,0:T(8,128)(2,1)S(1)}, u32[]{:S(2)}, u32[]{:S(2)}) %collective-permute-start.8) | collective-permute-done | bytes 131104 | tf_op jit(solution)/shard_map/ppermute | solution.py:21
  59.5 1.5 shard_map.42.values_ref
  61.1 9.1 %collective-permute-done.9.partner_ref = bf16[32,2048]{1,0:T(8,128)(2,1)S(1)} collective-permute-done((bf16[32,2048]{1,0:T(8,128)(2,1)S(1)}, bf16[32,2048]{1,0:T(8,128)(2,1)S(1)}, u32[]{:S(2)}, u32[]{:S(2)}) %collective-permute-start.9) | collective-permute-done | bytes 131104 | tf_op jit(solution)/shard_map/ppermute | solution.py:21
  70.2 1.5 shard_map.43.values_ref
  71.7 2.5 %shard_map.44 = bf16[32,2048]{1,0:T(8,128)(2,1)S(1)} custom-call(bf16[32,2048]{1,0:T(8,128)(2,1)S(1)} %shard_map.43.values_ref, bf16[2048,2048]{1,0:T(8,128)(2,1)S(1)} %bitcast.19), custom_call_target="tpu_custom_call" | custom-call | flops 268435456 | bytes 8781824 | tf_op jit(solution)/shard_map/pallas_call | solution.py:77
  74.3 7.7 %collective-permute-done.10 = bf16[32,2048]{1,0:T(8,128)(2,1)S(1)} collective-permute-done((bf16[32,2048]{1,0:T(8,128)(2,1)S(1)}, bf16[32,2048]{1,0:T(8,128)(2,1)S(1)}, u32[]{:S(2)}, u32[]{:S(2)}) %collective-permute-start.10) | collective-permute-done | bytes 131104 | tf_op jit(solution)/shard_map/ppermute | solution.py:21
  82.0 0.1 collective-permute-start.11
  82.1 4.6 %collective-permute-done.11 = bf16[32,2048]{1,0:T(8,128)(2,1)S(1)} collective-permute-done((bf16[32,2048]{1,0:T(8,128)(2,1)S(1)}, bf16[32,2048]{1,0:T(8,128)(2,1)S(1)}, u32[]{:S(2)}, u32[]{:S(2)}) %collective-permute-start.11) | collective-permute-done | bytes 131104 | tf_op jit(solution)/shard_map/ppermute | solution.py:21
  86.7 1.4 collective-permute-start.12
  88.2 1.0 collective-permute-done.12
  89.2 0.8 collective-permute-start.13
  90.1 0.4 collective-permute-start.14
  90.6 1.0 collective-permute-done.14.partner_ref
  91.5 1.5 shard_map.45.values_ref
  93.1 4.7 %collective-permute-done.15.partner_ref = bf16[32,2048]{1,0:T(8,128)(2,1)S(1)} collective-permute-done((bf16[32,2048]{1,0:T(8,128)(2,1)S(1)}, bf16[32,2048]{1,0:T(8,128)(2,1)S(1)}, u32[]{:S(2)}, u32[]{:S(2)}) %collective-permute-start.15) | collective-permute-done | bytes 131104 | tf_op jit(solution)/shard_map/ppermute | solution.py:21
  97.8 1.5 shard_map.46.values_ref
  99.3 1.2 collective-permute-start.16
  100.5 7.9 %collective-permute-done.16.partner_ref = bf16[32,2048]{1,0:T(8,128)(2,1)S(1)} collective-permute-done((bf16[32,2048]{1,0:T(8,128)(2,1)S(1)}, bf16[32,2048]{1,0:T(8,128)(2,1)S(1)}, u32[]{:S(2)}, u32[]{:S(2)}) %collective-permute-start.16) | collective-permute-done | bytes 131104 | tf_op jit(solution)/shard_map/ppermute | solution.py:21
  108.5 1.5 shard_map.47.values_ref
  110.0 2.5 %shard_map.48 = bf16[32,2048]{1,0:T(8,128)(2,1)S(1)} custom-call(bf16[32,2048]{1,0:T(8,128)(2,1)S(1)} %shard_map.47.values_ref, bf16[2048,2048]{1,0:T(8,128)(2,1)S(1)} %bitcast.23), custom_call_target="tpu_custom_call" | custom-call | flops 268435456 | bytes 8781824 | tf_op jit(solution)/shard_map/pallas_call | solution.py:77
  112.6 8.7 %collective-permute-done.17 = bf16[32,2048]{1,0:T(8,128)(2,1)S(1)} collective-permute-done((bf16[32,2048]{1,0:T(8,128)(2,1)S(1)}, bf16[32,2048]{1,0:T(8,128)(2,1)S(1)}, u32[]{:S(2)}, u32[]{:S(2)}) %collective-permute-start.17) | collective-permute-done | bytes 131104 | tf_op jit(solution)/shard_map/ppermute | solution.py:21
  121.3 0.1 collective-permute-start.18
  121.4 4.6 %collective-permute-done.18 = bf16[32,2048]{1,0:T(8,128)(2,1)S(1)} collective-permute-done((bf16[32,2048]{1,0:T(8,128)(2,1)S(1)}, bf16[32,2048]{1,0:T(8,128)(2,1)S(1)}, u32[]{:S(2)}, u32[]{:S(2)}) %collective-permute-start.18) | collective-permute-done | bytes 131104 | tf_op jit(solution)/shard_map/ppermute | solution.py:21
  126.0 1.4 collective-permute-start.19
  127.4 1.0 collective-permute-done.19
  128.5 1.3 collective-permute-start.20
  129.8 16.1 %collective-permute-done.20 = bf16[32,2048]{1,0:T(8,128)(2,1)S(1)} collective-permute-done((bf16[32,2048]{1,0:T(8,128)(2,1)S(1)}, bf16[32,2048]{1,0:T(8,128)(2,1)S(1)}, u32[]{:S(2)}, u32[]{:S(2)}) %collective-permute-start.20) | collective-permute-done | bytes 131104 | tf_op jit(solution)/shard_map/ppermute | solution.py:25
  146.0 1.0 collective-permute-start.21
  147.0 1.0 collective-permute-done.21.partner_ref
  147.9 1.5 shard_map.49.values_ref
  149.5 4.7 %collective-permute-done.22.partner_ref = bf16[32,2048]{1,0:T(8,128)(2,1)S(1)} collective-permute-done((bf16[32,2048]{1,0:T(8,128)(2,1)S(1)}, bf16[32,2048]{1,0:T(8,128)(2,1)S(1)}, u32[]{:S(2)}, u32[]{:S(2)}) %collective-permute-start.22) | collective-permute-done | bytes 131104 | tf_op jit(solution)/shard_map/ppermute | solution.py:21
  154.2 1.5 shard_map.50.values_ref
  155.7 0.2 collective-permute-start.23
  155.9 8.5 %collective-permute-done.23.partner_ref = bf16[32,2048]{1,0:T(8,128)(2,1)S(1)} collective-permute-done((bf16[32,2048]{1,0:T(8,128)(2,1)S(1)}, bf16[32,2048]{1,0:T(8,128)(2,1)S(1)}, u32[]{:S(2)}, u32[]{:S(2)}) %collective-permute-start.23) | collective-permute-done | bytes 131104 | tf_op jit(solution)/shard_map/ppermute | solution.py:21
  164.4 1.5 shard_map.51.values_ref
  166.0 2.5 %shard_map.52 = bf16[32,2048]{1,0:T(8,128)(2,1)S(1)} custom-call(bf16[32,2048]{1,0:T(8,128)(2,1)S(1)} %shard_map.51.values_ref, bf16[2048,2048]{1,0:T(8,128)(2,1)S(1)} %bitcast.27), custom_call_target="tpu_custom_call" | custom-call | flops 268435456 | bytes 8781824 | tf_op jit(solution)/shard_map/pallas_call | solution.py:77
  168.5 8.1 %collective-permute-done.24 = bf16[32,2048]{1,0:T(8,128)(2,1)S(1)} collective-permute-done((bf16[32,2048]{1,0:T(8,128)(2,1)S(1)}, bf16[32,2048]{1,0:T(8,128)(2,1)S(1)}, u32[]{:S(2)}, u32[]{:S(2)}) %collective-permute-start.24) | collective-permute-done | bytes 131104 | tf_op jit(solution)/shard_map/ppermute | solution.py:21
  176.7 0.1 collective-permute-start.25
  176.8 4.5 %collective-permute-done.25 = bf16[32,2048]{1,0:T(8,128)(2,1)S(1)} collective-permute-done((bf16[32,2048]{1,0:T(8,128)(2,1)S(1)}, bf16[32,2048]{1,0:T(8,128)(2,1)S(1)}, u32[]{:S(2)}, u32[]{:S(2)}) %collective-permute-start.25) | collective-permute-done | bytes 131104 | tf_op jit(solution)/shard_map/ppermute | solution.py:21
  181.4 1.4 collective-permute-start.26
  182.8 1.0 collective-permute-done.26
  183.8 0.8 fusion.53
  (35 shorter events, 1.0 us)
Async XLA Ops:
  1.6 1.7 collective-permute-start
  7.1 4.8 %collective-permute-start.1 = (bf16[32,2048]{1,0:T(8,128)(2,1)S(1)}, bf16[32,2048]{1,0:T(8,128)(2,1)S(1)}, u32[]{:S(2)}, u32[]{:S(2)}) collective-permute-start(bf16[32,2048]{1,0:T(8,128)(2,1)S(1)} %shard_map.37.refs_1_), channel_id=1, source_target_pairs={{0,2},{2,0},{1,3},{3,1},{4,6},{6,4},{5,7},{7,5},{8,10},{10,8},{9,1... | collective-permute-start | bytes 393224 | tf_op jit(solution)/shard_map/ppermute | solution.py:21
  15.7 8.2 %collective-permute-start.2 = (bf16[32,2048]{1,0:T(8,128)(2,1)S(1)}, bf16[32,2048]{1,0:T(8,128)(2,1)S(1)}, u32[]{:S(2)}, u32[]{:S(2)}) collective-permute-start(bf16[32,2048]{1,0:T(8,128)(2,1)S(1)} %shard_map.38.refs_1_), channel_id=1, source_target_pairs={{0,4},{4,0},{1,5},{5,1},{2,6},{6,2},{3,7},{7,3},{8,12},{12,8},{9,1... | collective-permute-start | bytes 393224 | tf_op jit(solution)/shard_map/ppermute | solution.py:21
  23.9 27.9 %copy-start = (bf16[1,1,32,2048]{3,2,1,0:T(8,128)(2,1)S(1)}, bf16[1,1,32,2048]{3,2,1,0:T(8,128)(2,1)}, u32[]{:S(2)}) copy-start(bf16[1,1,32,2048]{3,2,1,0:T(8,128)(2,1)} %param.3) | copy-start | bytes 393220
  23.9 27.9 %copy-start.1 = (f32[1,1,2048]{2,1,0:T(1,128)S(1)}, f32[1,1,2048]{2,1,0:T(1,128)}, u32[]{:S(2)}) copy-start(f32[1,1,2048]{2,1,0:T(1,128)} %param.4) | copy-start | bytes 24580
  23.9 29.4 %slice-start = ((s8[8388608]{0:T(1024)(128)(4,1)}), s8[4194304]{0:T(1024)(128)(4,1)S(1)}, s32[]{:S(2)}) async-start(s8[8388608]{0:T(1024)(128)(4,1)} %bitcast.14), calls=%async_computation | async-start | bytes 8388608
  28.0 25.3 %slice-start.1 = ((s8[8388608]{0:T(1024)(128)(4,1)}), s8[4194304]{0:T(1024)(128)(4,1)S(1)}, s32[]{:S(2)}) async-start(s8[8388608]{0:T(1024)(128)(4,1)} %bitcast.14), calls=%async_computation.1 | async-start | bytes 8388608
  34.8 4.8 %collective-permute-start.3 = (bf16[32,2048]{1,0:T(8,128)(2,1)S(1)}, bf16[32,2048]{1,0:T(8,128)(2,1)S(1)}, u32[]{:S(2)}, u32[]{:S(2)}) collective-permute-start(bf16[32,2048]{1,0:T(8,128)(2,1)S(1)} %shard_map.40), channel_id=1, source_target_pairs={{0,4},{4,0},{1,5},{5,1},{2,6},{6,2},{3,7},{7,3},{8,12},{12,8},{9,1... | collective-permute-start | bytes 393224 | tf_op jit(solution)/shard_map/ppermute | solution.py:21
  39.6 5.8 %collective-permute-start.4 = (bf16[32,2048]{1,0:T(8,128)(2,1)S(1)}, bf16[32,2048]{1,0:T(8,128)(2,1)S(1)}, u32[]{:S(2)}, u32[]{:S(2)}) collective-permute-start(bf16[32,2048]{1,0:T(8,128)(2,1)S(1)} %fusion.2), channel_id=1, source_target_pairs={{0,2},{2,0},{1,3},{3,1},{4,6},{6,4},{5,7},{7,5},{8,10},{10,8},{9,1... | collective-permute-start | bytes 393224 | tf_op jit(solution)/shard_map/ppermute | solution.py:21
  45.5 5.5 %collective-permute-start.5 = (bf16[32,2048]{1,0:T(8,128)(2,1)S(1)}, bf16[32,2048]{1,0:T(8,128)(2,1)S(1)}, u32[]{:S(2)}, u32[]{:S(2)}) collective-permute-start(bf16[32,2048]{1,0:T(8,128)(2,1)S(1)} %fusion.6), channel_id=1, source_target_pairs={{0,1},{1,0},{2,3},{3,2},{4,5},{5,4},{6,7},{7,6},{8,9},{9,8},{10,11... | collective-permute-start | bytes 393224 | tf_op jit(solution)/shard_map/ppermute | solution.py:21
  51.1 0.7 collective-permute-start.6
  51.9 1.4 collective-permute-start.7
  54.8 4.7 %collective-permute-start.8 = (bf16[32,2048]{1,0:T(8,128)(2,1)S(1)}, bf16[32,2048]{1,0:T(8,128)(2,1)S(1)}, u32[]{:S(2)}, u32[]{:S(2)}) collective-permute-start(bf16[32,2048]{1,0:T(8,128)(2,1)S(1)} %shard_map.41.values_ref), channel_id=1, source_target_pairs={{0,2},{2,0},{1,3},{3,1},{4,6},{6,4},{5,7},{7,5},{8,10},{10,8},{9,1... | collective-permute-start | bytes 393224 | tf_op jit(solution)/shard_map/ppermute | solution.py:21
  61.1 9.1 %collective-permute-start.9 = (bf16[32,2048]{1,0:T(8,128)(2,1)S(1)}, bf16[32,2048]{1,0:T(8,128)(2,1)S(1)}, u32[]{:S(2)}, u32[]{:S(2)}) collective-permute-start(bf16[32,2048]{1,0:T(8,128)(2,1)S(1)} %shard_map.42.values_ref), channel_id=1, source_target_pairs={{0,4},{4,0},{1,5},{5,1},{2,6},{6,2},{3,7},{7,3},{8,12},{12,8},{9,1... | collective-permute-start | bytes 393224 | tf_op jit(solution)/shard_map/ppermute | solution.py:21
  74.3 7.7 %collective-permute-start.10 = (bf16[32,2048]{1,0:T(8,128)(2,1)S(1)}, bf16[32,2048]{1,0:T(8,128)(2,1)S(1)}, u32[]{:S(2)}, u32[]{:S(2)}) collective-permute-start(bf16[32,2048]{1,0:T(8,128)(2,1)S(1)} %shard_map.44), channel_id=1, source_target_pairs={{0,4},{4,0},{1,5},{5,1},{2,6},{6,2},{3,7},{7,3},{8,12},{12,8},{9,1... | collective-permute-start | bytes 393224 | tf_op jit(solution)/shard_map/ppermute | solution.py:21
  82.0 4.6 %collective-permute-start.11 = (bf16[32,2048]{1,0:T(8,128)(2,1)S(1)}, bf16[32,2048]{1,0:T(8,128)(2,1)S(1)}, u32[]{:S(2)}, u32[]{:S(2)}) collective-permute-start(bf16[32,2048]{1,0:T(8,128)(2,1)S(1)} %fusion.14), channel_id=1, source_target_pairs={{0,2},{2,0},{1,3},{3,1},{4,6},{6,4},{5,7},{7,5},{8,10},{10,8},{9,1... | collective-permute-start | bytes 393224 | tf_op jit(solution)/shard_map/ppermute | solution.py:21
  86.7 2.4 %collective-permute-start.12 = (bf16[32,2048]{1,0:T(8,128)(2,1)S(1)}, bf16[32,2048]{1,0:T(8,128)(2,1)S(1)}, u32[]{:S(2)}, u32[]{:S(2)}) collective-permute-start(bf16[32,2048]{1,0:T(8,128)(2,1)S(1)} %fusion.18), channel_id=1, source_target_pairs={{0,1},{1,0},{2,3},{3,2},{4,5},{5,4},{6,7},{7,6},{8,9},{9,8},{10,11... | collective-permute-start | bytes 393224 | tf_op jit(solution)/shard_map/ppermute | solution.py:21
  89.2 0.9 collective-permute-start.13
  90.1 1.4 collective-permute-start.14
  93.1 4.7 %collective-permute-start.15 = (bf16[32,2048]{1,0:T(8,128)(2,1)S(1)}, bf16[32,2048]{1,0:T(8,128)(2,1)S(1)}, u32[]{:S(2)}, u32[]{:S(2)}) collective-permute-start(bf16[32,2048]{1,0:T(8,128)(2,1)S(1)} %shard_map.45.values_ref), channel_id=1, source_target_pairs={{0,2},{2,0},{1,3},{3,1},{4,6},{6,4},{5,7},{7,5},{8,10},{10,8},{9,1... | collective-permute-start | bytes 393224 | tf_op jit(solution)/shard_map/ppermute | solution.py:21
  99.3 9.1 %collective-permute-start.16 = (bf16[32,2048]{1,0:T(8,128)(2,1)S(1)}, bf16[32,2048]{1,0:T(8,128)(2,1)S(1)}, u32[]{:S(2)}, u32[]{:S(2)}) collective-permute-start(bf16[32,2048]{1,0:T(8,128)(2,1)S(1)} %shard_map.46.values_ref), channel_id=1, source_target_pairs={{0,4},{4,0},{1,5},{5,1},{2,6},{6,2},{3,7},{7,3},{8,12},{12,8},{9,1... | collective-permute-start | bytes 393224 | tf_op jit(solution)/shard_map/ppermute | solution.py:21
  112.5 8.7 %collective-permute-start.17 = (bf16[32,2048]{1,0:T(8,128)(2,1)S(1)}, bf16[32,2048]{1,0:T(8,128)(2,1)S(1)}, u32[]{:S(2)}, u32[]{:S(2)}) collective-permute-start(bf16[32,2048]{1,0:T(8,128)(2,1)S(1)} %shard_map.48), channel_id=1, source_target_pairs={{0,4},{4,0},{1,5},{5,1},{2,6},{6,2},{3,7},{7,3},{8,12},{12,8},{9,1... | collective-permute-start | bytes 393224 | tf_op jit(solution)/shard_map/ppermute | solution.py:21
  121.3 4.6 %collective-permute-start.18 = (bf16[32,2048]{1,0:T(8,128)(2,1)S(1)}, bf16[32,2048]{1,0:T(8,128)(2,1)S(1)}, u32[]{:S(2)}, u32[]{:S(2)}) collective-permute-start(bf16[32,2048]{1,0:T(8,128)(2,1)S(1)} %fusion.26), channel_id=1, source_target_pairs={{0,2},{2,0},{1,3},{3,1},{4,6},{6,4},{5,7},{7,5},{8,10},{10,8},{9,1... | collective-permute-start | bytes 393224 | tf_op jit(solution)/shard_map/ppermute | solution.py:21
  126.0 2.4 %collective-permute-start.19 = (bf16[32,2048]{1,0:T(8,128)(2,1)S(1)}, bf16[32,2048]{1,0:T(8,128)(2,1)S(1)}, u32[]{:S(2)}, u32[]{:S(2)}) collective-permute-start(bf16[32,2048]{1,0:T(8,128)(2,1)S(1)} %fusion.30), channel_id=1, source_target_pairs={{0,1},{1,0},{2,3},{3,2},{4,5},{5,4},{6,7},{7,6},{8,9},{9,8},{10,11... | collective-permute-start | bytes 393224 | tf_op jit(solution)/shard_map/ppermute | solution.py:21
  128.5 17.4 %collective-permute-start.20 = (bf16[32,2048]{1,0:T(8,128)(2,1)S(1)}, bf16[32,2048]{1,0:T(8,128)(2,1)S(1)}, u32[]{:S(2)}, u32[]{:S(2)}) collective-permute-start(bf16[32,2048]{1,0:T(8,128)(2,1)S(1)} %fusion.34), channel_id=1, source_target_pairs={{16,24},{17,25},{18,26},{19,27},{20,28},{21,29},{22,30},{23,31}} | collective-permute-start | bytes 393224 | tf_op jit(solution)/shard_map/ppermute | solution.py:25
  146.0 2.0 %collective-permute-start.21 = (bf16[32,2048]{1,0:T(8,128)(2,1)S(1)}, bf16[32,2048]{1,0:T(8,128)(2,1)S(1)}, u32[]{:S(2)}, u32[]{:S(2)}) collective-permute-start(bf16[32,2048]{1,0:T(8,128)(2,1)S(1)} %fusion.51.values_ref), channel_id=1, source_target_pairs={{0,1},{1,0},{2,3},{3,2},{4,5},{5,4},{6,7},{7,6},{8,9},{9,8},{10,11... | collective-permute-start | bytes 393224 | tf_op jit(solution)/shard_map/ppermute | solution.py:21
  149.5 4.7 %collective-permute-start.22 = (bf16[32,2048]{1,0:T(8,128)(2,1)S(1)}, bf16[32,2048]{1,0:T(8,128)(2,1)S(1)}, u32[]{:S(2)}, u32[]{:S(2)}) collective-permute-start(bf16[32,2048]{1,0:T(8,128)(2,1)S(1)} %shard_map.49.values_ref), channel_id=1, source_target_pairs={{0,2},{2,0},{1,3},{3,1},{4,6},{6,4},{5,7},{7,5},{8,10},{10,8},{9,1... | collective-permute-start | bytes 393224 | tf_op jit(solution)/shard_map/ppermute | solution.py:21
  155.7 8.7 %collective-permute-start.23 = (bf16[32,2048]{1,0:T(8,128)(2,1)S(1)}, bf16[32,2048]{1,0:T(8,128)(2,1)S(1)}, u32[]{:S(2)}, u32[]{:S(2)}) collective-permute-start(bf16[32,2048]{1,0:T(8,128)(2,1)S(1)} %shard_map.50.values_ref), channel_id=1, source_target_pairs={{0,4},{4,0},{1,5},{5,1},{2,6},{6,2},{3,7},{7,3},{8,12},{12,8},{9,1... | collective-permute-start | bytes 393224 | tf_op jit(solution)/shard_map/ppermute | solution.py:21
  168.5 8.1 %collective-permute-start.24 = (bf16[32,2048]{1,0:T(8,128)(2,1)S(1)}, bf16[32,2048]{1,0:T(8,128)(2,1)S(1)}, u32[]{:S(2)}, u32[]{:S(2)}) collective-permute-start(bf16[32,2048]{1,0:T(8,128)(2,1)S(1)} %shard_map.52), channel_id=1, source_target_pairs={{0,4},{4,0},{1,5},{5,1},{2,6},{6,2},{3,7},{7,3},{8,12},{12,8},{9,1... | collective-permute-start | bytes 393224 | tf_op jit(solution)/shard_map/ppermute | solution.py:21
  176.7 4.6 %collective-permute-start.25 = (bf16[32,2048]{1,0:T(8,128)(2,1)S(1)}, bf16[32,2048]{1,0:T(8,128)(2,1)S(1)}, u32[]{:S(2)}, u32[]{:S(2)}) collective-permute-start(bf16[32,2048]{1,0:T(8,128)(2,1)S(1)} %fusion.38), channel_id=1, source_target_pairs={{0,2},{2,0},{1,3},{3,1},{4,6},{6,4},{5,7},{7,5},{8,10},{10,8},{9,1... | collective-permute-start | bytes 393224 | tf_op jit(solution)/shard_map/ppermute | solution.py:21
  181.4 2.4 %collective-permute-start.26 = (bf16[32,2048]{1,0:T(8,128)(2,1)S(1)}, bf16[32,2048]{1,0:T(8,128)(2,1)S(1)}, u32[]{:S(2)}, u32[]{:S(2)}) collective-permute-start(bf16[32,2048]{1,0:T(8,128)(2,1)S(1)} %fusion.42), channel_id=1, source_target_pairs={{0,1},{1,0},{2,3},{3,2},{4,5},{5,4},{6,7},{7,6},{8,9},{9,8},{10,11... | collective-permute-start | bytes 393224 | tf_op jit(solution)/shard_map/ppermute | solution.py:21

commit v8 on v6

--- a/solution.py
+++ b/solution.py
@@ -11,14 +11,14 @@
 TILE = 512
 
 
-def partner_2(block, axis, apart):
+def partner_2(block, axis, apart, layer):
     count = lax.axis_size(axis)
     route = []
     for low in range(count):
         high = low | 1 << apart
         if high != low and high < count:
-            route += [(low, high), (high, low)]
-    return lax.ppermute(block, axis, route)
+            route += [(layer * count + low, layer * count + high), (layer * count + high, layer * count + low)]
+    return lax.ppermute(block, ("depth", axis), route)
 
 
 def handed_down(array, axis, layer):
@@ -98,18 +98,18 @@
     return jnp.full((1, width), jnp.where(is_lower, 1.0, -1.0), jnp.float32)
 
 
-def sweep_layer(leaf_data, merge_op):
+def sweep_layer(leaf_data, merge_op, layer):
     lat_count = lax.axis_size("lat")
     lat_index = lax.axis_index("lat")
     levels = lat_count.bit_length() - 1
     width = leaf_data.shape[1]
     values = leaf_data
     for bit_level in range(levels):
-        partner = partner_2(values, "lat", bit_level)
+        partner = partner_2(values, "lat", bit_level, layer)
         values = mixed_dot(level_sign(lat_index, bit_level, width), values, partner, merge_op)
     values = transposed_dot(values, merge_op)
     for bit_level in range(levels - 1, -1, -1):
-        partner = partner_2(values, "lat", bit_level)
+        partner = partner_2(values, "lat", bit_level, layer)
         values = haar_pair(values, partner, lat_index, bit_level)
     return values
 
@@ -126,7 +126,7 @@
         leaf_data = (
             shot_rows.astype(jnp.float32) + coupling_row * incoming.astype(jnp.float32)
         ).astype(jnp.bfloat16)
-        solved = sweep_layer(leaf_data, merge_op)
+        solved = sweep_layer(leaf_data, merge_op, sweep_step)
         result = jnp.where(depth_index == sweep_step, solved, result)
         if sweep_step + 1 < depth_count:
             incoming = handed_down(solved, "depth", sweep_step)

time: 184 us -> 227 us (1.23)
  waiting for transfers between devices: 119 us -> 154 us
  starting transfers between devices: 22.4 us -> 28.9 us
    ppermute x3, waiting for transfers between devices: 16.2 us -> 127 us  [handed_down(): return lax.ppermute(array, axis, [(layer, layer + 1)])]
    ppermute x24, waiting for transfers between devices: 102 us -> 27.7 us  [partner_2(): return lax.ppermute(block, ('depth', axis), route)]
    ppermute x24, starting transfers between devices: 19.6 us -> 26.3 us  [partner_2(): return lax.ppermute(block, ('depth', axis), route)]
  transfers between devices with their start and end apart: 27 -> 27, of which waited for: 25 -> 7; matrix products, arithmetic and copies ran while one was open for 0% -> 0% of each run, Pallas kernels for 0% -> 0%
where the time goes in v8:
time: 227 us; the launch traced here: 226 us
  waiting for transfers between devices  154 us (68%)
  starting transfers between devices  28.9 us (13%)
  Pallas kernels  28.6 us (13%)
  local copies, waits for them, and re-layouts  10.2 us (4%)
  other arithmetic  3.31 us (1%)
    ppermute x3, waiting for transfers between devices, handed_down(): return lax.ppermute(array, axis, [(layer, layer + 1)])  127 us
    ppermute x24, waiting for transfers between devices, partner_2(): return lax.ppermute(block, ('depth', axis), route)  27.7 us
    ppermute x24, starting transfers between devices, partner_2(): return lax.ppermute(block, ('depth', axis), route)  26.3 us
    pallas_call x12, Pallas kernels, mixed_dot(): pl.pallas_call(mixed_dot_kernel, out_shape=jax.ShapeDtypeStruct(values.sh...  18.4 us
    pallas_call x4, Pallas kernels, transposed_dot(): pl.pallas_call(transposed_dot_kernel, out_shape=jax.ShapeDtypeStruct(valu...  10.2 us
    unnamed x14, local copies, waits for them, and re-layouts  10.1 us
  transfers between devices with their start and end apart: 27, of which 7 were waited for; matrix products, arithmetic and copies ran while one was open for 0% of the time, Pallas kernels for 0%

profile of v8, /device:TPU:7, one launch (start us, length us, event | category | flops | bytes accessed | tf_op | source)
XLA Modules:
  0.0 226.0 jit_solution(8067411457735447103)
XLA Ops:
  0.0 0.7 broadcast_multiply_fusion
  0.7 0.9 fusion.48.values_ref
  1.6 0.7 collective-permute-start
  2.4 3.4 %copy-done = bf16[1,1,2048,2048]{3,2,1,0:T(8,128)(2,1)S(1)} copy-done((bf16[1,1,2048,2048]{3,2,1,0:T(8,128)(2,1)S(1)}, bf16[1,1,2048,2048]{3,2,1,0:T(8,128)(2,1)}, u32[]{:S(2)}) %copy-start) | copy-done | bytes 8388632
  5.7 1.5 shard_map.37.values_ref
  7.3 0.7 collective-permute-start.1
  8.0 3.4 %copy-done.1 = bf16[1,1,2048,2048]{3,2,1,0:T(8,128)(2,1)S(1)} copy-done((bf16[1,1,2048,2048]{3,2,1,0:T(8,128)(2,1)S(1)}, bf16[1,1,2048,2048]{3,2,1,0:T(8,128)(2,1)}, u32[]{:S(2)}) %copy-start.1) | copy-done | bytes 8388632
  11.4 1.5 shard_map.38.values_ref
  12.9 0.7 collective-permute-start.2
  13.7 3.4 %copy-done.2 = bf16[1,1,2048,2048]{3,2,1,0:T(8,128)(2,1)S(1)} copy-done((bf16[1,1,2048,2048]{3,2,1,0:T(8,128)(2,1)S(1)}, bf16[1,1,2048,2048]{3,2,1,0:T(8,128)(2,1)}, u32[]{:S(2)}) %copy-start.2) | copy-done | bytes 8388632
  17.1 1.5 shard_map.39.values_ref
  18.6 2.5 %shard_map.40 = bf16[32,2048]{1,0:T(8,128)(2,1)S(1)} custom-call(bf16[32,2048]{1,0:T(8,128)(2,1)S(1)} %shard_map.39.values_ref, bf16[2048,2048]{1,0:T(8,128)(2,1)S(1)} %bitcast.13), custom_call_target="tpu_custom_call" | custom-call | flops 268435456 | bytes 8781824 | tf_op jit(solution)/shard_map/pallas_call | solution.py:77
  21.1 0.7 collective-permute-start.3
  21.8 0.1 fusion.2
  21.9 0.7 collective-permute-start.4
  22.6 0.1 fusion.6
  22.7 0.7 collective-permute-start.5
  23.4 0.1 fusion.10
  23.4 0.7 collective-permute-start.6
  24.2 0.7 collective-permute-start.7
  24.9 1.5 shard_map.41.values_ref
  26.4 0.7 collective-permute-start.8
  27.1 1.5 shard_map.42.values_ref
  28.7 0.7 collective-permute-start.9
  29.4 1.5 shard_map.43.values_ref
  30.9 2.5 %shard_map.44 = bf16[32,2048]{1,0:T(8,128)(2,1)S(1)} custom-call(bf16[32,2048]{1,0:T(8,128)(2,1)S(1)} %shard_map.43.values_ref, bf16[2048,2048]{1,0:T(8,128)(2,1)S(1)} %bitcast.19), custom_call_target="tpu_custom_call" | custom-call | flops 268435456 | bytes 8781824 | tf_op jit(solution)/shard_map/pallas_call | solution.py:77
  33.4 0.7 collective-permute-start.10
  34.1 0.1 fusion.14
  34.2 0.7 collective-permute-start.11
  34.9 0.1 fusion.18
  35.0 0.7 collective-permute-start.12
  35.7 0.1 fusion.22
  35.7 0.7 collective-permute-start.13
  36.5 0.7 collective-permute-start.14
  37.2 1.5 shard_map.45.values_ref
  38.7 0.7 collective-permute-start.15
  39.4 1.5 shard_map.46.values_ref
  40.9 0.9 collective-permute-start.16
  41.8 1.5 shard_map.47.values_ref
  43.3 2.5 %shard_map.48 = bf16[32,2048]{1,0:T(8,128)(2,1)S(1)} custom-call(bf16[32,2048]{1,0:T(8,128)(2,1)S(1)} %shard_map.47.values_ref, bf16[2048,2048]{1,0:T(8,128)(2,1)S(1)} %bitcast.23), custom_call_target="tpu_custom_call" | custom-call | flops 268435456 | bytes 8781824 | tf_op jit(solution)/shard_map/pallas_call | solution.py:77
  45.9 0.7 collective-permute-start.17
  46.6 0.1 fusion.26
  46.7 0.7 collective-permute-start.18
  47.3 0.1 fusion.30
  47.4 0.7 collective-permute-start.19
  48.2 1.3 collective-permute-start.20
  49.5 126.7 %collective-permute-done.20 = bf16[32,2048]{1,0:T(8,128)(2,1)S(1)} collective-permute-done((bf16[32,2048]{1,0:T(8,128)(2,1)S(1)}, bf16[32,2048]{1,0:T(8,128)(2,1)S(1)}, u32[]{:S(2)}, u32[]{:S(2)}) %collective-permute-start.20) | collective-permute-done | bytes 131104 | tf_op jit(solution)/shard_map/ppermute | solution.py:25
  176.2 2.8 %collective-permute-start.21 = (bf16[32,2048]{1,0:T(8,128)(2,1)S(1)}, bf16[32,2048]{1,0:T(8,128)(2,1)S(1)}, u32[]{:S(2)}, u32[]{:S(2)}) collective-permute-start(bf16[32,2048]{1,0:T(8,128)(2,1)S(1)} %fusion.51.values_ref), channel_id=1, source_target_pairs={{24,25},{25,24},{26,27},{27,26},{28,29},{29,28},{30,31},{31,30}} | collective-permute-start | bytes 393224 | tf_op jit(solution)/shard_map/ppermute | solution.py:21
  179.1 1.0 collective-permute-done.21.partner_ref
  180.0 1.5 shard_map.49.values_ref
  181.5 1.9 collective-permute-start.22
  183.5 4.7 %collective-permute-done.22.partner_ref = bf16[32,2048]{1,0:T(8,128)(2,1)S(1)} collective-permute-done((bf16[32,2048]{1,0:T(8,128)(2,1)S(1)}, bf16[32,2048]{1,0:T(8,128)(2,1)S(1)}, u32[]{:S(2)}, u32[]{:S(2)}) %collective-permute-start.22) | collective-permute-done | bytes 131104 | tf_op jit(solution)/shard_map/ppermute | solution.py:21
  188.1 1.5 shard_map.50.values_ref
  189.7 2.1 collective-permute-start.23
  191.8 8.5 %collective-permute-done.23.partner_ref = bf16[32,2048]{1,0:T(8,128)(2,1)S(1)} collective-permute-done((bf16[32,2048]{1,0:T(8,128)(2,1)S(1)}, bf16[32,2048]{1,0:T(8,128)(2,1)S(1)}, u32[]{:S(2)}, u32[]{:S(2)}) %collective-permute-start.23) | collective-permute-done | bytes 131104 | tf_op jit(solution)/shard_map/ppermute | solution.py:21
  200.3 1.5 shard_map.51.values_ref
  201.8 2.5 %shard_map.52 = bf16[32,2048]{1,0:T(8,128)(2,1)S(1)} custom-call(bf16[32,2048]{1,0:T(8,128)(2,1)S(1)} %shard_map.51.values_ref, bf16[2048,2048]{1,0:T(8,128)(2,1)S(1)} %bitcast.27), custom_call_target="tpu_custom_call" | custom-call | flops 268435456 | bytes 8781824 | tf_op jit(solution)/shard_map/pallas_call | solution.py:77
  204.3 1.9 collective-permute-start.24
  206.3 8.1 %collective-permute-done.24 = bf16[32,2048]{1,0:T(8,128)(2,1)S(1)} collective-permute-done((bf16[32,2048]{1,0:T(8,128)(2,1)S(1)}, bf16[32,2048]{1,0:T(8,128)(2,1)S(1)}, u32[]{:S(2)}, u32[]{:S(2)}) %collective-permute-start.24) | collective-permute-done | bytes 131104 | tf_op jit(solution)/shard_map/ppermute | solution.py:21
  214.4 1.9 collective-permute-start.25
  216.3 4.5 %collective-permute-done.25 = bf16[32,2048]{1,0:T(8,128)(2,1)S(1)} collective-permute-done((bf16[32,2048]{1,0:T(8,128)(2,1)S(1)}, bf16[32,2048]{1,0:T(8,128)(2,1)S(1)}, u32[]{:S(2)}, u32[]{:S(2)}) %collective-permute-start.25) | collective-permute-done | bytes 131104 | tf_op jit(solution)/shard_map/ppermute | solution.py:21
  220.9 3.3 %collective-permute-start.26 = (bf16[32,2048]{1,0:T(8,128)(2,1)S(1)}, bf16[32,2048]{1,0:T(8,128)(2,1)S(1)}, u32[]{:S(2)}, u32[]{:S(2)}) collective-permute-start(bf16[32,2048]{1,0:T(8,128)(2,1)S(1)} %fusion.42), channel_id=1, source_target_pairs={{24,25},{25,24},{26,27},{27,26},{28,29},{29,28},{30,31},{31,30}} | collective-permute-start | bytes 393224 | tf_op jit(solution)/shard_map/ppermute | solution.py:21
  224.2 1.0 collective-permute-done.26
  225.2 0.8 fusion.53
  (41 shorter events, 0.4 us)
Async XLA Ops:
  1.6 0.7 collective-permute-start
  2.4 3.4 %copy-start = (bf16[1,1,2048,2048]{3,2,1,0:T(8,128)(2,1)S(1)}, bf16[1,1,2048,2048]{3,2,1,0:T(8,128)(2,1)}, u32[]{:S(2)}) copy-start(bf16[1,1,2048,2048]{3,2,1,0:T(8,128)(2,1)} %param.5) | copy-start | bytes 25165828
  7.3 0.7 collective-permute-start.1
  8.0 3.4 %copy-start.1 = (bf16[1,1,2048,2048]{3,2,1,0:T(8,128)(2,1)S(1)}, bf16[1,1,2048,2048]{3,2,1,0:T(8,128)(2,1)}, u32[]{:S(2)}) copy-start(bf16[1,1,2048,2048]{3,2,1,0:T(8,128)(2,1)} %param.5) | copy-start | bytes 25165828
  12.9 0.7 collective-permute-start.2
  13.7 3.4 %copy-start.2 = (bf16[1,1,2048,2048]{3,2,1,0:T(8,128)(2,1)S(1)}, bf16[1,1,2048,2048]{3,2,1,0:T(8,128)(2,1)}, u32[]{:S(2)}) copy-start(bf16[1,1,2048,2048]{3,2,1,0:T(8,128)(2,1)} %param.5) | copy-start | bytes 25165828
  17.1 7.1 %copy-start.3 = (bf16[1,1,32,2048]{3,2,1,0:T(8,128)(2,1)S(1)}, bf16[1,1,32,2048]{3,2,1,0:T(8,128)(2,1)}, u32[]{:S(2)}) copy-start(bf16[1,1,32,2048]{3,2,1,0:T(8,128)(2,1)} %param.3) | copy-start | bytes 393220
  17.1 7.1 %copy-start.4 = (f32[1,1,2048]{2,1,0:T(1,128)S(1)}, f32[1,1,2048]{2,1,0:T(1,128)}, u32[]{:S(2)}) copy-start(f32[1,1,2048]{2,1,0:T(1,128)} %param.4) | copy-start | bytes 24580
  17.1 7.8 %slice-start = ((s8[8388608]{0:T(1024)(128)(4,1)}), s8[4194304]{0:T(1024)(128)(4,1)S(1)}, s32[]{:S(2)}) async-start(s8[8388608]{0:T(1024)(128)(4,1)} %bitcast.14), calls=%async_computation | async-start | bytes 8388608
  18.6 6.3 %slice-start.1 = ((s8[8388608]{0:T(1024)(128)(4,1)}), s8[4194304]{0:T(1024)(128)(4,1)S(1)}, s32[]{:S(2)}) async-start(s8[8388608]{0:T(1024)(128)(4,1)} %bitcast.14), calls=%async_computation.1 | async-start | bytes 8388608
  21.1 0.7 collective-permute-start.3
  21.9 0.7 collective-permute-start.4
  22.7 0.7 collective-permute-start.5
  23.4 0.7 collective-permute-start.6
  24.2 0.7 collective-permute-start.7
  26.4 0.7 collective-permute-start.8
  28.7 0.7 collective-permute-start.9
  33.4 0.7 collective-permute-start.10
  34.2 0.7 collective-permute-start.11
  35.0 0.7 collective-permute-start.12
  35.7 0.7 collective-permute-start.13
  36.5 0.7 collective-permute-start.14
  38.7 0.7 collective-permute-start.15
  40.9 0.9 collective-permute-start.16
  45.9 0.7 collective-permute-start.17
  46.7 0.7 collective-permute-start.18
  47.4 0.7 collective-permute-start.19
  48.2 128.0 %collective-permute-start.20 = (bf16[32,2048]{1,0:T(8,128)(2,1)S(1)}, bf16[32,2048]{1,0:T(8,128)(2,1)S(1)}, u32[]{:S(2)}, u32[]{:S(2)}) collective-permute-start(bf16[32,2048]{1,0:T(8,128)(2,1)S(1)} %fusion.34), channel_id=1, source_target_pairs={{16,24},{17,25},{18,26},{19,27},{20,28},{21,29},{22,30},{23,31}} | collective-permute-start | bytes 393224 | tf_op jit(solution)/shard_map/ppermute | solution.py:25
  176.2 3.8 %collective-permute-start.21 = (bf16[32,2048]{1,0:T(8,128)(2,1)S(1)}, bf16[32,2048]{1,0:T(8,128)(2,1)S(1)}, u32[]{:S(2)}, u32[]{:S(2)}) collective-permute-start(bf16[32,2048]{1,0:T(8,128)(2,1)S(1)} %fusion.51.values_ref), channel_id=1, source_target_pairs={{24,25},{25,24},{26,27},{27,26},{28,29},{29,28},{30,31},{31,30}} | collective-permute-start | bytes 393224 | tf_op jit(solution)/shard_map/ppermute | solution.py:21
  181.5 6.6 %collective-permute-start.22 = (bf16[32,2048]{1,0:T(8,128)(2,1)S(1)}, bf16[32,2048]{1,0:T(8,128)(2,1)S(1)}, u32[]{:S(2)}, u32[]{:S(2)}) collective-permute-start(bf16[32,2048]{1,0:T(8,128)(2,1)S(1)} %shard_map.49.values_ref), channel_id=1, source_target_pairs={{24,26},{26,24},{25,27},{27,25},{28,30},{30,28},{29,31},{31,29}} | collective-permute-start | bytes 393224 | tf_op jit(solution)/shard_map/ppermute | solution.py:21
  189.7 10.6 %collective-permute-start.23 = (bf16[32,2048]{1,0:T(8,128)(2,1)S(1)}, bf16[32,2048]{1,0:T(8,128)(2,1)S(1)}, u32[]{:S(2)}, u32[]{:S(2)}) collective-permute-start(bf16[32,2048]{1,0:T(8,128)(2,1)S(1)} %shard_map.50.values_ref), channel_id=1, source_target_pairs={{24,28},{28,24},{25,29},{29,25},{26,30},{30,26},{27,31},{31,27}} | collective-permute-start | bytes 393224 | tf_op jit(solution)/shard_map/ppermute | solution.py:21
  204.3 10.0 %collective-permute-start.24 = (bf16[32,2048]{1,0:T(8,128)(2,1)S(1)}, bf16[32,2048]{1,0:T(8,128)(2,1)S(1)}, u32[]{:S(2)}, u32[]{:S(2)}) collective-permute-start(bf16[32,2048]{1,0:T(8,128)(2,1)S(1)} %shard_map.52), channel_id=1, source_target_pairs={{24,28},{28,24},{25,29},{29,25},{26,30},{30,26},{27,31},{31,27}} | collective-permute-start | bytes 393224 | tf_op jit(solution)/shard_map/ppermute | solution.py:21
  214.4 6.5 %collective-permute-start.25 = (bf16[32,2048]{1,0:T(8,128)(2,1)S(1)}, bf16[32,2048]{1,0:T(8,128)(2,1)S(1)}, u32[]{:S(2)}, u32[]{:S(2)}) collective-permute-start(bf16[32,2048]{1,0:T(8,128)(2,1)S(1)} %fusion.38), channel_id=1, source_target_pairs={{24,26},{26,24},{25,27},{27,25},{28,30},{30,28},{29,31},{31,29}} | collective-permute-start | bytes 393224 | tf_op jit(solution)/shard_map/ppermute | solution.py:21
  220.9 4.2 %collective-permute-start.26 = (bf16[32,2048]{1,0:T(8,128)(2,1)S(1)}, bf16[32,2048]{1,0:T(8,128)(2,1)S(1)}, u32[]{:S(2)}, u32[]{:S(2)}) collective-permute-start(bf16[32,2048]{1,0:T(8,128)(2,1)S(1)} %fusion.42), channel_id=1, source_target_pairs={{24,25},{25,24},{26,27},{27,26},{28,29},{29,28},{30,31},{31,30}} | collective-permute-start | bytes 393224 | tf_op jit(solution)/shard_map/ppermute | solution.py:21

commit v9 on v6

--- a/solution.py
+++ b/solution.py
@@ -121,11 +121,13 @@
     depth_count = lax.axis_size("depth")
     shot_rows = sources[0, 0]
     result = jnp.zeros_like(shot_rows)
-    incoming = jnp.zeros_like(shot_rows)
     for sweep_step in range(depth_count):
-        leaf_data = (
-            shot_rows.astype(jnp.float32) + coupling_row * incoming.astype(jnp.float32)
-        ).astype(jnp.bfloat16)
+        if sweep_step == 0:
+            leaf_data = shot_rows
+        else:
+            leaf_data = (
+                shot_rows.astype(jnp.float32) + coupling_row * incoming.astype(jnp.float32)
+            ).astype(jnp.bfloat16)
         solved = sweep_layer(leaf_data, merge_op)
         result = jnp.where(depth_index == sweep_step, solved, result)
         if sweep_step + 1 < depth_count:

time: 184 us -> 183 us (level)
    unnamed x14 -> x16, local copies, waits for them, and re-layouts: 10.2 us -> 11.1 us
where the time goes in v9:
time: 183 us
  waiting for transfers between devices  119 us (65%)
  Pallas kernels  28.5 us (16%)
  starting transfers between devices  22.3 us (12%)
  local copies, waits for them, and re-layouts  11.1 us (6%)
    ppermute x24, waiting for transfers between devices, partner_2(): return lax.ppermute(block, axis, route)  103 us
    ppermute x24, starting transfers between devices, partner_2(): return lax.ppermute(block, axis, route)  19.5 us
    pallas_call x12, Pallas kernels, mixed_dot(): pl.pallas_call(mixed_dot_kernel, out_shape=jax.ShapeDtypeStruct(values.sh...  18.4 us
    ppermute x3, waiting for transfers between devices, handed_down(): return lax.ppermute(array, axis, [(layer, layer + 1)])  16.2 us
    unnamed x16, local copies, waits for them, and re-layouts  11.1 us
    pallas_call x4, Pallas kernels, transposed_dot(): pl.pallas_call(transposed_dot_kernel, out_shape=jax.ShapeDtypeStruct(valu...  10.2 us
  transfers between devices with their start and end apart: 27, of which 25 were waited for; matrix products, arithmetic and copies ran while one was open for 0% of the time, Pallas kernels for 0%

profile of v9, /device:TPU:7, one launch (start us, length us, event | category | flops | bytes accessed | tf_op | source)
XLA Modules:
  0.0 182.7 jit_solution(1990046929055190330)
XLA Ops:
  0.0 0.7 collective-permute-start
  0.7 1.2 collective-permute-done.partner_ref
  1.9 3.4 %copy-done = bf16[1,1,2048,2048]{3,2,1,0:T(8,128)(2,1)S(1)} copy-done((bf16[1,1,2048,2048]{3,2,1,0:T(8,128)(2,1)S(1)}, bf16[1,1,2048,2048]{3,2,1,0:T(8,128)(2,1)}, u32[]{:S(2)}) %copy-start) | copy-done | bytes 8388632
  5.3 0.9 copy-done.3
  6.2 1.5 shard_map.37.values_ref
  7.7 1.3 collective-permute-start.1
  9.0 3.4 %collective-permute-done.1.partner_ref = bf16[32,2048]{1,0:T(8,128)(2,1)S(1)} collective-permute-done((bf16[32,2048]{1,0:T(8,128)(2,1)S(1)}, bf16[32,2048]{1,0:T(8,128)(2,1)S(1)}, u32[]{:S(2)}, u32[]{:S(2)}) %collective-permute-start.1) | collective-permute-done | bytes 131104 | tf_op jit(solution)/shard_map/ppermute | solution.py:21
  12.4 3.4 %copy-done.1 = bf16[1,1,2048,2048]{3,2,1,0:T(8,128)(2,1)S(1)} copy-done((bf16[1,1,2048,2048]{3,2,1,0:T(8,128)(2,1)S(1)}, bf16[1,1,2048,2048]{3,2,1,0:T(8,128)(2,1)}, u32[]{:S(2)}) %copy-start.1) | copy-done | bytes 8388632
  15.8 1.5 shard_map.38.values_ref
  17.3 2.3 %collective-permute-start.2 = (bf16[32,2048]{1,0:T(8,128)(2,1)S(1)}, bf16[32,2048]{1,0:T(8,128)(2,1)S(1)}, u32[]{:S(2)}, u32[]{:S(2)}) collective-permute-start(bf16[32,2048]{1,0:T(8,128)(2,1)S(1)} %shard_map.38.values_ref), channel_id=1, source_target_pairs={{0,4},{4,0},{1,5},{5,1},{2,6},{6,2},{3,7},{7,3},{8,12},{12,8},{9,1... | collective-permute-start | bytes 393224 | tf_op jit(solution)/shard_map/ppermute | solution.py:21
  19.7 5.8 %collective-permute-done.2.partner_ref = bf16[32,2048]{1,0:T(8,128)(2,1)S(1)} collective-permute-done((bf16[32,2048]{1,0:T(8,128)(2,1)S(1)}, bf16[32,2048]{1,0:T(8,128)(2,1)S(1)}, u32[]{:S(2)}, u32[]{:S(2)}) %collective-permute-start.2) | collective-permute-done | bytes 131104 | tf_op jit(solution)/shard_map/ppermute | solution.py:21
  25.5 3.4 %copy-done.2 = bf16[1,1,2048,2048]{3,2,1,0:T(8,128)(2,1)S(1)} copy-done((bf16[1,1,2048,2048]{3,2,1,0:T(8,128)(2,1)S(1)}, bf16[1,1,2048,2048]{3,2,1,0:T(8,128)(2,1)}, u32[]{:S(2)}) %copy-start.2) | copy-done | bytes 8388632
  28.9 1.5 shard_map.39.values_ref
  30.4 2.5 %shard_map.40 = bf16[32,2048]{1,0:T(8,128)(2,1)S(1)} custom-call(bf16[32,2048]{1,0:T(8,128)(2,1)S(1)} %shard_map.39.values_ref, bf16[2048,2048]{1,0:T(8,128)(2,1)S(1)} %bitcast.11), custom_call_target="tpu_custom_call" | custom-call | flops 268435456 | bytes 8781824 | tf_op jit(solution)/shard_map/pallas_call | solution.py:77
  33.0 4.7 %collective-permute-done.3 = bf16[32,2048]{1,0:T(8,128)(2,1)S(1)} collective-permute-done((bf16[32,2048]{1,0:T(8,128)(2,1)S(1)}, bf16[32,2048]{1,0:T(8,128)(2,1)S(1)}, u32[]{:S(2)}, u32[]{:S(2)}) %collective-permute-start.3) | collective-permute-done | bytes 131104 | tf_op jit(solution)/shard_map/ppermute | solution.py:21
  37.7 2.9 %collective-permute-start.4 = (bf16[32,2048]{1,0:T(8,128)(2,1)S(1)}, bf16[32,2048]{1,0:T(8,128)(2,1)S(1)}, u32[]{:S(2)}, u32[]{:S(2)}) collective-permute-start(bf16[32,2048]{1,0:T(8,128)(2,1)S(1)} %fusion.2), channel_id=1, source_target_pairs={{0,2},{2,0},{1,3},{3,1},{4,6},{6,4},{5,7},{7,5},{8,10},{10,8},{9,1... | collective-permute-start | bytes 393224 | tf_op jit(solution)/shard_map/ppermute | solution.py:21
  40.6 2.9 %collective-permute-done.4 = bf16[32,2048]{1,0:T(8,128)(2,1)S(1)} collective-permute-done((bf16[32,2048]{1,0:T(8,128)(2,1)S(1)}, bf16[32,2048]{1,0:T(8,128)(2,1)S(1)}, u32[]{:S(2)}, u32[]{:S(2)}) %collective-permute-start.4) | collective-permute-done | bytes 131104 | tf_op jit(solution)/shard_map/ppermute | solution.py:21
  43.6 4.5 %collective-permute-start.5 = (bf16[32,2048]{1,0:T(8,128)(2,1)S(1)}, bf16[32,2048]{1,0:T(8,128)(2,1)S(1)}, u32[]{:S(2)}, u32[]{:S(2)}) collective-permute-start(bf16[32,2048]{1,0:T(8,128)(2,1)S(1)} %fusion.6), channel_id=1, source_target_pairs={{0,1},{1,0},{2,3},{3,2},{4,5},{5,4},{6,7},{7,6},{8,9},{9,8},{10,11... | collective-permute-start | bytes 393224 | tf_op jit(solution)/shard_map/ppermute | solution.py:21
  48.2 1.0 collective-permute-done.5
  49.2 0.7 collective-permute-start.6
  50.0 0.4 collective-permute-start.7
  50.4 1.0 collective-permute-done.7.partner_ref
  51.4 1.5 shard_map.41.values_ref
  52.9 4.7 %collective-permute-done.8.partner_ref = bf16[32,2048]{1,0:T(8,128)(2,1)S(1)} collective-permute-done((bf16[32,2048]{1,0:T(8,128)(2,1)S(1)}, bf16[32,2048]{1,0:T(8,128)(2,1)S(1)}, u32[]{:S(2)}, u32[]{:S(2)}) %collective-permute-start.8) | collective-permute-done | bytes 131104 | tf_op jit(solution)/shard_map/ppermute | solution.py:21
  57.6 1.5 shard_map.42.values_ref
  59.2 9.1 %collective-permute-done.9.partner_ref = bf16[32,2048]{1,0:T(8,128)(2,1)S(1)} collective-permute-done((bf16[32,2048]{1,0:T(8,128)(2,1)S(1)}, bf16[32,2048]{1,0:T(8,128)(2,1)S(1)}, u32[]{:S(2)}, u32[]{:S(2)}) %collective-permute-start.9) | collective-permute-done | bytes 131104 | tf_op jit(solution)/shard_map/ppermute | solution.py:21
  68.3 1.5 shard_map.43.values_ref
  69.8 2.5 %shard_map.44 = bf16[32,2048]{1,0:T(8,128)(2,1)S(1)} custom-call(bf16[32,2048]{1,0:T(8,128)(2,1)S(1)} %shard_map.43.values_ref, bf16[2048,2048]{1,0:T(8,128)(2,1)S(1)} %bitcast.17), custom_call_target="tpu_custom_call" | custom-call | flops 268435456 | bytes 8781824 | tf_op jit(solution)/shard_map/pallas_call | solution.py:77
  72.4 7.7 %collective-permute-done.10 = bf16[32,2048]{1,0:T(8,128)(2,1)S(1)} collective-permute-done((bf16[32,2048]{1,0:T(8,128)(2,1)S(1)}, bf16[32,2048]{1,0:T(8,128)(2,1)S(1)}, u32[]{:S(2)}, u32[]{:S(2)}) %collective-permute-start.10) | collective-permute-done | bytes 131104 | tf_op jit(solution)/shard_map/ppermute | solution.py:21
  80.1 0.1 collective-permute-start.11
  80.2 4.6 %collective-permute-done.11 = bf16[32,2048]{1,0:T(8,128)(2,1)S(1)} collective-permute-done((bf16[32,2048]{1,0:T(8,128)(2,1)S(1)}, bf16[32,2048]{1,0:T(8,128)(2,1)S(1)}, u32[]{:S(2)}, u32[]{:S(2)}) %collective-permute-start.11) | collective-permute-done | bytes 131104 | tf_op jit(solution)/shard_map/ppermute | solution.py:21
  84.8 1.4 collective-permute-start.12
  86.3 1.0 collective-permute-done.12
  87.3 0.8 collective-permute-start.13
  88.2 0.4 collective-permute-start.14
  88.7 1.0 collective-permute-done.14.partner_ref
  89.6 1.5 shard_map.45.values_ref
  91.2 4.7 %collective-permute-done.15.partner_ref = bf16[32,2048]{1,0:T(8,128)(2,1)S(1)} collective-permute-done((bf16[32,2048]{1,0:T(8,128)(2,1)S(1)}, bf16[32,2048]{1,0:T(8,128)(2,1)S(1)}, u32[]{:S(2)}, u32[]{:S(2)}) %collective-permute-start.15) | collective-permute-done | bytes 131104 | tf_op jit(solution)/shard_map/ppermute | solution.py:21
  95.9 1.5 shard_map.46.values_ref
  97.4 1.2 collective-permute-start.16
  98.6 7.9 %collective-permute-done.16.partner_ref = bf16[32,2048]{1,0:T(8,128)(2,1)S(1)} collective-permute-done((bf16[32,2048]{1,0:T(8,128)(2,1)S(1)}, bf16[32,2048]{1,0:T(8,128)(2,1)S(1)}, u32[]{:S(2)}, u32[]{:S(2)}) %collective-permute-start.16) | collective-permute-done | bytes 131104 | tf_op jit(solution)/shard_map/ppermute | solution.py:21
  106.5 1.5 shard_map.47.values_ref
  108.1 2.5 %shard_map.48 = bf16[32,2048]{1,0:T(8,128)(2,1)S(1)} custom-call(bf16[32,2048]{1,0:T(8,128)(2,1)S(1)} %shard_map.47.values_ref, bf16[2048,2048]{1,0:T(8,128)(2,1)S(1)} %bitcast.21), custom_call_target="tpu_custom_call" | custom-call | flops 268435456 | bytes 8781824 | tf_op jit(solution)/shard_map/pallas_call | solution.py:77
  110.6 8.7 %collective-permute-done.17 = bf16[32,2048]{1,0:T(8,128)(2,1)S(1)} collective-permute-done((bf16[32,2048]{1,0:T(8,128)(2,1)S(1)}, bf16[32,2048]{1,0:T(8,128)(2,1)S(1)}, u32[]{:S(2)}, u32[]{:S(2)}) %collective-permute-start.17) | collective-permute-done | bytes 131104 | tf_op jit(solution)/shard_map/ppermute | solution.py:21
  119.4 0.1 collective-permute-start.18
  119.5 4.6 %collective-permute-done.18 = bf16[32,2048]{1,0:T(8,128)(2,1)S(1)} collective-permute-done((bf16[32,2048]{1,0:T(8,128)(2,1)S(1)}, bf16[32,2048]{1,0:T(8,128)(2,1)S(1)}, u32[]{:S(2)}, u32[]{:S(2)}) %collective-permute-start.18) | collective-permute-done | bytes 131104 | tf_op jit(solution)/shard_map/ppermute | solution.py:21
  124.1 1.4 collective-permute-start.19
  125.5 1.0 collective-permute-done.19
  126.6 1.3 collective-permute-start.20
  127.9 16.1 %collective-permute-done.20 = bf16[32,2048]{1,0:T(8,128)(2,1)S(1)} collective-permute-done((bf16[32,2048]{1,0:T(8,128)(2,1)S(1)}, bf16[32,2048]{1,0:T(8,128)(2,1)S(1)}, u32[]{:S(2)}, u32[]{:S(2)}) %collective-permute-start.20) | collective-permute-done | bytes 131104 | tf_op jit(solution)/shard_map/ppermute | solution.py:25
  144.1 1.0 collective-permute-start.21
  145.1 1.0 collective-permute-done.21.partner_ref
  146.0 1.5 shard_map.49.values_ref
  147.6 4.7 %collective-permute-done.22.partner_ref = bf16[32,2048]{1,0:T(8,128)(2,1)S(1)} collective-permute-done((bf16[32,2048]{1,0:T(8,128)(2,1)S(1)}, bf16[32,2048]{1,0:T(8,128)(2,1)S(1)}, u32[]{:S(2)}, u32[]{:S(2)}) %collective-permute-start.22) | collective-permute-done | bytes 131104 | tf_op jit(solution)/shard_map/ppermute | solution.py:21
  152.3 1.5 shard_map.50.values_ref
  153.8 0.2 collective-permute-start.23
  154.0 8.5 %collective-permute-done.23.partner_ref = bf16[32,2048]{1,0:T(8,128)(2,1)S(1)} collective-permute-done((bf16[32,2048]{1,0:T(8,128)(2,1)S(1)}, bf16[32,2048]{1,0:T(8,128)(2,1)S(1)}, u32[]{:S(2)}, u32[]{:S(2)}) %collective-permute-start.23) | collective-permute-done | bytes 131104 | tf_op jit(solution)/shard_map/ppermute | solution.py:21
  162.5 1.5 shard_map.51.values_ref
  164.1 2.5 %shard_map.52 = bf16[32,2048]{1,0:T(8,128)(2,1)S(1)} custom-call(bf16[32,2048]{1,0:T(8,128)(2,1)S(1)} %shard_map.51.values_ref, bf16[2048,2048]{1,0:T(8,128)(2,1)S(1)} %bitcast.25), custom_call_target="tpu_custom_call" | custom-call | flops 268435456 | bytes 8781824 | tf_op jit(solution)/shard_map/pallas_call | solution.py:77
  166.6 8.1 %collective-permute-done.24 = bf16[32,2048]{1,0:T(8,128)(2,1)S(1)} collective-permute-done((bf16[32,2048]{1,0:T(8,128)(2,1)S(1)}, bf16[32,2048]{1,0:T(8,128)(2,1)S(1)}, u32[]{:S(2)}, u32[]{:S(2)}) %collective-permute-start.24) | collective-permute-done | bytes 131104 | tf_op jit(solution)/shard_map/ppermute | solution.py:21
  174.9 4.5 %collective-permute-done.25 = bf16[32,2048]{1,0:T(8,128)(2,1)S(1)} collective-permute-done((bf16[32,2048]{1,0:T(8,128)(2,1)S(1)}, bf16[32,2048]{1,0:T(8,128)(2,1)S(1)}, u32[]{:S(2)}, u32[]{:S(2)}) %collective-permute-start.25) | collective-permute-done | bytes 131104 | tf_op jit(solution)/shard_map/ppermute | solution.py:21
  179.5 1.4 collective-permute-start.26
  180.9 1.0 collective-permute-done.26
  181.9 0.8 fusion.52
  (41 shorter events, 1.1 us)
Async XLA Ops:
  0.0 1.9 %collective-permute-start = (bf16[32,2048]{1,0:T(8,128)(2,1)}, bf16[32,2048]{1,0:T(8,128)(2,1)S(1)}, u32[]{:S(2)}, u32[]{:S(2)}) collective-permute-start(bf16[32,2048]{1,0:T(8,128)(2,1)} %bitcast.26), channel_id=1, source_target_pairs={{0,1},{1,0},{2,3},{3,2},{4,5},{5,4},{6,7},{7,6},{8,9},{9,8},{10,11... | collective-permute-start | bytes 393224 | tf_op jit(solution)/shard_map/ppermute | solution.py:21
  1.9 3.4 %copy-start = (bf16[1,1,2048,2048]{3,2,1,0:T(8,128)(2,1)S(1)}, bf16[1,1,2048,2048]{3,2,1,0:T(8,128)(2,1)}, u32[]{:S(2)}) copy-start(bf16[1,1,2048,2048]{3,2,1,0:T(8,128)(2,1)} %param.5) | copy-start | bytes 25165828
  5.3 0.9 copy-start.3
  7.7 4.7 %collective-permute-start.1 = (bf16[32,2048]{1,0:T(8,128)(2,1)S(1)}, bf16[32,2048]{1,0:T(8,128)(2,1)S(1)}, u32[]{:S(2)}, u32[]{:S(2)}) collective-permute-start(bf16[32,2048]{1,0:T(8,128)(2,1)S(1)} %shard_map.37.values_ref), channel_id=1, source_target_pairs={{0,2},{2,0},{1,3},{3,1},{4,6},{6,4},{5,7},{7,5},{8,10},{10,8},{9,1... | collective-permute-start | bytes 393224 | tf_op jit(solution)/shard_map/ppermute | solution.py:21
  12.4 3.4 %copy-start.1 = (bf16[1,1,2048,2048]{3,2,1,0:T(8,128)(2,1)S(1)}, bf16[1,1,2048,2048]{3,2,1,0:T(8,128)(2,1)}, u32[]{:S(2)}) copy-start(bf16[1,1,2048,2048]{3,2,1,0:T(8,128)(2,1)} %param.5) | copy-start | bytes 25165828
  17.3 8.1 %collective-permute-start.2 = (bf16[32,2048]{1,0:T(8,128)(2,1)S(1)}, bf16[32,2048]{1,0:T(8,128)(2,1)S(1)}, u32[]{:S(2)}, u32[]{:S(2)}) collective-permute-start(bf16[32,2048]{1,0:T(8,128)(2,1)S(1)} %shard_map.38.values_ref), channel_id=1, source_target_pairs={{0,4},{4,0},{1,5},{5,1},{2,6},{6,2},{3,7},{7,3},{8,12},{12,8},{9,1... | collective-permute-start | bytes 393224 | tf_op jit(solution)/shard_map/ppermute | solution.py:21
  25.5 3.4 %copy-start.2 = (bf16[1,1,2048,2048]{3,2,1,0:T(8,128)(2,1)S(1)}, bf16[1,1,2048,2048]{3,2,1,0:T(8,128)(2,1)}, u32[]{:S(2)}) copy-start(bf16[1,1,2048,2048]{3,2,1,0:T(8,128)(2,1)} %param.5) | copy-start | bytes 25165828
  28.9 21.1 %copy-start.4 = (bf16[1,1,32,2048]{3,2,1,0:T(8,128)(2,1)S(1)}, bf16[1,1,32,2048]{3,2,1,0:T(8,128)(2,1)}, u32[]{:S(2)}) copy-start(bf16[1,1,32,2048]{3,2,1,0:T(8,128)(2,1)} %param.3) | copy-start | bytes 393220
  28.9 21.1 %copy-start.5 = (f32[1,1,2048]{2,1,0:T(1,128)S(1)}, f32[1,1,2048]{2,1,0:T(1,128)}, u32[]{:S(2)}) copy-start(f32[1,1,2048]{2,1,0:T(1,128)} %param.4) | copy-start | bytes 24580
  28.9 22.5 %slice-start = ((s8[8388608]{0:T(1024)(128)(4,1)}), s8[4194304]{0:T(1024)(128)(4,1)S(1)}, s32[]{:S(2)}) async-start(s8[8388608]{0:T(1024)(128)(4,1)} %bitcast.12), calls=%async_computation | async-start | bytes 8388608
  30.4 21.0 %slice-start.1 = ((s8[8388608]{0:T(1024)(128)(4,1)}), s8[4194304]{0:T(1024)(128)(4,1)S(1)}, s32[]{:S(2)}) async-start(s8[8388608]{0:T(1024)(128)(4,1)} %bitcast.12), calls=%async_computation.1 | async-start | bytes 8388608
  32.9 4.7 %collective-permute-start.3 = (bf16[32,2048]{1,0:T(8,128)(2,1)S(1)}, bf16[32,2048]{1,0:T(8,128)(2,1)S(1)}, u32[]{:S(2)}, u32[]{:S(2)}) collective-permute-start(bf16[32,2048]{1,0:T(8,128)(2,1)S(1)} %shard_map.40), channel_id=1, source_target_pairs={{0,4},{4,0},{1,5},{5,1},{2,6},{6,2},{3,7},{7,3},{8,12},{12,8},{9,1... | collective-permute-start | bytes 393224 | tf_op jit(solution)/shard_map/ppermute | solution.py:21
  37.7 5.8 %collective-permute-start.4 = (bf16[32,2048]{1,0:T(8,128)(2,1)S(1)}, bf16[32,2048]{1,0:T(8,128)(2,1)S(1)}, u32[]{:S(2)}, u32[]{:S(2)}) collective-permute-start(bf16[32,2048]{1,0:T(8,128)(2,1)S(1)} %fusion.2), channel_id=1, source_target_pairs={{0,2},{2,0},{1,3},{3,1},{4,6},{6,4},{5,7},{7,5},{8,10},{10,8},{9,1... | collective-permute-start | bytes 393224 | tf_op jit(solution)/shard_map/ppermute | solution.py:21
  43.6 5.5 %collective-permute-start.5 = (bf16[32,2048]{1,0:T(8,128)(2,1)S(1)}, bf16[32,2048]{1,0:T(8,128)(2,1)S(1)}, u32[]{:S(2)}, u32[]{:S(2)}) collective-permute-start(bf16[32,2048]{1,0:T(8,128)(2,1)S(1)} %fusion.6), channel_id=1, source_target_pairs={{0,1},{1,0},{2,3},{3,2},{4,5},{5,4},{6,7},{7,6},{8,9},{9,8},{10,11... | collective-permute-start | bytes 393224 | tf_op jit(solution)/shard_map/ppermute | solution.py:21
  49.2 0.7 collective-permute-start.6
  50.0 1.4 collective-permute-start.7
  52.9 4.7 %collective-permute-start.8 = (bf16[32,2048]{1,0:T(8,128)(2,1)S(1)}, bf16[32,2048]{1,0:T(8,128)(2,1)S(1)}, u32[]{:S(2)}, u32[]{:S(2)}) collective-permute-start(bf16[32,2048]{1,0:T(8,128)(2,1)S(1)} %shard_map.41.values_ref), channel_id=1, source_target_pairs={{0,2},{2,0},{1,3},{3,1},{4,6},{6,4},{5,7},{7,5},{8,10},{10,8},{9,1... | collective-permute-start | bytes 393224 | tf_op jit(solution)/shard_map/ppermute | solution.py:21
  59.2 9.1 %collective-permute-start.9 = (bf16[32,2048]{1,0:T(8,128)(2,1)S(1)}, bf16[32,2048]{1,0:T(8,128)(2,1)S(1)}, u32[]{:S(2)}, u32[]{:S(2)}) collective-permute-start(bf16[32,2048]{1,0:T(8,128)(2,1)S(1)} %shard_map.42.values_ref), channel_id=1, source_target_pairs={{0,4},{4,0},{1,5},{5,1},{2,6},{6,2},{3,7},{7,3},{8,12},{12,8},{9,1... | collective-permute-start | bytes 393224 | tf_op jit(solution)/shard_map/ppermute | solution.py:21
  72.4 7.7 %collective-permute-start.10 = (bf16[32,2048]{1,0:T(8,128)(2,1)S(1)}, bf16[32,2048]{1,0:T(8,128)(2,1)S(1)}, u32[]{:S(2)}, u32[]{:S(2)}) collective-permute-start(bf16[32,2048]{1,0:T(8,128)(2,1)S(1)} %shard_map.44), channel_id=1, source_target_pairs={{0,4},{4,0},{1,5},{5,1},{2,6},{6,2},{3,7},{7,3},{8,12},{12,8},{9,1... | collective-permute-start | bytes 393224 | tf_op jit(solution)/shard_map/ppermute | solution.py:21
  80.1 4.6 %collective-permute-start.11 = (bf16[32,2048]{1,0:T(8,128)(2,1)S(1)}, bf16[32,2048]{1,0:T(8,128)(2,1)S(1)}, u32[]{:S(2)}, u32[]{:S(2)}) collective-permute-start(bf16[32,2048]{1,0:T(8,128)(2,1)S(1)} %fusion.14), channel_id=1, source_target_pairs={{0,2},{2,0},{1,3},{3,1},{4,6},{6,4},{5,7},{7,5},{8,10},{10,8},{9,1... | collective-permute-start | bytes 393224 | tf_op jit(solution)/shard_map/ppermute | solution.py:21
  84.8 2.4 %collective-permute-start.12 = (bf16[32,2048]{1,0:T(8,128)(2,1)S(1)}, bf16[32,2048]{1,0:T(8,128)(2,1)S(1)}, u32[]{:S(2)}, u32[]{:S(2)}) collective-permute-start(bf16[32,2048]{1,0:T(8,128)(2,1)S(1)} %fusion.18), channel_id=1, source_target_pairs={{0,1},{1,0},{2,3},{3,2},{4,5},{5,4},{6,7},{7,6},{8,9},{9,8},{10,11... | collective-permute-start | bytes 393224 | tf_op jit(solution)/shard_map/ppermute | solution.py:21
  87.3 0.9 collective-permute-start.13
  88.2 1.4 collective-permute-start.14
  91.2 4.7 %collective-permute-start.15 = (bf16[32,2048]{1,0:T(8,128)(2,1)S(1)}, bf16[32,2048]{1,0:T(8,128)(2,1)S(1)}, u32[]{:S(2)}, u32[]{:S(2)}) collective-permute-start(bf16[32,2048]{1,0:T(8,128)(2,1)S(1)} %shard_map.45.values_ref), channel_id=1, source_target_pairs={{0,2},{2,0},{1,3},{3,1},{4,6},{6,4},{5,7},{7,5},{8,10},{10,8},{9,1... | collective-permute-start | bytes 393224 | tf_op jit(solution)/shard_map/ppermute | solution.py:21
  97.4 9.1 %collective-permute-start.16 = (bf16[32,2048]{1,0:T(8,128)(2,1)S(1)}, bf16[32,2048]{1,0:T(8,128)(2,1)S(1)}, u32[]{:S(2)}, u32[]{:S(2)}) collective-permute-start(bf16[32,2048]{1,0:T(8,128)(2,1)S(1)} %shard_map.46.values_ref), channel_id=1, source_target_pairs={{0,4},{4,0},{1,5},{5,1},{2,6},{6,2},{3,7},{7,3},{8,12},{12,8},{9,1... | collective-permute-start | bytes 393224 | tf_op jit(solution)/shard_map/ppermute | solution.py:21
  110.6 8.7 %collective-permute-start.17 = (bf16[32,2048]{1,0:T(8,128)(2,1)S(1)}, bf16[32,2048]{1,0:T(8,128)(2,1)S(1)}, u32[]{:S(2)}, u32[]{:S(2)}) collective-permute-start(bf16[32,2048]{1,0:T(8,128)(2,1)S(1)} %shard_map.48), channel_id=1, source_target_pairs={{0,4},{4,0},{1,5},{5,1},{2,6},{6,2},{3,7},{7,3},{8,12},{12,8},{9,1... | collective-permute-start | bytes 393224 | tf_op jit(solution)/shard_map/ppermute | solution.py:21
  119.4 4.6 %collective-permute-start.18 = (bf16[32,2048]{1,0:T(8,128)(2,1)S(1)}, bf16[32,2048]{1,0:T(8,128)(2,1)S(1)}, u32[]{:S(2)}, u32[]{:S(2)}) collective-permute-start(bf16[32,2048]{1,0:T(8,128)(2,1)S(1)} %fusion.26), channel_id=1, source_target_pairs={{0,2},{2,0},{1,3},{3,1},{4,6},{6,4},{5,7},{7,5},{8,10},{10,8},{9,1... | collective-permute-start | bytes 393224 | tf_op jit(solution)/shard_map/ppermute | solution.py:21
  124.1 2.4 %collective-permute-start.19 = (bf16[32,2048]{1,0:T(8,128)(2,1)S(1)}, bf16[32,2048]{1,0:T(8,128)(2,1)S(1)}, u32[]{:S(2)}, u32[]{:S(2)}) collective-permute-start(bf16[32,2048]{1,0:T(8,128)(2,1)S(1)} %fusion.30), channel_id=1, source_target_pairs={{0,1},{1,0},{2,3},{3,2},{4,5},{5,4},{6,7},{7,6},{8,9},{9,8},{10,11... | collective-permute-start | bytes 393224 | tf_op jit(solution)/shard_map/ppermute | solution.py:21
  126.6 17.4 %collective-permute-start.20 = (bf16[32,2048]{1,0:T(8,128)(2,1)S(1)}, bf16[32,2048]{1,0:T(8,128)(2,1)S(1)}, u32[]{:S(2)}, u32[]{:S(2)}) collective-permute-start(bf16[32,2048]{1,0:T(8,128)(2,1)S(1)} %fusion.34), channel_id=1, source_target_pairs={{16,24},{17,25},{18,26},{19,27},{20,28},{21,29},{22,30},{23,31}} | collective-permute-start | bytes 393224 | tf_op jit(solution)/shard_map/ppermute | solution.py:25
  144.1 2.0 %collective-permute-start.21 = (bf16[32,2048]{1,0:T(8,128)(2,1)S(1)}, bf16[32,2048]{1,0:T(8,128)(2,1)S(1)}, u32[]{:S(2)}, u32[]{:S(2)}) collective-permute-start(bf16[32,2048]{1,0:T(8,128)(2,1)S(1)} %fusion.50.values_ref), channel_id=1, source_target_pairs={{0,1},{1,0},{2,3},{3,2},{4,5},{5,4},{6,7},{7,6},{8,9},{9,8},{10,11... | collective-permute-start | bytes 393224 | tf_op jit(solution)/shard_map/ppermute | solution.py:21
  147.6 4.7 %collective-permute-start.22 = (bf16[32,2048]{1,0:T(8,128)(2,1)S(1)}, bf16[32,2048]{1,0:T(8,128)(2,1)S(1)}, u32[]{:S(2)}, u32[]{:S(2)}) collective-permute-start(bf16[32,2048]{1,0:T(8,128)(2,1)S(1)} %shard_map.49.values_ref), channel_id=1, source_target_pairs={{0,2},{2,0},{1,3},{3,1},{4,6},{6,4},{5,7},{7,5},{8,10},{10,8},{9,1... | collective-permute-start | bytes 393224 | tf_op jit(solution)/shard_map/ppermute | solution.py:21
  153.8 8.7 %collective-permute-start.23 = (bf16[32,2048]{1,0:T(8,128)(2,1)S(1)}, bf16[32,2048]{1,0:T(8,128)(2,1)S(1)}, u32[]{:S(2)}, u32[]{:S(2)}) collective-permute-start(bf16[32,2048]{1,0:T(8,128)(2,1)S(1)} %shard_map.50.values_ref), channel_id=1, source_target_pairs={{0,4},{4,0},{1,5},{5,1},{2,6},{6,2},{3,7},{7,3},{8,12},{12,8},{9,1... | collective-permute-start | bytes 393224 | tf_op jit(solution)/shard_map/ppermute | solution.py:21
  166.6 8.1 %collective-permute-start.24 = (bf16[32,2048]{1,0:T(8,128)(2,1)S(1)}, bf16[32,2048]{1,0:T(8,128)(2,1)S(1)}, u32[]{:S(2)}, u32[]{:S(2)}) collective-permute-start(bf16[32,2048]{1,0:T(8,128)(2,1)S(1)} %shard_map.52), channel_id=1, source_target_pairs={{0,4},{4,0},{1,5},{5,1},{2,6},{6,2},{3,7},{7,3},{8,12},{12,8},{9,1... | collective-permute-start | bytes 393224 | tf_op jit(solution)/shard_map/ppermute | solution.py:21
  174.8 4.6 %collective-permute-start.25 = (bf16[32,2048]{1,0:T(8,128)(2,1)S(1)}, bf16[32,2048]{1,0:T(8,128)(2,1)S(1)}, u32[]{:S(2)}, u32[]{:S(2)}) collective-permute-start(bf16[32,2048]{1,0:T(8,128)(2,1)S(1)} %fusion.38), channel_id=1, source_target_pairs={{0,2},{2,0},{1,3},{3,1},{4,6},{6,4},{5,7},{7,5},{8,10},{10,8},{9,1... | collective-permute-start | bytes 393224 | tf_op jit(solution)/shard_map/ppermute | solution.py:21
  179.5 2.4 %collective-permute-start.26 = (bf16[32,2048]{1,0:T(8,128)(2,1)S(1)}, bf16[32,2048]{1,0:T(8,128)(2,1)S(1)}, u32[]{:S(2)}, u32[]{:S(2)}) collective-permute-start(bf16[32,2048]{1,0:T(8,128)(2,1)S(1)} %fusion.42), channel_id=1, source_target_pairs={{0,1},{1,0},{2,3},{3,2},{4,5},{5,4},{6,7},{7,6},{8,9},{9,8},{10,11... | collective-permute-start | bytes 393224 | tf_op jit(solution)/shard_map/ppermute | solution.py:21

commit v10 on v7

--- a/solution.py
+++ b/solution.py
@@ -159,14 +159,11 @@
     for bit_level in range(levels):
         partner = partner_2(values, "lat", bit_level)
         sign = level_sign(lat_index, bit_level, width)
-        if fetch:
+        if fetch and bit_level < levels - 1:
             values = fetched_dot((sign, values, partner), merge_op, True)
         else:
             values = mixed_dot(sign, values, partner, merge_op)
-    if fetch:
-        values = fetched_dot((values,), merge_op, False)
-    else:
-        values = transposed_dot(values, merge_op)
+    values = transposed_dot(values, merge_op)
     for bit_level in range(levels - 1, -1, -1):
         partner = partner_2(values, "lat", bit_level)
         values = haar_pair(values, partner, lat_index, bit_level)
@@ -180,11 +177,13 @@
     depth_count = lax.axis_size("depth")
     shot_rows = sources[0, 0]
     result = jnp.zeros_like(shot_rows)
-    incoming = jnp.zeros_like(shot_rows)
     for sweep_step in range(depth_count):
-        leaf_data = (
-            shot_rows.astype(jnp.float32) + coupling_row * incoming.astype(jnp.float32)
-        ).astype(jnp.bfloat16)
+        if sweep_step == 0:
+            leaf_data = shot_rows
+        else:
+            leaf_data = (
+                shot_rows.astype(jnp.float32) + coupling_row * incoming.astype(jnp.float32)
+            ).astype(jnp.bfloat16)
         solved = sweep_layer(leaf_data, merge_op, sweep_step == 0)
         result = jnp.where(depth_index == sweep_step, solved, result)
         if sweep_step + 1 < depth_count:

time: 185 us -> 181 us (0.978)
  Pallas kernels: 39.8 us -> 33 us
  local copies, waits for them, and re-layouts: 0.04 us -> 4.31 us
    pallas_call x4 -> x2, Pallas kernels: 18.4 us -> 7.53 us  [fetched_dot(): pl.pallas_call(functools.partial(fetched_dot_kernel, mix), out_shape=jax....]
    unnamed x8 -> x12, local copies, waits for them, and re-layouts: 0.03 us -> 4.3 us
    pallas_call x3 -> x4, Pallas kernels: 7.63 us -> 10.2 us  [transposed_dot(): pl.pallas_call(transposed_dot_kernel, out_shape=jax.ShapeDtypeStruct(valu...]
    pallas_call x9 -> x10, Pallas kernels: 13.8 us -> 15.3 us  [mixed_dot(): pl.pallas_call(mixed_dot_kernel, out_shape=jax.ShapeDtypeStruct(values.sh...]
where the time goes in v10:
time: 181 us; the launch traced here: 180 us
  waiting for transfers between devices  119 us (66%)
  Pallas kernels  33 us (18%)
  starting transfers between devices  22.4 us (12%)
  local copies, waits for them, and re-layouts  4.31 us (2%)
    ppermute x24, waiting for transfers between devices, partner_2(): return lax.ppermute(block, axis, route)  103 us
    ppermute x24, starting transfers between devices, partner_2(): return lax.ppermute(block, axis, route)  19.6 us
    ppermute x3, waiting for transfers between devices, handed_down(): return lax.ppermute(array, axis, [(layer, layer + 1)])  16.2 us
    pallas_call x10, Pallas kernels, mixed_dot(): pl.pallas_call(mixed_dot_kernel, out_shape=jax.ShapeDtypeStruct(values.sh...  15.3 us
    pallas_call x4, Pallas kernels, transposed_dot(): pl.pallas_call(transposed_dot_kernel, out_shape=jax.ShapeDtypeStruct(valu...  10.2 us
    pallas_call x2, Pallas kernels, fetched_dot(): pl.pallas_call(functools.partial(fetched_dot_kernel, mix), out_shape=jax....  7.53 us
    unnamed x12, local copies, waits for them, and re-layouts  4.3 us
  transfers between devices with their start and end apart: 27, of which 25 were waited for; matrix products, arithmetic and copies ran while one was open for 0% of the time, Pallas kernels for 0%

profile of v10, /device:TPU:7, one launch (start us, length us, event | category | flops | bytes accessed | tf_op | source)
XLA Modules:
  0.0 180.5 jit_solution(4193480940218255668)
XLA Ops:
  0.0 0.7 collective-permute-start
  0.7 1.2 collective-permute-done.refs_2_
  1.9 0.9 copy-done.1
  2.8 3.8 %shard_map.37.refs_1_ = bf16[32,2048]{1,0:T(8,128)(2,1)S(1)} custom-call(f32[1,2048]{1,0:T(1,128)S(1)} %broadcast_in_dim.12.refs_0_.sign_ref, bf16[32,2048]{1,0:T(8,128)(2,1)S(1)} %bitcast.27, bf16[32,2048]{1,0:T(8,128)(2,1)S(1)} %collective-permute-done.refs_2_, bf16[2048,2048]{1,0:T(8,128)(2,1)} %bitcast.8), custom_call_target="tpu_custom_call" | custom-call | flops 268435456 | bytes 8781824 | tf_op jit(solution)/shard_map/pallas_call | solution.py:125
  6.6 1.4 collective-permute-start.1
  7.9 3.4 %collective-permute-done.1.refs_2_ = bf16[32,2048]{1,0:T(8,128)(2,1)S(1)} collective-permute-done((bf16[32,2048]{1,0:T(8,128)(2,1)S(1)}, bf16[32,2048]{1,0:T(8,128)(2,1)S(1)}, u32[]{:S(2)}, u32[]{:S(2)}) %collective-permute-start.1) | collective-permute-done | bytes 131104 | tf_op jit(solution)/shard_map/ppermute | solution.py:21
  11.3 3.8 %shard_map.38.values_ref = bf16[32,2048]{1,0:T(8,128)(2,1)S(1)} custom-call(f32[1,2048]{1,0:T(1,128)S(1)} %broadcast_in_dim.11.refs_0_.sign_ref, bf16[32,2048]{1,0:T(8,128)(2,1)S(1)} %shard_map.37.refs_1_, bf16[32,2048]{1,0:T(8,128)(2,1)S(1)} %collective-permute-done.1.refs_2_, bf16[2048,2048]{1,0:T(8,128)(2,1)} %bitcast.9), custom_call_target="tpu_custom_call" | custom-call | flops 268435456 | bytes 8781824 | tf_op jit(solution)/shard_map/pallas_call | solution.py:125
  15.1 2.4 %collective-permute-start.2 = (bf16[32,2048]{1,0:T(8,128)(2,1)S(1)}, bf16[32,2048]{1,0:T(8,128)(2,1)S(1)}, u32[]{:S(2)}, u32[]{:S(2)}) collective-permute-start(bf16[32,2048]{1,0:T(8,128)(2,1)S(1)} %shard_map.38.values_ref), channel_id=1, source_target_pairs={{0,4},{4,0},{1,5},{5,1},{2,6},{6,2},{3,7},{7,3},{8,12},{12,8},{9,1... | collective-permute-start | bytes 393224 | tf_op jit(solution)/shard_map/ppermute | solution.py:21
  17.5 5.8 %collective-permute-done.2.partner_ref = bf16[32,2048]{1,0:T(8,128)(2,1)S(1)} collective-permute-done((bf16[32,2048]{1,0:T(8,128)(2,1)S(1)}, bf16[32,2048]{1,0:T(8,128)(2,1)S(1)}, u32[]{:S(2)}, u32[]{:S(2)}) %collective-permute-start.2) | collective-permute-done | bytes 131104 | tf_op jit(solution)/shard_map/ppermute | solution.py:21
  23.3 3.4 %copy-done = bf16[1,1,2048,2048]{3,2,1,0:T(8,128)(2,1)S(1)} copy-done((bf16[1,1,2048,2048]{3,2,1,0:T(8,128)(2,1)S(1)}, bf16[1,1,2048,2048]{3,2,1,0:T(8,128)(2,1)}, u32[]{:S(2)}) %copy-start) | copy-done | bytes 8388632
  26.7 1.5 shard_map.39.values_ref
  28.2 2.5 %shard_map.40 = bf16[32,2048]{1,0:T(8,128)(2,1)S(1)} custom-call(bf16[32,2048]{1,0:T(8,128)(2,1)S(1)} %shard_map.39.values_ref, bf16[2048,2048]{1,0:T(8,128)(2,1)S(1)} %bitcast.11), custom_call_target="tpu_custom_call" | custom-call | flops 268435456 | bytes 8781824 | tf_op jit(solution)/shard_map/pallas_call | solution.py:77
  30.8 4.7 %collective-permute-done.3 = bf16[32,2048]{1,0:T(8,128)(2,1)S(1)} collective-permute-done((bf16[32,2048]{1,0:T(8,128)(2,1)S(1)}, bf16[32,2048]{1,0:T(8,128)(2,1)S(1)}, u32[]{:S(2)}, u32[]{:S(2)}) %collective-permute-start.3) | collective-permute-done | bytes 131104 | tf_op jit(solution)/shard_map/ppermute | solution.py:21
  35.6 2.9 %collective-permute-start.4 = (bf16[32,2048]{1,0:T(8,128)(2,1)S(1)}, bf16[32,2048]{1,0:T(8,128)(2,1)S(1)}, u32[]{:S(2)}, u32[]{:S(2)}) collective-permute-start(bf16[32,2048]{1,0:T(8,128)(2,1)S(1)} %fusion.2), channel_id=1, source_target_pairs={{0,2},{2,0},{1,3},{3,1},{4,6},{6,4},{5,7},{7,5},{8,10},{10,8},{9,1... | collective-permute-start | bytes 393224 | tf_op jit(solution)/shard_map/ppermute | solution.py:21
  38.5 2.9 %collective-permute-done.4 = bf16[32,2048]{1,0:T(8,128)(2,1)S(1)} collective-permute-done((bf16[32,2048]{1,0:T(8,128)(2,1)S(1)}, bf16[32,2048]{1,0:T(8,128)(2,1)S(1)}, u32[]{:S(2)}, u32[]{:S(2)}) %collective-permute-start.4) | collective-permute-done | bytes 131104 | tf_op jit(solution)/shard_map/ppermute | solution.py:21
  41.4 0.1 fusion.6
  41.5 4.5 %collective-permute-start.5 = (bf16[32,2048]{1,0:T(8,128)(2,1)S(1)}, bf16[32,2048]{1,0:T(8,128)(2,1)S(1)}, u32[]{:S(2)}, u32[]{:S(2)}) collective-permute-start(bf16[32,2048]{1,0:T(8,128)(2,1)S(1)} %fusion.6), channel_id=1, source_target_pairs={{0,1},{1,0},{2,3},{3,2},{4,5},{5,4},{6,7},{7,6},{8,9},{9,8},{10,11... | collective-permute-start | bytes 393224 | tf_op jit(solution)/shard_map/ppermute | solution.py:21
  46.0 1.0 collective-permute-done.5
  47.0 0.7 collective-permute-start.6
  47.8 0.4 collective-permute-start.7
  48.2 1.0 collective-permute-done.7.partner_ref
  49.2 1.5 shard_map.41.values_ref
  50.8 4.7 %collective-permute-done.8.partner_ref = bf16[32,2048]{1,0:T(8,128)(2,1)S(1)} collective-permute-done((bf16[32,2048]{1,0:T(8,128)(2,1)S(1)}, bf16[32,2048]{1,0:T(8,128)(2,1)S(1)}, u32[]{:S(2)}, u32[]{:S(2)}) %collective-permute-start.8) | collective-permute-done | bytes 131104 | tf_op jit(solution)/shard_map/ppermute | solution.py:21
  55.5 1.5 shard_map.42.values_ref
  57.0 9.1 %collective-permute-done.9.partner_ref = bf16[32,2048]{1,0:T(8,128)(2,1)S(1)} collective-permute-done((bf16[32,2048]{1,0:T(8,128)(2,1)S(1)}, bf16[32,2048]{1,0:T(8,128)(2,1)S(1)}, u32[]{:S(2)}, u32[]{:S(2)}) %collective-permute-start.9) | collective-permute-done | bytes 131104 | tf_op jit(solution)/shard_map/ppermute | solution.py:21
  66.1 1.5 shard_map.43.values_ref
  67.7 2.5 %shard_map.44 = bf16[32,2048]{1,0:T(8,128)(2,1)S(1)} custom-call(bf16[32,2048]{1,0:T(8,128)(2,1)S(1)} %shard_map.43.values_ref, bf16[2048,2048]{1,0:T(8,128)(2,1)S(1)} %bitcast.17), custom_call_target="tpu_custom_call" | custom-call | flops 268435456 | bytes 8781824 | tf_op jit(solution)/shard_map/pallas_call | solution.py:77
  70.2 7.7 %collective-permute-done.10 = bf16[32,2048]{1,0:T(8,128)(2,1)S(1)} collective-permute-done((bf16[32,2048]{1,0:T(8,128)(2,1)S(1)}, bf16[32,2048]{1,0:T(8,128)(2,1)S(1)}, u32[]{:S(2)}, u32[]{:S(2)}) %collective-permute-start.10) | collective-permute-done | bytes 131104 | tf_op jit(solution)/shard_map/ppermute | solution.py:21
  77.9 0.1 collective-permute-start.11
  78.0 4.6 %collective-permute-done.11 = bf16[32,2048]{1,0:T(8,128)(2,1)S(1)} collective-permute-done((bf16[32,2048]{1,0:T(8,128)(2,1)S(1)}, bf16[32,2048]{1,0:T(8,128)(2,1)S(1)}, u32[]{:S(2)}, u32[]{:S(2)}) %collective-permute-start.11) | collective-permute-done | bytes 131104 | tf_op jit(solution)/shard_map/ppermute | solution.py:21
  82.7 1.4 collective-permute-start.12
  84.1 1.0 collective-permute-done.12
  85.1 0.8 collective-permute-start.13
  86.0 0.4 collective-permute-start.14
  86.5 1.0 collective-permute-done.14.partner_ref
  87.5 1.5 shard_map.45.values_ref
  89.0 4.7 %collective-permute-done.15.partner_ref = bf16[32,2048]{1,0:T(8,128)(2,1)S(1)} collective-permute-done((bf16[32,2048]{1,0:T(8,128)(2,1)S(1)}, bf16[32,2048]{1,0:T(8,128)(2,1)S(1)}, u32[]{:S(2)}, u32[]{:S(2)}) %collective-permute-start.15) | collective-permute-done | bytes 131104 | tf_op jit(solution)/shard_map/ppermute | solution.py:21
  93.7 1.5 shard_map.46.values_ref
  95.2 1.2 collective-permute-start.16
  96.4 7.9 %collective-permute-done.16.partner_ref = bf16[32,2048]{1,0:T(8,128)(2,1)S(1)} collective-permute-done((bf16[32,2048]{1,0:T(8,128)(2,1)S(1)}, bf16[32,2048]{1,0:T(8,128)(2,1)S(1)}, u32[]{:S(2)}, u32[]{:S(2)}) %collective-permute-start.16) | collective-permute-done | bytes 131104 | tf_op jit(solution)/shard_map/ppermute | solution.py:21
  104.4 1.5 shard_map.47.values_ref
  105.9 2.5 %shard_map.48 = bf16[32,2048]{1,0:T(8,128)(2,1)S(1)} custom-call(bf16[32,2048]{1,0:T(8,128)(2,1)S(1)} %shard_map.47.values_ref, bf16[2048,2048]{1,0:T(8,128)(2,1)S(1)} %bitcast.21), custom_call_target="tpu_custom_call" | custom-call | flops 268435456 | bytes 8781824 | tf_op jit(solution)/shard_map/pallas_call | solution.py:77
  108.5 8.7 %collective-permute-done.17 = bf16[32,2048]{1,0:T(8,128)(2,1)S(1)} collective-permute-done((bf16[32,2048]{1,0:T(8,128)(2,1)S(1)}, bf16[32,2048]{1,0:T(8,128)(2,1)S(1)}, u32[]{:S(2)}, u32[]{:S(2)}) %collective-permute-start.17) | collective-permute-done | bytes 131104 | tf_op jit(solution)/shard_map/ppermute | solution.py:21
  117.2 0.1 collective-permute-start.18
  117.3 4.6 %collective-permute-done.18 = bf16[32,2048]{1,0:T(8,128)(2,1)S(1)} collective-permute-done((bf16[32,2048]{1,0:T(8,128)(2,1)S(1)}, bf16[32,2048]{1,0:T(8,128)(2,1)S(1)}, u32[]{:S(2)}, u32[]{:S(2)}) %collective-permute-start.18) | collective-permute-done | bytes 131104 | tf_op jit(solution)/shard_map/ppermute | solution.py:21
  121.9 1.4 collective-permute-start.19
  123.3 1.0 collective-permute-done.19
  124.4 1.3 collective-permute-start.20
  125.7 16.1 %collective-permute-done.20 = bf16[32,2048]{1,0:T(8,128)(2,1)S(1)} collective-permute-done((bf16[32,2048]{1,0:T(8,128)(2,1)S(1)}, bf16[32,2048]{1,0:T(8,128)(2,1)S(1)}, u32[]{:S(2)}, u32[]{:S(2)}) %collective-permute-start.20) | collective-permute-done | bytes 131104 | tf_op jit(solution)/shard_map/ppermute | solution.py:25
  141.9 1.0 collective-permute-start.21
  142.9 1.0 collective-permute-done.21.partner_ref
  143.9 1.5 shard_map.49.values_ref
  145.4 4.7 %collective-permute-done.22.partner_ref = bf16[32,2048]{1,0:T(8,128)(2,1)S(1)} collective-permute-done((bf16[32,2048]{1,0:T(8,128)(2,1)S(1)}, bf16[32,2048]{1,0:T(8,128)(2,1)S(1)}, u32[]{:S(2)}, u32[]{:S(2)}) %collective-permute-start.22) | collective-permute-done | bytes 131104 | tf_op jit(solution)/shard_map/ppermute | solution.py:21
  150.1 1.5 shard_map.50.values_ref
  151.6 0.2 collective-permute-start.23
  151.8 8.5 %collective-permute-done.23.partner_ref = bf16[32,2048]{1,0:T(8,128)(2,1)S(1)} collective-permute-done((bf16[32,2048]{1,0:T(8,128)(2,1)S(1)}, bf16[32,2048]{1,0:T(8,128)(2,1)S(1)}, u32[]{:S(2)}, u32[]{:S(2)}) %collective-permute-start.23) | collective-permute-done | bytes 131104 | tf_op jit(solution)/shard_map/ppermute | solution.py:21
  160.3 1.5 shard_map.51.values_ref
  161.9 2.5 %shard_map.52 = bf16[32,2048]{1,0:T(8,128)(2,1)S(1)} custom-call(bf16[32,2048]{1,0:T(8,128)(2,1)S(1)} %shard_map.51.values_ref, bf16[2048,2048]{1,0:T(8,128)(2,1)S(1)} %bitcast.25), custom_call_target="tpu_custom_call" | custom-call | flops 268435456 | bytes 8781824 | tf_op jit(solution)/shard_map/pallas_call | solution.py:77
  164.4 8.1 %collective-permute-done.24 = bf16[32,2048]{1,0:T(8,128)(2,1)S(1)} collective-permute-done((bf16[32,2048]{1,0:T(8,128)(2,1)S(1)}, bf16[32,2048]{1,0:T(8,128)(2,1)S(1)}, u32[]{:S(2)}, u32[]{:S(2)}) %collective-permute-start.24) | collective-permute-done | bytes 131104 | tf_op jit(solution)/shard_map/ppermute | solution.py:21
  172.6 0.1 collective-permute-start.25
  172.7 4.5 %collective-permute-done.25 = bf16[32,2048]{1,0:T(8,128)(2,1)S(1)} collective-permute-done((bf16[32,2048]{1,0:T(8,128)(2,1)S(1)}, bf16[32,2048]{1,0:T(8,128)(2,1)S(1)}, u32[]{:S(2)}, u32[]{:S(2)}) %collective-permute-start.25) | collective-permute-done | bytes 131104 | tf_op jit(solution)/shard_map/ppermute | solution.py:21
  177.3 1.4 collective-permute-start.26
  178.7 1.0 collective-permute-done.26
  179.7 0.8 fusion.52
  (37 shorter events, 1.0 us)
Async XLA Ops:
  0.0 1.9 %collective-permute-start = (bf16[32,2048]{1,0:T(8,128)(2,1)}, bf16[32,2048]{1,0:T(8,128)(2,1)S(1)}, u32[]{:S(2)}, u32[]{:S(2)}) collective-permute-start(bf16[32,2048]{1,0:T(8,128)(2,1)} %bitcast.26), channel_id=1, source_target_pairs={{0,1},{1,0},{2,3},{3,2},{4,5},{5,4},{6,7},{7,6},{8,9},{9,8},{10,11... | collective-permute-start | bytes 393224 | tf_op jit(solution)/shard_map/ppermute | solution.py:21
  1.9 0.9 copy-start.1
  6.6 4.8 %collective-permute-start.1 = (bf16[32,2048]{1,0:T(8,128)(2,1)S(1)}, bf16[32,2048]{1,0:T(8,128)(2,1)S(1)}, u32[]{:S(2)}, u32[]{:S(2)}) collective-permute-start(bf16[32,2048]{1,0:T(8,128)(2,1)S(1)} %shard_map.37.refs_1_), channel_id=1, source_target_pairs={{0,2},{2,0},{1,3},{3,1},{4,6},{6,4},{5,7},{7,5},{8,10},{10,8},{9,1... | collective-permute-start | bytes 393224 | tf_op jit(solution)/shard_map/ppermute | solution.py:21
  15.1 8.2 %collective-permute-start.2 = (bf16[32,2048]{1,0:T(8,128)(2,1)S(1)}, bf16[32,2048]{1,0:T(8,128)(2,1)S(1)}, u32[]{:S(2)}, u32[]{:S(2)}) collective-permute-start(bf16[32,2048]{1,0:T(8,128)(2,1)S(1)} %shard_map.38.values_ref), channel_id=1, source_target_pairs={{0,4},{4,0},{1,5},{5,1},{2,6},{6,2},{3,7},{7,3},{8,12},{12,8},{9,1... | collective-permute-start | bytes 393224 | tf_op jit(solution)/shard_map/ppermute | solution.py:21
  23.3 3.4 %copy-start = (bf16[1,1,2048,2048]{3,2,1,0:T(8,128)(2,1)S(1)}, bf16[1,1,2048,2048]{3,2,1,0:T(8,128)(2,1)}, u32[]{:S(2)}) copy-start(bf16[1,1,2048,2048]{3,2,1,0:T(8,128)(2,1)} %param.5) | copy-start | bytes 25165828
  26.7 21.0 %copy-start.2 = (bf16[1,1,32,2048]{3,2,1,0:T(8,128)(2,1)S(1)}, bf16[1,1,32,2048]{3,2,1,0:T(8,128)(2,1)}, u32[]{:S(2)}) copy-start(bf16[1,1,32,2048]{3,2,1,0:T(8,128)(2,1)} %param.3) | copy-start | bytes 393220
  26.7 21.1 %copy-start.3 = (f32[1,1,2048]{2,1,0:T(1,128)S(1)}, f32[1,1,2048]{2,1,0:T(1,128)}, u32[]{:S(2)}) copy-start(f32[1,1,2048]{2,1,0:T(1,128)} %param.4) | copy-start | bytes 24580
  26.7 22.5 %slice-start = ((s8[8388608]{0:T(1024)(128)(4,1)}), s8[4194304]{0:T(1024)(128)(4,1)S(1)}, s32[]{:S(2)}) async-start(s8[8388608]{0:T(1024)(128)(4,1)} %bitcast.12), calls=%async_computation | async-start | bytes 8388608
  28.2 21.0 %slice-start.1 = ((s8[8388608]{0:T(1024)(128)(4,1)}), s8[4194304]{0:T(1024)(128)(4,1)S(1)}, s32[]{:S(2)}) async-start(s8[8388608]{0:T(1024)(128)(4,1)} %bitcast.12), calls=%async_computation.1 | async-start | bytes 8388608
  30.7 4.7 %collective-permute-start.3 = (bf16[32,2048]{1,0:T(8,128)(2,1)S(1)}, bf16[32,2048]{1,0:T(8,128)(2,1)S(1)}, u32[]{:S(2)}, u32[]{:S(2)}) collective-permute-start(bf16[32,2048]{1,0:T(8,128)(2,1)S(1)} %shard_map.40), channel_id=1, source_target_pairs={{0,4},{4,0},{1,5},{5,1},{2,6},{6,2},{3,7},{7,3},{8,12},{12,8},{9,1... | collective-permute-start | bytes 393224 | tf_op jit(solution)/shard_map/ppermute | solution.py:21
  35.6 5.8 %collective-permute-start.4 = (bf16[32,2048]{1,0:T(8,128)(2,1)S(1)}, bf16[32,2048]{1,0:T(8,128)(2,1)S(1)}, u32[]{:S(2)}, u32[]{:S(2)}) collective-permute-start(bf16[32,2048]{1,0:T(8,128)(2,1)S(1)} %fusion.2), channel_id=1, source_target_pairs={{0,2},{2,0},{1,3},{3,1},{4,6},{6,4},{5,7},{7,5},{8,10},{10,8},{9,1... | collective-permute-start | bytes 393224 | tf_op jit(solution)/shard_map/ppermute | solution.py:21
  41.5 5.5 %collective-permute-start.5 = (bf16[32,2048]{1,0:T(8,128)(2,1)S(1)}, bf16[32,2048]{1,0:T(8,128)(2,1)S(1)}, u32[]{:S(2)}, u32[]{:S(2)}) collective-permute-start(bf16[32,2048]{1,0:T(8,128)(2,1)S(1)} %fusion.6), channel_id=1, source_target_pairs={{0,1},{1,0},{2,3},{3,2},{4,5},{5,4},{6,7},{7,6},{8,9},{9,8},{10,11... | collective-permute-start | bytes 393224 | tf_op jit(solution)/shard_map/ppermute | solution.py:21
  47.0 0.7 collective-permute-start.6
  47.8 1.4 collective-permute-start.7
  50.7 4.7 %collective-permute-start.8 = (bf16[32,2048]{1,0:T(8,128)(2,1)S(1)}, bf16[32,2048]{1,0:T(8,128)(2,1)S(1)}, u32[]{:S(2)}, u32[]{:S(2)}) collective-permute-start(bf16[32,2048]{1,0:T(8,128)(2,1)S(1)} %shard_map.41.values_ref), channel_id=1, source_target_pairs={{0,2},{2,0},{1,3},{3,1},{4,6},{6,4},{5,7},{7,5},{8,10},{10,8},{9,1... | collective-permute-start | bytes 393224 | tf_op jit(solution)/shard_map/ppermute | solution.py:21
  57.0 9.1 %collective-permute-start.9 = (bf16[32,2048]{1,0:T(8,128)(2,1)S(1)}, bf16[32,2048]{1,0:T(8,128)(2,1)S(1)}, u32[]{:S(2)}, u32[]{:S(2)}) collective-permute-start(bf16[32,2048]{1,0:T(8,128)(2,1)S(1)} %shard_map.42.values_ref), channel_id=1, source_target_pairs={{0,4},{4,0},{1,5},{5,1},{2,6},{6,2},{3,7},{7,3},{8,12},{12,8},{9,1... | collective-permute-start | bytes 393224 | tf_op jit(solution)/shard_map/ppermute | solution.py:21
  70.2 7.7 %collective-permute-start.10 = (bf16[32,2048]{1,0:T(8,128)(2,1)S(1)}, bf16[32,2048]{1,0:T(8,128)(2,1)S(1)}, u32[]{:S(2)}, u32[]{:S(2)}) collective-permute-start(bf16[32,2048]{1,0:T(8,128)(2,1)S(1)} %shard_map.44), channel_id=1, source_target_pairs={{0,4},{4,0},{1,5},{5,1},{2,6},{6,2},{3,7},{7,3},{8,12},{12,8},{9,1... | collective-permute-start | bytes 393224 | tf_op jit(solution)/shard_map/ppermute | solution.py:21
  77.9 4.6 %collective-permute-start.11 = (bf16[32,2048]{1,0:T(8,128)(2,1)S(1)}, bf16[32,2048]{1,0:T(8,128)(2,1)S(1)}, u32[]{:S(2)}, u32[]{:S(2)}) collective-permute-start(bf16[32,2048]{1,0:T(8,128)(2,1)S(1)} %fusion.14), channel_id=1, source_target_pairs={{0,2},{2,0},{1,3},{3,1},{4,6},{6,4},{5,7},{7,5},{8,10},{10,8},{9,1... | collective-permute-start | bytes 393224 | tf_op jit(solution)/shard_map/ppermute | solution.py:21
  82.7 2.4 %collective-permute-start.12 = (bf16[32,2048]{1,0:T(8,128)(2,1)S(1)}, bf16[32,2048]{1,0:T(8,128)(2,1)S(1)}, u32[]{:S(2)}, u32[]{:S(2)}) collective-permute-start(bf16[32,2048]{1,0:T(8,128)(2,1)S(1)} %fusion.18), channel_id=1, source_target_pairs={{0,1},{1,0},{2,3},{3,2},{4,5},{5,4},{6,7},{7,6},{8,9},{9,8},{10,11... | collective-permute-start | bytes 393224 | tf_op jit(solution)/shard_map/ppermute | solution.py:21
  85.1 0.9 collective-permute-start.13
  86.0 1.4 collective-permute-start.14
  89.0 4.7 %collective-permute-start.15 = (bf16[32,2048]{1,0:T(8,128)(2,1)S(1)}, bf16[32,2048]{1,0:T(8,128)(2,1)S(1)}, u32[]{:S(2)}, u32[]{:S(2)}) collective-permute-start(bf16[32,2048]{1,0:T(8,128)(2,1)S(1)} %shard_map.45.values_ref), channel_id=1, source_target_pairs={{0,2},{2,0},{1,3},{3,1},{4,6},{6,4},{5,7},{7,5},{8,10},{10,8},{9,1... | collective-permute-start | bytes 393224 | tf_op jit(solution)/shard_map/ppermute | solution.py:21
  95.2 9.1 %collective-permute-start.16 = (bf16[32,2048]{1,0:T(8,128)(2,1)S(1)}, bf16[32,2048]{1,0:T(8,128)(2,1)S(1)}, u32[]{:S(2)}, u32[]{:S(2)}) collective-permute-start(bf16[32,2048]{1,0:T(8,128)(2,1)S(1)} %shard_map.46.values_ref), channel_id=1, source_target_pairs={{0,4},{4,0},{1,5},{5,1},{2,6},{6,2},{3,7},{7,3},{8,12},{12,8},{9,1... | collective-permute-start | bytes 393224 | tf_op jit(solution)/shard_map/ppermute | solution.py:21
  108.4 8.7 %collective-permute-start.17 = (bf16[32,2048]{1,0:T(8,128)(2,1)S(1)}, bf16[32,2048]{1,0:T(8,128)(2,1)S(1)}, u32[]{:S(2)}, u32[]{:S(2)}) collective-permute-start(bf16[32,2048]{1,0:T(8,128)(2,1)S(1)} %shard_map.48), channel_id=1, source_target_pairs={{0,4},{4,0},{1,5},{5,1},{2,6},{6,2},{3,7},{7,3},{8,12},{12,8},{9,1... | collective-permute-start | bytes 393224 | tf_op jit(solution)/shard_map/ppermute | solution.py:21
  117.2 4.6 %collective-permute-start.18 = (bf16[32,2048]{1,0:T(8,128)(2,1)S(1)}, bf16[32,2048]{1,0:T(8,128)(2,1)S(1)}, u32[]{:S(2)}, u32[]{:S(2)}) collective-permute-start(bf16[32,2048]{1,0:T(8,128)(2,1)S(1)} %fusion.26), channel_id=1, source_target_pairs={{0,2},{2,0},{1,3},{3,1},{4,6},{6,4},{5,7},{7,5},{8,10},{10,8},{9,1... | collective-permute-start | bytes 393224 | tf_op jit(solution)/shard_map/ppermute | solution.py:21
  121.9 2.4 %collective-permute-start.19 = (bf16[32,2048]{1,0:T(8,128)(2,1)S(1)}, bf16[32,2048]{1,0:T(8,128)(2,1)S(1)}, u32[]{:S(2)}, u32[]{:S(2)}) collective-permute-start(bf16[32,2048]{1,0:T(8,128)(2,1)S(1)} %fusion.30), channel_id=1, source_target_pairs={{0,1},{1,0},{2,3},{3,2},{4,5},{5,4},{6,7},{7,6},{8,9},{9,8},{10,11... | collective-permute-start | bytes 393224 | tf_op jit(solution)/shard_map/ppermute | solution.py:21
  124.4 17.4 %collective-permute-start.20 = (bf16[32,2048]{1,0:T(8,128)(2,1)S(1)}, bf16[32,2048]{1,0:T(8,128)(2,1)S(1)}, u32[]{:S(2)}, u32[]{:S(2)}) collective-permute-start(bf16[32,2048]{1,0:T(8,128)(2,1)S(1)} %fusion.34), channel_id=1, source_target_pairs={{16,24},{17,25},{18,26},{19,27},{20,28},{21,29},{22,30},{23,31}} | collective-permute-start | bytes 393224 | tf_op jit(solution)/shard_map/ppermute | solution.py:25
  141.9 2.0 %collective-permute-start.21 = (bf16[32,2048]{1,0:T(8,128)(2,1)S(1)}, bf16[32,2048]{1,0:T(8,128)(2,1)S(1)}, u32[]{:S(2)}, u32[]{:S(2)}) collective-permute-start(bf16[32,2048]{1,0:T(8,128)(2,1)S(1)} %fusion.50.values_ref), channel_id=1, source_target_pairs={{0,1},{1,0},{2,3},{3,2},{4,5},{5,4},{6,7},{7,6},{8,9},{9,8},{10,11... | collective-permute-start | bytes 393224 | tf_op jit(solution)/shard_map/ppermute | solution.py:21
  145.4 4.7 %collective-permute-start.22 = (bf16[32,2048]{1,0:T(8,128)(2,1)S(1)}, bf16[32,2048]{1,0:T(8,128)(2,1)S(1)}, u32[]{:S(2)}, u32[]{:S(2)}) collective-permute-start(bf16[32,2048]{1,0:T(8,128)(2,1)S(1)} %shard_map.49.values_ref), channel_id=1, source_target_pairs={{0,2},{2,0},{1,3},{3,1},{4,6},{6,4},{5,7},{7,5},{8,10},{10,8},{9,1... | collective-permute-start | bytes 393224 | tf_op jit(solution)/shard_map/ppermute | solution.py:21
  151.6 8.7 %collective-permute-start.23 = (bf16[32,2048]{1,0:T(8,128)(2,1)S(1)}, bf16[32,2048]{1,0:T(8,128)(2,1)S(1)}, u32[]{:S(2)}, u32[]{:S(2)}) collective-permute-start(bf16[32,2048]{1,0:T(8,128)(2,1)S(1)} %shard_map.50.values_ref), channel_id=1, source_target_pairs={{0,4},{4,0},{1,5},{5,1},{2,6},{6,2},{3,7},{7,3},{8,12},{12,8},{9,1... | collective-permute-start | bytes 393224 | tf_op jit(solution)/shard_map/ppermute | solution.py:21
  164.4 8.1 %collective-permute-start.24 = (bf16[32,2048]{1,0:T(8,128)(2,1)S(1)}, bf16[32,2048]{1,0:T(8,128)(2,1)S(1)}, u32[]{:S(2)}, u32[]{:S(2)}) collective-permute-start(bf16[32,2048]{1,0:T(8,128)(2,1)S(1)} %shard_map.52), channel_id=1, source_target_pairs={{0,4},{4,0},{1,5},{5,1},{2,6},{6,2},{3,7},{7,3},{8,12},{12,8},{9,1... | collective-permute-start | bytes 393224 | tf_op jit(solution)/shard_map/ppermute | solution.py:21
  172.6 4.6 %collective-permute-start.25 = (bf16[32,2048]{1,0:T(8,128)(2,1)S(1)}, bf16[32,2048]{1,0:T(8,128)(2,1)S(1)}, u32[]{:S(2)}, u32[]{:S(2)}) collective-permute-start(bf16[32,2048]{1,0:T(8,128)(2,1)S(1)} %fusion.38), channel_id=1, source_target_pairs={{0,2},{2,0},{1,3},{3,1},{4,6},{6,4},{5,7},{7,5},{8,10},{10,8},{9,1... | collective-permute-start | bytes 393224 | tf_op jit(solution)/shard_map/ppermute | solution.py:21
  177.3 2.4 %collective-permute-start.26 = (bf16[32,2048]{1,0:T(8,128)(2,1)S(1)}, bf16[32,2048]{1,0:T(8,128)(2,1)S(1)}, u32[]{:S(2)}, u32[]{:S(2)}) collective-permute-start(bf16[32,2048]{1,0:T(8,128)(2,1)S(1)} %fusion.42), channel_id=1, source_target_pairs={{0,1},{1,0},{2,3},{3,2},{4,5},{5,4},{6,7},{7,6},{8,9},{9,8},{10,11... | collective-permute-start | bytes 393224 | tf_op jit(solution)/shard_map/ppermute | solution.py:21

commit v11 on v9

--- a/solution.py
+++ b/solution.py
@@ -84,6 +84,57 @@
     )(values, pltpu.with_memory_space_constraint(merge_op, pltpu.VMEM))
 
 
+CHUNK = 256
+
+
+def fetched_dot_kernel(values_in_hbm, sign_ref, values_ref, partner_ref, op_hbm_ref, out_ref, op_ref, own_ref, sems):
+    width = op_ref.shape[0]
+    blocks = width // CHUNK
+    if values_in_hbm:
+        own_copy = pltpu.make_async_copy(values_ref, own_ref, sems.at[blocks])
+        own_copy.start()
+    copies = []
+    for index in range(blocks):
+        rows = pl.ds(index * CHUNK, CHUNK)
+        copy = pltpu.make_async_copy(op_hbm_ref.at[rows, :], op_ref.at[rows, :], sems.at[index])
+        copy.start()
+        copies.append(copy)
+    if values_in_hbm:
+        own_copy.wait()
+        first = own_ref[...].astype(jnp.float32)
+    else:
+        first = values_ref[...].astype(jnp.float32)
+    second = partner_ref[...].astype(jnp.float32)
+    mixed = ((second + sign_ref[...] * first) * half_root).astype(jnp.bfloat16)
+    total = jnp.zeros(out_ref.shape, jnp.float32)
+    for index, copy in enumerate(copies):
+        copy.wait()
+        rows = slice(index * CHUNK, (index + 1) * CHUNK)
+        total = total + jnp.dot(mixed[:, rows], op_ref[rows, :], preferred_element_type=jnp.float32)
+    out_ref[...] = total.astype(out_ref.dtype)
+
+
+def fetched_dot(sign, values, partner, merge_op, values_in_hbm):
+    rows, width = values.shape
+    if values_in_hbm:
+        values_spec = pl.BlockSpec(memory_space=pl.ANY)
+        values = pltpu.with_memory_space_constraint(values, pltpu.HBM)
+    else:
+        values_spec = vmem_spec()
+    return pl.pallas_call(
+        functools.partial(fetched_dot_kernel, values_in_hbm),
+        out_shape=jax.ShapeDtypeStruct(values.shape, jnp.bfloat16),
+        in_specs=[vmem_spec(), values_spec, vmem_spec(), pl.BlockSpec(memory_space=pl.ANY)],
+        out_specs=vmem_spec(),
+        scratch_shapes=[
+            pltpu.VMEM(merge_op.shape, merge_op.dtype),
+            pltpu.VMEM(values.shape, values.dtype),
+            pltpu.SemaphoreType.DMA((width // CHUNK + 1,)),
+        ],
+        cost_estimate=cost(rows, width),
+        compiler_params=pltpu.CompilerParams(vmem_limit_bytes=16 * 1024 * 1024),
+    )(sign, values, partner, pltpu.with_memory_space_constraint(merge_op, pltpu.HBM))
+
 def haar_pair(values, partner, lat_index, bit_level):
     is_lower = lat_index // 2**bit_level % 2 == 0
     first = values.astype(jnp.float32)
@@ -98,7 +149,7 @@
     return jnp.full((1, width), jnp.where(is_lower, 1.0, -1.0), jnp.float32)
 
 
-def sweep_layer(leaf_data, merge_op):
+def sweep_layer(leaf_data, merge_op, fetch):
     lat_count = lax.axis_size("lat")
     lat_index = lax.axis_index("lat")
     levels = lat_count.bit_length() - 1
@@ -106,7 +157,11 @@
     values = leaf_data
     for bit_level in range(levels):
         partner = partner_2(values, "lat", bit_level)
-        values = mixed_dot(level_sign(lat_index, bit_level, width), values, partner, merge_op)
+        sign = level_sign(lat_index, bit_level, width)
+        if fetch and bit_level < levels - 1:
+            values = fetched_dot(sign, values, partner, merge_op, bit_level == 0)
+        else:
+            values = mixed_dot(sign, values, partner, merge_op)
     values = transposed_dot(values, merge_op)
     for bit_level in range(levels - 1, -1, -1):
         partner = partner_2(values, "lat", bit_level)
@@ -128,7 +183,7 @@
             leaf_data = (
                 shot_rows.astype(jnp.float32) + coupling_row * incoming.astype(jnp.float32)
             ).astype(jnp.bfloat16)
-        solved = sweep_layer(leaf_data, merge_op)
+        solved = sweep_layer(leaf_data, merge_op, sweep_step == 0)
         result = jnp.where(depth_index == sweep_step, solved, result)
         if sweep_step + 1 < depth_count:
             incoming = handed_down(solved, "depth", sweep_step)

time: 183 us -> 180 us (0.984)
  local copies, waits for them, and re-layouts: 11.1 us -> 3.41 us
  Pallas kernels: 28.5 us -> 33.1 us
    unnamed x16 -> x10, local copies, waits for them, and re-layouts: 11.1 us -> 3.39 us
    pallas_call x0 -> x2, Pallas kernels: none -> 7.62 us  [fetched_dot(): pl.pallas_call(functools.partial(fetched_dot_kernel, values_in_hbm), out_...]
    pallas_call x12 -> x10, Pallas kernels: 18.4 us -> 15.3 us  [mixed_dot(): pl.pallas_call(mixed_dot_kernel, out_shape=jax.ShapeDtypeStruct(values.sh...]
where the time goes in v11:
time: 180 us
  waiting for transfers between devices  119 us (66%)
  Pallas kernels  33.1 us (18%)
  starting transfers between devices  22.4 us (12%)
  local copies, waits for them, and re-layouts  3.41 us (2%)
    ppermute x24, waiting for transfers between devices, partner_2(): return lax.ppermute(block, axis, route)  103 us
    ppermute x24, starting transfers between devices, partner_2(): return lax.ppermute(block, axis, route)  19.6 us
    ppermute x3, waiting for transfers between devices, handed_down(): return lax.ppermute(array, axis, [(layer, layer + 1)])  16.2 us
    pallas_call x10, Pallas kernels, mixed_dot(): pl.pallas_call(mixed_dot_kernel, out_shape=jax.ShapeDtypeStruct(values.sh...  15.3 us
    pallas_call x4, Pallas kernels, transposed_dot(): pl.pallas_call(transposed_dot_kernel, out_shape=jax.ShapeDtypeStruct(valu...  10.2 us
    pallas_call x2, Pallas kernels, fetched_dot(): pl.pallas_call(functools.partial(fetched_dot_kernel, values_in_hbm), out_...  7.62 us
  transfers between devices with their start and end apart: 27, of which 25 were waited for; matrix products, arithmetic and copies ran while one was open for 0% of the time, Pallas kernels for 0%

profile of v11, /device:TPU:7, one launch (start us, length us, event | category | flops | bytes accessed | tf_op | source)
XLA Modules:
  0.0 179.7 jit_solution(14366896404761300197)
XLA Ops:
  0.0 0.7 collective-permute-start
  0.7 1.2 collective-permute-done.partner_ref
  1.9 3.8 %shard_map.37.values_ref = bf16[32,2048]{1,0:T(8,128)(2,1)S(1)} custom-call(f32[1,2048]{1,0:T(1,128)S(1)} %broadcast_in_dim.12.sign_ref, bf16[32,2048]{1,0:T(8,128)(2,1)} %bitcast.27, bf16[32,2048]{1,0:T(8,128)(2,1)S(1)} %collective-permute-done.partner_ref, bf16[2048,2048]{1,0:T(8,128)(2,1)} %bitcast.8), custom_call_target="tpu_custom_call" | custom-call | flops 268435456 | bytes 8781824 | tf_op jit(solution)/shard_map/pallas_call | solution.py:124
  5.7 1.4 collective-permute-start.1
  7.1 3.4 %collective-permute-done.1.partner_ref = bf16[32,2048]{1,0:T(8,128)(2,1)S(1)} collective-permute-done((bf16[32,2048]{1,0:T(8,128)(2,1)S(1)}, bf16[32,2048]{1,0:T(8,128)(2,1)S(1)}, u32[]{:S(2)}, u32[]{:S(2)}) %collective-permute-start.1) | collective-permute-done | bytes 131104 | tf_op jit(solution)/shard_map/ppermute | solution.py:21
  10.5 3.8 %shard_map.38.values_ref = bf16[32,2048]{1,0:T(8,128)(2,1)S(1)} custom-call(f32[1,2048]{1,0:T(1,128)S(1)} %broadcast_in_dim.11.sign_ref, bf16[32,2048]{1,0:T(8,128)(2,1)S(1)} %shard_map.37.values_ref, bf16[32,2048]{1,0:T(8,128)(2,1)S(1)} %collective-permute-done.1.partner_ref, bf16[2048,2048]{1,0:T(8,128)(2,1)} %bitcast.9), custom_call_target="tpu_custom_call" | custom-call | flops 268435456 | bytes 8781824 | tf_op jit(solution)/shard_map/pallas_call | solution.py:124
  14.3 2.4 %collective-permute-start.2 = (bf16[32,2048]{1,0:T(8,128)(2,1)S(1)}, bf16[32,2048]{1,0:T(8,128)(2,1)S(1)}, u32[]{:S(2)}, u32[]{:S(2)}) collective-permute-start(bf16[32,2048]{1,0:T(8,128)(2,1)S(1)} %shard_map.38.values_ref), channel_id=1, source_target_pairs={{0,4},{4,0},{1,5},{5,1},{2,6},{6,2},{3,7},{7,3},{8,12},{12,8},{9,1... | collective-permute-start | bytes 393224 | tf_op jit(solution)/shard_map/ppermute | solution.py:21
  16.7 5.8 %collective-permute-done.2.partner_ref = bf16[32,2048]{1,0:T(8,128)(2,1)S(1)} collective-permute-done((bf16[32,2048]{1,0:T(8,128)(2,1)S(1)}, bf16[32,2048]{1,0:T(8,128)(2,1)S(1)}, u32[]{:S(2)}, u32[]{:S(2)}) %collective-permute-start.2) | collective-permute-done | bytes 131104 | tf_op jit(solution)/shard_map/ppermute | solution.py:21
  22.5 3.4 %copy-done = bf16[1,1,2048,2048]{3,2,1,0:T(8,128)(2,1)S(1)} copy-done((bf16[1,1,2048,2048]{3,2,1,0:T(8,128)(2,1)S(1)}, bf16[1,1,2048,2048]{3,2,1,0:T(8,128)(2,1)}, u32[]{:S(2)}) %copy-start) | copy-done | bytes 8388632
  25.9 1.5 shard_map.39.values_ref
  27.4 2.5 %shard_map.40 = bf16[32,2048]{1,0:T(8,128)(2,1)S(1)} custom-call(bf16[32,2048]{1,0:T(8,128)(2,1)S(1)} %shard_map.39.values_ref, bf16[2048,2048]{1,0:T(8,128)(2,1)S(1)} %bitcast.11), custom_call_target="tpu_custom_call" | custom-call | flops 268435456 | bytes 8781824 | tf_op jit(solution)/shard_map/pallas_call | solution.py:77
  30.0 4.7 %collective-permute-done.3 = bf16[32,2048]{1,0:T(8,128)(2,1)S(1)} collective-permute-done((bf16[32,2048]{1,0:T(8,128)(2,1)S(1)}, bf16[32,2048]{1,0:T(8,128)(2,1)S(1)}, u32[]{:S(2)}, u32[]{:S(2)}) %collective-permute-start.3) | collective-permute-done | bytes 131104 | tf_op jit(solution)/shard_map/ppermute | solution.py:21
  34.7 2.9 %collective-permute-start.4 = (bf16[32,2048]{1,0:T(8,128)(2,1)S(1)}, bf16[32,2048]{1,0:T(8,128)(2,1)S(1)}, u32[]{:S(2)}, u32[]{:S(2)}) collective-permute-start(bf16[32,2048]{1,0:T(8,128)(2,1)S(1)} %fusion.2), channel_id=1, source_target_pairs={{0,2},{2,0},{1,3},{3,1},{4,6},{6,4},{5,7},{7,5},{8,10},{10,8},{9,1... | collective-permute-start | bytes 393224 | tf_op jit(solution)/shard_map/ppermute | solution.py:21
  37.6 2.9 %collective-permute-done.4 = bf16[32,2048]{1,0:T(8,128)(2,1)S(1)} collective-permute-done((bf16[32,2048]{1,0:T(8,128)(2,1)S(1)}, bf16[32,2048]{1,0:T(8,128)(2,1)S(1)}, u32[]{:S(2)}, u32[]{:S(2)}) %collective-permute-start.4) | collective-permute-done | bytes 131104 | tf_op jit(solution)/shard_map/ppermute | solution.py:21
  40.6 4.5 %collective-permute-start.5 = (bf16[32,2048]{1,0:T(8,128)(2,1)S(1)}, bf16[32,2048]{1,0:T(8,128)(2,1)S(1)}, u32[]{:S(2)}, u32[]{:S(2)}) collective-permute-start(bf16[32,2048]{1,0:T(8,128)(2,1)S(1)} %fusion.6), channel_id=1, source_target_pairs={{0,1},{1,0},{2,3},{3,2},{4,5},{5,4},{6,7},{7,6},{8,9},{9,8},{10,11... | collective-permute-start | bytes 393224 | tf_op jit(solution)/shard_map/ppermute | solution.py:21
  45.1 1.0 collective-permute-done.5
  46.2 0.7 collective-permute-start.6
  47.0 0.4 collective-permute-start.7
  47.4 1.0 collective-permute-done.7.partner_ref
  48.4 1.5 shard_map.41.values_ref
  49.9 4.7 %collective-permute-done.8.partner_ref = bf16[32,2048]{1,0:T(8,128)(2,1)S(1)} collective-permute-done((bf16[32,2048]{1,0:T(8,128)(2,1)S(1)}, bf16[32,2048]{1,0:T(8,128)(2,1)S(1)}, u32[]{:S(2)}, u32[]{:S(2)}) %collective-permute-start.8) | collective-permute-done | bytes 131104 | tf_op jit(solution)/shard_map/ppermute | solution.py:21
  54.6 1.5 shard_map.42.values_ref
  56.2 9.1 %collective-permute-done.9.partner_ref = bf16[32,2048]{1,0:T(8,128)(2,1)S(1)} collective-permute-done((bf16[32,2048]{1,0:T(8,128)(2,1)S(1)}, bf16[32,2048]{1,0:T(8,128)(2,1)S(1)}, u32[]{:S(2)}, u32[]{:S(2)}) %collective-permute-start.9) | collective-permute-done | bytes 131104 | tf_op jit(solution)/shard_map/ppermute | solution.py:21
  65.3 1.5 shard_map.43.values_ref
  66.8 2.5 %shard_map.44 = bf16[32,2048]{1,0:T(8,128)(2,1)S(1)} custom-call(bf16[32,2048]{1,0:T(8,128)(2,1)S(1)} %shard_map.43.values_ref, bf16[2048,2048]{1,0:T(8,128)(2,1)S(1)} %bitcast.17), custom_call_target="tpu_custom_call" | custom-call | flops 268435456 | bytes 8781824 | tf_op jit(solution)/shard_map/pallas_call | solution.py:77
  69.4 7.7 %collective-permute-done.10 = bf16[32,2048]{1,0:T(8,128)(2,1)S(1)} collective-permute-done((bf16[32,2048]{1,0:T(8,128)(2,1)S(1)}, bf16[32,2048]{1,0:T(8,128)(2,1)S(1)}, u32[]{:S(2)}, u32[]{:S(2)}) %collective-permute-start.10) | collective-permute-done | bytes 131104 | tf_op jit(solution)/shard_map/ppermute | solution.py:21
  77.1 0.1 collective-permute-start.11
  77.2 4.6 %collective-permute-done.11 = bf16[32,2048]{1,0:T(8,128)(2,1)S(1)} collective-permute-done((bf16[32,2048]{1,0:T(8,128)(2,1)S(1)}, bf16[32,2048]{1,0:T(8,128)(2,1)S(1)}, u32[]{:S(2)}, u32[]{:S(2)}) %collective-permute-start.11) | collective-permute-done | bytes 131104 | tf_op jit(solution)/shard_map/ppermute | solution.py:21
  81.8 1.4 collective-permute-start.12
  83.2 1.0 collective-permute-done.12
  84.3 0.8 collective-permute-start.13
  85.2 0.4 collective-permute-start.14
  85.6 1.0 collective-permute-done.14.partner_ref
  86.6 1.5 shard_map.45.values_ref
  88.2 4.7 %collective-permute-done.15.partner_ref = bf16[32,2048]{1,0:T(8,128)(2,1)S(1)} collective-permute-done((bf16[32,2048]{1,0:T(8,128)(2,1)S(1)}, bf16[32,2048]{1,0:T(8,128)(2,1)S(1)}, u32[]{:S(2)}, u32[]{:S(2)}) %collective-permute-start.15) | collective-permute-done | bytes 131104 | tf_op jit(solution)/shard_map/ppermute | solution.py:21
  92.9 1.5 shard_map.46.values_ref
  94.4 1.2 collective-permute-start.16
  95.6 7.9 %collective-permute-done.16.partner_ref = bf16[32,2048]{1,0:T(8,128)(2,1)S(1)} collective-permute-done((bf16[32,2048]{1,0:T(8,128)(2,1)S(1)}, bf16[32,2048]{1,0:T(8,128)(2,1)S(1)}, u32[]{:S(2)}, u32[]{:S(2)}) %collective-permute-start.16) | collective-permute-done | bytes 131104 | tf_op jit(solution)/shard_map/ppermute | solution.py:21
  103.5 1.5 shard_map.47.values_ref
  105.1 2.5 %shard_map.48 = bf16[32,2048]{1,0:T(8,128)(2,1)S(1)} custom-call(bf16[32,2048]{1,0:T(8,128)(2,1)S(1)} %shard_map.47.values_ref, bf16[2048,2048]{1,0:T(8,128)(2,1)S(1)} %bitcast.21), custom_call_target="tpu_custom_call" | custom-call | flops 268435456 | bytes 8781824 | tf_op jit(solution)/shard_map/pallas_call | solution.py:77
  107.6 8.7 %collective-permute-done.17 = bf16[32,2048]{1,0:T(8,128)(2,1)S(1)} collective-permute-done((bf16[32,2048]{1,0:T(8,128)(2,1)S(1)}, bf16[32,2048]{1,0:T(8,128)(2,1)S(1)}, u32[]{:S(2)}, u32[]{:S(2)}) %collective-permute-start.17) | collective-permute-done | bytes 131104 | tf_op jit(solution)/shard_map/ppermute | solution.py:21
  116.3 0.1 fusion.26
  116.4 0.1 collective-permute-start.18
  116.5 4.6 %collective-permute-done.18 = bf16[32,2048]{1,0:T(8,128)(2,1)S(1)} collective-permute-done((bf16[32,2048]{1,0:T(8,128)(2,1)S(1)}, bf16[32,2048]{1,0:T(8,128)(2,1)S(1)}, u32[]{:S(2)}, u32[]{:S(2)}) %collective-permute-start.18) | collective-permute-done | bytes 131104 | tf_op jit(solution)/shard_map/ppermute | solution.py:21
  121.1 1.4 collective-permute-start.19
  122.5 1.0 collective-permute-done.19
  123.5 0.1 fusion.34
  123.6 1.3 collective-permute-start.20
  124.9 16.1 %collective-permute-done.20 = bf16[32,2048]{1,0:T(8,128)(2,1)S(1)} collective-permute-done((bf16[32,2048]{1,0:T(8,128)(2,1)S(1)}, bf16[32,2048]{1,0:T(8,128)(2,1)S(1)}, u32[]{:S(2)}, u32[]{:S(2)}) %collective-permute-start.20) | collective-permute-done | bytes 131104 | tf_op jit(solution)/shard_map/ppermute | solution.py:25
  141.1 1.0 collective-permute-start.21
  142.1 1.0 collective-permute-done.21.partner_ref
  143.0 1.5 shard_map.49.values_ref
  144.6 4.7 %collective-permute-done.22.partner_ref = bf16[32,2048]{1,0:T(8,128)(2,1)S(1)} collective-permute-done((bf16[32,2048]{1,0:T(8,128)(2,1)S(1)}, bf16[32,2048]{1,0:T(8,128)(2,1)S(1)}, u32[]{:S(2)}, u32[]{:S(2)}) %collective-permute-start.22) | collective-permute-done | bytes 131104 | tf_op jit(solution)/shard_map/ppermute | solution.py:21
  149.3 1.5 shard_map.50.values_ref
  150.8 0.2 collective-permute-start.23
  151.0 8.5 %collective-permute-done.23.partner_ref = bf16[32,2048]{1,0:T(8,128)(2,1)S(1)} collective-permute-done((bf16[32,2048]{1,0:T(8,128)(2,1)S(1)}, bf16[32,2048]{1,0:T(8,128)(2,1)S(1)}, u32[]{:S(2)}, u32[]{:S(2)}) %collective-permute-start.23) | collective-permute-done | bytes 131104 | tf_op jit(solution)/shard_map/ppermute | solution.py:21
  159.5 1.5 shard_map.51.values_ref
  161.0 2.5 %shard_map.52 = bf16[32,2048]{1,0:T(8,128)(2,1)S(1)} custom-call(bf16[32,2048]{1,0:T(8,128)(2,1)S(1)} %shard_map.51.values_ref, bf16[2048,2048]{1,0:T(8,128)(2,1)S(1)} %bitcast.25), custom_call_target="tpu_custom_call" | custom-call | flops 268435456 | bytes 8781824 | tf_op jit(solution)/shard_map/pallas_call | solution.py:77
  163.6 8.1 %collective-permute-done.24 = bf16[32,2048]{1,0:T(8,128)(2,1)S(1)} collective-permute-done((bf16[32,2048]{1,0:T(8,128)(2,1)S(1)}, bf16[32,2048]{1,0:T(8,128)(2,1)S(1)}, u32[]{:S(2)}, u32[]{:S(2)}) %collective-permute-start.24) | collective-permute-done | bytes 131104 | tf_op jit(solution)/shard_map/ppermute | solution.py:21
  171.8 0.1 collective-permute-start.25
  171.9 4.5 %collective-permute-done.25 = bf16[32,2048]{1,0:T(8,128)(2,1)S(1)} collective-permute-done((bf16[32,2048]{1,0:T(8,128)(2,1)S(1)}, bf16[32,2048]{1,0:T(8,128)(2,1)S(1)}, u32[]{:S(2)}, u32[]{:S(2)}) %collective-permute-start.25) | collective-permute-done | bytes 131104 | tf_op jit(solution)/shard_map/ppermute | solution.py:21
  176.5 1.4 collective-permute-start.26
  177.9 1.0 collective-permute-done.26
  178.9 0.8 fusion.52
  (35 shorter events, 0.9 us)
Async XLA Ops:
  0.0 1.9 %collective-permute-start = (bf16[32,2048]{1,0:T(8,128)(2,1)}, bf16[32,2048]{1,0:T(8,128)(2,1)S(1)}, u32[]{:S(2)}, u32[]{:S(2)}) collective-permute-start(bf16[32,2048]{1,0:T(8,128)(2,1)} %bitcast.26), channel_id=1, source_target_pairs={{0,1},{1,0},{2,3},{3,2},{4,5},{5,4},{6,7},{7,6},{8,9},{9,8},{10,11... | collective-permute-start | bytes 393224 | tf_op jit(solution)/shard_map/ppermute | solution.py:21
  5.7 4.8 %collective-permute-start.1 = (bf16[32,2048]{1,0:T(8,128)(2,1)S(1)}, bf16[32,2048]{1,0:T(8,128)(2,1)S(1)}, u32[]{:S(2)}, u32[]{:S(2)}) collective-permute-start(bf16[32,2048]{1,0:T(8,128)(2,1)S(1)} %shard_map.37.values_ref), channel_id=1, source_target_pairs={{0,2},{2,0},{1,3},{3,1},{4,6},{6,4},{5,7},{7,5},{8,10},{10,8},{9,1... | collective-permute-start | bytes 393224 | tf_op jit(solution)/shard_map/ppermute | solution.py:21
  14.3 8.2 %collective-permute-start.2 = (bf16[32,2048]{1,0:T(8,128)(2,1)S(1)}, bf16[32,2048]{1,0:T(8,128)(2,1)S(1)}, u32[]{:S(2)}, u32[]{:S(2)}) collective-permute-start(bf16[32,2048]{1,0:T(8,128)(2,1)S(1)} %shard_map.38.values_ref), channel_id=1, source_target_pairs={{0,4},{4,0},{1,5},{5,1},{2,6},{6,2},{3,7},{7,3},{8,12},{12,8},{9,1... | collective-permute-start | bytes 393224 | tf_op jit(solution)/shard_map/ppermute | solution.py:21
  22.5 3.4 %copy-start = (bf16[1,1,2048,2048]{3,2,1,0:T(8,128)(2,1)S(1)}, bf16[1,1,2048,2048]{3,2,1,0:T(8,128)(2,1)}, u32[]{:S(2)}) copy-start(bf16[1,1,2048,2048]{3,2,1,0:T(8,128)(2,1)} %param.5) | copy-start | bytes 25165828
  25.8 21.1 %copy-start.1 = (bf16[1,1,32,2048]{3,2,1,0:T(8,128)(2,1)S(1)}, bf16[1,1,32,2048]{3,2,1,0:T(8,128)(2,1)}, u32[]{:S(2)}) copy-start(bf16[1,1,32,2048]{3,2,1,0:T(8,128)(2,1)} %param.3) | copy-start | bytes 393220
  25.8 21.1 %copy-start.2 = (f32[1,1,2048]{2,1,0:T(1,128)S(1)}, f32[1,1,2048]{2,1,0:T(1,128)}, u32[]{:S(2)}) copy-start(f32[1,1,2048]{2,1,0:T(1,128)} %param.4) | copy-start | bytes 24580
  25.8 22.5 %slice-start = ((s8[8388608]{0:T(1024)(128)(4,1)}), s8[4194304]{0:T(1024)(128)(4,1)S(1)}, s32[]{:S(2)}) async-start(s8[8388608]{0:T(1024)(128)(4,1)} %bitcast.12), calls=%async_computation | async-start | bytes 8388608
  27.4 21.0 %slice-start.1 = ((s8[8388608]{0:T(1024)(128)(4,1)}), s8[4194304]{0:T(1024)(128)(4,1)S(1)}, s32[]{:S(2)}) async-start(s8[8388608]{0:T(1024)(128)(4,1)} %bitcast.12), calls=%async_computation.1 | async-start | bytes 8388608
  29.9 4.7 %collective-permute-start.3 = (bf16[32,2048]{1,0:T(8,128)(2,1)S(1)}, bf16[32,2048]{1,0:T(8,128)(2,1)S(1)}, u32[]{:S(2)}, u32[]{:S(2)}) collective-permute-start(bf16[32,2048]{1,0:T(8,128)(2,1)S(1)} %shard_map.40), channel_id=1, source_target_pairs={{0,4},{4,0},{1,5},{5,1},{2,6},{6,2},{3,7},{7,3},{8,12},{12,8},{9,1... | collective-permute-start | bytes 393224 | tf_op jit(solution)/shard_map/ppermute | solution.py:21
  34.7 5.8 %collective-permute-start.4 = (bf16[32,2048]{1,0:T(8,128)(2,1)S(1)}, bf16[32,2048]{1,0:T(8,128)(2,1)S(1)}, u32[]{:S(2)}, u32[]{:S(2)}) collective-permute-start(bf16[32,2048]{1,0:T(8,128)(2,1)S(1)} %fusion.2), channel_id=1, source_target_pairs={{0,2},{2,0},{1,3},{3,1},{4,6},{6,4},{5,7},{7,5},{8,10},{10,8},{9,1... | collective-permute-start | bytes 393224 | tf_op jit(solution)/shard_map/ppermute | solution.py:21
  40.6 5.5 %collective-permute-start.5 = (bf16[32,2048]{1,0:T(8,128)(2,1)S(1)}, bf16[32,2048]{1,0:T(8,128)(2,1)S(1)}, u32[]{:S(2)}, u32[]{:S(2)}) collective-permute-start(bf16[32,2048]{1,0:T(8,128)(2,1)S(1)} %fusion.6), channel_id=1, source_target_pairs={{0,1},{1,0},{2,3},{3,2},{4,5},{5,4},{6,7},{7,6},{8,9},{9,8},{10,11... | collective-permute-start | bytes 393224 | tf_op jit(solution)/shard_map/ppermute | solution.py:21
  46.2 0.7 collective-permute-start.6
  47.0 1.4 collective-permute-start.7
  49.9 4.7 %collective-permute-start.8 = (bf16[32,2048]{1,0:T(8,128)(2,1)S(1)}, bf16[32,2048]{1,0:T(8,128)(2,1)S(1)}, u32[]{:S(2)}, u32[]{:S(2)}) collective-permute-start(bf16[32,2048]{1,0:T(8,128)(2,1)S(1)} %shard_map.41.values_ref), channel_id=1, source_target_pairs={{0,2},{2,0},{1,3},{3,1},{4,6},{6,4},{5,7},{7,5},{8,10},{10,8},{9,1... | collective-permute-start | bytes 393224 | tf_op jit(solution)/shard_map/ppermute | solution.py:21
  56.2 9.1 %collective-permute-start.9 = (bf16[32,2048]{1,0:T(8,128)(2,1)S(1)}, bf16[32,2048]{1,0:T(8,128)(2,1)S(1)}, u32[]{:S(2)}, u32[]{:S(2)}) collective-permute-start(bf16[32,2048]{1,0:T(8,128)(2,1)S(1)} %shard_map.42.values_ref), channel_id=1, source_target_pairs={{0,4},{4,0},{1,5},{5,1},{2,6},{6,2},{3,7},{7,3},{8,12},{12,8},{9,1... | collective-permute-start | bytes 393224 | tf_op jit(solution)/shard_map/ppermute | solution.py:21
  69.4 7.7 %collective-permute-start.10 = (bf16[32,2048]{1,0:T(8,128)(2,1)S(1)}, bf16[32,2048]{1,0:T(8,128)(2,1)S(1)}, u32[]{:S(2)}, u32[]{:S(2)}) collective-permute-start(bf16[32,2048]{1,0:T(8,128)(2,1)S(1)} %shard_map.44), channel_id=1, source_target_pairs={{0,4},{4,0},{1,5},{5,1},{2,6},{6,2},{3,7},{7,3},{8,12},{12,8},{9,1... | collective-permute-start | bytes 393224 | tf_op jit(solution)/shard_map/ppermute | solution.py:21
  77.1 4.6 %collective-permute-start.11 = (bf16[32,2048]{1,0:T(8,128)(2,1)S(1)}, bf16[32,2048]{1,0:T(8,128)(2,1)S(1)}, u32[]{:S(2)}, u32[]{:S(2)}) collective-permute-start(bf16[32,2048]{1,0:T(8,128)(2,1)S(1)} %fusion.14), channel_id=1, source_target_pairs={{0,2},{2,0},{1,3},{3,1},{4,6},{6,4},{5,7},{7,5},{8,10},{10,8},{9,1... | collective-permute-start | bytes 393224 | tf_op jit(solution)/shard_map/ppermute | solution.py:21
  81.8 2.4 %collective-permute-start.12 = (bf16[32,2048]{1,0:T(8,128)(2,1)S(1)}, bf16[32,2048]{1,0:T(8,128)(2,1)S(1)}, u32[]{:S(2)}, u32[]{:S(2)}) collective-permute-start(bf16[32,2048]{1,0:T(8,128)(2,1)S(1)} %fusion.18), channel_id=1, source_target_pairs={{0,1},{1,0},{2,3},{3,2},{4,5},{5,4},{6,7},{7,6},{8,9},{9,8},{10,11... | collective-permute-start | bytes 393224 | tf_op jit(solution)/shard_map/ppermute | solution.py:21
  84.3 0.9 collective-permute-start.13
  85.2 1.4 collective-permute-start.14
  88.2 4.7 %collective-permute-start.15 = (bf16[32,2048]{1,0:T(8,128)(2,1)S(1)}, bf16[32,2048]{1,0:T(8,128)(2,1)S(1)}, u32[]{:S(2)}, u32[]{:S(2)}) collective-permute-start(bf16[32,2048]{1,0:T(8,128)(2,1)S(1)} %shard_map.45.values_ref), channel_id=1, source_target_pairs={{0,2},{2,0},{1,3},{3,1},{4,6},{6,4},{5,7},{7,5},{8,10},{10,8},{9,1... | collective-permute-start | bytes 393224 | tf_op jit(solution)/shard_map/ppermute | solution.py:21
  94.4 9.1 %collective-permute-start.16 = (bf16[32,2048]{1,0:T(8,128)(2,1)S(1)}, bf16[32,2048]{1,0:T(8,128)(2,1)S(1)}, u32[]{:S(2)}, u32[]{:S(2)}) collective-permute-start(bf16[32,2048]{1,0:T(8,128)(2,1)S(1)} %shard_map.46.values_ref), channel_id=1, source_target_pairs={{0,4},{4,0},{1,5},{5,1},{2,6},{6,2},{3,7},{7,3},{8,12},{12,8},{9,1... | collective-permute-start | bytes 393224 | tf_op jit(solution)/shard_map/ppermute | solution.py:21
  107.6 8.7 %collective-permute-start.17 = (bf16[32,2048]{1,0:T(8,128)(2,1)S(1)}, bf16[32,2048]{1,0:T(8,128)(2,1)S(1)}, u32[]{:S(2)}, u32[]{:S(2)}) collective-permute-start(bf16[32,2048]{1,0:T(8,128)(2,1)S(1)} %shard_map.48), channel_id=1, source_target_pairs={{0,4},{4,0},{1,5},{5,1},{2,6},{6,2},{3,7},{7,3},{8,12},{12,8},{9,1... | collective-permute-start | bytes 393224 | tf_op jit(solution)/shard_map/ppermute | solution.py:21
  116.4 4.6 %collective-permute-start.18 = (bf16[32,2048]{1,0:T(8,128)(2,1)S(1)}, bf16[32,2048]{1,0:T(8,128)(2,1)S(1)}, u32[]{:S(2)}, u32[]{:S(2)}) collective-permute-start(bf16[32,2048]{1,0:T(8,128)(2,1)S(1)} %fusion.26), channel_id=1, source_target_pairs={{0,2},{2,0},{1,3},{3,1},{4,6},{6,4},{5,7},{7,5},{8,10},{10,8},{9,1... | collective-permute-start | bytes 393224 | tf_op jit(solution)/shard_map/ppermute | solution.py:21
  121.1 2.4 %collective-permute-start.19 = (bf16[32,2048]{1,0:T(8,128)(2,1)S(1)}, bf16[32,2048]{1,0:T(8,128)(2,1)S(1)}, u32[]{:S(2)}, u32[]{:S(2)}) collective-permute-start(bf16[32,2048]{1,0:T(8,128)(2,1)S(1)} %fusion.30), channel_id=1, source_target_pairs={{0,1},{1,0},{2,3},{3,2},{4,5},{5,4},{6,7},{7,6},{8,9},{9,8},{10,11... | collective-permute-start | bytes 393224 | tf_op jit(solution)/shard_map/ppermute | solution.py:21
  123.6 17.4 %collective-permute-start.20 = (bf16[32,2048]{1,0:T(8,128)(2,1)S(1)}, bf16[32,2048]{1,0:T(8,128)(2,1)S(1)}, u32[]{:S(2)}, u32[]{:S(2)}) collective-permute-start(bf16[32,2048]{1,0:T(8,128)(2,1)S(1)} %fusion.34), channel_id=1, source_target_pairs={{16,24},{17,25},{18,26},{19,27},{20,28},{21,29},{22,30},{23,31}} | collective-permute-start | bytes 393224 | tf_op jit(solution)/shard_map/ppermute | solution.py:25
  141.1 2.0 %collective-permute-start.21 = (bf16[32,2048]{1,0:T(8,128)(2,1)S(1)}, bf16[32,2048]{1,0:T(8,128)(2,1)S(1)}, u32[]{:S(2)}, u32[]{:S(2)}) collective-permute-start(bf16[32,2048]{1,0:T(8,128)(2,1)S(1)} %fusion.50.values_ref), channel_id=1, source_target_pairs={{0,1},{1,0},{2,3},{3,2},{4,5},{5,4},{6,7},{7,6},{8,9},{9,8},{10,11... | collective-permute-start | bytes 393224 | tf_op jit(solution)/shard_map/ppermute | solution.py:21
  144.6 4.7 %collective-permute-start.22 = (bf16[32,2048]{1,0:T(8,128)(2,1)S(1)}, bf16[32,2048]{1,0:T(8,128)(2,1)S(1)}, u32[]{:S(2)}, u32[]{:S(2)}) collective-permute-start(bf16[32,2048]{1,0:T(8,128)(2,1)S(1)} %shard_map.49.values_ref), channel_id=1, source_target_pairs={{0,2},{2,0},{1,3},{3,1},{4,6},{6,4},{5,7},{7,5},{8,10},{10,8},{9,1... | collective-permute-start | bytes 393224 | tf_op jit(solution)/shard_map/ppermute | solution.py:21
  150.8 8.7 %collective-permute-start.23 = (bf16[32,2048]{1,0:T(8,128)(2,1)S(1)}, bf16[32,2048]{1,0:T(8,128)(2,1)S(1)}, u32[]{:S(2)}, u32[]{:S(2)}) collective-permute-start(bf16[32,2048]{1,0:T(8,128)(2,1)S(1)} %shard_map.50.values_ref), channel_id=1, source_target_pairs={{0,4},{4,0},{1,5},{5,1},{2,6},{6,2},{3,7},{7,3},{8,12},{12,8},{9,1... | collective-permute-start | bytes 393224 | tf_op jit(solution)/shard_map/ppermute | solution.py:21
  163.6 8.1 %collective-permute-start.24 = (bf16[32,2048]{1,0:T(8,128)(2,1)S(1)}, bf16[32,2048]{1,0:T(8,128)(2,1)S(1)}, u32[]{:S(2)}, u32[]{:S(2)}) collective-permute-start(bf16[32,2048]{1,0:T(8,128)(2,1)S(1)} %shard_map.52), channel_id=1, source_target_pairs={{0,4},{4,0},{1,5},{5,1},{2,6},{6,2},{3,7},{7,3},{8,12},{12,8},{9,1... | collective-permute-start | bytes 393224 | tf_op jit(solution)/shard_map/ppermute | solution.py:21
  171.8 4.6 %collective-permute-start.25 = (bf16[32,2048]{1,0:T(8,128)(2,1)S(1)}, bf16[32,2048]{1,0:T(8,128)(2,1)S(1)}, u32[]{:S(2)}, u32[]{:S(2)}) collective-permute-start(bf16[32,2048]{1,0:T(8,128)(2,1)S(1)} %fusion.38), channel_id=1, source_target_pairs={{0,2},{2,0},{1,3},{3,1},{4,6},{6,4},{5,7},{7,5},{8,10},{10,8},{9,1... | collective-permute-start | bytes 393224 | tf_op jit(solution)/shard_map/ppermute | solution.py:21
  176.5 2.4 %collective-permute-start.26 = (bf16[32,2048]{1,0:T(8,128)(2,1)S(1)}, bf16[32,2048]{1,0:T(8,128)(2,1)S(1)}, u32[]{:S(2)}, u32[]{:S(2)}) collective-permute-start(bf16[32,2048]{1,0:T(8,128)(2,1)S(1)} %fusion.42), channel_id=1, source_target_pairs={{0,1},{1,0},{2,3},{3,2},{4,5},{5,4},{6,7},{7,6},{8,9},{9,8},{10,11... | collective-permute-start | bytes 393224 | tf_op jit(solution)/shard_map/ppermute | solution.py:21

commit v12 on v11

--- a/solution.py
+++ b/solution.py
@@ -40,12 +40,13 @@
     values = values_ref[...]
     width = op_ref.shape[0]
     for start in range(0, width, TILE):
-        out_ref[:, start:start + TILE] = lax.dot_general(
+        block = lax.dot_general(
+            op_ref[start:start + TILE, :],
             values,
-            op_ref[start:start + TILE, :],
             (((1,), (1,)), ((), ())),
             preferred_element_type=jnp.float32,
-        ).astype(out_ref.dtype)
+        )
+        out_ref[:, start:start + TILE] = block.T.astype(out_ref.dtype)
 
 
 def vmem_spec():

time: 180 us -> 179 us (level)
  no operation moved by 1% of the time
where the time goes in v12:
time: 179 us
  waiting for transfers between devices  119 us (66%)
  Pallas kernels  32.5 us (18%)
  starting transfers between devices  22.6 us (13%)
  local copies, waits for them, and re-layouts  3.41 us (2%)
    ppermute x24, waiting for transfers between devices, partner_2(): return lax.ppermute(block, axis, route)  103 us
    ppermute x24, starting transfers between devices, partner_2(): return lax.ppermute(block, axis, route)  19.8 us
    ppermute x3, waiting for transfers between devices, handed_down(): return lax.ppermute(array, axis, [(layer, layer + 1)])  16.1 us
    pallas_call x10, Pallas kernels, mixed_dot(): pl.pallas_call(mixed_dot_kernel, out_shape=jax.ShapeDtypeStruct(values.sh...  15.3 us
    pallas_call x4, Pallas kernels, transposed_dot(): pl.pallas_call(transposed_dot_kernel, out_shape=jax.ShapeDtypeStruct(valu...  9.53 us
    pallas_call x2, Pallas kernels, fetched_dot(): pl.pallas_call(functools.partial(fetched_dot_kernel, values_in_hbm), out_...  7.62 us
  transfers between devices with their start and end apart: 27, of which 25 were waited for; matrix products, arithmetic and copies ran while one was open for 0% of the time, Pallas kernels for 0%

profile of v12, /device:TPU:7, one launch (start us, length us, event | category | flops | bytes accessed | tf_op | source)
XLA Modules:
  0.0 179.2 jit_solution(16993629762686129778)
XLA Ops:
  0.0 0.7 collective-permute-start
  0.7 1.2 collective-permute-done.partner_ref
  1.9 3.8 %shard_map.37.values_ref = bf16[32,2048]{1,0:T(8,128)(2,1)S(1)} custom-call(f32[1,2048]{1,0:T(1,128)S(1)} %broadcast_in_dim.12.sign_ref, bf16[32,2048]{1,0:T(8,128)(2,1)} %bitcast.27, bf16[32,2048]{1,0:T(8,128)(2,1)S(1)} %collective-permute-done.partner_ref, bf16[2048,2048]{1,0:T(8,128)(2,1)} %bitcast.8), custom_call_target="tpu_custom_call" | custom-call | flops 268435456 | bytes 8781824 | tf_op jit(solution)/shard_map/pallas_call | solution.py:125
  5.7 1.4 collective-permute-start.1
  7.1 3.4 %collective-permute-done.1.partner_ref = bf16[32,2048]{1,0:T(8,128)(2,1)S(1)} collective-permute-done((bf16[32,2048]{1,0:T(8,128)(2,1)S(1)}, bf16[32,2048]{1,0:T(8,128)(2,1)S(1)}, u32[]{:S(2)}, u32[]{:S(2)}) %collective-permute-start.1) | collective-permute-done | bytes 131104 | tf_op jit(solution)/shard_map/ppermute | solution.py:21
  10.5 3.8 %shard_map.38.values_ref = bf16[32,2048]{1,0:T(8,128)(2,1)S(1)} custom-call(f32[1,2048]{1,0:T(1,128)S(1)} %broadcast_in_dim.11.sign_ref, bf16[32,2048]{1,0:T(8,128)(2,1)S(1)} %shard_map.37.values_ref, bf16[32,2048]{1,0:T(8,128)(2,1)S(1)} %collective-permute-done.1.partner_ref, bf16[2048,2048]{1,0:T(8,128)(2,1)} %bitcast.9), custom_call_target="tpu_custom_call" | custom-call | flops 268435456 | bytes 8781824 | tf_op jit(solution)/shard_map/pallas_call | solution.py:125
  14.3 2.4 %collective-permute-start.2 = (bf16[32,2048]{1,0:T(8,128)(2,1)S(1)}, bf16[32,2048]{1,0:T(8,128)(2,1)S(1)}, u32[]{:S(2)}, u32[]{:S(2)}) collective-permute-start(bf16[32,2048]{1,0:T(8,128)(2,1)S(1)} %shard_map.38.values_ref), channel_id=1, source_target_pairs={{0,4},{4,0},{1,5},{5,1},{2,6},{6,2},{3,7},{7,3},{8,12},{12,8},{9,1... | collective-permute-start | bytes 393224 | tf_op jit(solution)/shard_map/ppermute | solution.py:21
  16.7 5.8 %collective-permute-done.2.partner_ref = bf16[32,2048]{1,0:T(8,128)(2,1)S(1)} collective-permute-done((bf16[32,2048]{1,0:T(8,128)(2,1)S(1)}, bf16[32,2048]{1,0:T(8,128)(2,1)S(1)}, u32[]{:S(2)}, u32[]{:S(2)}) %collective-permute-start.2) | collective-permute-done | bytes 131104 | tf_op jit(solution)/shard_map/ppermute | solution.py:21
  22.5 3.4 %copy-done = bf16[1,1,2048,2048]{3,2,1,0:T(8,128)(2,1)S(1)} copy-done((bf16[1,1,2048,2048]{3,2,1,0:T(8,128)(2,1)S(1)}, bf16[1,1,2048,2048]{3,2,1,0:T(8,128)(2,1)}, u32[]{:S(2)}) %copy-start) | copy-done | bytes 8388632
  25.9 1.5 shard_map.39.values_ref
  27.4 2.4 %shard_map.40 = bf16[32,2048]{1,0:T(8,128)(2,1)S(1)} custom-call(bf16[32,2048]{1,0:T(8,128)(2,1)S(1)} %shard_map.39.values_ref, bf16[2048,2048]{1,0:T(8,128)(2,1)S(1)} %bitcast.11), custom_call_target="tpu_custom_call" | custom-call | flops 268435456 | bytes 8781824 | tf_op jit(solution)/shard_map/pallas_call | solution.py:78
  29.8 4.7 %collective-permute-done.3 = bf16[32,2048]{1,0:T(8,128)(2,1)S(1)} collective-permute-done((bf16[32,2048]{1,0:T(8,128)(2,1)S(1)}, bf16[32,2048]{1,0:T(8,128)(2,1)S(1)}, u32[]{:S(2)}, u32[]{:S(2)}) %collective-permute-start.3) | collective-permute-done | bytes 131104 | tf_op jit(solution)/shard_map/ppermute | solution.py:21
  34.6 2.9 %collective-permute-start.4 = (bf16[32,2048]{1,0:T(8,128)(2,1)S(1)}, bf16[32,2048]{1,0:T(8,128)(2,1)S(1)}, u32[]{:S(2)}, u32[]{:S(2)}) collective-permute-start(bf16[32,2048]{1,0:T(8,128)(2,1)S(1)} %fusion.2), channel_id=1, source_target_pairs={{0,2},{2,0},{1,3},{3,1},{4,6},{6,4},{5,7},{7,5},{8,10},{10,8},{9,1... | collective-permute-start | bytes 393224 | tf_op jit(solution)/shard_map/ppermute | solution.py:21
  37.5 2.9 %collective-permute-done.4 = bf16[32,2048]{1,0:T(8,128)(2,1)S(1)} collective-permute-done((bf16[32,2048]{1,0:T(8,128)(2,1)S(1)}, bf16[32,2048]{1,0:T(8,128)(2,1)S(1)}, u32[]{:S(2)}, u32[]{:S(2)}) %collective-permute-start.4) | collective-permute-done | bytes 131104 | tf_op jit(solution)/shard_map/ppermute | solution.py:21
  40.4 0.1 fusion.6
  40.5 4.5 %collective-permute-start.5 = (bf16[32,2048]{1,0:T(8,128)(2,1)S(1)}, bf16[32,2048]{1,0:T(8,128)(2,1)S(1)}, u32[]{:S(2)}, u32[]{:S(2)}) collective-permute-start(bf16[32,2048]{1,0:T(8,128)(2,1)S(1)} %fusion.6), channel_id=1, source_target_pairs={{0,1},{1,0},{2,3},{3,2},{4,5},{5,4},{6,7},{7,6},{8,9},{9,8},{10,11... | collective-permute-start | bytes 393224 | tf_op jit(solution)/shard_map/ppermute | solution.py:21
  45.0 1.0 collective-permute-done.5
  46.1 0.7 collective-permute-start.6
  46.8 0.4 collective-permute-start.7
  47.3 1.0 collective-permute-done.7.partner_ref
  48.3 1.5 shard_map.41.values_ref
  49.8 4.7 %collective-permute-done.8.partner_ref = bf16[32,2048]{1,0:T(8,128)(2,1)S(1)} collective-permute-done((bf16[32,2048]{1,0:T(8,128)(2,1)S(1)}, bf16[32,2048]{1,0:T(8,128)(2,1)S(1)}, u32[]{:S(2)}, u32[]{:S(2)}) %collective-permute-start.8) | collective-permute-done | bytes 131104 | tf_op jit(solution)/shard_map/ppermute | solution.py:21
  54.5 1.5 shard_map.42.values_ref
  56.1 9.1 %collective-permute-done.9.partner_ref = bf16[32,2048]{1,0:T(8,128)(2,1)S(1)} collective-permute-done((bf16[32,2048]{1,0:T(8,128)(2,1)S(1)}, bf16[32,2048]{1,0:T(8,128)(2,1)S(1)}, u32[]{:S(2)}, u32[]{:S(2)}) %collective-permute-start.9) | collective-permute-done | bytes 131104 | tf_op jit(solution)/shard_map/ppermute | solution.py:21
  65.2 1.5 shard_map.43.values_ref
  66.7 2.4 %shard_map.44 = bf16[32,2048]{1,0:T(8,128)(2,1)S(1)} custom-call(bf16[32,2048]{1,0:T(8,128)(2,1)S(1)} %shard_map.43.values_ref, bf16[2048,2048]{1,0:T(8,128)(2,1)S(1)} %bitcast.17), custom_call_target="tpu_custom_call" | custom-call | flops 268435456 | bytes 8781824 | tf_op jit(solution)/shard_map/pallas_call | solution.py:78
  69.2 7.7 %collective-permute-done.10 = bf16[32,2048]{1,0:T(8,128)(2,1)S(1)} collective-permute-done((bf16[32,2048]{1,0:T(8,128)(2,1)S(1)}, bf16[32,2048]{1,0:T(8,128)(2,1)S(1)}, u32[]{:S(2)}, u32[]{:S(2)}) %collective-permute-start.10) | collective-permute-done | bytes 131104 | tf_op jit(solution)/shard_map/ppermute | solution.py:21
  76.9 0.1 collective-permute-start.11
  77.0 4.6 %collective-permute-done.11 = bf16[32,2048]{1,0:T(8,128)(2,1)S(1)} collective-permute-done((bf16[32,2048]{1,0:T(8,128)(2,1)S(1)}, bf16[32,2048]{1,0:T(8,128)(2,1)S(1)}, u32[]{:S(2)}, u32[]{:S(2)}) %collective-permute-start.11) | collective-permute-done | bytes 131104 | tf_op jit(solution)/shard_map/ppermute | solution.py:21
  81.6 1.4 collective-permute-start.12
  83.0 1.0 collective-permute-done.12
  84.1 0.8 collective-permute-start.13
  85.0 0.4 collective-permute-start.14
  85.4 1.0 collective-permute-done.14.partner_ref
  86.4 1.5 shard_map.45.values_ref
  87.9 4.7 %collective-permute-done.15.partner_ref = bf16[32,2048]{1,0:T(8,128)(2,1)S(1)} collective-permute-done((bf16[32,2048]{1,0:T(8,128)(2,1)S(1)}, bf16[32,2048]{1,0:T(8,128)(2,1)S(1)}, u32[]{:S(2)}, u32[]{:S(2)}) %collective-permute-start.15) | collective-permute-done | bytes 131104 | tf_op jit(solution)/shard_map/ppermute | solution.py:21
  92.6 1.5 shard_map.46.values_ref
  94.2 1.2 collective-permute-start.16
  95.3 7.9 %collective-permute-done.16.partner_ref = bf16[32,2048]{1,0:T(8,128)(2,1)S(1)} collective-permute-done((bf16[32,2048]{1,0:T(8,128)(2,1)S(1)}, bf16[32,2048]{1,0:T(8,128)(2,1)S(1)}, u32[]{:S(2)}, u32[]{:S(2)}) %collective-permute-start.16) | collective-permute-done | bytes 131104 | tf_op jit(solution)/shard_map/ppermute | solution.py:21
  103.3 1.5 shard_map.47.values_ref
  104.8 2.4 %shard_map.48 = bf16[32,2048]{1,0:T(8,128)(2,1)S(1)} custom-call(bf16[32,2048]{1,0:T(8,128)(2,1)S(1)} %shard_map.47.values_ref, bf16[2048,2048]{1,0:T(8,128)(2,1)S(1)} %bitcast.21), custom_call_target="tpu_custom_call" | custom-call | flops 268435456 | bytes 8781824 | tf_op jit(solution)/shard_map/pallas_call | solution.py:78
  107.3 8.7 %collective-permute-done.17 = bf16[32,2048]{1,0:T(8,128)(2,1)S(1)} collective-permute-done((bf16[32,2048]{1,0:T(8,128)(2,1)S(1)}, bf16[32,2048]{1,0:T(8,128)(2,1)S(1)}, u32[]{:S(2)}, u32[]{:S(2)}) %collective-permute-start.17) | collective-permute-done | bytes 131104 | tf_op jit(solution)/shard_map/ppermute | solution.py:21
  116.0 0.1 collective-permute-start.18
  116.1 4.6 %collective-permute-done.18 = bf16[32,2048]{1,0:T(8,128)(2,1)S(1)} collective-permute-done((bf16[32,2048]{1,0:T(8,128)(2,1)S(1)}, bf16[32,2048]{1,0:T(8,128)(2,1)S(1)}, u32[]{:S(2)}, u32[]{:S(2)}) %collective-permute-start.18) | collective-permute-done | bytes 131104 | tf_op jit(solution)/shard_map/ppermute | solution.py:21
  120.7 1.4 collective-permute-start.19
  122.1 1.0 collective-permute-done.19
  123.2 1.3 collective-permute-start.20
  124.5 16.1 %collective-permute-done.20 = bf16[32,2048]{1,0:T(8,128)(2,1)S(1)} collective-permute-done((bf16[32,2048]{1,0:T(8,128)(2,1)S(1)}, bf16[32,2048]{1,0:T(8,128)(2,1)S(1)}, u32[]{:S(2)}, u32[]{:S(2)}) %collective-permute-start.20) | collective-permute-done | bytes 131104 | tf_op jit(solution)/shard_map/ppermute | solution.py:25
  140.7 1.0 collective-permute-start.21
  141.7 1.0 collective-permute-done.21.partner_ref
  142.7 1.5 shard_map.49.values_ref
  144.2 4.7 %collective-permute-done.22.partner_ref = bf16[32,2048]{1,0:T(8,128)(2,1)S(1)} collective-permute-done((bf16[32,2048]{1,0:T(8,128)(2,1)S(1)}, bf16[32,2048]{1,0:T(8,128)(2,1)S(1)}, u32[]{:S(2)}, u32[]{:S(2)}) %collective-permute-start.22) | collective-permute-done | bytes 131104 | tf_op jit(solution)/shard_map/ppermute | solution.py:21
  148.9 1.5 shard_map.50.values_ref
  150.4 0.2 collective-permute-start.23
  150.6 8.5 %collective-permute-done.23.partner_ref = bf16[32,2048]{1,0:T(8,128)(2,1)S(1)} collective-permute-done((bf16[32,2048]{1,0:T(8,128)(2,1)S(1)}, bf16[32,2048]{1,0:T(8,128)(2,1)S(1)}, u32[]{:S(2)}, u32[]{:S(2)}) %collective-permute-start.23) | collective-permute-done | bytes 131104 | tf_op jit(solution)/shard_map/ppermute | solution.py:21
  159.1 1.5 shard_map.51.values_ref
  160.7 2.4 %shard_map.52 = bf16[32,2048]{1,0:T(8,128)(2,1)S(1)} custom-call(bf16[32,2048]{1,0:T(8,128)(2,1)S(1)} %shard_map.51.values_ref, bf16[2048,2048]{1,0:T(8,128)(2,1)S(1)} %bitcast.25), custom_call_target="tpu_custom_call" | custom-call | flops 268435456 | bytes 8781824 | tf_op jit(solution)/shard_map/pallas_call | solution.py:78
  163.1 8.1 %collective-permute-done.24 = bf16[32,2048]{1,0:T(8,128)(2,1)S(1)} collective-permute-done((bf16[32,2048]{1,0:T(8,128)(2,1)S(1)}, bf16[32,2048]{1,0:T(8,128)(2,1)S(1)}, u32[]{:S(2)}, u32[]{:S(2)}) %collective-permute-start.24) | collective-permute-done | bytes 131104 | tf_op jit(solution)/shard_map/ppermute | solution.py:21
  171.3 0.1 collective-permute-start.25
  171.4 4.5 %collective-permute-done.25 = bf16[32,2048]{1,0:T(8,128)(2,1)S(1)} collective-permute-done((bf16[32,2048]{1,0:T(8,128)(2,1)S(1)}, bf16[32,2048]{1,0:T(8,128)(2,1)S(1)}, u32[]{:S(2)}, u32[]{:S(2)}) %collective-permute-start.25) | collective-permute-done | bytes 131104 | tf_op jit(solution)/shard_map/ppermute | solution.py:21
  175.9 0.1 fusion.42
  176.0 1.4 collective-permute-start.26
  177.4 1.0 collective-permute-done.26
  178.4 0.8 fusion.52
  (35 shorter events, 1.1 us)
Async XLA Ops:
  0.0 1.9 %collective-permute-start = (bf16[32,2048]{1,0:T(8,128)(2,1)}, bf16[32,2048]{1,0:T(8,128)(2,1)S(1)}, u32[]{:S(2)}, u32[]{:S(2)}) collective-permute-start(bf16[32,2048]{1,0:T(8,128)(2,1)} %bitcast.26), channel_id=1, source_target_pairs={{0,1},{1,0},{2,3},{3,2},{4,5},{5,4},{6,7},{7,6},{8,9},{9,8},{10,11... | collective-permute-start | bytes 393224 | tf_op jit(solution)/shard_map/ppermute | solution.py:21
  5.7 4.8 %collective-permute-start.1 = (bf16[32,2048]{1,0:T(8,128)(2,1)S(1)}, bf16[32,2048]{1,0:T(8,128)(2,1)S(1)}, u32[]{:S(2)}, u32[]{:S(2)}) collective-permute-start(bf16[32,2048]{1,0:T(8,128)(2,1)S(1)} %shard_map.37.values_ref), channel_id=1, source_target_pairs={{0,2},{2,0},{1,3},{3,1},{4,6},{6,4},{5,7},{7,5},{8,10},{10,8},{9,1... | collective-permute-start | bytes 393224 | tf_op jit(solution)/shard_map/ppermute | solution.py:21
  14.3 8.2 %collective-permute-start.2 = (bf16[32,2048]{1,0:T(8,128)(2,1)S(1)}, bf16[32,2048]{1,0:T(8,128)(2,1)S(1)}, u32[]{:S(2)}, u32[]{:S(2)}) collective-permute-start(bf16[32,2048]{1,0:T(8,128)(2,1)S(1)} %shard_map.38.values_ref), channel_id=1, source_target_pairs={{0,4},{4,0},{1,5},{5,1},{2,6},{6,2},{3,7},{7,3},{8,12},{12,8},{9,1... | collective-permute-start | bytes 393224 | tf_op jit(solution)/shard_map/ppermute | solution.py:21
  22.5 3.4 %copy-start = (bf16[1,1,2048,2048]{3,2,1,0:T(8,128)(2,1)S(1)}, bf16[1,1,2048,2048]{3,2,1,0:T(8,128)(2,1)}, u32[]{:S(2)}) copy-start(bf16[1,1,2048,2048]{3,2,1,0:T(8,128)(2,1)} %param.5) | copy-start | bytes 25165828
  25.8 20.9 %copy-start.1 = (bf16[1,1,32,2048]{3,2,1,0:T(8,128)(2,1)S(1)}, bf16[1,1,32,2048]{3,2,1,0:T(8,128)(2,1)}, u32[]{:S(2)}) copy-start(bf16[1,1,32,2048]{3,2,1,0:T(8,128)(2,1)} %param.3) | copy-start | bytes 393220
  25.8 20.9 %copy-start.2 = (f32[1,1,2048]{2,1,0:T(1,128)S(1)}, f32[1,1,2048]{2,1,0:T(1,128)}, u32[]{:S(2)}) copy-start(f32[1,1,2048]{2,1,0:T(1,128)} %param.4) | copy-start | bytes 24580
  25.8 22.4 %slice-start = ((s8[8388608]{0:T(1024)(128)(4,1)}), s8[4194304]{0:T(1024)(128)(4,1)S(1)}, s32[]{:S(2)}) async-start(s8[8388608]{0:T(1024)(128)(4,1)} %bitcast.12), calls=%async_computation | async-start | bytes 8388608
  27.4 20.9 %slice-start.1 = ((s8[8388608]{0:T(1024)(128)(4,1)}), s8[4194304]{0:T(1024)(128)(4,1)S(1)}, s32[]{:S(2)}) async-start(s8[8388608]{0:T(1024)(128)(4,1)} %bitcast.12), calls=%async_computation.1 | async-start | bytes 8388608
  29.8 4.8 %collective-permute-start.3 = (bf16[32,2048]{1,0:T(8,128)(2,1)S(1)}, bf16[32,2048]{1,0:T(8,128)(2,1)S(1)}, u32[]{:S(2)}, u32[]{:S(2)}) collective-permute-start(bf16[32,2048]{1,0:T(8,128)(2,1)S(1)} %shard_map.40), channel_id=1, source_target_pairs={{0,4},{4,0},{1,5},{5,1},{2,6},{6,2},{3,7},{7,3},{8,12},{12,8},{9,1... | collective-permute-start | bytes 393224 | tf_op jit(solution)/shard_map/ppermute | solution.py:21
  34.6 5.8 %collective-permute-start.4 = (bf16[32,2048]{1,0:T(8,128)(2,1)S(1)}, bf16[32,2048]{1,0:T(8,128)(2,1)S(1)}, u32[]{:S(2)}, u32[]{:S(2)}) collective-permute-start(bf16[32,2048]{1,0:T(8,128)(2,1)S(1)} %fusion.2), channel_id=1, source_target_pairs={{0,2},{2,0},{1,3},{3,1},{4,6},{6,4},{5,7},{7,5},{8,10},{10,8},{9,1... | collective-permute-start | bytes 393224 | tf_op jit(solution)/shard_map/ppermute | solution.py:21
  40.5 5.5 %collective-permute-start.5 = (bf16[32,2048]{1,0:T(8,128)(2,1)S(1)}, bf16[32,2048]{1,0:T(8,128)(2,1)S(1)}, u32[]{:S(2)}, u32[]{:S(2)}) collective-permute-start(bf16[32,2048]{1,0:T(8,128)(2,1)S(1)} %fusion.6), channel_id=1, source_target_pairs={{0,1},{1,0},{2,3},{3,2},{4,5},{5,4},{6,7},{7,6},{8,9},{9,8},{10,11... | collective-permute-start | bytes 393224 | tf_op jit(solution)/shard_map/ppermute | solution.py:21
  46.1 0.7 collective-permute-start.6
  46.8 1.4 collective-permute-start.7
  49.8 4.7 %collective-permute-start.8 = (bf16[32,2048]{1,0:T(8,128)(2,1)S(1)}, bf16[32,2048]{1,0:T(8,128)(2,1)S(1)}, u32[]{:S(2)}, u32[]{:S(2)}) collective-permute-start(bf16[32,2048]{1,0:T(8,128)(2,1)S(1)} %shard_map.41.values_ref), channel_id=1, source_target_pairs={{0,2},{2,0},{1,3},{3,1},{4,6},{6,4},{5,7},{7,5},{8,10},{10,8},{9,1... | collective-permute-start | bytes 393224 | tf_op jit(solution)/shard_map/ppermute | solution.py:21
  56.0 9.1 %collective-permute-start.9 = (bf16[32,2048]{1,0:T(8,128)(2,1)S(1)}, bf16[32,2048]{1,0:T(8,128)(2,1)S(1)}, u32[]{:S(2)}, u32[]{:S(2)}) collective-permute-start(bf16[32,2048]{1,0:T(8,128)(2,1)S(1)} %shard_map.42.values_ref), channel_id=1, source_target_pairs={{0,4},{4,0},{1,5},{5,1},{2,6},{6,2},{3,7},{7,3},{8,12},{12,8},{9,1... | collective-permute-start | bytes 393224 | tf_op jit(solution)/shard_map/ppermute | solution.py:21
  69.1 7.7 %collective-permute-start.10 = (bf16[32,2048]{1,0:T(8,128)(2,1)S(1)}, bf16[32,2048]{1,0:T(8,128)(2,1)S(1)}, u32[]{:S(2)}, u32[]{:S(2)}) collective-permute-start(bf16[32,2048]{1,0:T(8,128)(2,1)S(1)} %shard_map.44), channel_id=1, source_target_pairs={{0,4},{4,0},{1,5},{5,1},{2,6},{6,2},{3,7},{7,3},{8,12},{12,8},{9,1... | collective-permute-start | bytes 393224 | tf_op jit(solution)/shard_map/ppermute | solution.py:21
  76.9 4.6 %collective-permute-start.11 = (bf16[32,2048]{1,0:T(8,128)(2,1)S(1)}, bf16[32,2048]{1,0:T(8,128)(2,1)S(1)}, u32[]{:S(2)}, u32[]{:S(2)}) collective-permute-start(bf16[32,2048]{1,0:T(8,128)(2,1)S(1)} %fusion.14), channel_id=1, source_target_pairs={{0,2},{2,0},{1,3},{3,1},{4,6},{6,4},{5,7},{7,5},{8,10},{10,8},{9,1... | collective-permute-start | bytes 393224 | tf_op jit(solution)/shard_map/ppermute | solution.py:21
  81.6 2.4 %collective-permute-start.12 = (bf16[32,2048]{1,0:T(8,128)(2,1)S(1)}, bf16[32,2048]{1,0:T(8,128)(2,1)S(1)}, u32[]{:S(2)}, u32[]{:S(2)}) collective-permute-start(bf16[32,2048]{1,0:T(8,128)(2,1)S(1)} %fusion.18), channel_id=1, source_target_pairs={{0,1},{1,0},{2,3},{3,2},{4,5},{5,4},{6,7},{7,6},{8,9},{9,8},{10,11... | collective-permute-start | bytes 393224 | tf_op jit(solution)/shard_map/ppermute | solution.py:21
  84.1 0.9 collective-permute-start.13
  85.0 1.4 collective-permute-start.14
  87.9 4.7 %collective-permute-start.15 = (bf16[32,2048]{1,0:T(8,128)(2,1)S(1)}, bf16[32,2048]{1,0:T(8,128)(2,1)S(1)}, u32[]{:S(2)}, u32[]{:S(2)}) collective-permute-start(bf16[32,2048]{1,0:T(8,128)(2,1)S(1)} %shard_map.45.values_ref), channel_id=1, source_target_pairs={{0,2},{2,0},{1,3},{3,1},{4,6},{6,4},{5,7},{7,5},{8,10},{10,8},{9,1... | collective-permute-start | bytes 393224 | tf_op jit(solution)/shard_map/ppermute | solution.py:21
  94.2 9.1 %collective-permute-start.16 = (bf16[32,2048]{1,0:T(8,128)(2,1)S(1)}, bf16[32,2048]{1,0:T(8,128)(2,1)S(1)}, u32[]{:S(2)}, u32[]{:S(2)}) collective-permute-start(bf16[32,2048]{1,0:T(8,128)(2,1)S(1)} %shard_map.46.values_ref), channel_id=1, source_target_pairs={{0,4},{4,0},{1,5},{5,1},{2,6},{6,2},{3,7},{7,3},{8,12},{12,8},{9,1... | collective-permute-start | bytes 393224 | tf_op jit(solution)/shard_map/ppermute | solution.py:21
  107.2 8.7 %collective-permute-start.17 = (bf16[32,2048]{1,0:T(8,128)(2,1)S(1)}, bf16[32,2048]{1,0:T(8,128)(2,1)S(1)}, u32[]{:S(2)}, u32[]{:S(2)}) collective-permute-start(bf16[32,2048]{1,0:T(8,128)(2,1)S(1)} %shard_map.48), channel_id=1, source_target_pairs={{0,4},{4,0},{1,5},{5,1},{2,6},{6,2},{3,7},{7,3},{8,12},{12,8},{9,1... | collective-permute-start | bytes 393224 | tf_op jit(solution)/shard_map/ppermute | solution.py:21
  116.0 4.6 %collective-permute-start.18 = (bf16[32,2048]{1,0:T(8,128)(2,1)S(1)}, bf16[32,2048]{1,0:T(8,128)(2,1)S(1)}, u32[]{:S(2)}, u32[]{:S(2)}) collective-permute-start(bf16[32,2048]{1,0:T(8,128)(2,1)S(1)} %fusion.26), channel_id=1, source_target_pairs={{0,2},{2,0},{1,3},{3,1},{4,6},{6,4},{5,7},{7,5},{8,10},{10,8},{9,1... | collective-permute-start | bytes 393224 | tf_op jit(solution)/shard_map/ppermute | solution.py:21
  120.7 2.4 %collective-permute-start.19 = (bf16[32,2048]{1,0:T(8,128)(2,1)S(1)}, bf16[32,2048]{1,0:T(8,128)(2,1)S(1)}, u32[]{:S(2)}, u32[]{:S(2)}) collective-permute-start(bf16[32,2048]{1,0:T(8,128)(2,1)S(1)} %fusion.30), channel_id=1, source_target_pairs={{0,1},{1,0},{2,3},{3,2},{4,5},{5,4},{6,7},{7,6},{8,9},{9,8},{10,11... | collective-permute-start | bytes 393224 | tf_op jit(solution)/shard_map/ppermute | solution.py:21
  123.2 17.4 %collective-permute-start.20 = (bf16[32,2048]{1,0:T(8,128)(2,1)S(1)}, bf16[32,2048]{1,0:T(8,128)(2,1)S(1)}, u32[]{:S(2)}, u32[]{:S(2)}) collective-permute-start(bf16[32,2048]{1,0:T(8,128)(2,1)S(1)} %fusion.34), channel_id=1, source_target_pairs={{16,24},{17,25},{18,26},{19,27},{20,28},{21,29},{22,30},{23,31}} | collective-permute-start | bytes 393224 | tf_op jit(solution)/shard_map/ppermute | solution.py:25
  140.7 2.0 %collective-permute-start.21 = (bf16[32,2048]{1,0:T(8,128)(2,1)S(1)}, bf16[32,2048]{1,0:T(8,128)(2,1)S(1)}, u32[]{:S(2)}, u32[]{:S(2)}) collective-permute-start(bf16[32,2048]{1,0:T(8,128)(2,1)S(1)} %fusion.50.values_ref), channel_id=1, source_target_pairs={{0,1},{1,0},{2,3},{3,2},{4,5},{5,4},{6,7},{7,6},{8,9},{9,8},{10,11... | collective-permute-start | bytes 393224 | tf_op jit(solution)/shard_map/ppermute | solution.py:21
  144.2 4.7 %collective-permute-start.22 = (bf16[32,2048]{1,0:T(8,128)(2,1)S(1)}, bf16[32,2048]{1,0:T(8,128)(2,1)S(1)}, u32[]{:S(2)}, u32[]{:S(2)}) collective-permute-start(bf16[32,2048]{1,0:T(8,128)(2,1)S(1)} %shard_map.49.values_ref), channel_id=1, source_target_pairs={{0,2},{2,0},{1,3},{3,1},{4,6},{6,4},{5,7},{7,5},{8,10},{10,8},{9,1... | collective-permute-start | bytes 393224 | tf_op jit(solution)/shard_map/ppermute | solution.py:21
  150.4 8.7 %collective-permute-start.23 = (bf16[32,2048]{1,0:T(8,128)(2,1)S(1)}, bf16[32,2048]{1,0:T(8,128)(2,1)S(1)}, u32[]{:S(2)}, u32[]{:S(2)}) collective-permute-start(bf16[32,2048]{1,0:T(8,128)(2,1)S(1)} %shard_map.50.values_ref), channel_id=1, source_target_pairs={{0,4},{4,0},{1,5},{5,1},{2,6},{6,2},{3,7},{7,3},{8,12},{12,8},{9,1... | collective-permute-start | bytes 393224 | tf_op jit(solution)/shard_map/ppermute | solution.py:21
  163.0 8.2 %collective-permute-start.24 = (bf16[32,2048]{1,0:T(8,128)(2,1)S(1)}, bf16[32,2048]{1,0:T(8,128)(2,1)S(1)}, u32[]{:S(2)}, u32[]{:S(2)}) collective-permute-start(bf16[32,2048]{1,0:T(8,128)(2,1)S(1)} %shard_map.52), channel_id=1, source_target_pairs={{0,4},{4,0},{1,5},{5,1},{2,6},{6,2},{3,7},{7,3},{8,12},{12,8},{9,1... | collective-permute-start | bytes 393224 | tf_op jit(solution)/shard_map/ppermute | solution.py:21
  171.3 4.6 %collective-permute-start.25 = (bf16[32,2048]{1,0:T(8,128)(2,1)S(1)}, bf16[32,2048]{1,0:T(8,128)(2,1)S(1)}, u32[]{:S(2)}, u32[]{:S(2)}) collective-permute-start(bf16[32,2048]{1,0:T(8,128)(2,1)S(1)} %fusion.38), channel_id=1, source_target_pairs={{0,2},{2,0},{1,3},{3,1},{4,6},{6,4},{5,7},{7,5},{8,10},{10,8},{9,1... | collective-permute-start | bytes 393224 | tf_op jit(solution)/shard_map/ppermute | solution.py:21
  176.0 2.4 %collective-permute-start.26 = (bf16[32,2048]{1,0:T(8,128)(2,1)S(1)}, bf16[32,2048]{1,0:T(8,128)(2,1)S(1)}, u32[]{:S(2)}, u32[]{:S(2)}) collective-permute-start(bf16[32,2048]{1,0:T(8,128)(2,1)S(1)} %fusion.42), channel_id=1, source_target_pairs={{0,1},{1,0},{2,3},{3,2},{4,5},{5,4},{6,7},{7,6},{8,9},{9,8},{10,11... | collective-permute-start | bytes 393224 | tf_op jit(solution)/shard_map/ppermute | solution.py:21
